TPU v7x, 256 devices: a whole 4x4x8 slice. The times are simulated.
256 devices in a mesh: ctx: 32 (over z, x), dp: 8 (over y, core).
Axes of the slice: x: 4, y: 4, z: 8, core: 2. Of those that a mesh axis runs over, the one named last changes fastest.
Arguments:
- layer_input: bfloat16 [8, 4096, 5376], P('dp', 'ctx'), may hold values from -12 to 12
- query_states: bfloat16 [8, 4096, 2048], P('dp', 'ctx'), may hold values from -6 to 6
- key_states: bfloat16 [8, 4096, 1024], P('dp', 'ctx'), may hold values from -6 to 6
- value_state_rows: bfloat16 [8, 4096, 1024], P('dp', 'ctx'), may hold values from -6 to 6
- grad_out: bfloat16 [8, 4096, 2048], P('dp', 'ctx'), may hold values from -180 to 180
- segments: int32 [8, 4096], P('dp', 'ctx'), may hold values from 0 to 7, never falling along the last dimension, each value on 1 to 2048 neighbouring positions
- master: float32 [5376, 1024], P(('ctx', 'dp')), may hold values from -0.078125 to 0.078125
- first_moment_value: float32 [5376, 1024], P(('ctx', 'dp')), may hold values from -0.0024 to 0.0024
- second_moment_value: float32 [5376, 1024], P(('ctx', 'dp')), may hold values from 1e-08 to 1e-06
Outputs:
- query_gradient: bfloat16 [8, 4096, 2048], P('dp', 'ctx')
- key_gradient: bfloat16 [8, 4096, 1024], P('dp', 'ctx')
- value_gradient: bfloat16 [8, 4096, 1024], P('dp', 'ctx')
- new_master: float32 [5376, 1024], P(('ctx', 'dp'))
- new_first: float32 [5376, 1024], P(('ctx', 'dp'))
- new_second: float32 [5376, 1024], P(('ctx', 'dp'))
- new_weight: bfloat16 [5376, 1024], P('ctx')
Inputs may be any that keep to these rules, and one draw needn't show every extreme that they name: `segments`: segment numbers never fall along a sequence; each document holds 1 to 2048 tokens and one holds exactly 2048.
All inputs are finite; a program needn't handle non-finite values.
Results may differ from a plain program's by a relative error of at most 0.01.
The roundings to bfloat16 on the way count: a program that leaves them out, or rounds other values in their place, can miss the bound.
Values may be sent and summed in bfloat16 or wider, within the bound.
No kernel may reach another device: no remote copies, remote signals or barrier semaphores. Data moves between devices by JAX's collectives and lax.ppermute only.
A program may use at most 128 MiB of HBM per device.

v0:
```python
import jax
import jax.numpy as jnp
from jax import lax
from jax.sharding import PartitionSpec as P

QUERY_HEADS = 16
KEY_VALUE_HEADS = 8
HEAD_SIZE = 128
WINDOW = 1024


query_scale = 168.0 ** (-0.5)
masked_score = -1e30
clip_norm = 1.0
beta_first = 0.9
beta_second = 0.95
learn_rate = 0.001
decay_rate = 0.1
adam_eps = 1e-08
correct_first = 0.9999734386011124
correct_second = 0.994079470779666


def from_behind(x, axis, by):
    count = lax.axis_size(axis)
    pairs = [(i, i + by) for i in range(count) if 0 <= i + by < count]
    return lax.ppermute(x, axis, pairs)


def attend(
    query_row_block,
    key_row_block,
    value_row_block,
    gradient_rows,
    seg_query,
    seg_key,
    index_query,
    index_key,
):
    shard_length = query_row_block.shape[0]
    extent_rows = key_row_block.shape[0]
    heads_ratio = QUERY_HEADS // KEY_VALUE_HEADS
    query_four_axes = query_row_block.reshape(shard_length, KEY_VALUE_HEADS, heads_ratio, HEAD_SIZE)
    gradient_four_axes = gradient_rows.reshape(
        shard_length, KEY_VALUE_HEADS, heads_ratio, HEAD_SIZE
    )
    key_three_axes = key_row_block.reshape(extent_rows, KEY_VALUE_HEADS, HEAD_SIZE)
    value_three_axes = value_row_block.reshape(extent_rows, KEY_VALUE_HEADS, HEAD_SIZE)
    scores = (
        jnp.einsum(
            "tgrd,egd->grte", query_four_axes, key_three_axes, preferred_element_type=jnp.float32
        )
        * query_scale
    )
    offset = index_query[:, None] - index_key[None, :]
    allowed = (
        (seg_query[:, None] == seg_key[None, :])
        & (offset >= 0)
        & (offset < WINDOW)
        & (index_key[None, :] >= 0)
    )
    scores = jnp.where(allowed, scores, masked_score)
    row_max = jnp.max(scores, axis=-1, keepdims=True)
    weights = jnp.exp(scores - row_max)
    probabilities = weights / jnp.sum(weights, axis=-1, keepdims=True)
    probs_low = probabilities.astype(jnp.bfloat16)
    attn_out = jnp.einsum(
        "grte,egd->tgrd", probs_low, value_three_axes, preferred_element_type=jnp.float32
    )
    row_delta = jnp.sum(gradient_four_axes.astype(jnp.float32) * attn_out, axis=-1)
    grad_probs = jnp.einsum(
        "tgrd,egd->grte", gradient_four_axes, value_three_axes, preferred_element_type=jnp.float32
    )
    grad_scores = probabilities * (grad_probs - jnp.transpose(row_delta, (1, 2, 0))[..., None])
    scores_low = grad_scores.astype(jnp.bfloat16)
    query_gradient = (
        jnp.einsum("grte,egd->tgrd", scores_low, key_three_axes, preferred_element_type=jnp.float32)
        * query_scale
    )
    query_gradient = query_gradient.astype(jnp.bfloat16).reshape(
        shard_length, QUERY_HEADS * HEAD_SIZE
    )
    key_gradient = (
        jnp.einsum(
            "grte,tgrd->egd", scores_low, query_four_axes, preferred_element_type=jnp.float32
        )
        * query_scale
    )
    value_gradient = jnp.einsum(
        "grte,tgrd->egd", probs_low, gradient_four_axes, preferred_element_type=jnp.float32
    )
    return (
        query_gradient,
        key_gradient.reshape(extent_rows, KEY_VALUE_HEADS * HEAD_SIZE),
        value_gradient.reshape(extent_rows, KEY_VALUE_HEADS * HEAD_SIZE),
    )


def shards(
    layer_input,
    query_states,
    key_states,
    value_state_rows,
    grad_out,
    segments,
    master,
    first_moment_value,
    second_moment_value,
):
    shard_length = query_states.shape[1]
    peer_count = min(WINDOW // shard_length, lax.axis_size("ctx") - 1)
    front_len = peer_count * shard_length
    position = lax.axis_index("ctx") * shard_length
    seg_low = segments[0].astype(jnp.bfloat16)
    own_piece = (key_states[0], value_state_rows[0], seg_low)
    incoming_list = []
    for distance in range(peer_count, 0, -1):
        incoming_list.append(
            from_behind((own_piece[0], own_piece[1], own_piece[2]), "ctx", distance)
        )
    halo_rows = tuple(
        (
            jnp.concatenate([incoming[member] for incoming in incoming_list], axis=0)
            for member in range(3)
        )
    )
    key_row_block = jnp.concatenate([halo_rows[0], key_states[0]], axis=0)
    value_row_block = jnp.concatenate([halo_rows[1], value_state_rows[0]], axis=0)
    seg_key = jnp.concatenate([halo_rows[2], seg_low], axis=0)
    index_query = position + jnp.arange(shard_length, dtype=jnp.int32)
    index_key = position - front_len + jnp.arange(front_len + shard_length, dtype=jnp.int32)
    query_gradient, key_gradient, value_gradient = attend(
        query_states[0],
        key_row_block,
        value_row_block,
        grad_out[0],
        seg_low,
        seg_key,
        index_query,
        index_key,
    )
    key_sum = key_gradient[front_len:]
    value_sum = value_gradient[front_len:]
    for distance in range(1, peer_count + 1):
        lower = (peer_count - distance) * shard_length
        key_part = key_gradient[lower : lower + shard_length].astype(jnp.bfloat16)
        value_part = value_gradient[lower : lower + shard_length].astype(jnp.bfloat16)
        returned = from_behind((key_part, value_part), "ctx", -distance)
        key_sum = key_sum + returned[0].astype(jnp.float32)
        value_sum = value_sum + returned[1].astype(jnp.float32)
    key_out = key_sum.astype(jnp.bfloat16)
    value_out = value_sum.astype(jnp.bfloat16)
    feature_block = lax.all_to_all(layer_input[0], "ctx", split_axis=1, concat_axis=0, tiled=True)
    sequence_grad = lax.dot_general(
        feature_block,
        lax.all_gather(value_out, "ctx", axis=0, tiled=True),
        (((0,), (0,)), ((), ())),
        preferred_element_type=jnp.float32,
    )
    weight_grad = lax.psum_scatter(sequence_grad, "dp", scatter_dimension=0, tiled=True)
    square_total = lax.psum(jnp.sum(weight_grad * weight_grad), ("ctx", "dp"))
    norm_total = jnp.sqrt(square_total + 1e-06)
    clipped = weight_grad * jnp.minimum(1.0, clip_norm / norm_total)
    new_first = beta_first * first_moment_value + (1.0 - beta_first) * clipped
    new_second = beta_second * second_moment_value + (1.0 - beta_second) * clipped * clipped
    step_dir = new_first / correct_first / (jnp.sqrt(new_second / correct_second) + adam_eps)
    new_master = master - learn_rate * (step_dir + decay_rate * master)
    new_weight = lax.all_gather(new_master.astype(jnp.bfloat16), "dp", axis=0, tiled=True)
    return (
        query_gradient[None],
        key_out[None],
        value_out[None],
        new_master,
        new_first,
        new_second,
        new_weight,
    )


def solution(mesh):
    return jax.shard_map(
        shards,
        mesh=mesh,
        in_specs=(
            P("dp", "ctx", None),
            P("dp", "ctx", None),
            P("dp", "ctx", None),
            P("dp", "ctx", None),
            P("dp", "ctx", None),
            P("dp", "ctx"),
            P(("ctx", "dp"), None),
            P(("ctx", "dp"), None),
            P(("ctx", "dp"), None),
        ),
        out_specs=(
            P("dp", "ctx", None),
            P("dp", "ctx", None),
            P("dp", "ctx", None),
            P(("ctx", "dp"), None),
            P(("ctx", "dp"), None),
            P(("ctx", "dp"), None),
            P("ctx", None),
        ),
        check_vma=False,
    )
```

profile of v0, /device:TPU:1, one launch (start us, length us, event | category | flops | bytes accessed | tf_op | source)
XLA Modules:
  0.0 551.0 jit_solution(3754582582561746699)
XLA Ops:
  7.9 5.7 %collective-permute-start.8 = (bf16[128]{0:T(256)(128)(2,1)S(1)}, bf16[128]{0:T(256)(128)(2,1)S(1)}, u32[]{:S(2)}, u32[]{:S(2)}) collective-permute-start(bf16[128]{0:T(256)(128)(2,1)S(1)} %convert_bitcast_fusion.1), channel_id=1, source_target_pairs={{0,64},{8,72},{16,80},{24,88},{32,96},{40,104},{48,112},{56,120},{... | collective-permute-start | bytes 776 | tf_op jit(solution)/shard_map/ppermute | solution.py:27
  13.6 5.7 %collective-permute-start.9 = (bf16[128]{0:T(256)(128)(2,1)S(1)}, bf16[128]{0:T(256)(128)(2,1)S(1)}, u32[]{:S(2)}, u32[]{:S(2)}) collective-permute-start(bf16[128]{0:T(256)(128)(2,1)S(1)} %convert_bitcast_fusion.1), channel_id=1, source_target_pairs={{0,56},{8,64},{16,72},{24,80},{32,88},{40,96},{48,104},{56,112},{6... | collective-permute-start | bytes 776 | tf_op jit(solution)/shard_map/ppermute | solution.py:27
  21.1 5.2 collective-permute-start
  26.4 3.4 collective-permute-start.1
  29.8 1.9 collective-permute-start.2
  34.6 2.0 copy.108
  36.5 3.6 collective-permute-start.10
  40.4 2.3 collective-permute-start.11
  42.9 8.8 %collective-permute-start.12 = (bf16[128]{0:T(256)(128)(2,1)S(1)}, bf16[128]{0:T(256)(128)(2,1)S(1)}, u32[]{:S(2)}, u32[]{:S(2)}) collective-permute-start(bf16[128]{0:T(256)(128)(2,1)S(1)} %convert_bitcast_fusion.1), channel_id=1, source_target_pairs={{0,32},{8,40},{16,48},{24,56},{32,64},{40,72},{48,80},{56,88},{64,... | collective-permute-start | bytes 776 | tf_op jit(solution)/shard_map/ppermute | solution.py:27
  52.0 14.1 %collective-permute-start.13 = (bf16[128]{0:T(256)(128)(2,1)S(1)}, bf16[128]{0:T(256)(128)(2,1)S(1)}, u32[]{:S(2)}, u32[]{:S(2)}) collective-permute-start(bf16[128]{0:T(256)(128)(2,1)S(1)} %convert_bitcast_fusion.1), channel_id=1, source_target_pairs={{0,24},{8,32},{16,40},{24,48},{32,56},{40,64},{48,72},{56,80},{64,... | collective-permute-start | bytes 776 | tf_op jit(solution)/shard_map/ppermute | solution.py:27
  67.9 3.1 collective-permute-start.15
  71.3 7.6 %collective-permute-start.3 = (bf16[128,1024]{0,1:T(8,128)(2,1)}, bf16[128,1024]{0,1:T(8,128)(2,1)S(1)}, u32[]{:S(2)}, u32[]{:S(2)}) collective-permute-start(bf16[128,1024]{0,1:T(8,128)(2,1)} %bitcast), channel_id=1, source_target_pairs={{0,40},{8,48},{16,56},{24,64},{32,72},{40,80},{48,88},{56,96},{64,... | collective-permute-start | bytes 786440 | tf_op jit(solution)/shard_map/ppermute | solution.py:27
  79.1 2.8 collective-permute-start.4
  82.2 3.5 collective-permute-start.5
  85.7 3.1 collective-permute-start.6
  88.8 3.2 collective-permute-start.7
  107.0 6.1 %fusion.54 = (f32[8,2,128]{2,1,0:T(2,128)}, f32[8,2,128,1152]{2,3,1,0:T(8,128)}) fusion(pred[128,1152]{0,1:T(8,128)(4,1)S(1)} %fusion.40, bf16[128,8,2,128]{0,3,2,1:T(8,128)(2,1)S(1)} %bitcast.154, bf16[1152,8,128]{2,0,1:T(8,128)(2,1)S(1)} %constant_dynamic-update-slice_fusion), kind=kOutput, calls=%fused_computation.72 | convolution fusion | flops 613418112 | bytes 12476416 | tf_op jit(solution)/shard_map/sub | solution.py:64
  113.1 4.8 fusion.9
  117.9 3.7 fusion.58
  123.1 1.8 copy.147
  140.2 28.3 %collective-permute-done.39 = bf16[128,1024]{1,0:T(8,128)(2,1)} collective-permute-done((bf16[128,1024]{1,0:T(8,128)(2,1)}, bf16[128,1024]{1,0:T(8,128)(2,1)}, u32[]{:S(2)}, u32[]{:S(2)}) %collective-permute-start.39) | collective-permute-done | bytes 262176 | tf_op jit(solution)/shard_map/ppermute | solution.py:27
  173.9 10.8 %collective-permute-done.34 = bf16[128,1024]{1,0:T(8,128)(2,1)} collective-permute-done((bf16[128,1024]{1,0:T(8,128)(2,1)}, bf16[128,1024]{1,0:T(8,128)(2,1)}, u32[]{:S(2)}, u32[]{:S(2)}) %collective-permute-start.34) | collective-permute-done | bytes 262176 | tf_op jit(solution)/shard_map/ppermute | solution.py:27
  184.7 4.5 collective-permute-done.32
  189.2 2.6 add_convert_fusion
  192.6 25.7 %collective-permute-start.16 = (bf16[128,1024]{0,1:T(8,128)(2,1)}, bf16[128,1024]{0,1:T(8,128)(2,1)}, u32[]{:S(2)}, u32[]{:S(2)}) collective-permute-start(bf16[128,1024]{0,1:T(8,128)(2,1)} %bitcast.15), channel_id=1, source_target_pairs={{0,64},{8,72},{16,80},{24,88},{32,96},{40,104},{48,112},{56,120},{... | collective-permute-start | bytes 786440 | tf_op jit(solution)/shard_map/ppermute | solution.py:27
  218.4 7.7 %collective-permute-start.17 = (bf16[128,1024]{0,1:T(8,128)(2,1)}, bf16[128,1024]{0,1:T(8,128)(2,1)}, u32[]{:S(2)}, u32[]{:S(2)}) collective-permute-start(bf16[128,1024]{0,1:T(8,128)(2,1)} %bitcast.15), channel_id=1, source_target_pairs={{0,56},{8,64},{16,72},{24,80},{32,88},{40,96},{48,104},{56,112},{6... | collective-permute-start | bytes 786440 | tf_op jit(solution)/shard_map/ppermute | solution.py:27
  226.1 2.0 collective-permute-start.18
  228.1 2.0 collective-permute-start.19
  230.1 2.4 collective-permute-start.20
  232.5 3.8 collective-permute-start.21
  236.3 2.3 collective-permute-start.22
  238.6 3.2 collective-permute-done.18
  241.9 2.0 collective-permute-start.23
  243.9 2.6 copy.148
  246.4 31.1 %all-to-all-start = ((bf16[128,32,168]{0,2,1:T(8,128)(2,1)}), bf16[128,32,168]{0,2,1:T(8,128)(2,1)}, u32[]{:S(2)}, u32[]{:S(2)}) async-start(bf16[128,32,168]{0,2,1:T(8,128)(2,1)} %bitcast.152), calls=%async_computation | async-start | bytes 2752512 | tf_op jit(solution)/shard_map/all_to_all | solution.py:153
  277.6 1.9 copy.120
  299.1 3.5 fusion.35
  305.6 3.7 fusion.57
  320.1 42.3 %all-gather.3.cloned.1.call-done = bf16[4096,1024]{1,0:T(8,128)(2,1)} async-done(((bf16[128,1024]{1,0:T(8,128)(2,1)}), bf16[4096,1024]{1,0:T(8,128)(2,1)}) %all-gather.3.cloned.1.call-update) | async-done | bytes 8388624 | tf_op jit(solution)/shard_map/all_gather | solution.py:156
  362.4 6.2 %fusion.32 = f32[168,1024]{1,0:T(8,128)} fusion(bf16[4096,1024]{1,0:T(8,128)(2,1)} %all-gather.3.cloned.1.call-done, bf16[128,32,168]{0,2,1:T(8,128)(2,1)} %all-to-all-done), kind=kOutput, calls=%fused_computation.29 | convolution fusion | flops 1409286144 | bytes 10452992 | tf_op jit(solution)/shard_map/dot_general | solution.py:154
  368.5 18.3 %fusion = f32[24,1024]{1,0:T(8,128)S(1)} fusion(f32[168,1024]{1,0:T(8,128)} %fusion.32), kind=kCustom, calls=%all-reduce-scatter | all-reduce-scatter fusion | flops 196609 | bytes 787456
  387.5 2.7 collective-permute-start.40
  402.1 3.4 fusion.29
  409.4 12.0 %collective-permute-done.28 = bf16[128,1024]{1,0:T(8,128)(2,1)} collective-permute-done((bf16[128,1024]{1,0:T(8,128)(2,1)}, bf16[128,1024]{1,0:T(8,128)(2,1)}, u32[]{:S(2)}, u32[]{:S(2)}) %collective-permute-start.28) | collective-permute-done | bytes 262176 | tf_op jit(solution)/shard_map/ppermute | solution.py:27
  421.5 7.7 %collective-permute-done.24 = bf16[128,1024]{1,0:T(8,128)(2,1)} collective-permute-done((bf16[128,1024]{1,0:T(8,128)(2,1)S(1)}, bf16[128,1024]{1,0:T(8,128)(2,1)}, u32[]{:S(2)}, u32[]{:S(2)}) %collective-permute-start.24) | collective-permute-done | bytes 262176 | tf_op jit(solution)/shard_map/ppermute | solution.py:27
  429.1 2.6 fusion.45
  431.7 96.6 %psum.7 = f32[]{:T(128)} all-reduce(f32[]{:T(128)} %multiply_reduce_fusion), channel_id=1, replica_groups=mesh['ctx'=32,'dp'=8] {'ctx','dp'}, use_global_device_ids=true, to_apply=%region_5.6 | all-reduce | flops 1 | bytes 8 | tf_op jit(solution)/shard_map/psum | solution.py:161
  529.8 13.5 %all-gather = bf16[8,21,1024]{2,1,0:T(8,128)(2,1)S(1)} all-gather(bf16[1,21,1024]{2,1,0:T(8,128)(2,1)S(1)} %get-tuple-element.28), channel_id=1, replica_groups=mesh['ctx'=32,'dp'=8] {'dp'}, dimensions={0}, use_global_device_ids=true | all-gather | bytes 387072 | tf_op jit(solution)/shard_map/all_gather | solution.py:168
  (184 shorter events, 96.9 us)
Async XLA Ops:
  7.2 75.1 %copy-start.19 = (s32[1,128]{1,0:T(1,128)S(1)}, s32[1,128]{1,0:T(1,128)}, u32[]{:S(2)}) copy-start(s32[1,128]{1,0:T(1,128)} %param.14) | copy-start | bytes 1540
  7.2 355.2 %all-gather.3.cloned.1.call-start = ((), (), s32[]{:S(2)}) async-start(), calls=%async_computation.1 | async-start | bytes 8650752 | tf_op jit(solution)/shard_map/all_gather | solution.py:156
  7.9 28.6 %collective-permute-start.8 = (bf16[128]{0:T(256)(128)(2,1)S(1)}, bf16[128]{0:T(256)(128)(2,1)S(1)}, u32[]{:S(2)}, u32[]{:S(2)}) collective-permute-start(bf16[128]{0:T(256)(128)(2,1)S(1)} %convert_bitcast_fusion.1), channel_id=1, source_target_pairs={{0,64},{8,72},{16,80},{24,88},{32,96},{40,104},{48,112},{56,120},{... | collective-permute-start | bytes 776 | tf_op jit(solution)/shard_map/ppermute | solution.py:27
  13.6 26.8 %collective-permute-start.9 = (bf16[128]{0:T(256)(128)(2,1)S(1)}, bf16[128]{0:T(256)(128)(2,1)S(1)}, u32[]{:S(2)}, u32[]{:S(2)}) collective-permute-start(bf16[128]{0:T(256)(128)(2,1)S(1)} %convert_bitcast_fusion.1), channel_id=1, source_target_pairs={{0,56},{8,64},{16,72},{24,80},{32,88},{40,96},{48,104},{56,112},{6... | collective-permute-start | bytes 776 | tf_op jit(solution)/shard_map/ppermute | solution.py:27
  21.1 61.1 %collective-permute-start = (bf16[128,1024]{0,1:T(8,128)(2,1)}, bf16[128,1024]{0,1:T(8,128)(2,1)S(1)}, u32[]{:S(2)}, u32[]{:S(2)}) collective-permute-start(bf16[128,1024]{0,1:T(8,128)(2,1)} %bitcast), channel_id=1, source_target_pairs={{0,64},{8,72},{16,80},{24,88},{32,96},{40,104},{48,112},{56,120},{... | collective-permute-start | bytes 786440 | tf_op jit(solution)/shard_map/ppermute | solution.py:27
  26.4 59.3 %collective-permute-start.1 = (bf16[128,1024]{0,1:T(8,128)(2,1)}, bf16[128,1024]{0,1:T(8,128)(2,1)S(1)}, u32[]{:S(2)}, u32[]{:S(2)}) collective-permute-start(bf16[128,1024]{0,1:T(8,128)(2,1)} %bitcast), channel_id=1, source_target_pairs={{0,56},{8,64},{16,72},{24,80},{32,88},{40,96},{48,104},{56,112},{6... | collective-permute-start | bytes 786440 | tf_op jit(solution)/shard_map/ppermute | solution.py:27
  29.8 59.0 %collective-permute-start.2 = (bf16[128,1024]{0,1:T(8,128)(2,1)}, bf16[128,1024]{0,1:T(8,128)(2,1)S(1)}, u32[]{:S(2)}, u32[]{:S(2)}) collective-permute-start(bf16[128,1024]{0,1:T(8,128)(2,1)} %bitcast), channel_id=1, source_target_pairs={{0,48},{8,56},{16,64},{24,72},{32,80},{40,88},{48,96},{56,104},{64... | collective-permute-start | bytes 786440 | tf_op jit(solution)/shard_map/ppermute | solution.py:27
  33.0 84.9 %copy-start.2 = (bf16[1,128,2048]{1,2,0:T(8,128)(2,1)}, bf16[1,128,2048]{1,2,0:T(8,128)(2,1)S(1)}, u32[]{:S(2)}) copy-start(bf16[1,128,2048]{1,2,0:T(8,128)(2,1)S(1)} %copy.121) | copy-start | bytes 1572868
  36.5 6.4 %collective-permute-start.10 = (bf16[128]{0:T(256)(128)(2,1)S(1)}, bf16[128]{0:T(256)(128)(2,1)S(1)}, u32[]{:S(2)}, u32[]{:S(2)}) collective-permute-start(bf16[128]{0:T(256)(128)(2,1)S(1)} %convert_bitcast_fusion.1), channel_id=1, source_target_pairs={{0,48},{8,56},{16,64},{24,72},{32,80},{40,88},{48,96},{56,104},{64... | collective-permute-start | bytes 776 | tf_op jit(solution)/shard_map/ppermute | solution.py:27
  40.4 11.6 %collective-permute-start.11 = (bf16[128]{0:T(256)(128)(2,1)S(1)}, bf16[128]{0:T(256)(128)(2,1)S(1)}, u32[]{:S(2)}, u32[]{:S(2)}) collective-permute-start(bf16[128]{0:T(256)(128)(2,1)S(1)} %convert_bitcast_fusion.1), channel_id=1, source_target_pairs={{0,40},{8,48},{16,56},{24,64},{32,72},{40,80},{48,88},{56,96},{64,... | collective-permute-start | bytes 776 | tf_op jit(solution)/shard_map/ppermute | solution.py:27
  42.9 23.5 %collective-permute-start.12 = (bf16[128]{0:T(256)(128)(2,1)S(1)}, bf16[128]{0:T(256)(128)(2,1)S(1)}, u32[]{:S(2)}, u32[]{:S(2)}) collective-permute-start(bf16[128]{0:T(256)(128)(2,1)S(1)} %convert_bitcast_fusion.1), channel_id=1, source_target_pairs={{0,32},{8,40},{16,48},{24,56},{32,64},{40,72},{48,80},{56,88},{64,... | collective-permute-start | bytes 776 | tf_op jit(solution)/shard_map/ppermute | solution.py:27
  52.0 15.9 %collective-permute-start.13 = (bf16[128]{0:T(256)(128)(2,1)S(1)}, bf16[128]{0:T(256)(128)(2,1)S(1)}, u32[]{:S(2)}, u32[]{:S(2)}) collective-permute-start(bf16[128]{0:T(256)(128)(2,1)S(1)} %convert_bitcast_fusion.1), channel_id=1, source_target_pairs={{0,24},{8,32},{16,40},{24,48},{32,56},{40,64},{48,72},{56,80},{64,... | collective-permute-start | bytes 776 | tf_op jit(solution)/shard_map/ppermute | solution.py:27
  66.4 4.9 collective-permute-start.14
  67.9 11.2 %collective-permute-start.15 = (bf16[128]{0:T(256)(128)(2,1)S(1)}, bf16[128]{0:T(256)(128)(2,1)S(1)}, u32[]{:S(2)}, u32[]{:S(2)}) collective-permute-start(bf16[128]{0:T(256)(128)(2,1)S(1)} %convert_bitcast_fusion.1), channel_id=1, source_target_pairs={{0,8},{8,16},{16,24},{24,32},{32,40},{40,48},{48,56},{56,64},{64,7... | collective-permute-start | bytes 776 | tf_op jit(solution)/shard_map/ppermute | solution.py:27
  71.3 24.3 %collective-permute-start.3 = (bf16[128,1024]{0,1:T(8,128)(2,1)}, bf16[128,1024]{0,1:T(8,128)(2,1)S(1)}, u32[]{:S(2)}, u32[]{:S(2)}) collective-permute-start(bf16[128,1024]{0,1:T(8,128)(2,1)} %bitcast), channel_id=1, source_target_pairs={{0,40},{8,48},{16,56},{24,64},{32,72},{40,80},{48,88},{56,96},{64,... | collective-permute-start | bytes 786440 | tf_op jit(solution)/shard_map/ppermute | solution.py:27
  79.1 17.3 %collective-permute-start.4 = (bf16[128,1024]{0,1:T(8,128)(2,1)}, bf16[128,1024]{0,1:T(8,128)(2,1)S(1)}, u32[]{:S(2)}, u32[]{:S(2)}) collective-permute-start(bf16[128,1024]{0,1:T(8,128)(2,1)} %bitcast), channel_id=1, source_target_pairs={{0,32},{8,40},{16,48},{24,56},{32,64},{40,72},{48,80},{56,88},{64,... | collective-permute-start | bytes 786440 | tf_op jit(solution)/shard_map/ppermute | solution.py:27
  82.2 15.1 %collective-permute-start.5 = (bf16[128,1024]{0,1:T(8,128)(2,1)}, bf16[128,1024]{0,1:T(8,128)(2,1)S(1)}, u32[]{:S(2)}, u32[]{:S(2)}) collective-permute-start(bf16[128,1024]{0,1:T(8,128)(2,1)} %bitcast), channel_id=1, source_target_pairs={{0,24},{8,32},{16,40},{24,48},{32,56},{40,64},{48,72},{56,80},{64,... | collective-permute-start | bytes 786440 | tf_op jit(solution)/shard_map/ppermute | solution.py:27
  85.7 12.5 %collective-permute-start.6 = (bf16[128,1024]{0,1:T(8,128)(2,1)}, bf16[128,1024]{0,1:T(8,128)(2,1)S(1)}, u32[]{:S(2)}, u32[]{:S(2)}) collective-permute-start(bf16[128,1024]{0,1:T(8,128)(2,1)} %bitcast), channel_id=1, source_target_pairs={{0,16},{8,24},{16,32},{24,40},{32,48},{40,56},{48,64},{56,72},{64,... | collective-permute-start | bytes 786440 | tf_op jit(solution)/shard_map/ppermute | solution.py:27
  88.8 11.2 %collective-permute-start.7 = (bf16[128,1024]{0,1:T(8,128)(2,1)}, bf16[128,1024]{0,1:T(8,128)(2,1)}, u32[]{:S(2)}, u32[]{:S(2)}) collective-permute-start(bf16[128,1024]{0,1:T(8,128)(2,1)} %bitcast), channel_id=1, source_target_pairs={{0,8},{8,16},{16,24},{24,32},{32,40},{40,48},{48,56},{56,64},{64,7... | collective-permute-start | bytes 786440 | tf_op jit(solution)/shard_map/ppermute | solution.py:27
  124.9 43.6 %collective-permute-start.39 = (bf16[128,1024]{1,0:T(8,128)(2,1)}, bf16[128,1024]{1,0:T(8,128)(2,1)}, u32[]{:S(2)}, u32[]{:S(2)}) collective-permute-start(bf16[128,1024]{1,0:T(8,128)(2,1)} %copy.147), channel_id=1, source_target_pairs={{64,0},{72,8},{80,16},{88,24},{96,32},{104,40},{112,48},{120,56},{... | collective-permute-start | bytes 786440 | tf_op jit(solution)/shard_map/ppermute | solution.py:27
  128.0 41.8 %collective-permute-start.38 = (bf16[128,1024]{1,0:T(8,128)(2,1)}, bf16[128,1024]{1,0:T(8,128)(2,1)}, u32[]{:S(2)}, u32[]{:S(2)}) collective-permute-start(bf16[128,1024]{1,0:T(8,128)(2,1)} %copy.146), channel_id=1, source_target_pairs={{56,0},{64,8},{72,16},{80,24},{88,32},{96,40},{104,48},{112,56},{1... | collective-permute-start | bytes 786440 | tf_op jit(solution)/shard_map/ppermute | solution.py:27
  131.1 40.0 %collective-permute-start.37 = (bf16[128,1024]{1,0:T(8,128)(2,1)}, bf16[128,1024]{1,0:T(8,128)(2,1)}, u32[]{:S(2)}, u32[]{:S(2)}) collective-permute-start(bf16[128,1024]{1,0:T(8,128)(2,1)} %copy.145), channel_id=1, source_target_pairs={{48,0},{56,8},{64,16},{72,24},{80,32},{88,40},{96,48},{104,56},{11... | collective-permute-start | bytes 786440 | tf_op jit(solution)/shard_map/ppermute | solution.py:27
  134.1 39.7 %collective-permute-start.36 = (bf16[128,1024]{1,0:T(8,128)(2,1)}, bf16[128,1024]{1,0:T(8,128)(2,1)}, u32[]{:S(2)}, u32[]{:S(2)}) collective-permute-start(bf16[128,1024]{1,0:T(8,128)(2,1)} %copy.144), channel_id=1, source_target_pairs={{40,0},{48,8},{56,16},{64,24},{72,32},{80,40},{88,48},{96,56},{104... | collective-permute-start | bytes 786440 | tf_op jit(solution)/shard_map/ppermute | solution.py:27
  136.3 37.6 %collective-permute-start.35 = (bf16[128,1024]{1,0:T(8,128)(2,1)}, bf16[128,1024]{1,0:T(8,128)(2,1)}, u32[]{:S(2)}, u32[]{:S(2)}) collective-permute-start(bf16[128,1024]{1,0:T(8,128)(2,1)} %copy.143), channel_id=1, source_target_pairs={{32,0},{40,8},{48,16},{56,24},{64,32},{72,40},{80,48},{88,56},{96,... | collective-permute-start | bytes 786440 | tf_op jit(solution)/shard_map/ppermute | solution.py:27
  168.5 16.2 %collective-permute-start.34 = (bf16[128,1024]{1,0:T(8,128)(2,1)}, bf16[128,1024]{1,0:T(8,128)(2,1)}, u32[]{:S(2)}, u32[]{:S(2)}) collective-permute-start(bf16[128,1024]{1,0:T(8,128)(2,1)} %copy.142), channel_id=1, source_target_pairs={{24,0},{32,8},{40,16},{48,24},{56,32},{64,40},{72,48},{80,56},{88,... | collective-permute-start | bytes 786440 | tf_op jit(solution)/shard_map/ppermute | solution.py:27
  169.8 14.9 %collective-permute-start.33 = (bf16[128,1024]{1,0:T(8,128)(2,1)}, bf16[128,1024]{1,0:T(8,128)(2,1)}, u32[]{:S(2)}, u32[]{:S(2)}) collective-permute-start(bf16[128,1024]{1,0:T(8,128)(2,1)} %copy.141), channel_id=1, source_target_pairs={{16,0},{24,8},{32,16},{40,24},{48,32},{56,40},{64,48},{72,56},{80,... | collective-permute-start | bytes 786440 | tf_op jit(solution)/shard_map/ppermute | solution.py:27
  171.1 18.1 %collective-permute-start.32 = (bf16[128,1024]{1,0:T(8,128)(2,1)}, bf16[128,1024]{1,0:T(8,128)(2,1)}, u32[]{:S(2)}, u32[]{:S(2)}) collective-permute-start(bf16[128,1024]{1,0:T(8,128)(2,1)} %copy.139), channel_id=1, source_target_pairs={{8,0},{16,8},{24,16},{32,24},{40,32},{48,40},{56,48},{64,56},{72,6... | collective-permute-start | bytes 786440 | tf_op jit(solution)/shard_map/ppermute | solution.py:27
  192.6 39.8 %collective-permute-start.16 = (bf16[128,1024]{0,1:T(8,128)(2,1)}, bf16[128,1024]{0,1:T(8,128)(2,1)}, u32[]{:S(2)}, u32[]{:S(2)}) collective-permute-start(bf16[128,1024]{0,1:T(8,128)(2,1)} %bitcast.15), channel_id=1, source_target_pairs={{0,64},{8,72},{16,80},{24,88},{32,96},{40,104},{48,112},{56,120},{... | collective-permute-start | bytes 786440 | tf_op jit(solution)/shard_map/ppermute | solution.py:27
  218.4 17.9 %collective-permute-start.17 = (bf16[128,1024]{0,1:T(8,128)(2,1)}, bf16[128,1024]{0,1:T(8,128)(2,1)}, u32[]{:S(2)}, u32[]{:S(2)}) collective-permute-start(bf16[128,1024]{0,1:T(8,128)(2,1)} %bitcast.15), channel_id=1, source_target_pairs={{0,56},{8,64},{16,72},{24,80},{32,88},{40,96},{48,104},{56,112},{6... | collective-permute-start | bytes 786440 | tf_op jit(solution)/shard_map/ppermute | solution.py:27
  226.1 15.8 %collective-permute-start.18 = (bf16[128,1024]{0,1:T(8,128)(2,1)}, bf16[128,1024]{0,1:T(8,128)(2,1)}, u32[]{:S(2)}, u32[]{:S(2)}) collective-permute-start(bf16[128,1024]{0,1:T(8,128)(2,1)} %bitcast.15), channel_id=1, source_target_pairs={{0,48},{8,56},{16,64},{24,72},{32,80},{40,88},{48,96},{56,104},{64... | collective-permute-start | bytes 786440 | tf_op jit(solution)/shard_map/ppermute | solution.py:27
  228.1 56.7 %collective-permute-start.19 = (bf16[128,1024]{0,1:T(8,128)(2,1)}, bf16[128,1024]{0,1:T(8,128)(2,1)}, u32[]{:S(2)}, u32[]{:S(2)}) collective-permute-start(bf16[128,1024]{0,1:T(8,128)(2,1)} %bitcast.15), channel_id=1, source_target_pairs={{0,40},{8,48},{16,56},{24,64},{32,72},{40,80},{48,88},{56,96},{64,... | collective-permute-start | bytes 786440 | tf_op jit(solution)/shard_map/ppermute | solution.py:27
  230.1 56.5 %collective-permute-start.20 = (bf16[128,1024]{0,1:T(8,128)(2,1)}, bf16[128,1024]{0,1:T(8,128)(2,1)}, u32[]{:S(2)}, u32[]{:S(2)}) collective-permute-start(bf16[128,1024]{0,1:T(8,128)(2,1)} %bitcast.15), channel_id=1, source_target_pairs={{0,32},{8,40},{16,48},{24,56},{32,64},{40,72},{48,80},{56,88},{64,... | collective-permute-start | bytes 786440 | tf_op jit(solution)/shard_map/ppermute | solution.py:27
  232.5 55.9 %collective-permute-start.21 = (bf16[128,1024]{0,1:T(8,128)(2,1)}, bf16[128,1024]{0,1:T(8,128)(2,1)}, u32[]{:S(2)}, u32[]{:S(2)}) collective-permute-start(bf16[128,1024]{0,1:T(8,128)(2,1)} %bitcast.15), channel_id=1, source_target_pairs={{0,24},{8,32},{16,40},{24,48},{32,56},{40,64},{48,72},{56,80},{64,... | collective-permute-start | bytes 786440 | tf_op jit(solution)/shard_map/ppermute | solution.py:27
  236.3 54.0 %collective-permute-start.22 = (bf16[128,1024]{0,1:T(8,128)(2,1)}, bf16[128,1024]{0,1:T(8,128)(2,1)}, u32[]{:S(2)}, u32[]{:S(2)}) collective-permute-start(bf16[128,1024]{0,1:T(8,128)(2,1)} %bitcast.15), channel_id=1, source_target_pairs={{0,16},{8,24},{16,32},{24,40},{32,48},{40,56},{48,64},{56,72},{64,... | collective-permute-start | bytes 786440 | tf_op jit(solution)/shard_map/ppermute | solution.py:27
  241.9 50.1 %collective-permute-start.23 = (bf16[128,1024]{0,1:T(8,128)(2,1)}, bf16[128,1024]{0,1:T(8,128)(2,1)}, u32[]{:S(2)}, u32[]{:S(2)}) collective-permute-start(bf16[128,1024]{0,1:T(8,128)(2,1)} %bitcast.15), channel_id=1, source_target_pairs={{0,8},{8,16},{16,24},{24,32},{32,40},{40,48},{48,56},{56,64},{64,7... | collective-permute-start | bytes 786440 | tf_op jit(solution)/shard_map/ppermute | solution.py:27
  246.4 73.7 %all-to-all-start = ((bf16[128,32,168]{0,2,1:T(8,128)(2,1)}), bf16[128,32,168]{0,2,1:T(8,128)(2,1)}, u32[]{:S(2)}, u32[]{:S(2)}) async-start(bf16[128,32,168]{0,2,1:T(8,128)(2,1)} %bitcast.152), calls=%async_computation | async-start | bytes 2752512 | tf_op jit(solution)/shard_map/all_to_all | solution.py:153
  312.5 84.1 %collective-permute-start.31 = (bf16[128,1024]{1,0:T(8,128)(2,1)}, bf16[128,1024]{1,0:T(8,128)(2,1)}, u32[]{:S(2)}, u32[]{:S(2)}) collective-permute-start(bf16[128,1024]{1,0:T(8,128)(2,1)} %copy.137), channel_id=1, source_target_pairs={{64,0},{72,8},{80,16},{88,24},{96,32},{104,40},{112,48},{120,56},{... | collective-permute-start | bytes 786440 | tf_op jit(solution)/shard_map/ppermute | solution.py:27
  315.6 82.3 %collective-permute-start.30 = (bf16[128,1024]{1,0:T(8,128)(2,1)}, bf16[128,1024]{1,0:T(8,128)(2,1)}, u32[]{:S(2)}, u32[]{:S(2)}) collective-permute-start(bf16[128,1024]{1,0:T(8,128)(2,1)} %copy.136), channel_id=1, source_target_pairs={{56,0},{64,8},{72,16},{80,24},{88,32},{96,40},{104,48},{112,56},{1... | collective-permute-start | bytes 786440 | tf_op jit(solution)/shard_map/ppermute | solution.py:27
  318.7 80.5 %collective-permute-start.29 = (bf16[128,1024]{1,0:T(8,128)(2,1)}, bf16[128,1024]{1,0:T(8,128)(2,1)}, u32[]{:S(2)}, u32[]{:S(2)}) collective-permute-start(bf16[128,1024]{1,0:T(8,128)(2,1)} %copy.135), channel_id=1, source_target_pairs={{48,0},{56,8},{64,16},{72,24},{80,32},{88,40},{96,48},{104,56},{11... | collective-permute-start | bytes 786440 | tf_op jit(solution)/shard_map/ppermute | solution.py:27
  387.5 13.0 %collective-permute-start.40 = (f32[21,1024]{1,0:T(8,128)}, f32[21,1024]{1,0:T(8,128)}, u32[]{:S(2)}, u32[]{:S(2)}) collective-permute-start(f32[21,1024]{1,0:T(8,128)} %slice.130), channel_id=1, source_target_pairs={{0,1},{1,2},{2,3},{3,4},{4,5},{5,6},{6,7},{8,9},{9,10},{10,11},{11... | collective-permute-start | bytes 258056
  393.3 28.1 %collective-permute-start.28 = (bf16[128,1024]{1,0:T(8,128)(2,1)}, bf16[128,1024]{1,0:T(8,128)(2,1)}, u32[]{:S(2)}, u32[]{:S(2)}) collective-permute-start(bf16[128,1024]{1,0:T(8,128)(2,1)} %copy.134), channel_id=1, source_target_pairs={{40,0},{48,8},{56,16},{64,24},{72,32},{80,40},{88,48},{96,56},{104... | collective-permute-start | bytes 786440 | tf_op jit(solution)/shard_map/ppermute | solution.py:27
  396.6 24.8 %collective-permute-start.27 = (bf16[128,1024]{1,0:T(8,128)(2,1)}, bf16[128,1024]{1,0:T(8,128)(2,1)}, u32[]{:S(2)}, u32[]{:S(2)}) collective-permute-start(bf16[128,1024]{1,0:T(8,128)(2,1)} %copy.133), channel_id=1, source_target_pairs={{32,0},{40,8},{48,16},{56,24},{64,32},{72,40},{80,48},{88,56},{96,... | collective-permute-start | bytes 786440 | tf_op jit(solution)/shard_map/ppermute | solution.py:27
  397.9 23.5 %collective-permute-start.26 = (bf16[128,1024]{1,0:T(8,128)(2,1)}, bf16[128,1024]{1,0:T(8,128)(2,1)}, u32[]{:S(2)}, u32[]{:S(2)}) collective-permute-start(bf16[128,1024]{1,0:T(8,128)(2,1)} %copy.132), channel_id=1, source_target_pairs={{24,0},{32,8},{40,16},{48,24},{56,32},{64,40},{72,48},{80,56},{88,... | collective-permute-start | bytes 786440 | tf_op jit(solution)/shard_map/ppermute | solution.py:27
  399.2 22.2 %collective-permute-start.25 = (bf16[128,1024]{1,0:T(8,128)(2,1)S(1)}, bf16[128,1024]{1,0:T(8,128)(2,1)}, u32[]{:S(2)}, u32[]{:S(2)}) collective-permute-start(bf16[128,1024]{1,0:T(8,128)(2,1)S(1)} %copy.131), channel_id=1, source_target_pairs={{16,0},{24,8},{32,16},{40,24},{48,32},{56,40},{64,48},{72,56},{80,... | collective-permute-start | bytes 786440 | tf_op jit(solution)/shard_map/ppermute | solution.py:27
  400.5 28.6 %collective-permute-start.24 = (bf16[128,1024]{1,0:T(8,128)(2,1)S(1)}, bf16[128,1024]{1,0:T(8,128)(2,1)}, u32[]{:S(2)}, u32[]{:S(2)}) collective-permute-start(bf16[128,1024]{1,0:T(8,128)(2,1)S(1)} %copy.129), channel_id=1, source_target_pairs={{8,0},{16,8},{24,16},{32,24},{40,32},{48,40},{56,48},{64,56},{72,6... | collective-permute-start | bytes 786440 | tf_op jit(solution)/shard_map/ppermute | solution.py:27
  407.5 121.5 %copy-start.14 = (f32[21,1024]{1,0:T(8,128)S(1)}, f32[21,1024]{1,0:T(8,128)}, u32[]{:S(2)}) copy-start(f32[21,1024]{1,0:T(8,128)} %param.15) | copy-start | bytes 258052
  407.5 121.5 %copy-start.15 = (f32[21,1024]{1,0:T(8,128)S(1)}, f32[21,1024]{1,0:T(8,128)}, u32[]{:S(2)}) copy-start(f32[21,1024]{1,0:T(8,128)} %param.16) | copy-start | bytes 258052
  407.5 121.5 %copy-start.16 = (f32[21,1024]{1,0:T(8,128)S(1)}, f32[21,1024]{1,0:T(8,128)}, u32[]{:S(2)}) copy-start(f32[21,1024]{1,0:T(8,128)} %param.17) | copy-start | bytes 258052
  (18 other events, 250.8 us)
Sparse Core Ops, SparseCore 0:
  191.9 170.4 all-gather.2
where the time goes:
time: 554 us; the launch traced here: 551 us
  starting transfers between devices  178 us (32%)
  blocking collectives  128 us (23%)
  waiting for transfers between devices  109 us (20%)
  local copies, waits for them, and re-layouts  77.8 us (14%)
  matrix products  28.2 us (5%)
  between operations  16.3 us (3%)
  other arithmetic  13.1 us (2%)
    ppermute x40, starting transfers between devices, from_behind(): return lax.ppermute(x, axis, pairs)  144 us
    psum x1, blocking collectives, shards(): square_total = lax.psum(jnp.sum(weight_grad * weight_grad), ('ctx', 'dp'))  96.6 us
    ppermute x40, waiting for transfers between devices, from_behind(): return lax.ppermute(x, axis, pairs)  66.6 us
    all_gather x1, waiting for transfers between devices, shards(): lax.all_gather(value_out, 'ctx', axis=0, tiled=True)  42.3 us
    all_to_all x1, starting transfers between devices, shards(): lax.all_to_all(layer_input[0], 'ctx', split_axis=1, concat_axis=0, tiled=...  31.1 us
    unnamed x79, local copies, waits for them, and re-layouts  25.1 us
    unnamed x1, blocking collectives  18.3 us
    concatenate x10, local copies, waits for them, and re-layouts, shards(): jnp.concatenate([halo_rows[1], value_state_rows[0]], axis=0)  16.3 us
  transfers between devices with their start and end apart: 43, of which 7 were waited for; matrix products, arithmetic and copies ran while one was open for 19% of the time, Pallas kernels for 0%

commit v1 on v0

--- a/solution.py
+++ b/solution.py
@@ -1,13 +1,16 @@
 import jax
 import jax.numpy as jnp
 from jax import lax
+from jax.sharding import Mesh
 from jax.sharding import PartitionSpec as P
 
 QUERY_HEADS = 16
 KEY_VALUE_HEADS = 8
 HEAD_SIZE = 128
 WINDOW = 1024
-
+Z_SIZE = 8
+
+CTX = ("cz", "cx")
 
 query_scale = 168.0 ** (-0.5)
 masked_score = -1e30
@@ -21,10 +24,18 @@
 correct_second = 0.994079470779666
 
 
-def from_behind(x, axis, by):
-    count = lax.axis_size(axis)
+def ctx_size():
+    return lax.axis_size("cz") * lax.axis_size("cx")
+
+
+def ctx_index():
+    return lax.axis_index("cz") * lax.axis_size("cx") + lax.axis_index("cx")
+
+
+def from_behind(x, by):
+    count = ctx_size()
     pairs = [(i, i + by) for i in range(count) if 0 <= i + by < count]
-    return lax.ppermute(x, axis, pairs)
+    return lax.ppermute(x, CTX, pairs)
 
 
 def attend(
@@ -108,25 +119,21 @@
     second_moment_value,
 ):
     shard_length = query_states.shape[1]
-    peer_count = min(WINDOW // shard_length, lax.axis_size("ctx") - 1)
+    kv_width = key_states.shape[2]
+    peer_count = min(WINDOW // shard_length, ctx_size() - 1)
     front_len = peer_count * shard_length
-    position = lax.axis_index("ctx") * shard_length
-    seg_low = segments[0].astype(jnp.bfloat16)
-    own_piece = (key_states[0], value_state_rows[0], seg_low)
-    incoming_list = []
-    for distance in range(peer_count, 0, -1):
-        incoming_list.append(
-            from_behind((own_piece[0], own_piece[1], own_piece[2]), "ctx", distance)
-        )
-    halo_rows = tuple(
-        (
-            jnp.concatenate([incoming[member] for incoming in incoming_list], axis=0)
-            for member in range(3)
-        )
-    )
-    key_row_block = jnp.concatenate([halo_rows[0], key_states[0]], axis=0)
-    value_row_block = jnp.concatenate([halo_rows[1], value_state_rows[0]], axis=0)
-    seg_key = jnp.concatenate([halo_rows[2], seg_low], axis=0)
+    position = ctx_index() * shard_length
+
+    seg_all = lax.all_gather(segments[0], CTX, axis=0, tiled=True)
+    seg_pad = jnp.concatenate([jnp.full((front_len,), -1, jnp.int32), seg_all], axis=0)
+    seg_key = lax.dynamic_slice_in_dim(seg_pad, position, front_len + shard_length, 0)
+    seg_query = segments[0]
+
+    own_kv = jnp.concatenate([key_states[0], value_state_rows[0]], axis=1)
+    incoming = [from_behind(own_kv, distance) for distance in range(peer_count, 0, -1)]
+    kv_rows = jnp.concatenate(incoming + [own_kv], axis=0)
+    key_row_block = kv_rows[:, :kv_width]
+    value_row_block = kv_rows[:, kv_width:]
     index_query = position + jnp.arange(shard_length, dtype=jnp.int32)
     index_key = position - front_len + jnp.arange(front_len + shard_length, dtype=jnp.int32)
     query_gradient, key_gradient, value_gradient = attend(
@@ -134,7 +141,7 @@
         key_row_block,
         value_row_block,
         grad_out[0],
-        seg_low,
+        seg_query,
         seg_key,
         index_query,
         index_key,
@@ -143,22 +150,40 @@
     value_sum = value_gradient[front_len:]
     for distance in range(1, peer_count + 1):
         lower = (peer_count - distance) * shard_length
-        key_part = key_gradient[lower : lower + shard_length].astype(jnp.bfloat16)
-        value_part = value_gradient[lower : lower + shard_length].astype(jnp.bfloat16)
-        returned = from_behind((key_part, value_part), "ctx", -distance)
-        key_sum = key_sum + returned[0].astype(jnp.float32)
-        value_sum = value_sum + returned[1].astype(jnp.float32)
+        part = jnp.concatenate(
+            [
+                key_gradient[lower : lower + shard_length].astype(jnp.bfloat16),
+                value_gradient[lower : lower + shard_length].astype(jnp.bfloat16),
+            ],
+            axis=1,
+        )
+        returned = from_behind(part, -distance).astype(jnp.float32)
+        key_sum = key_sum + returned[:, :kv_width]
+        value_sum = value_sum + returned[:, kv_width:]
     key_out = key_sum.astype(jnp.bfloat16)
     value_out = value_sum.astype(jnp.bfloat16)
-    feature_block = lax.all_to_all(layer_input[0], "ctx", split_axis=1, concat_axis=0, tiled=True)
-    sequence_grad = lax.dot_general(
+
+    feature_block = lax.all_to_all(layer_input[0], "cz", split_axis=1, concat_axis=0, tiled=True)
+    value_group = lax.all_gather(value_out, "cz", axis=0, tiled=True)
+    partial = lax.dot_general(
         feature_block,
-        lax.all_gather(value_out, "ctx", axis=0, tiled=True),
+        value_group,
         (((0,), (0,)), ((), ())),
         preferred_element_type=jnp.float32,
     )
-    weight_grad = lax.psum_scatter(sequence_grad, "dp", scatter_dimension=0, tiled=True)
-    square_total = lax.psum(jnp.sum(weight_grad * weight_grad), ("ctx", "dp"))
+    owners = lax.axis_size("cx") * lax.axis_size("dp")
+    rows = partial.shape[0] // owners
+    padded_rows = -(-rows // 8) * 8
+    partial = partial.reshape(owners, rows, kv_width)
+    partial = jnp.pad(partial, ((0, 0), (0, padded_rows - rows), (0, 0)))
+    partial = partial.reshape(owners * padded_rows, kv_width)
+    weight_grad = lax.psum_scatter(partial, ("cx", "dp"), scatter_dimension=0, tiled=True)
+    weight_grad = weight_grad[:rows]
+
+    square_total = jnp.sum(weight_grad * weight_grad)
+    square_total = lax.psum(square_total, "dp")
+    square_total = lax.psum(square_total, "cx")
+    square_total = lax.psum(square_total, "cz")
     norm_total = jnp.sqrt(square_total + 1e-06)
     clipped = weight_grad * jnp.minimum(1.0, clip_norm / norm_total)
     new_first = beta_first * first_moment_value + (1.0 - beta_first) * clipped
@@ -178,28 +203,34 @@
 
 
 def solution(mesh):
+    n_ctx = mesh.shape["ctx"]
+    n_dp = mesh.shape["dp"]
+    z_size = Z_SIZE if n_ctx % Z_SIZE == 0 else n_ctx
+    grid = Mesh(mesh.devices.reshape(z_size, n_ctx // z_size, n_dp), ("cz", "cx", "dp"))
+    tokens = P("dp", CTX, None)
+    owner = P(("cz", "cx", "dp"), None)
     return jax.shard_map(
         shards,
-        mesh=mesh,
+        mesh=grid,
         in_specs=(
-            P("dp", "ctx", None),
-            P("dp", "ctx", None),
-            P("dp", "ctx", None),
-            P("dp", "ctx", None),
-            P("dp", "ctx", None),
-            P("dp", "ctx"),
-            P(("ctx", "dp"), None),
-            P(("ctx", "dp"), None),
-            P(("ctx", "dp"), None),
+            tokens,
+            tokens,
+            tokens,
+            tokens,
+            tokens,
+            P("dp", CTX),
+            owner,
+            owner,
+            owner,
         ),
         out_specs=(
-            P("dp", "ctx", None),
-            P("dp", "ctx", None),
-            P("dp", "ctx", None),
-            P(("ctx", "dp"), None),
-            P(("ctx", "dp"), None),
-            P(("ctx", "dp"), None),
-            P("ctx", None),
+            tokens,
+            tokens,
+            tokens,
+            owner,
+            owner,
+            owner,
+            P(CTX, None),
         ),
         check_vma=False,
     )

time: 554 us -> 595 us (1.074)
  blocking collectives: 128 us -> 273 us
  starting transfers between devices: 178 us -> 40.9 us
  waiting for transfers between devices: 109 us -> 148 us
  local copies, waits for them, and re-layouts: 77.8 us -> 52.2 us
  other arithmetic: 13.1 us -> 33.6 us
    all_gather x0 -> x1, blocking collectives: none -> 113 us  [shards(): seg_all = lax.all_gather(segments[0], CTX, axis=0, tiled=True)]
    ppermute x40 -> x16, starting transfers between devices: 144 us -> 40.8 us  [from_behind(): return lax.ppermute(x, CTX, pairs)]
    all_to_all x0 -> x1, blocking collectives: none -> 103 us  [shards(): lax.all_to_all(layer_input[0], 'cz', split_axis=1, concat_axis=0, tiled=T...]
    reduce_scatter x0 -> x1, waiting for transfers between devices: none -> 88.4 us  [shards(): lax.psum_scatter(partial, ('cx', 'dp'), scatter_dimension=0, tiled=True)]
    psum x1 -> x3, blocking collectives: 96.6 us -> 37.8 us  [the longest x1 14.7 us: shards(): square_total = lax.psum(square_total, 'dp')]
    all_to_all x1 -> x0, starting transfers between devices: 31.1 us -> none  [shards(): lax.all_to_all(layer_input[0], 'ctx', split_axis=1, concat_axis=0, tiled=...]
    all_gather x1, waiting for transfers between devices: 42.3 us -> 12.9 us  [shards(): value_group = lax.all_gather(value_out, 'cz', axis=0, tiled=True)]
    concatenate x20 -> x0, local copies, waits for them, and re-layouts: 26 us -> none  [the longest x10 16.3 us: shards(): jnp.concatenate([halo_rows[1], value_state_rows[0]], axis=0)]
  transfers between devices with their start and end apart: 43 -> 18, of which waited for: 7 -> 8; matrix products, arithmetic and copies ran while one was open for 19% -> 9% of each run, Pallas kernels for 0% -> 0%
where the time goes in v1:
time: 595 us; the launch traced here: 593 us
  blocking collectives  273 us (46%)
  waiting for transfers between devices  148 us (25%)
  local copies, waits for them, and re-layouts  52.2 us (9%)
  starting transfers between devices  40.9 us (7%)
  other arithmetic  33.6 us (6%)
  matrix products  29.5 us (5%)
  between operations  15.3 us (3%)
    all_gather x1, blocking collectives, shards(): seg_all = lax.all_gather(segments[0], CTX, axis=0, tiled=True)  113 us
    all_to_all x1, blocking collectives, shards(): lax.all_to_all(layer_input[0], 'cz', split_axis=1, concat_axis=0, tiled=T...  103 us
    reduce_scatter x1, waiting for transfers between devices, shards(): lax.psum_scatter(partial, ('cx', 'dp'), scatter_dimension=0, tiled=True)  88.4 us
    ppermute x16, waiting for transfers between devices, from_behind(): return lax.ppermute(x, CTX, pairs)  47 us
    ppermute x16, starting transfers between devices, from_behind(): return lax.ppermute(x, CTX, pairs)  40.8 us
    all_gather x1, blocking collectives, shards(): lax.all_gather(new_master.astype(jnp.bfloat16), 'dp', axis=0, tiled=True)  19.2 us
    psum x1, blocking collectives, shards(): square_total = lax.psum(square_total, 'dp')  14.7 us
    psum x1, blocking collectives, shards(): square_total = lax.psum(square_total, 'cz')  14.4 us
  transfers between devices with their start and end apart: 18, of which 8 were waited for; matrix products, arithmetic and copies ran while one was open for 9% of the time, Pallas kernels for 0%

profile of v1, /device:TPU:1, one launch (start us, length us, event | category | flops | bytes accessed | tf_op | source)
XLA Modules:
  0.0 592.8 jit_solution(1941559451615078641)
XLA Ops:
  9.5 6.5 %collective-permute-start = (bf16[128,2048]{0,1:T(8,128)(2,1)S(1)}, bf16[128,2048]{0,1:T(8,128)(2,1)}, u32[]{:S(2)}, u32[]{:S(2)}) collective-permute-start(bf16[128,2048]{0,1:T(8,128)(2,1)S(1)} %pad_maximum_fusion), channel_id=1, source_target_pairs={{0,64},{8,72},{16,80},{24,88},{32,96},{40,104},{48,112},{56,120},{... | collective-permute-start | bytes 1572872 | tf_op jit(solution)/shard_map/ppermute | solution.py:38
  16.0 6.5 %collective-permute-start.1 = (bf16[128,2048]{0,1:T(8,128)(2,1)S(1)}, bf16[128,2048]{0,1:T(8,128)(2,1)}, u32[]{:S(2)}, u32[]{:S(2)}) collective-permute-start(bf16[128,2048]{0,1:T(8,128)(2,1)S(1)} %pad_maximum_fusion), channel_id=1, source_target_pairs={{0,56},{8,64},{16,72},{24,80},{32,88},{40,96},{48,104},{56,112},{6... | collective-permute-start | bytes 1572872 | tf_op jit(solution)/shard_map/ppermute | solution.py:38
  22.6 5.5 collective-permute-start.2
  28.0 2.2 collective-permute-start.3
  30.2 1.9 collective-permute-start.4
  32.2 113.3 %all-gather = s32[1,4096]{1,0:T(1,128)S(1)} all-gather(s32[1,128]{1,0:T(1,128)} %param.14), channel_id=2, replica_groups=mesh['cz'=8,'cx'=4,'dp'=8] {'cz','cx'}, dimensions={1}, use_global_device_ids=true | all-gather | bytes 16896 | tf_op jit(solution)/shard_map/all_gather | solution.py:127
  149.9 1.8 collective-permute-start.5
  152.8 4.7 collective-permute-start.6
  161.5 3.4 collective-permute-done.5
  165.2 5.2 collective-permute-done.7
  170.7 1.8 fusion.26
  172.4 6.3 %fusion.29 = (f32[8,2,128]{2,1,0:T(2,128)}, f32[8,2,128,1152]{2,3,1,0:T(8,128)}) fusion(pred[128,1152]{0,1:T(8,128)(4,1)S(1)} %fusion.18, bf16[1152,8,128,1]{0,2,3,1:T(8,128)(2,1)S(1)} %bitcast.105, bf16[128,8,2,128]{0,3,2,1:T(8,128)(2,1)S(1)} %bitcast.121), kind=kOutput, calls=%fused_computation.82 | convolution fusion | flops 613418112 | bytes 12476416 | tf_op jit(solution)/shard_map/sub | solution.py:75
  178.7 4.8 fusion.8
  183.6 3.9 fusion.30
  189.7 3.5 fusion.2
  194.7 1.8 copy.106
  196.5 6.0 %fusion.31 = (bf16[1152,8,128]{0,2,1:T(8,128)(2,1)S(1)}, f32[1152,8,128]{0,2,1:T(8,128)}) fusion(bf16[8,2,128,1152]{2,3,1,0:T(8,128)(2,1)} %fusion.2, bf16[128,8,2,128]{0,3,2,1:T(8,128)(2,1)S(1)} %bitcast.122), kind=kOutput, calls=%fused_computation.84 | convolution fusion | flops 606339072 | bytes 12320768 | tf_op jit(solution)/shard_map/grte,tgrd->egd/dot_general | solution.py:95
  204.9 1.9 pad_maximum_fusion.8
  208.3 1.8 copy.104
  210.1 1.8 copy.103
  211.9 1.9 pad_maximum_fusion.7
  215.0 1.8 copy.102
  216.8 1.8 copy.101
  218.6 1.9 pad_maximum_fusion.6
  221.8 1.8 copy.100
  223.6 1.8 copy.99
  225.4 1.9 pad_maximum_fusion.5
  228.5 1.8 copy.98
  230.3 1.8 copy.97
  232.1 1.9 pad_maximum_fusion.4
  237.2 1.8 pad_maximum_fusion.3
  242.1 1.8 pad_maximum_fusion.1
  250.6 1.9 slice.190
  259.4 6.1 %collective-permute-done.10 = bf16[128,2048]{1,0:T(8,128)(2,1)} collective-permute-done((bf16[128,2048]{1,0:T(8,128)(2,1)}, bf16[128,2048]{1,0:T(8,128)(2,1)}, u32[]{:S(2)}, u32[]{:S(2)}) %collective-permute-start.10) | collective-permute-done | bytes 524320 | tf_op jit(solution)/shard_map/ppermute | solution.py:38
  266.7 8.8 %collective-permute-done.9 = bf16[128,2048]{1,0:T(8,128)(2,1)} collective-permute-done((bf16[128,2048]{1,0:T(8,128)(2,1)}, bf16[128,2048]{1,0:T(8,128)(2,1)}, u32[]{:S(2)}, u32[]{:S(2)}) %collective-permute-start.9) | collective-permute-done | bytes 524320 | tf_op jit(solution)/shard_map/ppermute | solution.py:38
  276.6 21.9 %collective-permute-done.8 = bf16[128,2048]{1,0:T(8,128)(2,1)} collective-permute-done((bf16[128,2048]{1,0:T(8,128)(2,1)}, bf16[128,2048]{1,0:T(8,128)(2,1)}, u32[]{:S(2)}, u32[]{:S(2)}) %collective-permute-start.8) | collective-permute-done | bytes 524320 | tf_op jit(solution)/shard_map/ppermute | solution.py:38
  301.4 2.5 copy.108
  304.0 102.7 %all_to_all.19 = bf16[128,8,672]{0,2,1:T(8,128)(2,1)} all-to-all(bf16[128,8,672]{0,2,1:T(8,128)(2,1)} %bitcast.115), channel_id=1, replica_groups=mesh['cz'=8,'cx'=4,'dp'=8] {'cz'}, dimensions={1} | all-to-all | bytes 2752512 | tf_op jit(solution)/shard_map/all_to_all | solution.py:166
  406.7 12.9 %all-gather.4.cloned.1.call-done = bf16[1024,1024]{1,0:T(8,128)(2,1)} async-done(((bf16[128,1024]{1,0:T(8,128)(2,1)}), bf16[1024,1024]{1,0:T(8,128)(2,1)}) %all-gather.4.cloned.1.call-update) | async-done | bytes 2097168 | tf_op jit(solution)/shard_map/all_gather | solution.py:167
  419.6 5.2 convolution_bitcast_fusion.1
  424.8 3.1 reshape.85
  428.0 4.2 pad.5
  432.2 88.4 %reduce-scatter.2.cloned.1.call-done = f32[24,1024]{1,0:T(8,128)} async-done(((f32[768,1024]{1,0:T(8,128)}), f32[24,1024]{1,0:T(8,128)}) %reduce-scatter.2.cloned.1.call-update) | async-done | bytes 98320 | tf_op jit(solution)/shard_map/reduce_scatter | solution.py:180
  522.1 14.7 %psum.21 = f32[]{:T(128)} all-reduce(f32[]{:T(128)} %multiply_reduce_fusion), channel_id=1, replica_groups=mesh['cz'=8,'cx'=4,'dp'=8] {'dp'}, use_global_device_ids=true, to_apply=%region_5.6 | all-reduce | flops 1 | bytes 8 | tf_op jit(solution)/shard_map/psum | solution.py:184
  536.8 3.4 fusion.12
  540.3 8.7 %psum.22 = f32[]{:T(128)} all-reduce(f32[]{:T(128)} %psum.21), channel_id=1, replica_groups=mesh['cz'=8,'cx'=4,'dp'=8] {'cx'}, use_global_device_ids=true, to_apply=%region_6.7 | all-reduce | flops 1 | bytes 8 | tf_op jit(solution)/shard_map/psum | solution.py:185
  550.0 14.4 %psum.23 = f32[]{:T(128)} all-reduce(f32[]{:T(128)} %psum.22), channel_id=1, replica_groups=mesh['cz'=8,'cx'=4,'dp'=8] {'cz'}, use_global_device_ids=true, to_apply=%region_7.8 | all-reduce | flops 1 | bytes 8 | tf_op jit(solution)/shard_map/psum | solution.py:186
  565.9 19.2 %all-gather.1 = bf16[8,21,1024]{2,1,0:T(8,128)(2,1)S(1)} all-gather(bf16[1,21,1024]{2,1,0:T(8,128)(2,1)S(1)} %get-tuple-element.28), channel_id=1, replica_groups=mesh['cz'=8,'cx'=4,'dp'=8] {'dp'}, dimensions={0}, use_global_device_ids=true | all-gather | bytes 387072 | tf_op jit(solution)/shard_map/all_gather | solution.py:193
  (91 shorter events, 52.7 us)
Async XLA Ops:
  7.2 412.4 %all-gather.4.cloned.1.call-start = ((), (), s32[]{:S(2)}) async-start(), calls=%async_computation.2 | async-start | bytes 2359296 | tf_op jit(solution)/shard_map/all_gather | solution.py:167
  9.5 140.4 %collective-permute-start = (bf16[128,2048]{0,1:T(8,128)(2,1)S(1)}, bf16[128,2048]{0,1:T(8,128)(2,1)}, u32[]{:S(2)}, u32[]{:S(2)}) collective-permute-start(bf16[128,2048]{0,1:T(8,128)(2,1)S(1)} %pad_maximum_fusion), channel_id=1, source_target_pairs={{0,64},{8,72},{16,80},{24,88},{32,96},{40,104},{48,112},{56,120},{... | collective-permute-start | bytes 1572872 | tf_op jit(solution)/shard_map/ppermute | solution.py:38
  16.0 136.8 %collective-permute-start.1 = (bf16[128,2048]{0,1:T(8,128)(2,1)S(1)}, bf16[128,2048]{0,1:T(8,128)(2,1)}, u32[]{:S(2)}, u32[]{:S(2)}) collective-permute-start(bf16[128,2048]{0,1:T(8,128)(2,1)S(1)} %pad_maximum_fusion), channel_id=1, source_target_pairs={{0,56},{8,64},{16,72},{24,80},{32,88},{40,96},{48,104},{56,112},{6... | collective-permute-start | bytes 1572872 | tf_op jit(solution)/shard_map/ppermute | solution.py:38
  22.6 136.2 %collective-permute-start.2 = (bf16[128,2048]{0,1:T(8,128)(2,1)S(1)}, bf16[128,2048]{0,1:T(8,128)(2,1)}, u32[]{:S(2)}, u32[]{:S(2)}) collective-permute-start(bf16[128,2048]{0,1:T(8,128)(2,1)S(1)} %pad_maximum_fusion), channel_id=1, source_target_pairs={{0,48},{8,56},{16,64},{24,72},{32,80},{40,88},{48,96},{56,104},{64... | collective-permute-start | bytes 1572872 | tf_op jit(solution)/shard_map/ppermute | solution.py:38
  28.0 133.2 %collective-permute-start.3 = (bf16[128,2048]{0,1:T(8,128)(2,1)S(1)}, bf16[128,2048]{0,1:T(8,128)(2,1)S(1)}, u32[]{:S(2)}, u32[]{:S(2)}) collective-permute-start(bf16[128,2048]{0,1:T(8,128)(2,1)S(1)} %pad_maximum_fusion), channel_id=1, source_target_pairs={{0,40},{8,48},{16,56},{24,64},{32,72},{40,80},{48,88},{56,96},{64,... | collective-permute-start | bytes 1572872 | tf_op jit(solution)/shard_map/ppermute | solution.py:38
  30.2 131.1 %collective-permute-start.4 = (bf16[128,2048]{0,1:T(8,128)(2,1)S(1)}, bf16[128,2048]{0,1:T(8,128)(2,1)S(1)}, u32[]{:S(2)}, u32[]{:S(2)}) collective-permute-start(bf16[128,2048]{0,1:T(8,128)(2,1)S(1)} %pad_maximum_fusion), channel_id=1, source_target_pairs={{0,32},{8,40},{16,48},{24,56},{32,64},{40,72},{48,80},{56,88},{64,... | collective-permute-start | bytes 1572872 | tf_op jit(solution)/shard_map/ppermute | solution.py:38
  149.9 15.0 %collective-permute-start.5 = (bf16[128,2048]{0,1:T(8,128)(2,1)S(1)}, bf16[128,2048]{0,1:T(8,128)(2,1)S(1)}, u32[]{:S(2)}, u32[]{:S(2)}) collective-permute-start(bf16[128,2048]{0,1:T(8,128)(2,1)S(1)} %pad_maximum_fusion), channel_id=1, source_target_pairs={{0,24},{8,32},{16,40},{24,48},{32,56},{40,64},{48,72},{56,80},{64,... | collective-permute-start | bytes 1572872 | tf_op jit(solution)/shard_map/ppermute | solution.py:38
  152.8 12.2 %collective-permute-start.6 = (bf16[128,2048]{0,1:T(8,128)(2,1)S(1)}, bf16[128,2048]{0,1:T(8,128)(2,1)S(1)}, u32[]{:S(2)}, u32[]{:S(2)}) collective-permute-start(bf16[128,2048]{0,1:T(8,128)(2,1)S(1)} %pad_maximum_fusion), channel_id=1, source_target_pairs={{0,16},{8,24},{16,32},{24,40},{32,48},{40,56},{48,64},{56,72},{64,... | collective-permute-start | bytes 1572872 | tf_op jit(solution)/shard_map/ppermute | solution.py:38
  158.7 11.7 %collective-permute-start.7 = (bf16[128,2048]{0,1:T(8,128)(2,1)S(1)}, bf16[128,2048]{0,1:T(8,128)(2,1)S(1)}, u32[]{:S(2)}, u32[]{:S(2)}) collective-permute-start(bf16[128,2048]{0,1:T(8,128)(2,1)S(1)} %pad_maximum_fusion), channel_id=1, source_target_pairs={{0,8},{8,16},{16,24},{24,32},{32,40},{40,48},{48,56},{56,64},{64,7... | collective-permute-start | bytes 1572872 | tf_op jit(solution)/shard_map/ppermute | solution.py:38
  183.6 4.0 copy-start
  183.6 5.0 slice-start
  183.6 5.8 slice-start.1
  187.5 2.1 slice-start.2
  187.5 2.1 copy-start.6
  204.9 30.4 %copy-start.1 = (bf16[128,8,128]{0,2,1:T(8,128)(2,1)S(1)}, bf16[128,8,128]{0,2,1:T(8,128)(2,1)}, u32[]{:S(2)}) copy-start(bf16[128,8,128]{0,2,1:T(8,128)(2,1)} %get-tuple-element.50) | copy-start | bytes 786436
  206.8 37.1 %collective-permute-start.15 = (bf16[128,2048]{1,0:T(8,128)(2,1)}, bf16[128,2048]{1,0:T(8,128)(2,1)}, u32[]{:S(2)}, u32[]{:S(2)}) collective-permute-start(bf16[128,2048]{1,0:T(8,128)(2,1)} %pad_maximum_fusion.8), channel_id=1, source_target_pairs={{64,0},{72,8},{80,16},{88,24},{96,32},{104,40},{112,48},{120,56},{... | collective-permute-start | bytes 1572872 | tf_op jit(solution)/shard_map/ppermute | solution.py:38
  213.8 32.9 %collective-permute-start.14 = (bf16[128,2048]{1,0:T(8,128)(2,1)}, bf16[128,2048]{1,0:T(8,128)(2,1)}, u32[]{:S(2)}, u32[]{:S(2)}) collective-permute-start(bf16[128,2048]{1,0:T(8,128)(2,1)} %pad_maximum_fusion.7), channel_id=1, source_target_pairs={{56,0},{64,8},{72,16},{80,24},{88,32},{96,40},{104,48},{112,56},{1... | collective-permute-start | bytes 1572872 | tf_op jit(solution)/shard_map/ppermute | solution.py:38
  220.5 27.5 %collective-permute-start.13 = (bf16[128,2048]{1,0:T(8,128)(2,1)}, bf16[128,2048]{1,0:T(8,128)(2,1)}, u32[]{:S(2)}, u32[]{:S(2)}) collective-permute-start(bf16[128,2048]{1,0:T(8,128)(2,1)} %pad_maximum_fusion.6), channel_id=1, source_target_pairs={{48,0},{56,8},{64,16},{72,24},{80,32},{88,40},{96,48},{104,56},{11... | collective-permute-start | bytes 1572872 | tf_op jit(solution)/shard_map/ppermute | solution.py:38
  227.3 29.8 %collective-permute-start.12 = (bf16[128,2048]{1,0:T(8,128)(2,1)}, bf16[128,2048]{1,0:T(8,128)(2,1)}, u32[]{:S(2)}, u32[]{:S(2)}) collective-permute-start(bf16[128,2048]{1,0:T(8,128)(2,1)} %pad_maximum_fusion.5), channel_id=1, source_target_pairs={{40,0},{48,8},{56,16},{64,24},{72,32},{80,40},{88,48},{96,56},{104... | collective-permute-start | bytes 1572872 | tf_op jit(solution)/shard_map/ppermute | solution.py:38
  234.0 24.3 %collective-permute-start.11 = (bf16[128,2048]{1,0:T(8,128)(2,1)}, bf16[128,2048]{1,0:T(8,128)(2,1)}, u32[]{:S(2)}, u32[]{:S(2)}) collective-permute-start(bf16[128,2048]{1,0:T(8,128)(2,1)} %pad_maximum_fusion.4), channel_id=1, source_target_pairs={{32,0},{40,8},{48,16},{56,24},{64,32},{72,40},{80,48},{88,56},{96,... | collective-permute-start | bytes 1572872 | tf_op jit(solution)/shard_map/ppermute | solution.py:38
  243.9 21.6 %collective-permute-start.10 = (bf16[128,2048]{1,0:T(8,128)(2,1)}, bf16[128,2048]{1,0:T(8,128)(2,1)}, u32[]{:S(2)}, u32[]{:S(2)}) collective-permute-start(bf16[128,2048]{1,0:T(8,128)(2,1)} %pad_maximum_fusion.3), channel_id=1, source_target_pairs={{24,0},{32,8},{40,16},{48,24},{56,32},{64,40},{72,48},{80,56},{88,... | collective-permute-start | bytes 1572872 | tf_op jit(solution)/shard_map/ppermute | solution.py:38
  246.7 28.7 %collective-permute-start.9 = (bf16[128,2048]{1,0:T(8,128)(2,1)}, bf16[128,2048]{1,0:T(8,128)(2,1)}, u32[]{:S(2)}, u32[]{:S(2)}) collective-permute-start(bf16[128,2048]{1,0:T(8,128)(2,1)} %pad_maximum_fusion.2), channel_id=1, source_target_pairs={{16,0},{24,8},{32,16},{40,24},{48,32},{56,40},{64,48},{72,56},{80,... | collective-permute-start | bytes 1572872 | tf_op jit(solution)/shard_map/ppermute | solution.py:38
  248.0 50.5 %collective-permute-start.8 = (bf16[128,2048]{1,0:T(8,128)(2,1)}, bf16[128,2048]{1,0:T(8,128)(2,1)}, u32[]{:S(2)}, u32[]{:S(2)}) collective-permute-start(bf16[128,2048]{1,0:T(8,128)(2,1)} %pad_maximum_fusion.1), channel_id=1, source_target_pairs={{8,0},{16,8},{24,16},{32,24},{40,32},{48,40},{56,48},{64,56},{72,6... | collective-permute-start | bytes 1572872 | tf_op jit(solution)/shard_map/ppermute | solution.py:38
  301.4 219.2 %reduce-scatter.2.cloned.1.call-start = ((), (), s32[]{:S(2)}) async-start(), calls=%async_computation.3 | async-start | bytes 3244032 | tf_op jit(solution)/shard_map/reduce_scatter | solution.py:180
  536.8 28.2 %copy-start.2 = (f32[24,1024]{1,0:T(8,128)S(1)}, f32[24,1024]{1,0:T(8,128)}, u32[]{:S(2)}) copy-start(f32[24,1024]{1,0:T(8,128)} %reduce-scatter.2.cloned.1.call-done) | copy-start | bytes 294916
  536.8 28.3 %copy-start.3 = (f32[21,1024]{1,0:T(8,128)S(1)}, f32[21,1024]{1,0:T(8,128)}, u32[]{:S(2)}) copy-start(f32[21,1024]{1,0:T(8,128)} %param.15) | copy-start | bytes 258052
  536.8 28.3 %copy-start.4 = (f32[21,1024]{1,0:T(8,128)S(1)}, f32[21,1024]{1,0:T(8,128)}, u32[]{:S(2)}) copy-start(f32[21,1024]{1,0:T(8,128)} %param.16) | copy-start | bytes 258052
  536.8 28.3 %copy-start.5 = (f32[21,1024]{1,0:T(8,128)S(1)}, f32[21,1024]{1,0:T(8,128)}, u32[]{:S(2)}) copy-start(f32[21,1024]{1,0:T(8,128)} %param.17) | copy-start | bytes 258052
Sparse Core Ops, SparseCore 0:
  301.5 118.0 all-gather.3
  432.3 88.2 reduce-scatter.1

commit v2 on v1

--- a/solution.py
+++ b/solution.py
@@ -36,6 +36,11 @@
     count = ctx_size()
     pairs = [(i, i + by) for i in range(count) if 0 <= i + by < count]
     return lax.ppermute(x, CTX, pairs)
+
+
+def cyclic(x, axis, by):
+    count = lax.axis_size(axis)
+    return lax.ppermute(x, axis, [(i, (i + by) % count) for i in range(count)])
 
 
 def attend(
@@ -124,16 +129,14 @@
     front_len = peer_count * shard_length
     position = ctx_index() * shard_length
 
-    seg_all = lax.all_gather(segments[0], CTX, axis=0, tiled=True)
-    seg_pad = jnp.concatenate([jnp.full((front_len,), -1, jnp.int32), seg_all], axis=0)
-    seg_key = lax.dynamic_slice_in_dim(seg_pad, position, front_len + shard_length, 0)
     seg_query = segments[0]
-
-    own_kv = jnp.concatenate([key_states[0], value_state_rows[0]], axis=1)
+    seg_cols = jnp.broadcast_to(seg_query.astype(jnp.bfloat16)[:, None], (shard_length, 128))
+    own_kv = jnp.concatenate([key_states[0], value_state_rows[0], seg_cols], axis=1)
     incoming = [from_behind(own_kv, distance) for distance in range(peer_count, 0, -1)]
     kv_rows = jnp.concatenate(incoming + [own_kv], axis=0)
     key_row_block = kv_rows[:, :kv_width]
-    value_row_block = kv_rows[:, kv_width:]
+    value_row_block = kv_rows[:, kv_width : 2 * kv_width]
+    seg_key = kv_rows[:, 2 * kv_width]
     index_query = position + jnp.arange(shard_length, dtype=jnp.int32)
     index_key = position - front_len + jnp.arange(front_len + shard_length, dtype=jnp.int32)
     query_gradient, key_gradient, value_gradient = attend(
@@ -141,7 +144,7 @@
         key_row_block,
         value_row_block,
         grad_out[0],
-        seg_query,
+        seg_query.astype(jnp.bfloat16),
         seg_key,
         index_query,
         index_key,
@@ -163,22 +166,40 @@
     key_out = key_sum.astype(jnp.bfloat16)
     value_out = value_sum.astype(jnp.bfloat16)
 
-    feature_block = lax.all_to_all(layer_input[0], "cz", split_axis=1, concat_axis=0, tiled=True)
-    value_group = lax.all_gather(value_out, "cz", axis=0, tiled=True)
+    nz = lax.axis_size("cz")
+    iz = lax.axis_index("cz")
+    x_own = layer_input[0]
+    width = x_own.shape[1] // nz
+    x_list = [lax.dynamic_slice_in_dim(x_own, iz * width, width, 1)]
+    v_list = [value_out]
+    for shift in range(1, nz):
+        target = (iz + shift) % nz
+        piece = jnp.concatenate(
+            [lax.dynamic_slice_in_dim(x_own, target * width, width, 1), value_out], axis=1
+        )
+        got = cyclic(piece, "cz", shift)
+        x_list.append(got[:, :width])
+        v_list.append(got[:, width:])
     partial = lax.dot_general(
-        feature_block,
-        value_group,
+        jnp.concatenate(x_list, axis=0),
+        jnp.concatenate(v_list, axis=0),
         (((0,), (0,)), ((), ())),
         preferred_element_type=jnp.float32,
     )
-    owners = lax.axis_size("cx") * lax.axis_size("dp")
-    rows = partial.shape[0] // owners
-    padded_rows = -(-rows // 8) * 8
-    partial = partial.reshape(owners, rows, kv_width)
-    partial = jnp.pad(partial, ((0, 0), (0, padded_rows - rows), (0, 0)))
-    partial = partial.reshape(owners * padded_rows, kv_width)
-    weight_grad = lax.psum_scatter(partial, ("cx", "dp"), scatter_dimension=0, tiled=True)
-    weight_grad = weight_grad[:rows]
+    ncx = lax.axis_size("cx")
+    ndp = lax.axis_size("dp")
+    rows = width // (ncx * ndp)
+    partial = partial.reshape(ncx, ndp, rows, kv_width)
+    idp = lax.axis_index("dp")
+    stage = lax.dynamic_index_in_dim(partial, idp, 1, keepdims=False)
+    for shift in range(1, ndp):
+        target = (idp + shift) % ndp
+        stage = stage + cyclic(lax.dynamic_index_in_dim(partial, target, 1, keepdims=False), "dp", shift)
+    icx = lax.axis_index("cx")
+    weight_grad = lax.dynamic_index_in_dim(stage, icx, 0, keepdims=False)
+    for shift in range(1, ncx):
+        target = (icx + shift) % ncx
+        weight_grad = weight_grad + cyclic(lax.dynamic_index_in_dim(stage, target, 0, keepdims=False), "cx", shift)
 
     square_total = jnp.sum(weight_grad * weight_grad)
     square_total = lax.psum(square_total, "dp")

time: 595 us -> 573 us (0.963)
  blocking collectives: 273 us -> 62.4 us
  starting transfers between devices: 40.9 us -> 200 us
  waiting for transfers between devices: 148 us -> 173 us
  between operations: 15.3 us -> 2.26 us
  other arithmetic: 33.6 us -> 42.9 us
  local copies, waits for them, and re-layouts: 52.2 us -> 60.3 us
    ppermute x0 -> x17, starting transfers between devices: none -> 128 us  [cyclic(): return lax.ppermute(x, axis, [(i, (i + by) % count) for i in range(count)])]
    all_gather x1 -> x0, blocking collectives: 113 us -> none  [shards(): seg_all = lax.all_gather(segments[0], CTX, axis=0, tiled=True)]
    all_to_all x1 -> x0, blocking collectives: 103 us -> none  [shards(): lax.all_to_all(layer_input[0], 'cz', split_axis=1, concat_axis=0, tiled=T...]
    reduce_scatter x1 -> x0, waiting for transfers between devices: 88.4 us -> none  [shards(): lax.psum_scatter(partial, ('cx', 'dp'), scatter_dimension=0, tiled=True)]
    ppermute x16, waiting for transfers between devices: 47 us -> 128 us  [from_behind(): return lax.ppermute(x, CTX, pairs)]
    ppermute x0 -> x17, waiting for transfers between devices: none -> 44.8 us  [cyclic(): return lax.ppermute(x, axis, [(i, (i + by) % count) for i in range(count)])]
    ppermute x16, starting transfers between devices: 40.8 us -> 71.7 us  [from_behind(): return lax.ppermute(x, CTX, pairs)]
    all_gather x1 -> x0, waiting for transfers between devices: 12.9 us -> none  [shards(): value_group = lax.all_gather(value_out, 'cz', axis=0, tiled=True)]
  transfers between devices with their start and end apart: 18 -> 33, of which waited for: 8 -> 11; matrix products, arithmetic and copies ran while one was open for 9% -> 11% of each run, Pallas kernels for 0% -> 0%
where the time goes in v2:
time: 573 us; the launch traced here: 570 us
  starting transfers between devices  200 us (35%)
  waiting for transfers between devices  173 us (30%)
  blocking collectives  62.4 us (11%)
  local copies, waits for them, and re-layouts  60.3 us (11%)
  other arithmetic  42.9 us (7%)
  matrix products  30.3 us (5%)
    ppermute x17, starting transfers between devices, cyclic(): return lax.ppermute(x, axis, [(i, (i + by) % count) for i in range(count)])  128 us
    ppermute x16, waiting for transfers between devices, from_behind(): return lax.ppermute(x, CTX, pairs)  128 us
    ppermute x16, starting transfers between devices, from_behind(): return lax.ppermute(x, CTX, pairs)  71.7 us
    ppermute x17, waiting for transfers between devices, cyclic(): return lax.ppermute(x, axis, [(i, (i + by) % count) for i in range(count)])  44.8 us
    unnamed x98, local copies, waits for them, and re-layouts  21.1 us
    psum x1, blocking collectives, shards(): square_total = lax.psum(square_total, 'dp')  20.1 us
    all_gather x1, blocking collectives, shards(): lax.all_gather(new_master.astype(jnp.bfloat16), 'dp', axis=0, tiled=True)  19.2 us
    psum x1, blocking collectives, shards(): square_total = lax.psum(square_total, 'cz')  14.1 us
  transfers between devices with their start and end apart: 33, of which 11 were waited for; matrix products, arithmetic and copies ran while one was open for 11% of the time, Pallas kernels for 0%

profile of v2, /device:TPU:1, one launch (start us, length us, event | category | flops | bytes accessed | tf_op | source)
XLA Modules:
  0.0 570.3 jit_solution(13902186449127180422)
XLA Ops:
  3.6 6.6 %collective-permute-start = (bf16[128,2176]{0,1:T(8,128)(2,1)S(1)}, bf16[128,2176]{0,1:T(8,128)(2,1)}, u32[]{:S(2)}, u32[]{:S(2)}) collective-permute-start(bf16[128,2176]{0,1:T(8,128)(2,1)S(1)} %pad_maximum_fusion.7), channel_id=1, source_target_pairs={{0,64},{8,72},{16,80},{24,88},{32,96},{40,104},{48,112},{56,120},{... | collective-permute-start | bytes 1671176 | tf_op jit(solution)/shard_map/ppermute | solution.py:38
  10.2 6.5 %collective-permute-start.1 = (bf16[128,2176]{0,1:T(8,128)(2,1)S(1)}, bf16[128,2176]{0,1:T(8,128)(2,1)}, u32[]{:S(2)}, u32[]{:S(2)}) collective-permute-start(bf16[128,2176]{0,1:T(8,128)(2,1)S(1)} %pad_maximum_fusion.7), channel_id=1, source_target_pairs={{0,56},{8,64},{16,72},{24,80},{32,88},{40,96},{48,104},{56,112},{6... | collective-permute-start | bytes 1671176 | tf_op jit(solution)/shard_map/ppermute | solution.py:38
  16.7 4.7 collective-permute-start.2
  21.4 2.2 collective-permute-start.3
  23.6 2.6 collective-permute-start.4
  27.6 2.0 copy.122
  29.6 3.3 collective-permute-start.5
  34.1 20.4 %collective-permute-start.6 = (bf16[128,2176]{0,1:T(8,128)(2,1)S(1)}, bf16[128,2176]{0,1:T(8,128)(2,1)S(1)}, u32[]{:S(2)}, u32[]{:S(2)}) collective-permute-start(bf16[128,2176]{0,1:T(8,128)(2,1)S(1)} %pad_maximum_fusion.7), channel_id=1, source_target_pairs={{0,16},{8,24},{16,32},{24,40},{32,48},{40,56},{48,64},{56,72},{64,... | collective-permute-start | bytes 1671176 | tf_op jit(solution)/shard_map/ppermute | solution.py:38
  55.7 14.5 %collective-permute-start.7 = (bf16[128,2176]{0,1:T(8,128)(2,1)S(1)}, bf16[128,2176]{0,1:T(8,128)(2,1)S(1)}, u32[]{:S(2)}, u32[]{:S(2)}) collective-permute-start(bf16[128,2176]{0,1:T(8,128)(2,1)S(1)} %pad_maximum_fusion.7), channel_id=1, source_target_pairs={{0,8},{8,16},{16,24},{24,32},{32,40},{40,48},{48,56},{56,64},{64,7... | collective-permute-start | bytes 1671176 | tf_op jit(solution)/shard_map/ppermute | solution.py:38
  70.9 10.0 %collective-permute-done.7 = bf16[128,2176]{0,1:T(8,128)(2,1)S(1)} collective-permute-done((bf16[128,2176]{0,1:T(8,128)(2,1)S(1)}, bf16[128,2176]{0,1:T(8,128)(2,1)S(1)}, u32[]{:S(2)}, u32[]{:S(2)}) %collective-permute-start.7) | collective-permute-done | bytes 557088 | tf_op jit(solution)/shard_map/ppermute | solution.py:38
  84.7 6.6 %fusion.37 = (f32[8,2,128]{2,1,0:T(2,128)S(1)}, f32[8,2,128,1152]{2,3,1,0:T(8,128)}) fusion(pred[128,1152]{0,1:T(8,128)(4,1)} %fusion.16, bf16[1152,8,128,1]{0,2,3,1:T(8,128)(2,1)S(1)} %bitcast.151, bf16[128,8,2,128]{0,3,2,1:T(8,128)(2,1)S(1)} %bitcast.165), kind=kOutput, calls=%fused_computation.129 | convolution fusion | flops 613418112 | bytes 12476416 | tf_op jit(solution)/shard_map/sub | solution.py:80
  91.3 4.8 fusion.8
  96.2 3.9 fusion.38
  102.2 3.6 fusion.2
  109.2 6.1 %fusion.39 = (bf16[1152,8,128]{0,2,1:T(8,128)(2,1)S(1)}, f32[1152,8,128]{0,2,1:T(8,128)}) fusion(bf16[8,2,128,1152]{2,3,1,0:T(8,128)(2,1)} %fusion.2, bf16[128,8,2,128]{0,3,2,1:T(8,128)(2,1)S(1)} %bitcast.166), kind=kOutput, calls=%fused_computation.131 | convolution fusion | flops 606339072 | bytes 12320768 | tf_op jit(solution)/shard_map/grte,tgrd->egd/dot_general | solution.py:100
  151.0 104.6 %collective-permute-done.15 = bf16[128,2048]{1,0:T(8,128)(2,1)} collective-permute-done((bf16[128,2048]{1,0:T(8,128)(2,1)}, bf16[128,2048]{1,0:T(8,128)(2,1)}, u32[]{:S(2)}, u32[]{:S(2)}) %collective-permute-start.15) | collective-permute-done | bytes 524320 | tf_op jit(solution)/shard_map/ppermute | solution.py:38
  259.6 3.2 dynamic-slice_bitcast_fusion.7
  271.8 10.7 %collective-permute-done.10 = bf16[128,2048]{1,0:T(8,128)(2,1)} collective-permute-done((bf16[128,2048]{1,0:T(8,128)(2,1)}, bf16[128,2048]{1,0:T(8,128)(2,1)}, u32[]{:S(2)}, u32[]{:S(2)}) %collective-permute-start.10) | collective-permute-done | bytes 524320 | tf_op jit(solution)/shard_map/ppermute | solution.py:38
  285.2 2.3 collective-permute-done.8
  290.6 2.0 pad_maximum_fusion
  292.6 23.8 %collective-permute-start.16 = (bf16[128,1696]{1,0:T(8,128)(2,1)}, bf16[128,1696]{1,0:T(8,128)(2,1)}, u32[]{:S(2)}, u32[]{:S(2)}) collective-permute-start(bf16[128,1696]{1,0:T(8,128)(2,1)} %get-tuple-element.77), channel_id=1, source_target_pairs={{0,32},{32,64},{64,96},{96,128},{128,160},{160,192},{192,224},{224... | collective-permute-start | bytes 1302536 | tf_op jit(solution)/shard_map/ppermute | solution.py:43
  317.4 24.0 %collective-permute-start.17 = (bf16[128,1696]{1,0:T(8,128)(2,1)}, bf16[128,1696]{1,0:T(8,128)(2,1)S(1)}, u32[]{:S(2)}, u32[]{:S(2)}) collective-permute-start(bf16[128,1696]{1,0:T(8,128)(2,1)} %get-tuple-element.76), channel_id=1, source_target_pairs={{0,64},{32,96},{64,128},{96,160},{128,192},{160,224},{192,0},{224,... | collective-permute-start | bytes 1302536 | tf_op jit(solution)/shard_map/ppermute | solution.py:43
  341.4 4.8 collective-permute-start.18
  346.3 4.2 collective-permute-start.20
  350.5 6.3 %collective-permute-start.21 = (bf16[128,1696]{1,0:T(8,128)(2,1)}, bf16[128,1696]{1,0:T(8,128)(2,1)S(1)}, u32[]{:S(2)}, u32[]{:S(2)}) collective-permute-start(bf16[128,1696]{1,0:T(8,128)(2,1)} %get-tuple-element.75), channel_id=1, source_target_pairs={{0,192},{32,224},{64,0},{96,32},{128,64},{160,96},{192,128},{224,1... | collective-permute-start | bytes 1302536 | tf_op jit(solution)/shard_map/ppermute | solution.py:43
  359.6 5.4 collective-permute-done.17
  364.9 39.4 %collective-permute-start.22 = (bf16[128,1696]{1,0:T(8,128)(2,1)}, bf16[128,1696]{1,0:T(8,128)(2,1)S(1)}, u32[]{:S(2)}, u32[]{:S(2)}) collective-permute-start(bf16[128,1696]{1,0:T(8,128)(2,1)} %get-tuple-element.71), channel_id=1, source_target_pairs={{0,224},{32,0},{64,32},{96,64},{128,96},{160,128},{192,160},{224,1... | collective-permute-start | bytes 1302536 | tf_op jit(solution)/shard_map/ppermute | solution.py:43
  405.2 6.9 %collective-permute-done.18 = bf16[128,1696]{1,0:T(8,128)(2,1)S(1)} collective-permute-done((bf16[128,1696]{1,0:T(8,128)(2,1)}, bf16[128,1696]{1,0:T(8,128)(2,1)S(1)}, u32[]{:S(2)}, u32[]{:S(2)}) %collective-permute-start.18) | collective-permute-done | bytes 434208 | tf_op jit(solution)/shard_map/ppermute | solution.py:43
  414.7 5.6 collective-permute-done.21
  421.1 5.6 collective-permute-done.22
  427.6 4.7 fusion.40
  432.4 3.3 reshape.91
  435.6 3.1 dynamic-slice_bitcast_fusion.6
  439.6 2.7 collective-permute-start.28
  443.1 2.0 collective-permute-start.26
  446.2 4.6 collective-permute-done.29
  452.9 8.6 %collective-permute-start.23 = (f32[4,21,1024]{2,1,0:T(8,128)}, f32[4,21,1024]{2,1,0:T(8,128)}, u32[]{:S(2)}, u32[]{:S(2)}) collective-permute-start(f32[4,21,1024]{2,1,0:T(8,128)} %get-tuple-element.38), channel_id=1, source_target_pairs={{0,1},{1,2},{2,3},{3,4},{4,5},{5,6},{6,7},{7,0},{8,9},{9,10},{10,1... | collective-permute-start | bytes 1032200 | tf_op jit(solution)/shard_map/ppermute | solution.py:43
  461.5 14.7 %collective-permute-done.27 = f32[4,21,1024]{2,1,0:T(8,128)} collective-permute-done((f32[4,21,1024]{2,1,0:T(8,128)}, f32[4,21,1024]{2,1,0:T(8,128)}, u32[]{:S(2)}, u32[]{:S(2)}) %collective-permute-start.27) | collective-permute-done | bytes 344096 | tf_op jit(solution)/shard_map/ppermute | solution.py:43
  478.2 2.1 fusion.24
  481.8 7.4 %collective-permute-start.32 = (f32[21,1024]{1,0:T(8,128)}, f32[21,1024]{1,0:T(8,128)S(1)}, u32[]{:S(2)}, u32[]{:S(2)}) collective-permute-start(f32[21,1024]{1,0:T(8,128)} %get-tuple-element.69), channel_id=1, source_target_pairs={{0,24},{8,0},{16,8},{24,16},{1,25},{9,1},{17,9},{25,17},{2,26},{10... | collective-permute-start | bytes 258056 | tf_op jit(solution)/shard_map/ppermute | solution.py:43
  489.7 4.2 fusion.10
  493.9 2.2 copy.106
  499.6 20.1 %psum.21 = f32[]{:T(128)} all-reduce(f32[]{:T(128)} %get-tuple-element.32), channel_id=1, replica_groups=mesh['cz'=8,'cx'=4,'dp'=8] {'dp'}, use_global_device_ids=true, to_apply=%region_4.5 | all-reduce | flops 1 | bytes 8 | tf_op jit(solution)/shard_map/psum | solution.py:205
  519.7 2.1 copy.90
  521.8 8.9 %psum.22 = f32[]{:T(128)} all-reduce(f32[]{:T(128)} %psum.21), channel_id=1, replica_groups=mesh['cz'=8,'cx'=4,'dp'=8] {'cx'}, use_global_device_ids=true, to_apply=%region_5.6 | all-reduce | flops 1 | bytes 8 | tf_op jit(solution)/shard_map/psum | solution.py:206
  530.8 3.0 fusion.25
  533.7 14.1 %psum.23 = f32[]{:T(128)} all-reduce(f32[]{:T(128)} %psum.22), channel_id=1, replica_groups=mesh['cz'=8,'cx'=4,'dp'=8] {'cz'}, use_global_device_ids=true, to_apply=%region_6.7 | all-reduce | flops 1 | bytes 8 | tf_op jit(solution)/shard_map/psum | solution.py:207
  550.2 19.2 %all-gather = bf16[8,21,1024]{2,1,0:T(8,128)(2,1)S(1)} all-gather(bf16[1,21,1024]{2,1,0:T(8,128)(2,1)S(1)} %get-tuple-element.28), channel_id=1, replica_groups=mesh['cz'=8,'cx'=4,'dp'=8] {'dp'}, dimensions={0}, use_global_device_ids=true | all-gather | bytes 387072 | tf_op jit(solution)/shard_map/all_gather | solution.py:214
  (190 shorter events, 94.3 us)
Async XLA Ops:
  3.6 26.0 %collective-permute-start = (bf16[128,2176]{0,1:T(8,128)(2,1)S(1)}, bf16[128,2176]{0,1:T(8,128)(2,1)}, u32[]{:S(2)}, u32[]{:S(2)}) collective-permute-start(bf16[128,2176]{0,1:T(8,128)(2,1)S(1)} %pad_maximum_fusion.7), channel_id=1, source_target_pairs={{0,64},{8,72},{16,80},{24,88},{32,96},{40,104},{48,112},{56,120},{... | collective-permute-start | bytes 1671176 | tf_op jit(solution)/shard_map/ppermute | solution.py:38
  10.2 23.9 %collective-permute-start.1 = (bf16[128,2176]{0,1:T(8,128)(2,1)S(1)}, bf16[128,2176]{0,1:T(8,128)(2,1)}, u32[]{:S(2)}, u32[]{:S(2)}) collective-permute-start(bf16[128,2176]{0,1:T(8,128)(2,1)S(1)} %pad_maximum_fusion.7), channel_id=1, source_target_pairs={{0,56},{8,64},{16,72},{24,80},{32,88},{40,96},{48,104},{56,112},{6... | collective-permute-start | bytes 1671176 | tf_op jit(solution)/shard_map/ppermute | solution.py:38
  16.7 39.0 %collective-permute-start.2 = (bf16[128,2176]{0,1:T(8,128)(2,1)S(1)}, bf16[128,2176]{0,1:T(8,128)(2,1)S(1)}, u32[]{:S(2)}, u32[]{:S(2)}) collective-permute-start(bf16[128,2176]{0,1:T(8,128)(2,1)S(1)} %pad_maximum_fusion.7), channel_id=1, source_target_pairs={{0,48},{8,56},{16,64},{24,72},{32,80},{40,88},{48,96},{56,104},{64... | collective-permute-start | bytes 1671176 | tf_op jit(solution)/shard_map/ppermute | solution.py:38
  21.4 49.0 %collective-permute-start.3 = (bf16[128,2176]{0,1:T(8,128)(2,1)S(1)}, bf16[128,2176]{0,1:T(8,128)(2,1)S(1)}, u32[]{:S(2)}, u32[]{:S(2)}) collective-permute-start(bf16[128,2176]{0,1:T(8,128)(2,1)S(1)} %pad_maximum_fusion.7), channel_id=1, source_target_pairs={{0,40},{8,48},{16,56},{24,64},{32,72},{40,80},{48,88},{56,96},{64,... | collective-permute-start | bytes 1671176 | tf_op jit(solution)/shard_map/ppermute | solution.py:38
  23.6 46.9 %collective-permute-start.4 = (bf16[128,2176]{0,1:T(8,128)(2,1)S(1)}, bf16[128,2176]{0,1:T(8,128)(2,1)S(1)}, u32[]{:S(2)}, u32[]{:S(2)}) collective-permute-start(bf16[128,2176]{0,1:T(8,128)(2,1)S(1)} %pad_maximum_fusion.7), channel_id=1, source_target_pairs={{0,32},{8,40},{16,48},{24,56},{32,64},{40,72},{48,80},{56,88},{64,... | collective-permute-start | bytes 1671176 | tf_op jit(solution)/shard_map/ppermute | solution.py:38
  29.6 41.0 %collective-permute-start.5 = (bf16[128,2176]{0,1:T(8,128)(2,1)S(1)}, bf16[128,2176]{0,1:T(8,128)(2,1)S(1)}, u32[]{:S(2)}, u32[]{:S(2)}) collective-permute-start(bf16[128,2176]{0,1:T(8,128)(2,1)S(1)} %pad_maximum_fusion.7), channel_id=1, source_target_pairs={{0,24},{8,32},{16,40},{24,48},{32,56},{40,64},{48,72},{56,80},{64,... | collective-permute-start | bytes 1671176 | tf_op jit(solution)/shard_map/ppermute | solution.py:38
  34.1 36.7 %collective-permute-start.6 = (bf16[128,2176]{0,1:T(8,128)(2,1)S(1)}, bf16[128,2176]{0,1:T(8,128)(2,1)S(1)}, u32[]{:S(2)}, u32[]{:S(2)}) collective-permute-start(bf16[128,2176]{0,1:T(8,128)(2,1)S(1)} %pad_maximum_fusion.7), channel_id=1, source_target_pairs={{0,16},{8,24},{16,32},{24,40},{32,48},{40,56},{48,64},{56,72},{64,... | collective-permute-start | bytes 1671176 | tf_op jit(solution)/shard_map/ppermute | solution.py:38
  55.7 25.2 %collective-permute-start.7 = (bf16[128,2176]{0,1:T(8,128)(2,1)S(1)}, bf16[128,2176]{0,1:T(8,128)(2,1)S(1)}, u32[]{:S(2)}, u32[]{:S(2)}) collective-permute-start(bf16[128,2176]{0,1:T(8,128)(2,1)S(1)} %pad_maximum_fusion.7), channel_id=1, source_target_pairs={{0,8},{8,16},{16,24},{24,32},{32,40},{40,48},{48,56},{56,64},{64,7... | collective-permute-start | bytes 1671176 | tf_op jit(solution)/shard_map/ppermute | solution.py:38
  116.7 9.3 %copy-start.20 = (bf16[128,8,128]{0,2,1:T(8,128)(2,1)S(1)}, bf16[128,8,128]{0,2,1:T(8,128)(2,1)}, u32[]{:S(2)}) copy-start(bf16[128,8,128]{0,2,1:T(8,128)(2,1)} %get-tuple-element.56) | copy-start | bytes 786436
  119.4 11.8 %copy-start.19 = (bf16[128,8,128]{0,2,1:T(8,128)(2,1)S(1)}, bf16[128,8,128]{0,2,1:T(8,128)(2,1)}, u32[]{:S(2)}) copy-start(bf16[128,8,128]{0,2,1:T(8,128)(2,1)} %get-tuple-element.57) | copy-start | bytes 786436
  119.4 136.2 %collective-permute-start.15 = (bf16[128,2048]{1,0:T(8,128)(2,1)}, bf16[128,2048]{1,0:T(8,128)(2,1)}, u32[]{:S(2)}, u32[]{:S(2)}) collective-permute-start(bf16[128,2048]{1,0:T(8,128)(2,1)} %pad_maximum_fusion.15), channel_id=1, source_target_pairs={{64,0},{72,8},{80,16},{88,24},{96,32},{104,40},{112,48},{120,56},{... | collective-permute-start | bytes 1572872 | tf_op jit(solution)/shard_map/ppermute | solution.py:38
  124.6 11.8 %copy-start.18 = (bf16[128,8,128]{0,2,1:T(8,128)(2,1)S(1)}, bf16[128,8,128]{0,2,1:T(8,128)(2,1)}, u32[]{:S(2)}) copy-start(bf16[128,8,128]{0,2,1:T(8,128)(2,1)} %get-tuple-element.58) | copy-start | bytes 786436
  124.6 132.3 %collective-permute-start.14 = (bf16[128,2048]{1,0:T(8,128)(2,1)}, bf16[128,2048]{1,0:T(8,128)(2,1)}, u32[]{:S(2)}, u32[]{:S(2)}) collective-permute-start(bf16[128,2048]{1,0:T(8,128)(2,1)} %pad_maximum_fusion.14), channel_id=1, source_target_pairs={{56,0},{64,8},{72,16},{80,24},{88,32},{96,40},{104,48},{112,56},{1... | collective-permute-start | bytes 1572872 | tf_op jit(solution)/shard_map/ppermute | solution.py:38
  129.8 12.6 %copy-start.17 = (bf16[128,8,128]{0,2,1:T(8,128)(2,1)S(1)}, bf16[128,8,128]{0,2,1:T(8,128)(2,1)}, u32[]{:S(2)}) copy-start(bf16[128,8,128]{0,2,1:T(8,128)(2,1)} %get-tuple-element.59) | copy-start | bytes 786436
  129.8 128.4 %collective-permute-start.13 = (bf16[128,2048]{1,0:T(8,128)(2,1)}, bf16[128,2048]{1,0:T(8,128)(2,1)}, u32[]{:S(2)}, u32[]{:S(2)}) collective-permute-start(bf16[128,2048]{1,0:T(8,128)(2,1)} %pad_maximum_fusion.13), channel_id=1, source_target_pairs={{48,0},{56,8},{64,16},{72,24},{80,32},{88,40},{96,48},{104,56},{11... | collective-permute-start | bytes 1572872 | tf_op jit(solution)/shard_map/ppermute | solution.py:38
  134.9 11.2 %copy-start.16 = (bf16[128,8,128]{0,2,1:T(8,128)(2,1)S(1)}, bf16[128,8,128]{0,2,1:T(8,128)(2,1)}, u32[]{:S(2)}) copy-start(bf16[128,8,128]{0,2,1:T(8,128)(2,1)} %get-tuple-element.60) | copy-start | bytes 786436
  134.9 133.8 %collective-permute-start.12 = (bf16[128,2048]{1,0:T(8,128)(2,1)}, bf16[128,2048]{1,0:T(8,128)(2,1)}, u32[]{:S(2)}, u32[]{:S(2)}) collective-permute-start(bf16[128,2048]{1,0:T(8,128)(2,1)} %pad_maximum_fusion.12), channel_id=1, source_target_pairs={{40,0},{48,8},{56,16},{64,24},{72,32},{80,40},{88,48},{96,56},{104... | collective-permute-start | bytes 1572872 | tf_op jit(solution)/shard_map/ppermute | solution.py:38
  137.2 10.2 %copy-start.15 = (bf16[128,8,128]{0,2,1:T(8,128)(2,1)S(1)}, bf16[128,8,128]{0,2,1:T(8,128)(2,1)}, u32[]{:S(2)}) copy-start(bf16[128,8,128]{0,2,1:T(8,128)(2,1)} %get-tuple-element.53) | copy-start | bytes 786436
  140.9 129.3 %collective-permute-start.11 = (bf16[128,2048]{1,0:T(8,128)(2,1)}, bf16[128,2048]{1,0:T(8,128)(2,1)}, u32[]{:S(2)}, u32[]{:S(2)}) collective-permute-start(bf16[128,2048]{1,0:T(8,128)(2,1)} %pad_maximum_fusion.11), channel_id=1, source_target_pairs={{32,0},{40,8},{48,16},{56,24},{64,32},{72,40},{80,48},{88,56},{96,... | collective-permute-start | bytes 1572872 | tf_op jit(solution)/shard_map/ppermute | solution.py:38
  255.6 26.9 %collective-permute-start.10 = (bf16[128,2048]{1,0:T(8,128)(2,1)}, bf16[128,2048]{1,0:T(8,128)(2,1)}, u32[]{:S(2)}, u32[]{:S(2)}) collective-permute-start(bf16[128,2048]{1,0:T(8,128)(2,1)} %pad_maximum_fusion.10), channel_id=1, source_target_pairs={{24,0},{32,8},{40,16},{48,24},{56,32},{64,40},{72,48},{80,56},{88,... | collective-permute-start | bytes 1572872 | tf_op jit(solution)/shard_map/ppermute | solution.py:38
  256.9 26.7 %collective-permute-start.9 = (bf16[128,2048]{1,0:T(8,128)(2,1)}, bf16[128,2048]{1,0:T(8,128)(2,1)}, u32[]{:S(2)}, u32[]{:S(2)}) collective-permute-start(bf16[128,2048]{1,0:T(8,128)(2,1)} %pad_maximum_fusion.9), channel_id=1, source_target_pairs={{16,0},{24,8},{32,16},{40,24},{48,32},{56,40},{64,48},{72,56},{80,... | collective-permute-start | bytes 1572872 | tf_op jit(solution)/shard_map/ppermute | solution.py:38
  258.2 29.3 %collective-permute-start.8 = (bf16[128,2048]{1,0:T(8,128)(2,1)}, bf16[128,2048]{1,0:T(8,128)(2,1)}, u32[]{:S(2)}, u32[]{:S(2)}) collective-permute-start(bf16[128,2048]{1,0:T(8,128)(2,1)} %pad_maximum_fusion.8), channel_id=1, source_target_pairs={{8,0},{16,8},{24,16},{32,24},{40,32},{48,40},{56,48},{64,56},{72,6... | collective-permute-start | bytes 1572872 | tf_op jit(solution)/shard_map/ppermute | solution.py:38
  267.2 21.5 %copy-start.1 = (f32[128,2048]{1,0:T(8,128)}, f32[128,2048]{1,0:T(8,128)S(1)}, u32[]{:S(2)}) copy-start(f32[128,2048]{1,0:T(8,128)S(1)} %convert_element_type.150) | copy-start | bytes 3145732
  268.7 20.0 %copy-start.3 = (f32[128,2048]{1,0:T(8,128)}, f32[128,2048]{1,0:T(8,128)S(1)}, u32[]{:S(2)}) copy-start(f32[128,2048]{1,0:T(8,128)S(1)} %convert_element_type.147) | copy-start | bytes 3145732
  270.2 18.4 %copy-start.5 = (f32[128,2048]{1,0:T(8,128)}, f32[128,2048]{1,0:T(8,128)S(1)}, u32[]{:S(2)}) copy-start(f32[128,2048]{1,0:T(8,128)S(1)} %convert_element_type.144) | copy-start | bytes 3145732
  271.8 16.9 %copy-start.6 = (f32[128,2048]{1,0:T(8,128)}, f32[128,2048]{1,0:T(8,128)S(1)}, u32[]{:S(2)}) copy-start(f32[128,2048]{1,0:T(8,128)S(1)} %convert_element_type.141) | copy-start | bytes 3145732
  271.8 16.9 %copy-start.12 = (f32[128,1024]{1,0:T(8,128)S(1)}, f32[128,1024]{1,0:T(8,128)}, u32[]{:S(2)}) copy-start(f32[128,1024]{1,0:T(8,128)} %copy.105) | copy-start | bytes 1572868
  292.6 57.9 %collective-permute-start.16 = (bf16[128,1696]{1,0:T(8,128)(2,1)}, bf16[128,1696]{1,0:T(8,128)(2,1)}, u32[]{:S(2)}, u32[]{:S(2)}) collective-permute-start(bf16[128,1696]{1,0:T(8,128)(2,1)} %get-tuple-element.77), channel_id=1, source_target_pairs={{0,32},{32,64},{64,96},{96,128},{128,160},{160,192},{192,224},{224... | collective-permute-start | bytes 1302536 | tf_op jit(solution)/shard_map/ppermute | solution.py:43
  317.4 47.5 %collective-permute-start.17 = (bf16[128,1696]{1,0:T(8,128)(2,1)}, bf16[128,1696]{1,0:T(8,128)(2,1)S(1)}, u32[]{:S(2)}, u32[]{:S(2)}) collective-permute-start(bf16[128,1696]{1,0:T(8,128)(2,1)} %get-tuple-element.76), channel_id=1, source_target_pairs={{0,64},{32,96},{64,128},{96,160},{128,192},{160,224},{192,0},{224,... | collective-permute-start | bytes 1302536 | tf_op jit(solution)/shard_map/ppermute | solution.py:43
  341.4 70.7 %collective-permute-start.18 = (bf16[128,1696]{1,0:T(8,128)(2,1)}, bf16[128,1696]{1,0:T(8,128)(2,1)S(1)}, u32[]{:S(2)}, u32[]{:S(2)}) collective-permute-start(bf16[128,1696]{1,0:T(8,128)(2,1)} %get-tuple-element.72), channel_id=1, source_target_pairs={{0,96},{32,128},{64,160},{96,192},{128,224},{160,0},{192,32},{224,... | collective-permute-start | bytes 1302536 | tf_op jit(solution)/shard_map/ppermute | solution.py:43
  346.3 66.7 %collective-permute-start.19 = (bf16[128,1696]{1,0:T(8,128)(2,1)}, bf16[128,1696]{1,0:T(8,128)(2,1)S(1)}, u32[]{:S(2)}, u32[]{:S(2)}) collective-permute-start(bf16[128,1696]{1,0:T(8,128)(2,1)} %get-tuple-element.73), channel_id=1, source_target_pairs={{0,128},{32,160},{64,192},{96,224},{128,0},{160,32},{192,64},{224,... | collective-permute-start | bytes 1302536 | tf_op jit(solution)/shard_map/ppermute | solution.py:43
  346.3 67.6 %collective-permute-start.20 = (bf16[128,1696]{1,0:T(8,128)(2,1)}, bf16[128,1696]{1,0:T(8,128)(2,1)S(1)}, u32[]{:S(2)}, u32[]{:S(2)}) collective-permute-start(bf16[128,1696]{1,0:T(8,128)(2,1)} %get-tuple-element.74), channel_id=1, source_target_pairs={{0,160},{32,192},{64,224},{96,0},{128,32},{160,64},{192,96},{224,1... | collective-permute-start | bytes 1302536 | tf_op jit(solution)/shard_map/ppermute | solution.py:43
  350.5 69.8 %collective-permute-start.21 = (bf16[128,1696]{1,0:T(8,128)(2,1)}, bf16[128,1696]{1,0:T(8,128)(2,1)S(1)}, u32[]{:S(2)}, u32[]{:S(2)}) collective-permute-start(bf16[128,1696]{1,0:T(8,128)(2,1)} %get-tuple-element.75), channel_id=1, source_target_pairs={{0,192},{32,224},{64,0},{96,32},{128,64},{160,96},{192,128},{224,1... | collective-permute-start | bytes 1302536 | tf_op jit(solution)/shard_map/ppermute | solution.py:43
  364.9 61.8 %collective-permute-start.22 = (bf16[128,1696]{1,0:T(8,128)(2,1)}, bf16[128,1696]{1,0:T(8,128)(2,1)S(1)}, u32[]{:S(2)}, u32[]{:S(2)}) collective-permute-start(bf16[128,1696]{1,0:T(8,128)(2,1)} %get-tuple-element.71), channel_id=1, source_target_pairs={{0,224},{32,0},{64,32},{96,64},{128,96},{160,128},{192,160},{224,1... | collective-permute-start | bytes 1302536 | tf_op jit(solution)/shard_map/ppermute | solution.py:43
  438.7 12.2 %collective-permute-start.29 = (f32[4,21,1024]{2,1,0:T(8,128)S(1)}, f32[4,21,1024]{2,1,0:T(8,128)S(1)}, u32[]{:S(2)}, u32[]{:S(2)}) collective-permute-start(f32[4,21,1024]{2,1,0:T(8,128)S(1)} %get-tuple-element.39), channel_id=1, source_target_pairs={{0,7},{1,0},{2,1},{3,2},{4,3},{5,4},{6,5},{7,6},{8,15},{9,8},{10,9... | collective-permute-start | bytes 1032200 | tf_op jit(solution)/shard_map/ppermute | solution.py:43
  439.6 12.6 %collective-permute-start.28 = (f32[4,21,1024]{2,1,0:T(8,128)S(1)}, f32[4,21,1024]{2,1,0:T(8,128)S(1)}, u32[]{:S(2)}, u32[]{:S(2)}) collective-permute-start(f32[4,21,1024]{2,1,0:T(8,128)S(1)} %get-tuple-element.40), channel_id=1, source_target_pairs={{0,6},{1,7},{2,0},{3,1},{4,2},{5,3},{6,4},{7,5},{8,14},{9,15},{10,... | collective-permute-start | bytes 1032200 | tf_op jit(solution)/shard_map/ppermute | solution.py:43
  442.3 33.9 %collective-permute-start.27 = (f32[4,21,1024]{2,1,0:T(8,128)}, f32[4,21,1024]{2,1,0:T(8,128)}, u32[]{:S(2)}, u32[]{:S(2)}) collective-permute-start(f32[4,21,1024]{2,1,0:T(8,128)} %get-tuple-element.41), channel_id=1, source_target_pairs={{0,5},{1,6},{2,7},{3,0},{4,1},{5,2},{6,3},{7,4},{8,13},{9,14},{10,... | collective-permute-start | bytes 1032200 | tf_op jit(solution)/shard_map/ppermute | solution.py:43
  443.1 33.1 %collective-permute-start.26 = (f32[4,21,1024]{2,1,0:T(8,128)}, f32[4,21,1024]{2,1,0:T(8,128)}, u32[]{:S(2)}, u32[]{:S(2)}) collective-permute-start(f32[4,21,1024]{2,1,0:T(8,128)} %get-tuple-element.42), channel_id=1, source_target_pairs={{0,4},{1,5},{2,6},{3,7},{4,0},{5,1},{6,2},{7,3},{8,12},{9,13},{10,... | collective-permute-start | bytes 1032200 | tf_op jit(solution)/shard_map/ppermute | solution.py:43
  445.1 31.1 %collective-permute-start.25 = (f32[4,21,1024]{2,1,0:T(8,128)}, f32[4,21,1024]{2,1,0:T(8,128)}, u32[]{:S(2)}, u32[]{:S(2)}) collective-permute-start(f32[4,21,1024]{2,1,0:T(8,128)} %get-tuple-element.43), channel_id=1, source_target_pairs={{0,3},{1,4},{2,5},{3,6},{4,7},{5,0},{6,1},{7,2},{8,11},{9,12},{10,... | collective-permute-start | bytes 1032200 | tf_op jit(solution)/shard_map/ppermute | solution.py:43
  450.8 25.4 %collective-permute-start.24 = (f32[4,21,1024]{2,1,0:T(8,128)}, f32[4,21,1024]{2,1,0:T(8,128)}, u32[]{:S(2)}, u32[]{:S(2)}) collective-permute-start(f32[4,21,1024]{2,1,0:T(8,128)} %get-tuple-element.44), channel_id=1, source_target_pairs={{0,2},{1,3},{2,4},{3,5},{4,6},{5,7},{6,0},{7,1},{8,10},{9,11},{10,... | collective-permute-start | bytes 1032200 | tf_op jit(solution)/shard_map/ppermute | solution.py:43
  452.9 25.3 %collective-permute-start.23 = (f32[4,21,1024]{2,1,0:T(8,128)}, f32[4,21,1024]{2,1,0:T(8,128)}, u32[]{:S(2)}, u32[]{:S(2)}) collective-permute-start(f32[4,21,1024]{2,1,0:T(8,128)} %get-tuple-element.38), channel_id=1, source_target_pairs={{0,1},{1,2},{2,3},{3,4},{4,5},{5,6},{6,7},{7,0},{8,9},{9,10},{10,1... | collective-permute-start | bytes 1032200 | tf_op jit(solution)/shard_map/ppermute | solution.py:43
  481.8 16.2 %collective-permute-start.32 = (f32[21,1024]{1,0:T(8,128)}, f32[21,1024]{1,0:T(8,128)S(1)}, u32[]{:S(2)}, u32[]{:S(2)}) collective-permute-start(f32[21,1024]{1,0:T(8,128)} %get-tuple-element.69), channel_id=1, source_target_pairs={{0,24},{8,0},{16,8},{24,16},{1,25},{9,1},{17,9},{25,17},{2,26},{10... | collective-permute-start | bytes 258056 | tf_op jit(solution)/shard_map/ppermute | solution.py:43
  489.1 8.9 %collective-permute-start.31 = (f32[21,1024]{1,0:T(8,128)}, f32[21,1024]{1,0:T(8,128)}, u32[]{:S(2)}, u32[]{:S(2)}) collective-permute-start(f32[21,1024]{1,0:T(8,128)} %get-tuple-element.70), channel_id=1, source_target_pairs={{0,16},{8,24},{16,0},{24,8},{1,17},{9,25},{17,1},{25,9},{2,18},{10... | collective-permute-start | bytes 258056 | tf_op jit(solution)/shard_map/ppermute | solution.py:43
  489.1 8.9 %collective-permute-start.30 = (f32[21,1024]{1,0:T(8,128)}, f32[21,1024]{1,0:T(8,128)}, u32[]{:S(2)}, u32[]{:S(2)}) collective-permute-start(f32[21,1024]{1,0:T(8,128)} %get-tuple-element.68), channel_id=1, source_target_pairs={{0,8},{8,16},{16,24},{24,0},{1,9},{9,17},{17,25},{25,1},{2,10},{10... | collective-permute-start | bytes 258056 | tf_op jit(solution)/shard_map/ppermute | solution.py:43
  493.9 36.8 %copy-start.2 = (f32[128,2048]{1,0:T(8,128)S(1)}, f32[128,2048]{1,0:T(8,128)}, u32[]{:S(2)}) copy-start(f32[128,2048]{1,0:T(8,128)} %copy-done.1) | copy-start | bytes 3145732
  493.9 36.8 %copy-start.4 = (f32[128,2048]{1,0:T(8,128)S(1)}, f32[128,2048]{1,0:T(8,128)}, u32[]{:S(2)}) copy-start(f32[128,2048]{1,0:T(8,128)} %copy-done.3) | copy-start | bytes 3145732
  530.8 17.8 %copy-start.31 = (f32[21,1024]{1,0:T(8,128)S(1)}, f32[21,1024]{1,0:T(8,128)}, u32[]{:S(2)}) copy-start(f32[21,1024]{1,0:T(8,128)} %param.15) | copy-start | bytes 258052
  530.8 17.8 %copy-start.32 = (f32[21,1024]{1,0:T(8,128)S(1)}, f32[21,1024]{1,0:T(8,128)}, u32[]{:S(2)}) copy-start(f32[21,1024]{1,0:T(8,128)} %param.16) | copy-start | bytes 258052
  (21 other events, 58.2 us)

commit v3 on v2

--- a/solution.py
+++ b/solution.py
@@ -11,6 +11,7 @@
 Z_SIZE = 8
 
 CTX = ("cz", "cx")
+DP = ("y", "core")
 
 query_scale = 168.0 ** (-0.5)
 masked_score = -1e30
@@ -30,12 +31,6 @@
 
 def ctx_index():
     return lax.axis_index("cz") * lax.axis_size("cx") + lax.axis_index("cx")
-
-
-def from_behind(x, by):
-    count = ctx_size()
-    pairs = [(i, i + by) for i in range(count) if 0 <= i + by < count]
-    return lax.ppermute(x, CTX, pairs)
 
 
 def cyclic(x, axis, by):
@@ -112,6 +107,22 @@
     )
 
 
+def shift(x, axis, by):
+    count = lax.axis_size(axis)
+    pairs = [(i, i + by) for i in range(count) if 0 <= i + by < count]
+    return lax.ppermute(x, axis, pairs)
+
+
+def all_sum(x, axes):
+    for axis in axes:
+        count = lax.axis_size(axis)
+        step = 1
+        while step < count:
+            x = x + cyclic(x, axis, step)
+            step *= 2
+    return x
+
+
 def shards(
     layer_input,
     query_states,
@@ -125,20 +136,37 @@
 ):
     shard_length = query_states.shape[1]
     kv_width = key_states.shape[2]
-    peer_count = min(WINDOW // shard_length, ctx_size() - 1)
-    front_len = peer_count * shard_length
-    position = ctx_index() * shard_length
+    ncx = lax.axis_size("cx")
+    icx = lax.axis_index("cx")
+    iz = lax.axis_index("cz")
+    assert WINDOW // shard_length == 2 * ncx
+    block = ctx_index()
 
     seg_query = segments[0]
     seg_cols = jnp.broadcast_to(seg_query.astype(jnp.bfloat16)[:, None], (shard_length, 128))
     own_kv = jnp.concatenate([key_states[0], value_state_rows[0], seg_cols], axis=1)
-    incoming = [from_behind(own_kv, distance) for distance in range(peer_count, 0, -1)]
-    kv_rows = jnp.concatenate(incoming + [own_kv], axis=0)
+    plane_one = shift(own_kv, "cz", 1)
+    plane_two = shift(plane_one, "cz", 1)
+    slots = [own_kv, plane_one, plane_two]
+    sources = [block, block - ncx, block - 2 * ncx]
+    wraps = []
+    for by in range(1, ncx):
+        slots.append(cyclic(plane_one, "cx", by))
+        sources.append((iz - 1) * ncx + (icx - by) % ncx)
+    for by in range(1, ncx):
+        sending_wraps = icx + by >= ncx
+        slots.append(cyclic(jnp.where(sending_wraps, plane_two, own_kv), "cx", by))
+        got_wrap = icx - by < 0
+        wraps.append(sending_wraps)
+        sources.append(jnp.where(got_wrap, block - ncx - by, block - by))
+    kv_rows = jnp.concatenate(slots, axis=0)
     key_row_block = kv_rows[:, :kv_width]
     value_row_block = kv_rows[:, kv_width : 2 * kv_width]
     seg_key = kv_rows[:, 2 * kv_width]
-    index_query = position + jnp.arange(shard_length, dtype=jnp.int32)
-    index_key = position - front_len + jnp.arange(front_len + shard_length, dtype=jnp.int32)
+    index_query = block * shard_length + jnp.arange(shard_length, dtype=jnp.int32)
+    index_key = jnp.concatenate(
+        [src * shard_length + jnp.arange(shard_length, dtype=jnp.int32) for src in sources]
+    )
     query_gradient, key_gradient, value_gradient = attend(
         query_states[0],
         key_row_block,
@@ -149,69 +177,73 @@
         index_query,
         index_key,
     )
-    key_sum = key_gradient[front_len:]
-    value_sum = value_gradient[front_len:]
-    for distance in range(1, peer_count + 1):
-        lower = (peer_count - distance) * shard_length
-        part = jnp.concatenate(
-            [
-                key_gradient[lower : lower + shard_length].astype(jnp.bfloat16),
-                value_gradient[lower : lower + shard_length].astype(jnp.bfloat16),
-            ],
-            axis=1,
-        )
-        returned = from_behind(part, -distance).astype(jnp.float32)
-        key_sum = key_sum + returned[:, :kv_width]
-        value_sum = value_sum + returned[:, kv_width:]
-    key_out = key_sum.astype(jnp.bfloat16)
-    value_out = value_sum.astype(jnp.bfloat16)
+    grads = jnp.concatenate([key_gradient, value_gradient], axis=1)
+    slot_grads = [grads[i * shard_length : (i + 1) * shard_length] for i in range(len(slots))]
+    low = lambda x: x.astype(jnp.bfloat16)
+    own_acc = slot_grads[0]
+    one_acc = low(slot_grads[1]).astype(jnp.float32)
+    two_acc = low(slot_grads[2]).astype(jnp.float32)
+    for k, by in enumerate(range(1, ncx)):
+        back = cyclic(low(slot_grads[3 + k]), "cx", -by).astype(jnp.float32)
+        one_acc = one_acc + back
+    for k, by in enumerate(range(1, ncx)):
+        back = cyclic(low(slot_grads[3 + (ncx - 1) + k]), "cx", -by).astype(jnp.float32)
+        zero = jnp.zeros_like(back)
+        two_acc = two_acc + jnp.where(wraps[k], back, zero)
+        own_acc = own_acc + jnp.where(wraps[k], zero, back)
+    one_acc = one_acc + shift(low(two_acc), "cz", -1).astype(jnp.float32)
+    own_acc = own_acc + shift(low(one_acc), "cz", -1).astype(jnp.float32)
+    key_out = own_acc[:, :kv_width].astype(jnp.bfloat16)
+    value_out = own_acc[:, kv_width:].astype(jnp.bfloat16)
 
     nz = lax.axis_size("cz")
-    iz = lax.axis_index("cz")
+    ny = lax.axis_size("y")
+    nc = lax.axis_size("core")
     x_own = layer_input[0]
-    width = x_own.shape[1] // nz
-    x_list = [lax.dynamic_slice_in_dim(x_own, iz * width, width, 1)]
+    rows = x_own.shape[1] // (nz * ncx * ny * nc)
+    x_view = x_own.reshape(shard_length, nz, ncx, ny * nc * rows)
+
+    def columns(target):
+        picked = lax.dynamic_index_in_dim(x_view, target, 2, keepdims=False)
+        return picked.reshape(shard_length, nz * ny * nc * rows)
+
+    x_list = [columns(icx)]
     v_list = [value_out]
-    for shift in range(1, nz):
-        target = (iz + shift) % nz
-        piece = jnp.concatenate(
-            [lax.dynamic_slice_in_dim(x_own, target * width, width, 1), value_out], axis=1
-        )
-        got = cyclic(piece, "cz", shift)
-        x_list.append(got[:, :width])
-        v_list.append(got[:, width:])
+    for by in range(1, ncx):
+        piece = jnp.concatenate([columns((icx + by) % ncx), value_out], axis=1)
+        got = cyclic(piece, "cx", by)
+        x_list.append(got[:, : -kv_width])
+        v_list.append(got[:, -kv_width:])
     partial = lax.dot_general(
         jnp.concatenate(x_list, axis=0),
         jnp.concatenate(v_list, axis=0),
         (((0,), (0,)), ((), ())),
         preferred_element_type=jnp.float32,
     )
-    ncx = lax.axis_size("cx")
-    ndp = lax.axis_size("dp")
-    rows = width // (ncx * ndp)
-    partial = partial.reshape(ncx, ndp, rows, kv_width)
-    idp = lax.axis_index("dp")
-    stage = lax.dynamic_index_in_dim(partial, idp, 1, keepdims=False)
-    for shift in range(1, ndp):
-        target = (idp + shift) % ndp
-        stage = stage + cyclic(lax.dynamic_index_in_dim(partial, target, 1, keepdims=False), "dp", shift)
-    icx = lax.axis_index("cx")
-    weight_grad = lax.dynamic_index_in_dim(stage, icx, 0, keepdims=False)
-    for shift in range(1, ncx):
-        target = (icx + shift) % ncx
-        weight_grad = weight_grad + cyclic(lax.dynamic_index_in_dim(stage, target, 0, keepdims=False), "cx", shift)
-
-    square_total = jnp.sum(weight_grad * weight_grad)
-    square_total = lax.psum(square_total, "dp")
-    square_total = lax.psum(square_total, "cx")
-    square_total = lax.psum(square_total, "cz")
+    partial = partial.reshape(nz, ny, nc, rows, kv_width)
+    icore = lax.axis_index("core")
+    stage = lax.dynamic_index_in_dim(partial, icore, 2, keepdims=False)
+    for by in range(1, nc):
+        sent = lax.dynamic_index_in_dim(partial, (icore + by) % nc, 2, keepdims=False)
+        stage = stage + cyclic(low(sent), "core", by).astype(jnp.float32)
+    iy = lax.axis_index("y")
+    stage_y = lax.dynamic_index_in_dim(stage, iy, 1, keepdims=False)
+    for by in range(1, ny):
+        sent = lax.dynamic_index_in_dim(stage, (iy + by) % ny, 1, keepdims=False)
+        stage_y = stage_y + cyclic(low(sent), "y", by).astype(jnp.float32)
+    weight_grad = lax.dynamic_index_in_dim(stage_y, iz, 0, keepdims=False)
+    for by in range(1, nz):
+        sent = lax.dynamic_index_in_dim(stage_y, (iz + by) % nz, 0, keepdims=False)
+        weight_grad = weight_grad + cyclic(sent, "cz", by)
+
+    square_total = all_sum(jnp.sum(weight_grad * weight_grad), ("core", "y", "cx", "cz"))
     norm_total = jnp.sqrt(square_total + 1e-06)
     clipped = weight_grad * jnp.minimum(1.0, clip_norm / norm_total)
     new_first = beta_first * first_moment_value + (1.0 - beta_first) * clipped
     new_second = beta_second * second_moment_value + (1.0 - beta_second) * clipped * clipped
     step_dir = new_first / correct_first / (jnp.sqrt(new_second / correct_second) + adam_eps)
     new_master = master - learn_rate * (step_dir + decay_rate * master)
-    new_weight = lax.all_gather(new_master.astype(jnp.bfloat16), "dp", axis=0, tiled=True)
+    new_weight = lax.all_gather(new_master.astype(jnp.bfloat16), DP, axis=0, tiled=True)
     return (
         query_gradient[None],
         key_out[None],
@@ -227,9 +259,11 @@
     n_ctx = mesh.shape["ctx"]
     n_dp = mesh.shape["dp"]
     z_size = Z_SIZE if n_ctx % Z_SIZE == 0 else n_ctx
-    grid = Mesh(mesh.devices.reshape(z_size, n_ctx // z_size, n_dp), ("cz", "cx", "dp"))
-    tokens = P("dp", CTX, None)
-    owner = P(("cz", "cx", "dp"), None)
+    grid = Mesh(
+        mesh.devices.reshape(z_size, n_ctx // z_size, n_dp // 2, 2), ("cz", "cx", "y", "core")
+    )
+    tokens = P(DP, CTX, None)
+    owner = P(("cz", "cx", "y", "core"), None)
     return jax.shard_map(
         shards,
         mesh=grid,
@@ -239,7 +273,7 @@
             tokens,
             tokens,
             tokens,
-            P("dp", CTX),
+            P(DP, CTX),
             owner,
             owner,
             owner,

time: 573 us -> 359 us (0.63)
  starting transfers between devices: 200 us -> 63.5 us
  blocking collectives: 62.4 us -> 22.3 us
  local copies, waits for them, and re-layouts: 60.3 us -> 36.1 us
  other arithmetic: 42.9 us -> 23.2 us
  matrix products: 30.3 us -> 24 us
    ppermute x17 -> x34, waiting for transfers between devices: 44.8 us -> 149 us  [cyclic(): return lax.ppermute(x, axis, [(i, (i + by) % count) for i in range(count)])]
    ppermute x16 -> x4, waiting for transfers between devices: 128 us -> 28.6 us  [shift(): return lax.ppermute(x, axis, pairs)]
    ppermute x17 -> x34, starting transfers between devices: 128 us -> 52.4 us  [cyclic(): return lax.ppermute(x, axis, [(i, (i + by) % count) for i in range(count)])]
    ppermute x16 -> x4, starting transfers between devices: 71.7 us -> 11.1 us  [shift(): return lax.ppermute(x, axis, pairs)]
    psum x3 -> x0, blocking collectives: 43.2 us -> none  [the longest x1 20.1 us: shards(): square_total = lax.psum(square_total, 'dp')]
    concatenate x10 -> x2, other arithmetic: 15.7 us -> 1.25 us  [the longest x1 1.25 us: shards(): piece = jnp.concatenate([columns((icx + by) % ncx), value_out], axis=1)]
    convert_element_type x16 -> x3, local copies, waits for them, and re-layouts: 15.3 us -> 3.92 us  [shards(): low = lambda x: x.astype(jnp.bfloat16)]
    convert_element_type x8 -> x2, other arithmetic: 10.6 us -> 3.59 us  [shards(): low = lambda x: x.astype(jnp.bfloat16)]
  transfers between devices with their start and end apart: 33 -> 38, of which waited for: 11 -> 27; matrix products, arithmetic and copies ran while one was open for 11% -> 6% of each run, Pallas kernels for 0% -> 0%
where the time goes in v3:
time: 359 us; the launch traced here: 354 us
  waiting for transfers between devices  177 us (49%)
  starting transfers between devices  63.5 us (18%)
  local copies, waits for them, and re-layouts  36.1 us (10%)
  matrix products  24 us (7%)
  other arithmetic  23.2 us (6%)
  blocking collectives  22.3 us (6%)
  between operations  7.36 us (2%)
    ppermute x34, waiting for transfers between devices, cyclic(): return lax.ppermute(x, axis, [(i, (i + by) % count) for i in range(count)])  149 us
    ppermute x34, starting transfers between devices, cyclic(): return lax.ppermute(x, axis, [(i, (i + by) % count) for i in range(count)])  52.4 us
    ppermute x4, waiting for transfers between devices, shift(): return lax.ppermute(x, axis, pairs)  28.6 us
    all_gather x1, blocking collectives, shards(): lax.all_gather(new_master.astype(jnp.bfloat16), DP, axis=0, tiled=True)  22.3 us
    unnamed x54, local copies, waits for them, and re-layouts  16.8 us
    ppermute x4, starting transfers between devices, shift(): return lax.ppermute(x, axis, pairs)  11.1 us
  transfers between devices with their start and end apart: 38, of which 27 were waited for; matrix products, arithmetic and copies ran while one was open for 6% of the time, Pallas kernels for 0%

profile of v3, /device:TPU:1, one launch (start us, length us, event | category | flops | bytes accessed | tf_op | source)
XLA Modules:
  0.0 353.8 jit_solution(10527359843591712066)
XLA Ops:
  3.6 4.4 %collective-permute-start = (bf16[128,2176]{0,1:T(8,128)(2,1)S(1)}, bf16[128,2176]{0,1:T(8,128)(2,1)S(1)}, u32[]{:S(2)}, u32[]{:S(2)}) collective-permute-start(bf16[128,2176]{0,1:T(8,128)(2,1)S(1)} %pad_maximum_fusion.4), channel_id=1, source_target_pairs={{0,32},{32,64},{64,96},{96,128},{128,160},{160,192},{192,224},{1,3... | collective-permute-start | bytes 1671176 | tf_op jit(solution)/shard_map/ppermute | solution.py:113
  10.9 8.4 %collective-permute-done = bf16[128,2176]{0,1:T(8,128)(2,1)S(1)} collective-permute-done((bf16[128,2176]{0,1:T(8,128)(2,1)S(1)}, bf16[128,2176]{0,1:T(8,128)(2,1)S(1)}, u32[]{:S(2)}, u32[]{:S(2)}) %collective-permute-start) | collective-permute-done | bytes 557088 | tf_op jit(solution)/shard_map/ppermute | solution.py:113
  19.3 4.1 %collective-permute-start.1 = (bf16[128,2176]{0,1:T(8,128)(2,1)S(1)}, bf16[128,2176]{0,1:T(8,128)(2,1)S(1)}, u32[]{:S(2)}, u32[]{:S(2)}) collective-permute-start(bf16[128,2176]{0,1:T(8,128)(2,1)S(1)} %collective-permute-done), channel_id=1, source_target_pairs={{0,32},{32,64},{64,96},{96,128},{128,160},{160,192},{192,224},{1,3... | collective-permute-start | bytes 1671176 | tf_op jit(solution)/shard_map/ppermute | solution.py:113
  24.8 2.5 collective-permute-start.3
  28.4 5.4 %collective-permute-done.1 = bf16[128,2176]{0,1:T(8,128)(2,1)S(1)} collective-permute-done((bf16[128,2176]{0,1:T(8,128)(2,1)S(1)}, bf16[128,2176]{0,1:T(8,128)(2,1)S(1)}, u32[]{:S(2)}, u32[]{:S(2)}) %collective-permute-start.1) | collective-permute-done | bytes 557088 | tf_op jit(solution)/shard_map/ppermute | solution.py:113
  35.4 2.5 collective-permute-start.6
  39.7 10.4 %collective-permute-done.3 = bf16[128,2176]{0,1:T(8,128)(2,1)S(1)} collective-permute-done((bf16[128,2176]{0,1:T(8,128)(2,1)S(1)}, bf16[128,2176]{0,1:T(8,128)(2,1)S(1)}, u32[]{:S(2)}, u32[]{:S(2)}) %collective-permute-start.3) | collective-permute-done | bytes 557088 | tf_op jit(solution)/shard_map/ppermute | solution.py:38
  50.3 2.5 collective-permute-done.4
  52.9 9.2 %collective-permute-done.5 = bf16[128,2176]{0,1:T(8,128)(2,1)S(1)} collective-permute-done((bf16[128,2176]{0,1:T(8,128)(2,1)S(1)}, bf16[128,2176]{0,1:T(8,128)(2,1)S(1)}, u32[]{:S(2)}, u32[]{:S(2)}) %collective-permute-start.5) | collective-permute-done | bytes 557088 | tf_op jit(solution)/shard_map/ppermute | solution.py:38
  62.2 11.8 %collective-permute-done.6 = bf16[128,2176]{0,1:T(8,128)(2,1)S(1)} collective-permute-done((bf16[128,2176]{0,1:T(8,128)(2,1)S(1)}, bf16[128,2176]{0,1:T(8,128)(2,1)S(1)}, u32[]{:S(2)}, u32[]{:S(2)}) %collective-permute-start.6) | collective-permute-done | bytes 557088 | tf_op jit(solution)/shard_map/ppermute | solution.py:38
  77.8 6.3 %fusion.63 = (f32[8,2,128]{2,1,0:T(2,128)}, f32[8,2,128,1152]{2,3,1,0:T(8,128)}) fusion(pred[128,1152]{0,1:T(8,128)(4,1)S(1)} %fusion.44, bf16[1152,8,128,1]{0,2,3,1:T(8,128)(2,1)S(1)} %bitcast.136, bf16[128,8,2,128]{0,3,2,1:T(8,128)(2,1)S(1)} %bitcast.149), kind=kOutput, calls=%fused_computation.142 | convolution fusion | flops 613418112 | bytes 12476416 | tf_op jit(solution)/shard_map/sub | solution.py:75
  84.1 4.8 %fusion.8 = bf16[8,2,128,1152]{2,3,1,0:T(8,128)(2,1)S(1)} fusion(f32[8,2,128,1152]{2,3,1,0:T(8,128)} %get-tuple-element.75, f32[8,2,128]{2,1,0:T(2,128)} %get-tuple-element.74), kind=kLoop, calls=%fused_computation.16 | loop fusion | flops 4718592 | bytes 14163968 | tf_op jit(solution)/shard_map/convert_element_type | solution.py:77
  91.7 5.3 %fusion.3 = bf16[8,2,128,1152]{2,3,1,0:T(8,128)(2,1)S(1)} fusion(bf16[1152,8,128,1]{0,2,3,1:T(8,128)(2,1)S(1)} %bitcast.139, bf16[128,8,2,128]{0,3,2,1:T(8,128)(2,1)S(1)} %bitcast.142, f32[8,2,128]{2,1,0:T(2,128)S(1)} %bitcast.157, f32[8,2,128,1152]{2,3,1,0:T(8,128)} %get-tuple-element.75, f32[8,2,128]{2,1,0:T(2,128)S(1)} %copy-done.13), kind=kOutput, calls=%fused_computation.7 | convolution fusion | flops 613416960 | bytes 17055744 | tf_op jit(solution)/shard_map/tgrd,egd->grte/dot_general | solution.py:82
  99.1 2.9 fusion.1
  102.7 2.1 fusion.61
  104.8 3.5 collective-permute-start.8
  108.9 2.4 collective-permute-start.13
  112.7 28.7 %collective-permute-done.8 = bf16[128,2048]{0,1:T(8,128)(2,1)S(1)} collective-permute-done((bf16[128,2048]{0,1:T(8,128)(2,1)S(1)}, bf16[128,2048]{0,1:T(8,128)(2,1)S(1)}, u32[]{:S(2)}, u32[]{:S(2)}) %collective-permute-start.8) | collective-permute-done | bytes 524320 | tf_op jit(solution)/shard_map/ppermute | solution.py:38
  141.4 3.6 %collective-permute-start.11 = (bf16[128,2048]{0,1:T(8,128)(2,1)S(1)}, bf16[128,2048]{0,1:T(8,128)(2,1)S(1)}, u32[]{:S(2)}, u32[]{:S(2)}) collective-permute-start(bf16[128,2048]{0,1:T(8,128)(2,1)S(1)} %get-tuple-element.43), channel_id=1, source_target_pairs={{0,24},{8,0},{16,8},{24,16},{1,25},{9,1},{17,9},{25,17},{2,26},{10... | collective-permute-start | bytes 1572872 | tf_op jit(solution)/shard_map/ppermute | solution.py:38
  147.7 8.6 %collective-permute-done.12 = bf16[128,2048]{0,1:T(8,128)(2,1)S(1)} collective-permute-done((bf16[128,2048]{0,1:T(8,128)(2,1)S(1)}, bf16[128,2048]{0,1:T(8,128)(2,1)S(1)}, u32[]{:S(2)}, u32[]{:S(2)}) %collective-permute-start.12) | collective-permute-done | bytes 524320 | tf_op jit(solution)/shard_map/ppermute | solution.py:38
  156.3 4.1 %collective-permute-done.14 = bf16[128,2048]{0,1:T(8,128)(2,1)S(1)} collective-permute-done((bf16[128,2048]{0,1:T(8,128)(2,1)S(1)}, bf16[128,2048]{0,1:T(8,128)(2,1)S(1)}, u32[]{:S(2)}, u32[]{:S(2)}) %collective-permute-start.14) | collective-permute-done | bytes 524320 | tf_op jit(solution)/shard_map/ppermute | solution.py:113
  160.4 2.2 add_convert_fusion
  166.6 10.7 %collective-permute-done.15 = bf16[128,2048]{0,1:T(8,128)(2,1)S(1)} collective-permute-done((bf16[128,2048]{0,1:T(8,128)(2,1)}, bf16[128,2048]{0,1:T(8,128)(2,1)S(1)}, u32[]{:S(2)}, u32[]{:S(2)}) %collective-permute-start.15) | collective-permute-done | bytes 524320 | tf_op jit(solution)/shard_map/ppermute | solution.py:113
  181.7 11.2 %collective-permute-done.18 = bf16[128,2368]{0,1:T(8,128)(2,1)S(1)} collective-permute-done((bf16[128,2368]{0,1:T(8,128)(2,1)}, bf16[128,2368]{0,1:T(8,128)(2,1)S(1)}, u32[]{:S(2)}, u32[]{:S(2)}) %collective-permute-start.18) | collective-permute-done | bytes 606240 | tf_op jit(solution)/shard_map/ppermute | solution.py:38
  192.9 2.1 collective-permute-done.17
  195.1 16.0 %collective-permute-done.16 = bf16[128,2368]{0,1:T(8,128)(2,1)S(1)} collective-permute-done((bf16[128,2368]{0,1:T(8,128)(2,1)S(1)}, bf16[128,2368]{0,1:T(8,128)(2,1)S(1)}, u32[]{:S(2)}, u32[]{:S(2)}) %collective-permute-start.16) | collective-permute-done | bytes 606240 | tf_op jit(solution)/shard_map/ppermute | solution.py:38
  211.1 5.0 %fusion.10 = f32[1344,1024]{1,0:T(8,128)} fusion(bf16[128,1344]{0,1:T(8,128)(2,1)S(1)} %slice.107, bf16[128,1344]{0,1:T(8,128)(2,1)S(1)} %slice.106, bf16[128,1344]{0,1:T(8,128)(2,1)S(1)} %slice.105, bf16[128,1344]{0,1:T(8,128)(2,1)} %bitcast.154, bf16[128,1024]{0,1:T(8,128)(2,1)S(1)} %slice.110, bf16[128,1024]{0,1:T(8,128)(2,1)S(1)} %slice.109, ...), kind=kOutput, calls=%fused_computation.20 | convolution fusion | flops 1418985472 | bytes 7929856 | tf_op jit(solution)/shard_map/dot_general | solution.py:217
  216.1 5.9 %reshape.128 = f32[8,4,2,21,1024]{4,3,2,1,0:T(8,128)} reshape(f32[1344,1024]{1,0:T(8,128)} %fusion.10) | data formatting | bytes 11010048 | tf_op jit(solution)/shard_map/reshape | solution.py:223
  222.0 2.1 fusion.9
  225.5 2.3 constant_dynamic-slice_fusion.8
  232.5 2.7 collective-permute-start.22
  236.4 13.4 %collective-permute-done.22 = bf16[8,21,1024]{2,0,1:T(8,128)(2,1)} collective-permute-done((bf16[8,21,1024]{2,0,1:T(8,128)(2,1)}, bf16[8,21,1024]{2,0,1:T(8,128)(2,1)}, u32[]{:S(2)}, u32[]{:S(2)}) %collective-permute-start.22) | collective-permute-done | bytes 344096 | tf_op jit(solution)/shard_map/ppermute | solution.py:38
  249.8 4.5 %collective-permute-done.20 = bf16[8,21,1024]{2,0,1:T(8,128)(2,1)} collective-permute-done((bf16[8,21,1024]{2,0,1:T(8,128)(2,1)S(1)}, bf16[8,21,1024]{2,0,1:T(8,128)(2,1)}, u32[]{:S(2)}, u32[]{:S(2)}) %collective-permute-start.20) | collective-permute-done | bytes 344096 | tf_op jit(solution)/shard_map/ppermute | solution.py:38
  258.2 2.6 collective-permute-start.28
  261.5 5.7 %collective-permute-start.27 = (f32[21,1024]{1,0:T(8,128)}, f32[21,1024]{1,0:T(8,128)}, u32[]{:S(2)}, u32[]{:S(2)}) collective-permute-start(f32[21,1024]{1,0:T(8,128)} %bitcast.127), channel_id=1, source_target_pairs={{0,160},{32,192},{64,224},{96,0},{128,32},{160,64},{192,96},{224,1... | collective-permute-start | bytes 258056 | tf_op jit(solution)/shard_map/ppermute | solution.py:38
  268.5 3.3 collective-permute-start.25
  273.1 3.6 %collective-permute-start.24 = (f32[21,1024]{1,0:T(8,128)}, f32[21,1024]{1,0:T(8,128)}, u32[]{:S(2)}, u32[]{:S(2)}) collective-permute-start(f32[21,1024]{1,0:T(8,128)} %bitcast.130), channel_id=1, source_target_pairs={{0,64},{32,96},{64,128},{96,160},{128,192},{160,224},{192,0},{224,... | collective-permute-start | bytes 258056 | tf_op jit(solution)/shard_map/ppermute | solution.py:38
  277.3 3.4 fusion.19
  284.9 4.5 %collective-permute-done.23 = f32[21,1024]{1,0:T(8,128)} collective-permute-done((f32[21,1024]{1,0:T(8,128)}, f32[21,1024]{1,0:T(8,128)}, u32[]{:S(2)}, u32[]{:S(2)}) %collective-permute-start.23) | collective-permute-done | bytes 86048 | tf_op jit(solution)/shard_map/ppermute | solution.py:38
  295.2 2.9 collective-permute-done.31
  299.5 3.1 collective-permute-done.32
  304.1 2.9 collective-permute-done.33
  308.4 3.1 collective-permute-done.34
  313.0 2.9 collective-permute-done.35
  317.3 3.8 %collective-permute-done.36 = f32[]{:T(128)} collective-permute-done((f32[]{:T(128)}, f32[]{:T(128)}, u32[]{:S(2)}, u32[]{:S(2)}) %collective-permute-start.36) | collective-permute-done | bytes 36 | tf_op jit(solution)/shard_map/ppermute | solution.py:38
  321.7 2.7 collective-permute-start.37
  324.4 3.7 %collective-permute-done.37 = f32[]{:T(128)} collective-permute-done((f32[]{:T(128)}, f32[]{:T(128)}, u32[]{:S(2)}, u32[]{:S(2)}) %collective-permute-start.37) | collective-permute-done | bytes 36 | tf_op jit(solution)/shard_map/ppermute | solution.py:38
  330.5 22.3 %all-gather = bf16[8,21,1024]{2,1,0:T(8,128)(2,1)S(1)} all-gather(bf16[1,21,1024]{2,1,0:T(8,128)(2,1)S(1)} %get-tuple-element.35), channel_id=1, replica_groups=mesh['cz'=8,'cx'=4,'y'=4,'core'=2] {'y','core'}, dimensions={0}, use_global_device_ids=true | all-gather | bytes 387072 | tf_op jit(solution)/shard_map/all_gather | solution.py:246
  (135 shorter events, 64.9 us)
Async XLA Ops:
  1.3 2.3 copy-start.14
  3.6 15.7 %collective-permute-start = (bf16[128,2176]{0,1:T(8,128)(2,1)S(1)}, bf16[128,2176]{0,1:T(8,128)(2,1)S(1)}, u32[]{:S(2)}, u32[]{:S(2)}) collective-permute-start(bf16[128,2176]{0,1:T(8,128)(2,1)S(1)} %pad_maximum_fusion.4), channel_id=1, source_target_pairs={{0,32},{32,64},{64,96},{96,128},{128,160},{160,192},{192,224},{1,3... | collective-permute-start | bytes 1671176 | tf_op jit(solution)/shard_map/ppermute | solution.py:113
  10.8 67.0 %copy-start.7 = (bf16[1,128,2048]{1,2,0:T(8,128)(2,1)}, bf16[1,128,2048]{1,2,0:T(8,128)(2,1)S(1)}, u32[]{:S(2)}) copy-start(bf16[1,128,2048]{1,2,0:T(8,128)(2,1)S(1)} %copy.111) | copy-start | bytes 1572868
  19.3 14.5 %collective-permute-start.1 = (bf16[128,2176]{0,1:T(8,128)(2,1)S(1)}, bf16[128,2176]{0,1:T(8,128)(2,1)S(1)}, u32[]{:S(2)}, u32[]{:S(2)}) collective-permute-start(bf16[128,2176]{0,1:T(8,128)(2,1)S(1)} %collective-permute-done), channel_id=1, source_target_pairs={{0,32},{32,64},{64,96},{96,128},{128,160},{160,192},{192,224},{1,3... | collective-permute-start | bytes 1671176 | tf_op jit(solution)/shard_map/ppermute | solution.py:113
  23.5 38.7 %copy-start.11 = (s32[1152]{0:T(1024)}, s32[1152]{0:T(1024)S(1)}, u32[]{:S(2)}) copy-start(s32[1152]{0:T(1024)S(1)} %get-tuple-element.76) | copy-start | bytes 13828
  23.5 14.7 %collective-permute-start.2 = (bf16[128,2176]{0,1:T(8,128)(2,1)S(1)}, bf16[128,2176]{0,1:T(8,128)(2,1)S(1)}, u32[]{:S(2)}, u32[]{:S(2)}) collective-permute-start(bf16[128,2176]{0,1:T(8,128)(2,1)S(1)} %collective-permute-done), channel_id=1, source_target_pairs={{0,8},{8,16},{16,24},{24,0},{1,9},{9,17},{17,25},{25,1},{2,10},{10... | collective-permute-start | bytes 1671176 | tf_op jit(solution)/shard_map/ppermute | solution.py:38
  24.8 25.3 %collective-permute-start.3 = (bf16[128,2176]{0,1:T(8,128)(2,1)S(1)}, bf16[128,2176]{0,1:T(8,128)(2,1)S(1)}, u32[]{:S(2)}, u32[]{:S(2)}) collective-permute-start(bf16[128,2176]{0,1:T(8,128)(2,1)S(1)} %collective-permute-done), channel_id=1, source_target_pairs={{0,16},{8,24},{16,0},{24,8},{1,17},{9,25},{17,1},{25,9},{2,18},{10... | collective-permute-start | bytes 1671176 | tf_op jit(solution)/shard_map/ppermute | solution.py:38
  27.2 25.5 %collective-permute-start.4 = (bf16[128,2176]{0,1:T(8,128)(2,1)S(1)}, bf16[128,2176]{0,1:T(8,128)(2,1)S(1)}, u32[]{:S(2)}, u32[]{:S(2)}) collective-permute-start(bf16[128,2176]{0,1:T(8,128)(2,1)S(1)} %collective-permute-done), channel_id=1, source_target_pairs={{0,24},{8,0},{16,8},{24,16},{1,25},{9,1},{17,9},{25,17},{2,26},{10... | collective-permute-start | bytes 1671176 | tf_op jit(solution)/shard_map/ppermute | solution.py:38
  34.2 27.9 %collective-permute-start.5 = (bf16[128,2176]{0,1:T(8,128)(2,1)S(1)}, bf16[128,2176]{0,1:T(8,128)(2,1)S(1)}, u32[]{:S(2)}, u32[]{:S(2)}) collective-permute-start(bf16[128,2176]{0,1:T(8,128)(2,1)S(1)} %get-tuple-element.58), channel_id=1, source_target_pairs={{0,8},{8,16},{16,24},{24,0},{1,9},{9,17},{17,25},{25,1},{2,10},{10... | collective-permute-start | bytes 1671176 | tf_op jit(solution)/shard_map/ppermute | solution.py:38
  35.4 38.5 %collective-permute-start.6 = (bf16[128,2176]{0,1:T(8,128)(2,1)S(1)}, bf16[128,2176]{0,1:T(8,128)(2,1)S(1)}, u32[]{:S(2)}, u32[]{:S(2)}) collective-permute-start(bf16[128,2176]{0,1:T(8,128)(2,1)S(1)} %get-tuple-element.57), channel_id=1, source_target_pairs={{0,16},{8,24},{16,0},{24,8},{1,17},{9,25},{17,1},{25,9},{2,18},{10... | collective-permute-start | bytes 1671176 | tf_op jit(solution)/shard_map/ppermute | solution.py:38
  38.2 36.5 %collective-permute-start.7 = (bf16[128,2176]{0,1:T(8,128)(2,1)S(1)}, bf16[128,2176]{0,1:T(8,128)(2,1)S(1)}, u32[]{:S(2)}, u32[]{:S(2)}) collective-permute-start(bf16[128,2176]{0,1:T(8,128)(2,1)S(1)} %get-tuple-element.56), channel_id=1, source_target_pairs={{0,24},{8,0},{16,8},{24,16},{1,25},{9,1},{17,9},{25,17},{2,26},{10... | collective-permute-start | bytes 1671176 | tf_op jit(solution)/shard_map/ppermute | solution.py:38
  76.7 7.4 %copy-start.3 = (bf16[1152,1024]{0,1:T(8,128)(2,1)}, bf16[1152,1024]{0,1:T(8,128)(2,1)S(1)}, u32[]{:S(2)}) copy-start(bf16[1152,1024]{0,1:T(8,128)(2,1)S(1)} %get-tuple-element.42) | copy-start | bytes 7077892
  90.4 8.6 %copy-start = (f32[8,1152,128,1]{1,2,3,0:T(8,128)}, f32[8,1152,128,1]{1,2,3,0:T(8,128)S(1)}, u32[]{:S(2)}) copy-start(f32[8,1152,128,1]{1,2,3,0:T(8,128)S(1)} %fusion.64) | copy-start | bytes 14155780
  91.6 5.3 %copy-start.8 = (bf16[1,128,2048]{1,2,0:T(8,128)(2,1)S(1)}, bf16[1,128,2048]{1,2,0:T(8,128)(2,1)}, u32[]{:S(2)}) copy-start(bf16[1,128,2048]{1,2,0:T(8,128)(2,1)} %copy-done.7) | copy-start | bytes 1572868
  96.9 2.1 copy-start.2
  99.1 3.6 %copy-start.1 = (f32[8,1152,128]{1,2,0:T(8,128)}, f32[8,1152,128]{1,2,0:T(8,128)S(1)}, u32[]{:S(2)}) copy-start(f32[8,1152,128]{1,2,0:T(8,128)S(1)} %bitcast_multiply_fusion) | copy-start | bytes 14155780
  104.8 36.6 %collective-permute-start.8 = (bf16[128,2048]{0,1:T(8,128)(2,1)S(1)}, bf16[128,2048]{0,1:T(8,128)(2,1)S(1)}, u32[]{:S(2)}, u32[]{:S(2)}) collective-permute-start(bf16[128,2048]{0,1:T(8,128)(2,1)S(1)} %get-tuple-element.48), channel_id=1, source_target_pairs={{0,24},{8,0},{16,8},{24,16},{1,25},{9,1},{17,9},{25,17},{2,26},{10... | collective-permute-start | bytes 1572872 | tf_op jit(solution)/shard_map/ppermute | solution.py:38
  108.3 36.7 %collective-permute-start.9 = (bf16[128,2048]{0,1:T(8,128)(2,1)S(1)}, bf16[128,2048]{0,1:T(8,128)(2,1)S(1)}, u32[]{:S(2)}, u32[]{:S(2)}) collective-permute-start(bf16[128,2048]{0,1:T(8,128)(2,1)S(1)} %get-tuple-element.47), channel_id=1, source_target_pairs={{0,16},{8,24},{16,0},{24,8},{1,17},{9,25},{17,1},{25,9},{2,18},{10... | collective-permute-start | bytes 1572872 | tf_op jit(solution)/shard_map/ppermute | solution.py:38
  108.4 36.5 %collective-permute-start.10 = (bf16[128,2048]{0,1:T(8,128)(2,1)S(1)}, bf16[128,2048]{0,1:T(8,128)(2,1)S(1)}, u32[]{:S(2)}, u32[]{:S(2)}) collective-permute-start(bf16[128,2048]{0,1:T(8,128)(2,1)S(1)} %get-tuple-element.46), channel_id=1, source_target_pairs={{0,8},{8,16},{16,24},{24,0},{1,9},{9,17},{17,25},{25,1},{2,10},{10... | collective-permute-start | bytes 1572872 | tf_op jit(solution)/shard_map/ppermute | solution.py:38
  108.9 38.7 %collective-permute-start.13 = (bf16[128,2048]{0,1:T(8,128)(2,1)S(1)}, bf16[128,2048]{0,1:T(8,128)(2,1)S(1)}, u32[]{:S(2)}, u32[]{:S(2)}) collective-permute-start(bf16[128,2048]{0,1:T(8,128)(2,1)S(1)} %get-tuple-element.44), channel_id=1, source_target_pairs={{0,8},{8,16},{16,24},{24,0},{1,9},{9,17},{17,25},{25,1},{2,10},{10... | collective-permute-start | bytes 1572872 | tf_op jit(solution)/shard_map/ppermute | solution.py:38
  111.3 45.0 %collective-permute-start.12 = (bf16[128,2048]{0,1:T(8,128)(2,1)S(1)}, bf16[128,2048]{0,1:T(8,128)(2,1)S(1)}, u32[]{:S(2)}, u32[]{:S(2)}) collective-permute-start(bf16[128,2048]{0,1:T(8,128)(2,1)S(1)} %get-tuple-element.45), channel_id=1, source_target_pairs={{0,16},{8,24},{16,0},{24,8},{1,17},{9,25},{17,1},{25,9},{2,18},{10... | collective-permute-start | bytes 1572872 | tf_op jit(solution)/shard_map/ppermute | solution.py:38
  141.4 14.9 %collective-permute-start.11 = (bf16[128,2048]{0,1:T(8,128)(2,1)S(1)}, bf16[128,2048]{0,1:T(8,128)(2,1)S(1)}, u32[]{:S(2)}, u32[]{:S(2)}) collective-permute-start(bf16[128,2048]{0,1:T(8,128)(2,1)S(1)} %get-tuple-element.43), channel_id=1, source_target_pairs={{0,24},{8,0},{16,8},{24,16},{1,25},{9,1},{17,9},{25,17},{2,26},{10... | collective-permute-start | bytes 1572872 | tf_op jit(solution)/shard_map/ppermute | solution.py:38
  146.4 14.0 %collective-permute-start.14 = (bf16[128,2048]{0,1:T(8,128)(2,1)S(1)}, bf16[128,2048]{0,1:T(8,128)(2,1)S(1)}, u32[]{:S(2)}, u32[]{:S(2)}) collective-permute-start(bf16[128,2048]{0,1:T(8,128)(2,1)S(1)} %fusion.31), channel_id=1, source_target_pairs={{32,0},{64,32},{96,64},{128,96},{160,128},{192,160},{224,192},{33,... | collective-permute-start | bytes 1572872 | tf_op jit(solution)/shard_map/ppermute | solution.py:113
  162.6 14.7 %collective-permute-start.15 = (bf16[128,2048]{0,1:T(8,128)(2,1)}, bf16[128,2048]{0,1:T(8,128)(2,1)S(1)}, u32[]{:S(2)}, u32[]{:S(2)}) collective-permute-start(bf16[128,2048]{0,1:T(8,128)(2,1)} %add_convert_fusion), channel_id=1, source_target_pairs={{32,0},{64,32},{96,64},{128,96},{160,128},{192,160},{224,192},{33,... | collective-permute-start | bytes 1572872 | tf_op jit(solution)/shard_map/ppermute | solution.py:113
  180.2 12.7 %collective-permute-start.18 = (bf16[128,2368]{0,1:T(8,128)(2,1)}, bf16[128,2368]{0,1:T(8,128)(2,1)S(1)}, u32[]{:S(2)}, u32[]{:S(2)}) collective-permute-start(bf16[128,2368]{0,1:T(8,128)(2,1)} %get-tuple-element.72), channel_id=1, source_target_pairs={{0,24},{8,0},{16,8},{24,16},{1,25},{9,1},{17,9},{25,17},{2,26},{10... | collective-permute-start | bytes 1818632 | tf_op jit(solution)/shard_map/ppermute | solution.py:38
  180.8 14.3 %collective-permute-start.17 = (bf16[128,2368]{0,1:T(8,128)(2,1)}, bf16[128,2368]{0,1:T(8,128)(2,1)S(1)}, u32[]{:S(2)}, u32[]{:S(2)}) collective-permute-start(bf16[128,2368]{0,1:T(8,128)(2,1)} %get-tuple-element.73), channel_id=1, source_target_pairs={{0,16},{8,24},{16,0},{24,8},{1,17},{9,25},{17,1},{25,9},{2,18},{10... | collective-permute-start | bytes 1818632 | tf_op jit(solution)/shard_map/ppermute | solution.py:38
  180.8 30.3 %collective-permute-start.16 = (bf16[128,2368]{0,1:T(8,128)(2,1)S(1)}, bf16[128,2368]{0,1:T(8,128)(2,1)S(1)}, u32[]{:S(2)}, u32[]{:S(2)}) collective-permute-start(bf16[128,2368]{0,1:T(8,128)(2,1)S(1)} %get-tuple-element.71), channel_id=1, source_target_pairs={{0,8},{8,16},{16,24},{24,0},{1,9},{9,17},{17,25},{25,1},{2,10},{10... | collective-permute-start | bytes 1818632 | tf_op jit(solution)/shard_map/ppermute | solution.py:38
  224.9 3.3 collective-permute-start.19
  231.5 45.7 %copy-start.4 = (bf16[1152,1024]{0,1:T(8,128)(2,1)S(1)}, bf16[1152,1024]{0,1:T(8,128)(2,1)}, u32[]{:S(2)}) copy-start(bf16[1152,1024]{0,1:T(8,128)(2,1)} %copy-done.3) | copy-start | bytes 7077892
  232.5 17.3 %collective-permute-start.22 = (bf16[8,21,1024]{2,0,1:T(8,128)(2,1)}, bf16[8,21,1024]{2,0,1:T(8,128)(2,1)}, u32[]{:S(2)}, u32[]{:S(2)}) collective-permute-start(bf16[8,21,1024]{2,0,1:T(8,128)(2,1)} %get-tuple-element.50), channel_id=1, source_target_pairs={{0,6},{2,0},{4,2},{6,4},{1,7},{3,1},{5,3},{7,5},{8,14},{10,8},{12,... | collective-permute-start | bytes 1032200 | tf_op jit(solution)/shard_map/ppermute | solution.py:38
  235.2 14.6 %collective-permute-start.21 = (bf16[8,21,1024]{2,0,1:T(8,128)(2,1)}, bf16[8,21,1024]{2,0,1:T(8,128)(2,1)}, u32[]{:S(2)}, u32[]{:S(2)}) collective-permute-start(bf16[8,21,1024]{2,0,1:T(8,128)(2,1)} %get-tuple-element.51), channel_id=1, source_target_pairs={{0,4},{2,6},{4,0},{6,2},{1,5},{3,7},{5,1},{7,3},{8,12},{10,14},{12... | collective-permute-start | bytes 1032200 | tf_op jit(solution)/shard_map/ppermute | solution.py:38
  235.7 18.5 %collective-permute-start.20 = (bf16[8,21,1024]{2,0,1:T(8,128)(2,1)S(1)}, bf16[8,21,1024]{2,0,1:T(8,128)(2,1)}, u32[]{:S(2)}, u32[]{:S(2)}) collective-permute-start(bf16[8,21,1024]{2,0,1:T(8,128)(2,1)S(1)} %get-tuple-element.49), channel_id=1, source_target_pairs={{0,2},{2,4},{4,6},{6,0},{1,3},{3,5},{5,7},{7,1},{8,10},{10,12},{12... | collective-permute-start | bytes 1032200 | tf_op jit(solution)/shard_map/ppermute | solution.py:38
  256.7 16.4 %collective-permute-start.29 = (f32[21,1024]{1,0:T(8,128)S(1)}, f32[21,1024]{1,0:T(8,128)S(1)}, u32[]{:S(2)}, u32[]{:S(2)}) collective-permute-start(f32[21,1024]{1,0:T(8,128)S(1)} %bitcast.156), channel_id=1, source_target_pairs={{0,224},{32,0},{64,32},{96,64},{128,96},{160,128},{192,160},{224,1... | collective-permute-start | bytes 258056 | tf_op jit(solution)/shard_map/ppermute | solution.py:38
  258.2 18.5 %collective-permute-start.28 = (f32[21,1024]{1,0:T(8,128)S(1)}, f32[21,1024]{1,0:T(8,128)S(1)}, u32[]{:S(2)}, u32[]{:S(2)}) collective-permute-start(f32[21,1024]{1,0:T(8,128)S(1)} %bitcast.155), channel_id=1, source_target_pairs={{0,192},{32,224},{64,0},{96,32},{128,64},{160,96},{192,128},{224,1... | collective-permute-start | bytes 258056 | tf_op jit(solution)/shard_map/ppermute | solution.py:38
  261.5 21.9 %collective-permute-start.27 = (f32[21,1024]{1,0:T(8,128)}, f32[21,1024]{1,0:T(8,128)}, u32[]{:S(2)}, u32[]{:S(2)}) collective-permute-start(f32[21,1024]{1,0:T(8,128)} %bitcast.127), channel_id=1, source_target_pairs={{0,160},{32,192},{64,224},{96,0},{128,32},{160,64},{192,96},{224,1... | collective-permute-start | bytes 258056 | tf_op jit(solution)/shard_map/ppermute | solution.py:38
  267.9 15.5 %collective-permute-start.26 = (f32[21,1024]{1,0:T(8,128)}, f32[21,1024]{1,0:T(8,128)}, u32[]{:S(2)}, u32[]{:S(2)}) collective-permute-start(f32[21,1024]{1,0:T(8,128)} %bitcast.128), channel_id=1, source_target_pairs={{0,128},{32,160},{64,192},{96,224},{128,0},{160,32},{192,64},{224,... | collective-permute-start | bytes 258056 | tf_op jit(solution)/shard_map/ppermute | solution.py:38
  268.5 16.4 %collective-permute-start.25 = (f32[21,1024]{1,0:T(8,128)}, f32[21,1024]{1,0:T(8,128)}, u32[]{:S(2)}, u32[]{:S(2)}) collective-permute-start(f32[21,1024]{1,0:T(8,128)} %bitcast.129), channel_id=1, source_target_pairs={{0,96},{32,128},{64,160},{96,192},{128,224},{160,0},{192,32},{224,... | collective-permute-start | bytes 258056 | tf_op jit(solution)/shard_map/ppermute | solution.py:38
  273.1 3.6 %copy-start.9 = (f32[21,1024]{1,0:T(8,128)}, f32[21,1024]{1,0:T(8,128)S(1)}, u32[]{:S(2)}) copy-start(f32[21,1024]{1,0:T(8,128)S(1)} %collective-permute-done.29) | copy-start | bytes 258052
  273.1 11.8 %collective-permute-start.24 = (f32[21,1024]{1,0:T(8,128)}, f32[21,1024]{1,0:T(8,128)}, u32[]{:S(2)}, u32[]{:S(2)}) collective-permute-start(f32[21,1024]{1,0:T(8,128)} %bitcast.130), channel_id=1, source_target_pairs={{0,64},{32,96},{64,128},{96,160},{128,192},{160,224},{192,0},{224,... | collective-permute-start | bytes 258056 | tf_op jit(solution)/shard_map/ppermute | solution.py:38
  277.3 12.1 %collective-permute-start.23 = (f32[21,1024]{1,0:T(8,128)}, f32[21,1024]{1,0:T(8,128)}, u32[]{:S(2)}, u32[]{:S(2)}) collective-permute-start(f32[21,1024]{1,0:T(8,128)} %bitcast.131), channel_id=1, source_target_pairs={{0,32},{32,64},{64,96},{96,128},{128,160},{160,192},{192,224},{224... | collective-permute-start | bytes 258056 | tf_op jit(solution)/shard_map/ppermute | solution.py:38
  291.2 1.9 collective-permute-start.30
  294.4 3.7 %collective-permute-start.31 = (f32[]{:T(128)}, f32[]{:T(128)}, u32[]{:S(2)}, u32[]{:S(2)}) collective-permute-start(f32[]{:T(128)} %add.464), channel_id=1, source_target_pairs={{0,2},{2,4},{4,6},{6,0},{1,3},{3,5},{5,7},{7,1},{8,10},{10,12},{12... | collective-permute-start | bytes 20 | tf_op jit(solution)/shard_map/ppermute | solution.py:38
  298.7 4.0 %collective-permute-start.32 = (f32[]{:T(128)}, f32[]{:T(128)}, u32[]{:S(2)}, u32[]{:S(2)}) collective-permute-start(f32[]{:T(128)} %add.465), channel_id=1, source_target_pairs={{0,4},{2,6},{4,0},{6,2},{1,5},{3,7},{5,1},{7,3},{8,12},{10,14},{12... | collective-permute-start | bytes 20 | tf_op jit(solution)/shard_map/ppermute | solution.py:38
  303.3 3.7 %collective-permute-start.33 = (f32[]{:T(128)}, f32[]{:T(128)}, u32[]{:S(2)}, u32[]{:S(2)}) collective-permute-start(f32[]{:T(128)} %add.466), channel_id=1, source_target_pairs={{0,8},{8,16},{16,24},{24,0},{1,9},{9,17},{17,25},{25,1},{2,10},{10... | collective-permute-start | bytes 20 | tf_op jit(solution)/shard_map/ppermute | solution.py:38
  307.6 4.0 %collective-permute-start.34 = (f32[]{:T(128)}, f32[]{:T(128)}, u32[]{:S(2)}, u32[]{:S(2)}) collective-permute-start(f32[]{:T(128)} %add.467), channel_id=1, source_target_pairs={{0,16},{8,24},{16,0},{24,8},{1,17},{9,25},{17,1},{25,9},{2,18},{10... | collective-permute-start | bytes 20 | tf_op jit(solution)/shard_map/ppermute | solution.py:38
  312.2 3.7 %collective-permute-start.35 = (f32[]{:T(128)}, f32[]{:T(128)}, u32[]{:S(2)}, u32[]{:S(2)}) collective-permute-start(f32[]{:T(128)} %add.468), channel_id=1, source_target_pairs={{0,32},{32,64},{64,96},{96,128},{128,160},{160,192},{192,224},{224... | collective-permute-start | bytes 20 | tf_op jit(solution)/shard_map/ppermute | solution.py:38
  316.5 4.6 %collective-permute-start.36 = (f32[]{:T(128)}, f32[]{:T(128)}, u32[]{:S(2)}, u32[]{:S(2)}) collective-permute-start(f32[]{:T(128)} %add.469), channel_id=1, source_target_pairs={{0,64},{32,96},{64,128},{96,160},{128,192},{160,224},{192,0},{224,... | collective-permute-start | bytes 20 | tf_op jit(solution)/shard_map/ppermute | solution.py:38
  321.7 6.4 %collective-permute-start.37 = (f32[]{:T(128)}, f32[]{:T(128)}, u32[]{:S(2)}, u32[]{:S(2)}) collective-permute-start(f32[]{:T(128)} %add.470), channel_id=1, source_target_pairs={{0,128},{32,160},{64,192},{96,224},{128,0},{160,32},{192,64},{224,... | collective-permute-start | bytes 20 | tf_op jit(solution)/shard_map/ppermute | solution.py:38
  (6 other events, 8.7 us)

commit v4 on v3

--- a/solution.py
+++ b/solution.py
@@ -115,12 +115,26 @@
 
 def all_sum(x, axes):
     for axis in axes:
-        count = lax.axis_size(axis)
-        step = 1
-        while step < count:
-            x = x + cyclic(x, axis, step)
-            step *= 2
+        total = x
+        for by in range(1, lax.axis_size(axis)):
+            total = total + cyclic(x, axis, by)
+        x = total
     return x
+
+
+def halving_scatter(data, axis):
+    count = lax.axis_size(axis)
+    me = lax.axis_index(axis)
+    distance = count // 2
+    while distance >= 1:
+        bit = (me // distance) % 2
+        halves = data.reshape((2, data.shape[0] // 2) + data.shape[1:])
+        keep = lax.dynamic_index_in_dim(halves, bit, 0, keepdims=False)
+        sent = lax.dynamic_index_in_dim(halves, 1 - bit, 0, keepdims=False)
+        pairs = [(i, i ^ distance) for i in range(count)]
+        data = keep + lax.ppermute(sent, axis, pairs)
+        distance //= 2
+    return data[0]
 
 
 def shards(
@@ -209,11 +223,11 @@
 
     x_list = [columns(icx)]
     v_list = [value_out]
+    x_late, _ = lax.optimization_barrier((x_view, kv_rows))
+    x_view = x_late
     for by in range(1, ncx):
-        piece = jnp.concatenate([columns((icx + by) % ncx), value_out], axis=1)
-        got = cyclic(piece, "cx", by)
-        x_list.append(got[:, : -kv_width])
-        v_list.append(got[:, -kv_width:])
+        x_list.append(cyclic(columns((icx + by) % ncx), "cx", by))
+        v_list.append(cyclic(value_out, "cx", by))
     partial = lax.dot_general(
         jnp.concatenate(x_list, axis=0),
         jnp.concatenate(v_list, axis=0),
@@ -231,10 +245,7 @@
     for by in range(1, ny):
         sent = lax.dynamic_index_in_dim(stage, (iy + by) % ny, 1, keepdims=False)
         stage_y = stage_y + cyclic(low(sent), "y", by).astype(jnp.float32)
-    weight_grad = lax.dynamic_index_in_dim(stage_y, iz, 0, keepdims=False)
-    for by in range(1, nz):
-        sent = lax.dynamic_index_in_dim(stage_y, (iz + by) % nz, 0, keepdims=False)
-        weight_grad = weight_grad + cyclic(sent, "cz", by)
+    weight_grad = halving_scatter(stage_y, "cz")
 
     square_total = all_sum(jnp.sum(weight_grad * weight_grad), ("core", "y", "cx", "cz"))
     norm_total = jnp.sqrt(square_total + 1e-06)

time: 359 us -> 384 us (1.070)
  local copies, waits for them, and re-layouts: 36.1 us -> 45.4 us
  starting transfers between devices: 63.5 us -> 69.6 us
  matrix products: 24 us -> 29.7 us
    ppermute x0 -> x3, waiting for transfers between devices: none -> 25.8 us  [halving_scatter(): data = keep + lax.ppermute(sent, axis, pairs)]
    ppermute x34 -> x36, waiting for transfers between devices: 149 us -> 129 us  [cyclic(): return lax.ppermute(x, axis, [(i, (i + by) % count) for i in range(count)])]
    reshape x0 -> x4, local copies, waits for them, and re-layouts: none -> 13.7 us  [the longest x1 6.06 us: attend(): value_gradient.reshape(extent_rows, KEY_VALUE_HEADS * HEAD_SIZE)]
    ppermute x0 -> x3, starting transfers between devices: none -> 10 us  [halving_scatter(): data = keep + lax.ppermute(sent, axis, pairs)]
    ppermute x4, waiting for transfers between devices: 28.6 us -> 19.3 us  [shift(): return lax.ppermute(x, axis, pairs)]
    unnamed x54 -> x39, local copies, waits for them, and re-layouts: 16.8 us -> 11.1 us
    ppermute x34 -> x36, starting transfers between devices: 52.4 us -> 48.5 us  [cyclic(): return lax.ppermute(x, axis, [(i, (i + by) % count) for i in range(count)])]
  transfers between devices with their start and end apart: 38 -> 43, of which waited for: 27 -> 24; matrix products, arithmetic and copies ran while one was open for 6% -> 5% of each run, Pallas kernels for 0% -> 0%
where the time goes in v4:
time: 384 us; the launch traced here: 379 us
  waiting for transfers between devices  174 us (45%)
  starting transfers between devices  69.6 us (18%)
  local copies, waits for them, and re-layouts  45.4 us (12%)
  matrix products  29.7 us (8%)
  blocking collectives  24.6 us (6%)
  other arithmetic  23.8 us (6%)
  between operations  11.1 us (3%)
    ppermute x36, waiting for transfers between devices, cyclic(): return lax.ppermute(x, axis, [(i, (i + by) % count) for i in range(count)])  129 us
    ppermute x36, starting transfers between devices, cyclic(): return lax.ppermute(x, axis, [(i, (i + by) % count) for i in range(count)])  48.5 us
    ppermute x3, waiting for transfers between devices, halving_scatter(): data = keep + lax.ppermute(sent, axis, pairs)  25.8 us
    all_gather x1, blocking collectives, shards(): lax.all_gather(new_master.astype(jnp.bfloat16), DP, axis=0, tiled=True)  24.6 us
    ppermute x4, waiting for transfers between devices, shift(): return lax.ppermute(x, axis, pairs)  19.3 us
    unnamed x39, local copies, waits for them, and re-layouts  11.1 us
    ppermute x4, starting transfers between devices, shift(): return lax.ppermute(x, axis, pairs)  11.1 us
    ppermute x3, starting transfers between devices, halving_scatter(): data = keep + lax.ppermute(sent, axis, pairs)  10 us
  transfers between devices with their start and end apart: 43, of which 24 were waited for; matrix products, arithmetic and copies ran while one was open for 5% of the time, Pallas kernels for 0%

profile of v4, /device:TPU:1, one launch (start us, length us, event | category | flops | bytes accessed | tf_op | source)
XLA Modules:
  0.0 378.7 jit_solution(5709284791297274787)
XLA Ops:
  3.6 4.4 %collective-permute-start = (bf16[128,2176]{0,1:T(8,128)(2,1)S(1)}, bf16[128,2176]{0,1:T(8,128)(2,1)S(1)}, u32[]{:S(2)}, u32[]{:S(2)}) collective-permute-start(bf16[128,2176]{0,1:T(8,128)(2,1)S(1)} %pad_maximum_fusion.1), channel_id=1, source_target_pairs={{0,32},{32,64},{64,96},{96,128},{128,160},{160,192},{192,224},{1,3... | collective-permute-start | bytes 1671176 | tf_op jit(solution)/shard_map/ppermute | solution.py:113
  10.9 8.4 %collective-permute-done = bf16[128,2176]{0,1:T(8,128)(2,1)S(1)} collective-permute-done((bf16[128,2176]{0,1:T(8,128)(2,1)S(1)}, bf16[128,2176]{0,1:T(8,128)(2,1)S(1)}, u32[]{:S(2)}, u32[]{:S(2)}) %collective-permute-start) | collective-permute-done | bytes 557088 | tf_op jit(solution)/shard_map/ppermute | solution.py:113
  19.3 4.1 %collective-permute-start.1 = (bf16[128,2176]{0,1:T(8,128)(2,1)S(1)}, bf16[128,2176]{0,1:T(8,128)(2,1)S(1)}, u32[]{:S(2)}, u32[]{:S(2)}) collective-permute-start(bf16[128,2176]{0,1:T(8,128)(2,1)S(1)} %collective-permute-done), channel_id=1, source_target_pairs={{0,32},{32,64},{64,96},{96,128},{128,160},{160,192},{192,224},{1,3... | collective-permute-start | bytes 1671176 | tf_op jit(solution)/shard_map/ppermute | solution.py:113
  23.5 2.6 collective-permute-start.4
  27.2 6.6 %collective-permute-done.1 = bf16[128,2176]{0,1:T(8,128)(2,1)S(1)} collective-permute-done((bf16[128,2176]{0,1:T(8,128)(2,1)S(1)}, bf16[128,2176]{0,1:T(8,128)(2,1)S(1)}, u32[]{:S(2)}, u32[]{:S(2)}) %collective-permute-start.1) | collective-permute-done | bytes 557088 | tf_op jit(solution)/shard_map/ppermute | solution.py:113
  34.2 2.6 collective-permute-start.7
  37.5 18.9 %collective-permute-done.2 = bf16[128,2176]{0,1:T(8,128)(2,1)S(1)} collective-permute-done((bf16[128,2176]{0,1:T(8,128)(2,1)S(1)}, bf16[128,2176]{0,1:T(8,128)(2,1)S(1)}, u32[]{:S(2)}, u32[]{:S(2)}) %collective-permute-start.2) | collective-permute-done | bytes 557088 | tf_op jit(solution)/shard_map/ppermute | solution.py:38
  57.0 20.9 %collective-permute-done.5 = bf16[128,2176]{0,1:T(8,128)(2,1)S(1)} collective-permute-done((bf16[128,2176]{0,1:T(8,128)(2,1)S(1)}, bf16[128,2176]{0,1:T(8,128)(2,1)S(1)}, u32[]{:S(2)}, u32[]{:S(2)}) %collective-permute-start.5) | collective-permute-done | bytes 557088 | tf_op jit(solution)/shard_map/ppermute | solution.py:38
  81.2 6.3 %fusion.58 = (f32[8,2,128]{2,1,0:T(2,128)}, f32[8,2,128,1152]{2,3,1,0:T(8,128)}) fusion(pred[128,1152]{0,1:T(8,128)(4,1)S(1)} %fusion.44, bf16[1152,8,128,1]{0,2,3,1:T(8,128)(2,1)S(1)} %bitcast.122, bf16[128,8,2,128]{0,3,2,1:T(8,128)(2,1)S(1)} %bitcast.136), kind=kOutput, calls=%fused_computation.126 | convolution fusion | flops 613418112 | bytes 12476416 | tf_op jit(solution)/shard_map/sub | solution.py:75
  87.6 4.8 %fusion.8 = bf16[8,2,128,1152]{2,3,1,0:T(8,128)(2,1)S(1)} fusion(f32[8,2,128,1152]{2,3,1,0:T(8,128)} %get-tuple-element.67, f32[8,2,128]{2,1,0:T(2,128)} %get-tuple-element.66), kind=kLoop, calls=%fused_computation.16 | loop fusion | flops 4718592 | bytes 14163968 | tf_op jit(solution)/shard_map/convert_element_type | solution.py:77
  92.4 3.8 fusion.59
  97.3 6.1 %copy.79 = f32[1152,1024]{1,0:T(8,128)} copy(f32[1152,1024]{0,1:T(8,128)} %bitcast.120) | data formatting | bytes 9437184 | tf_op jit(solution)/shard_map/reshape | solution.py:106
  103.3 6.3 %fusion.3 = bf16[8,2,128,1152]{2,3,1,0:T(8,128)(2,1)S(1)} fusion(bf16[1152,8,128,1]{0,2,3,1:T(8,128)(2,1)} %bitcast.124, bf16[128,8,2,128]{0,3,2,1:T(8,128)(2,1)S(1)} %bitcast.128, f32[8,2,128]{2,1,0:T(2,128)S(1)} %bitcast.141, f32[8,2,128,1152]{2,3,1,0:T(8,128)} %get-tuple-element.67, f32[8,2,128]{2,1,0:T(2,128)S(1)} %copy-done.9), kind=kOutput, calls=%fused_computation.7 | convolution fusion | flops 613416960 | bytes 17055744 | tf_op jit(solution)/shard_map/tgrd,egd->grte/dot_general | solution.py:82
  109.6 3.7 bitcast_multiply_fusion
  113.3 6.1 %copy.78 = f32[1152,1024]{1,0:T(8,128)} copy(f32[1152,1024]{0,1:T(8,128)} %bitcast.121) | data formatting | bytes 9437184 | tf_op jit(solution)/shard_map/reshape | solution.py:105
  119.4 4.5 %fusion.1 = bf16[1152,2048]{1,0:T(8,128)(2,1)S(1)} fusion(f32[1152,1024]{1,0:T(8,128)} %copy.79, f32[1152,1024]{1,0:T(8,128)} %copy.78), kind=kLoop, calls=%fused_computation.4 | loop fusion | flops 9437184 | bytes 14155776 | tf_op jit(solution)/shard_map/convert.9
  125.3 2.1 collective-permute-start.8
  128.9 20.0 %collective-permute-done.10 = bf16[128,2048]{1,0:T(8,128)(2,1)S(1)} collective-permute-done((bf16[128,2048]{1,0:T(8,128)(2,1)S(1)}, bf16[128,2048]{1,0:T(8,128)(2,1)S(1)}, u32[]{:S(2)}, u32[]{:S(2)}) %collective-permute-start.10) | collective-permute-done | bytes 524320 | tf_op jit(solution)/shard_map/ppermute | solution.py:38
  152.2 9.6 %collective-permute-done.11 = bf16[128,2048]{1,0:T(8,128)(2,1)S(1)} collective-permute-done((bf16[128,2048]{1,0:T(8,128)(2,1)S(1)}, bf16[128,2048]{1,0:T(8,128)(2,1)S(1)}, u32[]{:S(2)}, u32[]{:S(2)}) %collective-permute-start.11) | collective-permute-done | bytes 524320 | tf_op jit(solution)/shard_map/ppermute | solution.py:38
  161.7 10.5 %collective-permute-done.13 = bf16[128,2048]{1,0:T(8,128)(2,1)S(1)} collective-permute-done((bf16[128,2048]{1,0:T(8,128)(2,1)S(1)}, bf16[128,2048]{1,0:T(8,128)(2,1)S(1)}, u32[]{:S(2)}, u32[]{:S(2)}) %collective-permute-start.13) | collective-permute-done | bytes 524320 | tf_op jit(solution)/shard_map/ppermute | solution.py:38
  174.8 2.5 copy.80
  179.4 3.2 collective-permute-start.18
  183.8 4.3 %collective-permute-done.15 = bf16[128,2048]{1,0:T(8,128)(2,1)} collective-permute-done((bf16[128,2048]{1,0:T(8,128)(2,1)}, bf16[128,2048]{1,0:T(8,128)(2,1)}, u32[]{:S(2)}, u32[]{:S(2)}) %collective-permute-start.15) | collective-permute-done | bytes 524320 | tf_op jit(solution)/shard_map/ppermute | solution.py:113
  190.9 2.9 collective-permute-start.21
  198.1 4.9 %collective-permute-done.21 = bf16[128,1024]{1,0:T(8,128)(2,1)S(1)} collective-permute-done((bf16[128,1024]{1,0:T(8,128)(2,1)S(1)}, bf16[128,1024]{1,0:T(8,128)(2,1)S(1)}, u32[]{:S(2)}, u32[]{:S(2)}) %collective-permute-start.21) | collective-permute-done | bytes 262176 | tf_op jit(solution)/shard_map/ppermute | solution.py:38
  203.6 7.7 %collective-permute-done.19 = bf16[128,1024]{1,0:T(8,128)(2,1)S(1)} collective-permute-done((bf16[128,1024]{1,0:T(8,128)(2,1)S(1)}, bf16[128,1024]{1,0:T(8,128)(2,1)S(1)}, u32[]{:S(2)}, u32[]{:S(2)}) %collective-permute-start.19) | collective-permute-done | bytes 262176 | tf_op jit(solution)/shard_map/ppermute | solution.py:38
  211.3 5.1 %fusion.10 = f32[1344,1024]{1,0:T(8,128)} fusion(bf16[128,1344]{0,1:T(8,128)(2,1)} %copy-done.12, bf16[128,1344]{0,1:T(8,128)(2,1)} %collective-permute-done.17, bf16[128,1344]{0,1:T(8,128)(2,1)} %collective-permute-done.16, bf16[128,1344]{0,1:T(8,128)(2,1)S(1)} %bitcast.138, bf16[128,1024]{1,0:T(8,128)(2,1)S(1)} %collective-permute-done.21, ...), kind=kOutput, calls=%fused_computation.20 | convolution fusion | flops 1418985472 | bytes 7929856 | tf_op jit(solution)/shard_map/dot_general | solution.py:231
  216.4 5.8 %reshape.142 = f32[8,4,2,21,1024]{4,3,2,1,0:T(8,128)} reshape(f32[1344,1024]{1,0:T(8,128)} %fusion.10) | data formatting | bytes 11010048 | tf_op jit(solution)/shard_map/reshape | solution.py:237
  222.2 2.1 fusion.9
  228.2 2.3 constant_dynamic-slice_fusion.3
  231.3 3.0 bitcast_add_fusion
  241.1 6.4 %collective-permute-done.23 = bf16[8,21,1024]{2,0,1:T(8,128)(2,1)S(1)} collective-permute-done((bf16[8,21,1024]{2,0,1:T(8,128)(2,1)}, bf16[8,21,1024]{2,0,1:T(8,128)(2,1)S(1)}, u32[]{:S(2)}, u32[]{:S(2)}) %collective-permute-start.23) | collective-permute-done | bytes 344096 | tf_op jit(solution)/shard_map/ppermute | solution.py:38
  247.5 8.6 %collective-permute-done.24 = bf16[8,21,1024]{2,0,1:T(8,128)(2,1)} collective-permute-done((bf16[8,21,1024]{2,0,1:T(8,128)(2,1)S(1)}, bf16[8,21,1024]{2,0,1:T(8,128)(2,1)}, u32[]{:S(2)}, u32[]{:S(2)}) %collective-permute-start.24) | collective-permute-done | bytes 344096 | tf_op jit(solution)/shard_map/ppermute | solution.py:38
  256.1 2.4 fusion.41
  259.8 9.8 %collective-permute-start.26 = (f32[4,21,1024]{2,0,1:T(4,128)S(1)}, f32[4,21,1024]{2,0,1:T(4,128)}, u32[]{:S(2)}, u32[]{:S(2)}) collective-permute-start(f32[4,21,1024]{2,0,1:T(4,128)S(1)} %dynamic-slice_bitcast_fusion), channel_id=1, source_target_pairs={{0,128},{32,160},{64,192},{96,224},{128,0},{160,32},{192,64},{224,... | collective-permute-start | bytes 1032200 | tf_op jit(solution)/shard_map/ppermute | solution.py:135
  269.6 14.7 %collective-permute-done.26 = f32[4,21,1024]{2,0,1:T(4,128)} collective-permute-done((f32[4,21,1024]{2,0,1:T(4,128)S(1)}, f32[4,21,1024]{2,0,1:T(4,128)}, u32[]{:S(2)}, u32[]{:S(2)}) %collective-permute-start.26) | collective-permute-done | bytes 344096 | tf_op jit(solution)/shard_map/ppermute | solution.py:135
  285.9 11.1 %collective-permute-done.27 = f32[2,21,1024]{2,1,0:T(8,128)S(1)} collective-permute-done((f32[2,21,1024]{2,1,0:T(8,128)S(1)}, f32[2,21,1024]{2,1,0:T(8,128)S(1)}, u32[]{:S(2)}, u32[]{:S(2)}) %collective-permute-start.27) | collective-permute-done | bytes 172064 | tf_op jit(solution)/shard_map/ppermute | solution.py:135
  297.3 3.4 fusion.19
  310.7 2.8 collective-permute-done.30
  319.3 2.7 collective-permute-done.33
  323.9 2.3 collective-permute-start.42
  326.2 3.3 collective-permute-start.41
  329.5 2.2 collective-permute-start.40
  331.7 3.5 collective-permute-start.39
  335.9 3.0 collective-permute-done.36
  340.2 3.3 collective-permute-done.37
  344.9 4.1 %collective-permute-done.38 = f32[]{:T(128)} collective-permute-done((f32[]{:T(128)}, f32[]{:T(128)}, u32[]{:S(2)}, u32[]{:S(2)}) %collective-permute-start.38) | collective-permute-done | bytes 36 | tf_op jit(solution)/shard_map/ppermute | solution.py:38
  353.0 24.6 %all-gather = bf16[8,21,1024]{2,1,0:T(8,128)(2,1)S(1)} all-gather(bf16[1,21,1024]{2,1,0:T(8,128)(2,1)S(1)} %get-tuple-element.37), channel_id=1, replica_groups=mesh['cz'=8,'cx'=4,'y'=4,'core'=2] {'y','core'}, dimensions={0}, use_global_device_ids=true | all-gather | bytes 387072 | tf_op jit(solution)/shard_map/all_gather | solution.py:257
  (133 shorter events, 63.3 us)
Async XLA Ops:
  3.6 15.7 %collective-permute-start = (bf16[128,2176]{0,1:T(8,128)(2,1)S(1)}, bf16[128,2176]{0,1:T(8,128)(2,1)S(1)}, u32[]{:S(2)}, u32[]{:S(2)}) collective-permute-start(bf16[128,2176]{0,1:T(8,128)(2,1)S(1)} %pad_maximum_fusion.1), channel_id=1, source_target_pairs={{0,32},{32,64},{64,96},{96,128},{128,160},{160,192},{192,224},{1,3... | collective-permute-start | bytes 1671176 | tf_op jit(solution)/shard_map/ppermute | solution.py:113
  19.3 14.5 %collective-permute-start.1 = (bf16[128,2176]{0,1:T(8,128)(2,1)S(1)}, bf16[128,2176]{0,1:T(8,128)(2,1)S(1)}, u32[]{:S(2)}, u32[]{:S(2)}) collective-permute-start(bf16[128,2176]{0,1:T(8,128)(2,1)S(1)} %collective-permute-done), channel_id=1, source_target_pairs={{0,32},{32,64},{64,96},{96,128},{128,160},{160,192},{192,224},{1,3... | collective-permute-start | bytes 1671176 | tf_op jit(solution)/shard_map/ppermute | solution.py:113
  23.5 54.6 %copy-start.7 = (s32[1152]{0:T(1024)}, s32[1152]{0:T(1024)S(1)}, u32[]{:S(2)}) copy-start(s32[1152]{0:T(1024)S(1)} %get-tuple-element.68) | copy-start | bytes 13828
  23.5 33.4 %collective-permute-start.4 = (bf16[128,2176]{0,1:T(8,128)(2,1)S(1)}, bf16[128,2176]{0,1:T(8,128)(2,1)S(1)}, u32[]{:S(2)}, u32[]{:S(2)}) collective-permute-start(bf16[128,2176]{0,1:T(8,128)(2,1)S(1)} %collective-permute-done), channel_id=1, source_target_pairs={{0,24},{8,0},{16,8},{24,16},{1,25},{9,1},{17,9},{25,17},{2,26},{10... | collective-permute-start | bytes 1671176 | tf_op jit(solution)/shard_map/ppermute | solution.py:38
  26.0 30.7 %collective-permute-start.3 = (bf16[128,2176]{0,1:T(8,128)(2,1)S(1)}, bf16[128,2176]{0,1:T(8,128)(2,1)S(1)}, u32[]{:S(2)}, u32[]{:S(2)}) collective-permute-start(bf16[128,2176]{0,1:T(8,128)(2,1)S(1)} %collective-permute-done), channel_id=1, source_target_pairs={{0,16},{8,24},{16,0},{24,8},{1,17},{9,25},{17,1},{25,9},{2,18},{10... | collective-permute-start | bytes 1671176 | tf_op jit(solution)/shard_map/ppermute | solution.py:38
  26.6 29.8 %collective-permute-start.2 = (bf16[128,2176]{0,1:T(8,128)(2,1)S(1)}, bf16[128,2176]{0,1:T(8,128)(2,1)S(1)}, u32[]{:S(2)}, u32[]{:S(2)}) collective-permute-start(bf16[128,2176]{0,1:T(8,128)(2,1)S(1)} %collective-permute-done), channel_id=1, source_target_pairs={{0,8},{8,16},{16,24},{24,0},{1,9},{9,17},{17,25},{25,1},{2,10},{10... | collective-permute-start | bytes 1671176 | tf_op jit(solution)/shard_map/ppermute | solution.py:38
  34.2 44.1 %collective-permute-start.7 = (bf16[128,2176]{0,1:T(8,128)(2,1)S(1)}, bf16[128,2176]{0,1:T(8,128)(2,1)S(1)}, u32[]{:S(2)}, u32[]{:S(2)}) collective-permute-start(bf16[128,2176]{0,1:T(8,128)(2,1)S(1)} %get-tuple-element.57), channel_id=1, source_target_pairs={{0,24},{8,0},{16,8},{24,16},{1,25},{9,1},{17,9},{25,17},{2,26},{10... | collective-permute-start | bytes 1671176 | tf_op jit(solution)/shard_map/ppermute | solution.py:38
  36.7 41.4 %collective-permute-start.6 = (bf16[128,2176]{0,1:T(8,128)(2,1)S(1)}, bf16[128,2176]{0,1:T(8,128)(2,1)S(1)}, u32[]{:S(2)}, u32[]{:S(2)}) collective-permute-start(bf16[128,2176]{0,1:T(8,128)(2,1)S(1)} %get-tuple-element.58), channel_id=1, source_target_pairs={{0,16},{8,24},{16,0},{24,8},{1,17},{9,25},{17,1},{25,9},{2,18},{10... | collective-permute-start | bytes 1671176 | tf_op jit(solution)/shard_map/ppermute | solution.py:38
  56.4 21.6 %collective-permute-start.5 = (bf16[128,2176]{0,1:T(8,128)(2,1)S(1)}, bf16[128,2176]{0,1:T(8,128)(2,1)S(1)}, u32[]{:S(2)}, u32[]{:S(2)}) collective-permute-start(bf16[128,2176]{0,1:T(8,128)(2,1)S(1)} %get-tuple-element.59), channel_id=1, source_target_pairs={{0,8},{8,16},{16,24},{24,0},{1,9},{9,17},{17,25},{25,1},{2,10},{10... | collective-permute-start | bytes 1671176 | tf_op jit(solution)/shard_map/ppermute | solution.py:38
  124.2 24.8 %collective-permute-start.10 = (bf16[128,2048]{1,0:T(8,128)(2,1)S(1)}, bf16[128,2048]{1,0:T(8,128)(2,1)S(1)}, u32[]{:S(2)}, u32[]{:S(2)}) collective-permute-start(bf16[128,2048]{1,0:T(8,128)(2,1)S(1)} %get-tuple-element.48), channel_id=1, source_target_pairs={{0,8},{8,16},{16,24},{24,0},{1,9},{9,17},{17,25},{25,1},{2,10},{10... | collective-permute-start | bytes 1572872 | tf_op jit(solution)/shard_map/ppermute | solution.py:38
  124.3 24.7 %collective-permute-start.9 = (bf16[128,2048]{1,0:T(8,128)(2,1)S(1)}, bf16[128,2048]{1,0:T(8,128)(2,1)S(1)}, u32[]{:S(2)}, u32[]{:S(2)}) collective-permute-start(bf16[128,2048]{1,0:T(8,128)(2,1)S(1)} %get-tuple-element.49), channel_id=1, source_target_pairs={{0,16},{8,24},{16,0},{24,8},{1,17},{9,25},{17,1},{25,9},{2,18},{10... | collective-permute-start | bytes 1572872 | tf_op jit(solution)/shard_map/ppermute | solution.py:38
  125.3 25.2 %collective-permute-start.8 = (bf16[128,2048]{1,0:T(8,128)(2,1)S(1)}, bf16[128,2048]{1,0:T(8,128)(2,1)S(1)}, u32[]{:S(2)}, u32[]{:S(2)}) collective-permute-start(bf16[128,2048]{1,0:T(8,128)(2,1)S(1)} %get-tuple-element.50), channel_id=1, source_target_pairs={{0,24},{8,0},{16,8},{24,16},{1,25},{9,1},{17,9},{25,17},{2,26},{10... | collective-permute-start | bytes 1572872 | tf_op jit(solution)/shard_map/ppermute | solution.py:38
  127.4 34.3 %collective-permute-start.11 = (bf16[128,2048]{1,0:T(8,128)(2,1)S(1)}, bf16[128,2048]{1,0:T(8,128)(2,1)S(1)}, u32[]{:S(2)}, u32[]{:S(2)}) collective-permute-start(bf16[128,2048]{1,0:T(8,128)(2,1)S(1)} %get-tuple-element.45), channel_id=1, source_target_pairs={{0,24},{8,0},{16,8},{24,16},{1,25},{9,1},{17,9},{25,17},{2,26},{10... | collective-permute-start | bytes 1572872 | tf_op jit(solution)/shard_map/ppermute | solution.py:38
  128.0 44.2 %collective-permute-start.13 = (bf16[128,2048]{1,0:T(8,128)(2,1)S(1)}, bf16[128,2048]{1,0:T(8,128)(2,1)S(1)}, u32[]{:S(2)}, u32[]{:S(2)}) collective-permute-start(bf16[128,2048]{1,0:T(8,128)(2,1)S(1)} %get-tuple-element.46), channel_id=1, source_target_pairs={{0,8},{8,16},{16,24},{24,0},{1,9},{9,17},{17,25},{25,1},{2,10},{10... | collective-permute-start | bytes 1572872 | tf_op jit(solution)/shard_map/ppermute | solution.py:38
  148.9 23.2 %collective-permute-start.12 = (bf16[128,2048]{1,0:T(8,128)(2,1)S(1)}, bf16[128,2048]{1,0:T(8,128)(2,1)S(1)}, u32[]{:S(2)}, u32[]{:S(2)}) collective-permute-start(bf16[128,2048]{1,0:T(8,128)(2,1)S(1)} %get-tuple-element.47), channel_id=1, source_target_pairs={{0,16},{8,24},{16,0},{24,8},{1,17},{9,25},{17,1},{25,9},{2,18},{10... | collective-permute-start | bytes 1572872 | tf_op jit(solution)/shard_map/ppermute | solution.py:38
  150.5 23.0 %copy-start.3 = (bf16[128,2048]{1,0:T(8,128)(2,1)}, bf16[128,2048]{1,0:T(8,128)(2,1)S(1)}, u32[]{:S(2)}) copy-start(bf16[128,2048]{1,0:T(8,128)(2,1)S(1)} %collective-permute-done.8) | copy-start | bytes 1572868
  150.9 21.3 %collective-permute-start.14 = (bf16[128,2048]{1,0:T(8,128)(2,1)S(1)}, bf16[128,2048]{1,0:T(8,128)(2,1)S(1)}, u32[]{:S(2)}, u32[]{:S(2)}) collective-permute-start(bf16[128,2048]{1,0:T(8,128)(2,1)S(1)} %fusion.31), channel_id=1, source_target_pairs={{32,0},{64,32},{96,64},{128,96},{160,128},{192,160},{224,192},{33,... | collective-permute-start | bytes 1572872 | tf_op jit(solution)/shard_map/ppermute | solution.py:113
  173.5 14.6 %collective-permute-start.15 = (bf16[128,2048]{1,0:T(8,128)(2,1)}, bf16[128,2048]{1,0:T(8,128)(2,1)}, u32[]{:S(2)}, u32[]{:S(2)}) collective-permute-start(bf16[128,2048]{1,0:T(8,128)(2,1)} %add_convert_fusion), channel_id=1, source_target_pairs={{32,0},{64,32},{96,64},{128,96},{160,128},{192,160},{224,192},{33,... | collective-permute-start | bytes 1572872 | tf_op jit(solution)/shard_map/ppermute | solution.py:113
  179.4 14.4 %collective-permute-start.18 = (bf16[128,1344]{0,1:T(8,128)(2,1)S(1)}, bf16[128,1344]{0,1:T(8,128)(2,1)S(1)}, u32[]{:S(2)}, u32[]{:S(2)}) collective-permute-start(bf16[128,1344]{0,1:T(8,128)(2,1)S(1)} %bitcast.139), channel_id=1, source_target_pairs={{0,24},{8,0},{16,8},{24,16},{1,25},{9,1},{17,9},{25,17},{2,26},{10... | collective-permute-start | bytes 1032200 | tf_op jit(solution)/shard_map/ppermute | solution.py:38
  182.6 13.5 %collective-permute-start.16 = (bf16[128,1344]{0,1:T(8,128)(2,1)}, bf16[128,1344]{0,1:T(8,128)(2,1)}, u32[]{:S(2)}, u32[]{:S(2)}) collective-permute-start(bf16[128,1344]{0,1:T(8,128)(2,1)} %bitcast.30), channel_id=1, source_target_pairs={{0,8},{8,16},{16,24},{24,0},{1,9},{9,17},{17,25},{25,1},{2,10},{10... | collective-permute-start | bytes 1032200 | tf_op jit(solution)/shard_map/ppermute | solution.py:38
  182.6 15.5 %collective-permute-start.17 = (bf16[128,1344]{0,1:T(8,128)(2,1)}, bf16[128,1344]{0,1:T(8,128)(2,1)}, u32[]{:S(2)}, u32[]{:S(2)}) collective-permute-start(bf16[128,1344]{0,1:T(8,128)(2,1)} %bitcast.31), channel_id=1, source_target_pairs={{0,16},{8,24},{16,0},{24,8},{1,17},{9,25},{17,1},{25,9},{2,18},{10... | collective-permute-start | bytes 1032200 | tf_op jit(solution)/shard_map/ppermute | solution.py:38
  190.9 12.1 %collective-permute-start.21 = (bf16[128,1024]{1,0:T(8,128)(2,1)S(1)}, bf16[128,1024]{1,0:T(8,128)(2,1)S(1)}, u32[]{:S(2)}, u32[]{:S(2)}) collective-permute-start(bf16[128,1024]{1,0:T(8,128)(2,1)S(1)} %get-tuple-element.61), channel_id=1, source_target_pairs={{0,24},{8,0},{16,8},{24,16},{1,25},{9,1},{17,9},{25,17},{2,26},{10... | collective-permute-start | bytes 786440 | tf_op jit(solution)/shard_map/ppermute | solution.py:38
  193.8 9.8 %collective-permute-start.20 = (bf16[128,1024]{1,0:T(8,128)(2,1)S(1)}, bf16[128,1024]{1,0:T(8,128)(2,1)S(1)}, u32[]{:S(2)}, u32[]{:S(2)}) collective-permute-start(bf16[128,1024]{1,0:T(8,128)(2,1)S(1)} %get-tuple-element.61), channel_id=1, source_target_pairs={{0,16},{8,24},{16,0},{24,8},{1,17},{9,25},{17,1},{25,9},{2,18},{10... | collective-permute-start | bytes 786440 | tf_op jit(solution)/shard_map/ppermute | solution.py:38
  194.5 16.8 %collective-permute-start.19 = (bf16[128,1024]{1,0:T(8,128)(2,1)S(1)}, bf16[128,1024]{1,0:T(8,128)(2,1)S(1)}, u32[]{:S(2)}, u32[]{:S(2)}) collective-permute-start(bf16[128,1024]{1,0:T(8,128)(2,1)S(1)} %get-tuple-element.61), channel_id=1, source_target_pairs={{0,8},{8,16},{16,24},{24,0},{1,9},{9,17},{17,25},{25,1},{2,10},{10... | collective-permute-start | bytes 786440 | tf_op jit(solution)/shard_map/ppermute | solution.py:38
  226.3 5.0 %collective-permute-start.22 = (bf16[8,4,21,1024]{3,0,2,1:T(8,128)(2,1)}, bf16[8,4,21,1024]{3,0,2,1:T(8,128)(2,1)}, u32[]{:S(2)}, u32[]{:S(2)}) collective-permute-start(bf16[8,4,21,1024]{3,0,2,1:T(8,128)(2,1)} %copy.82), channel_id=1, source_target_pairs={{0,1},{1,0},{2,3},{3,2},{4,5},{5,4},{6,7},{7,6},{8,9},{9,8},{10,11... | collective-permute-start | bytes 4128776 | tf_op jit(solution)/shard_map/ppermute | solution.py:38
  236.7 10.7 %collective-permute-start.23 = (bf16[8,21,1024]{2,0,1:T(8,128)(2,1)}, bf16[8,21,1024]{2,0,1:T(8,128)(2,1)S(1)}, u32[]{:S(2)}, u32[]{:S(2)}) collective-permute-start(bf16[8,21,1024]{2,0,1:T(8,128)(2,1)} %get-tuple-element.51), channel_id=1, source_target_pairs={{0,2},{2,4},{4,6},{6,0},{1,3},{3,5},{5,7},{7,1},{8,10},{10,12},{12... | collective-permute-start | bytes 1032200 | tf_op jit(solution)/shard_map/ppermute | solution.py:38
  238.0 9.5 %collective-permute-start.25 = (bf16[8,21,1024]{2,0,1:T(8,128)(2,1)S(1)}, bf16[8,21,1024]{2,0,1:T(8,128)(2,1)}, u32[]{:S(2)}, u32[]{:S(2)}) collective-permute-start(bf16[8,21,1024]{2,0,1:T(8,128)(2,1)S(1)} %get-tuple-element.52), channel_id=1, source_target_pairs={{0,6},{2,0},{4,2},{6,4},{1,7},{3,1},{5,3},{7,5},{8,14},{10,8},{12,... | collective-permute-start | bytes 1032200 | tf_op jit(solution)/shard_map/ppermute | solution.py:38
  239.4 16.6 %collective-permute-start.24 = (bf16[8,21,1024]{2,0,1:T(8,128)(2,1)S(1)}, bf16[8,21,1024]{2,0,1:T(8,128)(2,1)}, u32[]{:S(2)}, u32[]{:S(2)}) collective-permute-start(bf16[8,21,1024]{2,0,1:T(8,128)(2,1)S(1)} %get-tuple-element.53), channel_id=1, source_target_pairs={{0,4},{2,6},{4,0},{6,2},{1,5},{3,7},{5,1},{7,3},{8,12},{10,14},{12... | collective-permute-start | bytes 1032200 | tf_op jit(solution)/shard_map/ppermute | solution.py:38
  259.8 24.6 %collective-permute-start.26 = (f32[4,21,1024]{2,0,1:T(4,128)S(1)}, f32[4,21,1024]{2,0,1:T(4,128)}, u32[]{:S(2)}, u32[]{:S(2)}) collective-permute-start(f32[4,21,1024]{2,0,1:T(4,128)S(1)} %dynamic-slice_bitcast_fusion), channel_id=1, source_target_pairs={{0,128},{32,160},{64,192},{96,224},{128,0},{160,32},{192,64},{224,... | collective-permute-start | bytes 1032200 | tf_op jit(solution)/shard_map/ppermute | solution.py:135
  285.8 11.2 %collective-permute-start.27 = (f32[2,21,1024]{2,1,0:T(8,128)S(1)}, f32[2,21,1024]{2,1,0:T(8,128)S(1)}, u32[]{:S(2)}, u32[]{:S(2)}) collective-permute-start(f32[2,21,1024]{2,1,0:T(8,128)S(1)} %bitcast.140), channel_id=1, source_target_pairs={{0,64},{32,96},{64,0},{96,32},{128,192},{160,224},{192,128},{224,1... | collective-permute-start | bytes 516104 | tf_op jit(solution)/shard_map/ppermute | solution.py:135
  297.1 55.1 %copy-start.4 = (f32[21,1024]{1,0:T(8,128)S(1)}, f32[21,1024]{1,0:T(8,128)}, u32[]{:S(2)}) copy-start(f32[21,1024]{1,0:T(8,128)} %param.15) | copy-start | bytes 258052
  297.2 55.1 %copy-start.5 = (f32[21,1024]{1,0:T(8,128)S(1)}, f32[21,1024]{1,0:T(8,128)}, u32[]{:S(2)}) copy-start(f32[21,1024]{1,0:T(8,128)} %param.16) | copy-start | bytes 258052
  297.2 55.1 %copy-start.6 = (f32[21,1024]{1,0:T(8,128)S(1)}, f32[21,1024]{1,0:T(8,128)}, u32[]{:S(2)}) copy-start(f32[21,1024]{1,0:T(8,128)} %param.17) | copy-start | bytes 258052
  297.2 4.5 %collective-permute-start.28 = (f32[1,21,1024]{2,1,0:T(8,128)S(1)}, f32[1,21,1024]{2,1,0:T(8,128)}, u32[]{:S(2)}, u32[]{:S(2)}) collective-permute-start(f32[1,21,1024]{2,1,0:T(8,128)S(1)} %constant_dynamic-slice_fusion), channel_id=1, source_target_pairs={{0,32},{32,0},{64,96},{96,64},{128,160},{160,128},{192,224},{224,1... | collective-permute-start | bytes 258056 | tf_op jit(solution)/shard_map/ppermute | solution.py:135
  303.2 2.5 collective-permute-start.29
  307.0 7.7 %collective-permute-start.32 = (f32[]{:T(128)}, f32[]{:T(128)}, u32[]{:S(2)}, u32[]{:S(2)}) collective-permute-start(f32[]{:T(128)} %add.422), channel_id=1, source_target_pairs={{0,6},{2,0},{4,2},{6,4},{1,7},{3,1},{5,3},{7,5},{8,14},{10,8},{12,... | collective-permute-start | bytes 20 | tf_op jit(solution)/shard_map/ppermute | solution.py:38
  307.8 6.3 %collective-permute-start.31 = (f32[]{:T(128)}, f32[]{:T(128)}, u32[]{:S(2)}, u32[]{:S(2)}) collective-permute-start(f32[]{:T(128)} %add.422), channel_id=1, source_target_pairs={{0,4},{2,6},{4,0},{6,2},{1,5},{3,7},{5,1},{7,3},{8,12},{10,14},{12... | collective-permute-start | bytes 20 | tf_op jit(solution)/shard_map/ppermute | solution.py:38
  309.7 3.7 collective-permute-start.30
  315.4 7.9 %collective-permute-start.35 = (f32[]{:T(128)}, f32[]{:T(128)}, u32[]{:S(2)}, u32[]{:S(2)}) collective-permute-start(f32[]{:T(128)} %add.425), channel_id=1, source_target_pairs={{0,24},{8,0},{16,8},{24,16},{1,25},{9,1},{17,9},{25,17},{2,26},{10... | collective-permute-start | bytes 20 | tf_op jit(solution)/shard_map/ppermute | solution.py:38
  316.2 6.5 %collective-permute-start.34 = (f32[]{:T(128)}, f32[]{:T(128)}, u32[]{:S(2)}, u32[]{:S(2)}) collective-permute-start(f32[]{:T(128)} %add.425), channel_id=1, source_target_pairs={{0,16},{8,24},{16,0},{24,8},{1,17},{9,25},{17,1},{25,9},{2,18},{10... | collective-permute-start | bytes 20 | tf_op jit(solution)/shard_map/ppermute | solution.py:38
  317.5 4.5 %collective-permute-start.33 = (f32[]{:T(128)}, f32[]{:T(128)}, u32[]{:S(2)}, u32[]{:S(2)}) collective-permute-start(f32[]{:T(128)} %add.425), channel_id=1, source_target_pairs={{0,8},{8,16},{16,24},{24,0},{1,9},{9,17},{17,25},{25,1},{2,10},{10... | collective-permute-start | bytes 20 | tf_op jit(solution)/shard_map/ppermute | solution.py:38
  323.9 27.7 %collective-permute-start.42 = (f32[]{:T(128)}, f32[]{:T(128)}, u32[]{:S(2)}, u32[]{:S(2)}) collective-permute-start(f32[]{:T(128)} %add.428), channel_id=1, source_target_pairs={{0,224},{32,0},{64,32},{96,64},{128,96},{160,128},{192,160},{224,1... | collective-permute-start | bytes 20 | tf_op jit(solution)/shard_map/ppermute | solution.py:38
  326.2 24.8 %collective-permute-start.41 = (f32[]{:T(128)}, f32[]{:T(128)}, u32[]{:S(2)}, u32[]{:S(2)}) collective-permute-start(f32[]{:T(128)} %add.428), channel_id=1, source_target_pairs={{0,192},{32,224},{64,0},{96,32},{128,64},{160,96},{192,128},{224,1... | collective-permute-start | bytes 20 | tf_op jit(solution)/shard_map/ppermute | solution.py:38
  329.5 20.8 %collective-permute-start.40 = (f32[]{:T(128)}, f32[]{:T(128)}, u32[]{:S(2)}, u32[]{:S(2)}) collective-permute-start(f32[]{:T(128)} %add.428), channel_id=1, source_target_pairs={{0,160},{32,192},{64,224},{96,0},{128,32},{160,64},{192,96},{224,1... | collective-permute-start | bytes 20 | tf_op jit(solution)/shard_map/ppermute | solution.py:38
  331.7 18.0 %collective-permute-start.39 = (f32[]{:T(128)}, f32[]{:T(128)}, u32[]{:S(2)}, u32[]{:S(2)}) collective-permute-start(f32[]{:T(128)} %add.428), channel_id=1, source_target_pairs={{0,128},{32,160},{64,192},{96,224},{128,0},{160,32},{192,64},{224,... | collective-permute-start | bytes 20 | tf_op jit(solution)/shard_map/ppermute | solution.py:38
  335.2 3.7 collective-permute-start.36
  338.9 4.6 %collective-permute-start.37 = (f32[]{:T(128)}, f32[]{:T(128)}, u32[]{:S(2)}, u32[]{:S(2)}) collective-permute-start(f32[]{:T(128)} %add.428), channel_id=1, source_target_pairs={{0,64},{32,96},{64,128},{96,160},{128,192},{160,224},{192,0},{224,... | collective-permute-start | bytes 20 | tf_op jit(solution)/shard_map/ppermute | solution.py:38
  343.5 5.5 %collective-permute-start.38 = (f32[]{:T(128)}, f32[]{:T(128)}, u32[]{:S(2)}, u32[]{:S(2)}) collective-permute-start(f32[]{:T(128)} %add.428), channel_id=1, source_target_pairs={{0,96},{32,128},{64,160},{96,192},{128,224},{160,0},{192,32},{224,... | collective-permute-start | bytes 20 | tf_op jit(solution)/shard_map/ppermute | solution.py:38
  (8 other events, 21.6 us)

commit v5 on v3

--- a/solution.py
+++ b/solution.py
@@ -1,3 +1,5 @@
+import math
+
 import jax
 import jax.numpy as jnp
 from jax import lax
@@ -34,7 +36,7 @@
 
 
 def cyclic(x, axis, by):
-    count = lax.axis_size(axis)
+    count = lax.axis_size(axis) if isinstance(axis, str) else math.prod(lax.axis_size(a) for a in axis)
     return lax.ppermute(x, axis, [(i, (i + by) % count) for i in range(count)])
 
 
@@ -110,6 +112,14 @@
 def shift(x, axis, by):
     count = lax.axis_size(axis)
     pairs = [(i, i + by) for i in range(count) if 0 <= i + by < count]
+    return lax.ppermute(x, axis, pairs)
+
+
+def wrapped(x, axis, by, back=False):
+    count = lax.axis_size(axis)
+    pairs = [(i, i + by - count) for i in range(count) if i + by >= count]
+    if back:
+        pairs = [(b, a) for a, b in pairs]
     return lax.ppermute(x, axis, pairs)
 
 
@@ -154,10 +164,10 @@
         slots.append(cyclic(plane_one, "cx", by))
         sources.append((iz - 1) * ncx + (icx - by) % ncx)
     for by in range(1, ncx):
-        sending_wraps = icx + by >= ncx
-        slots.append(cyclic(jnp.where(sending_wraps, plane_two, own_kv), "cx", by))
         got_wrap = icx - by < 0
-        wraps.append(sending_wraps)
+        plain = shift(own_kv, "cx", by)
+        far = wrapped(plane_two, "cx", by)
+        slots.append(jnp.where(got_wrap, far, plain))
         sources.append(jnp.where(got_wrap, block - ncx - by, block - by))
     kv_rows = jnp.concatenate(slots, axis=0)
     key_row_block = kv_rows[:, :kv_width]
@@ -187,53 +197,44 @@
         back = cyclic(low(slot_grads[3 + k]), "cx", -by).astype(jnp.float32)
         one_acc = one_acc + back
     for k, by in enumerate(range(1, ncx)):
-        back = cyclic(low(slot_grads[3 + (ncx - 1) + k]), "cx", -by).astype(jnp.float32)
-        zero = jnp.zeros_like(back)
-        two_acc = two_acc + jnp.where(wraps[k], back, zero)
-        own_acc = own_acc + jnp.where(wraps[k], zero, back)
+        sent = low(slot_grads[3 + (ncx - 1) + k])
+        own_acc = own_acc + shift(sent, "cx", -by).astype(jnp.float32)
+        two_acc = two_acc + wrapped(sent, "cx", by, back=True).astype(jnp.float32)
     one_acc = one_acc + shift(low(two_acc), "cz", -1).astype(jnp.float32)
     own_acc = own_acc + shift(low(one_acc), "cz", -1).astype(jnp.float32)
     key_out = own_acc[:, :kv_width].astype(jnp.bfloat16)
     value_out = own_acc[:, kv_width:].astype(jnp.bfloat16)
 
     nz = lax.axis_size("cz")
-    ny = lax.axis_size("y")
-    nc = lax.axis_size("core")
+    ndp = lax.axis_size("y") * lax.axis_size("core")
+    idp = lax.axis_index("y") * lax.axis_size("core") + lax.axis_index("core")
     x_own = layer_input[0]
-    rows = x_own.shape[1] // (nz * ncx * ny * nc)
-    x_view = x_own.reshape(shard_length, nz, ncx, ny * nc * rows)
+    rows = x_own.shape[1] // (nz * ncx * ndp)
+    x_view = x_own.reshape(shard_length, nz * ncx, ndp, rows)
 
     def columns(target):
         picked = lax.dynamic_index_in_dim(x_view, target, 2, keepdims=False)
-        return picked.reshape(shard_length, nz * ny * nc * rows)
-
-    x_list = [columns(icx)]
+        return picked.reshape(shard_length, nz * ncx * rows)
+
+    x_list = [columns(idp)]
     v_list = [value_out]
-    for by in range(1, ncx):
-        piece = jnp.concatenate([columns((icx + by) % ncx), value_out], axis=1)
-        got = cyclic(piece, "cx", by)
-        x_list.append(got[:, : -kv_width])
-        v_list.append(got[:, -kv_width:])
+    for by in range(1, ndp):
+        x_list.append(cyclic(columns((idp + by) % ndp), DP, by))
+        v_list.append(cyclic(value_out, DP, by))
     partial = lax.dot_general(
         jnp.concatenate(x_list, axis=0),
         jnp.concatenate(v_list, axis=0),
         (((0,), (0,)), ((), ())),
         preferred_element_type=jnp.float32,
     )
-    partial = partial.reshape(nz, ny, nc, rows, kv_width)
-    icore = lax.axis_index("core")
-    stage = lax.dynamic_index_in_dim(partial, icore, 2, keepdims=False)
-    for by in range(1, nc):
-        sent = lax.dynamic_index_in_dim(partial, (icore + by) % nc, 2, keepdims=False)
-        stage = stage + cyclic(low(sent), "core", by).astype(jnp.float32)
-    iy = lax.axis_index("y")
-    stage_y = lax.dynamic_index_in_dim(stage, iy, 1, keepdims=False)
-    for by in range(1, ny):
-        sent = lax.dynamic_index_in_dim(stage, (iy + by) % ny, 1, keepdims=False)
-        stage_y = stage_y + cyclic(low(sent), "y", by).astype(jnp.float32)
-    weight_grad = lax.dynamic_index_in_dim(stage_y, iz, 0, keepdims=False)
+    partial = partial.reshape(nz, ncx, rows, kv_width)
+    stage = lax.dynamic_index_in_dim(partial, icx, 1, keepdims=False)
+    for by in range(1, ncx):
+        sent = lax.dynamic_index_in_dim(partial, (icx + by) % ncx, 1, keepdims=False)
+        stage = stage + cyclic(low(sent), "cx", by).astype(jnp.float32)
+    weight_grad = lax.dynamic_index_in_dim(stage, iz, 0, keepdims=False)
     for by in range(1, nz):
-        sent = lax.dynamic_index_in_dim(stage_y, (iz + by) % nz, 0, keepdims=False)
+        sent = lax.dynamic_index_in_dim(stage, (iz + by) % nz, 0, keepdims=False)
         weight_grad = weight_grad + cyclic(sent, "cz", by)
 
     square_total = all_sum(jnp.sum(weight_grad * weight_grad), ("core", "y", "cx", "cz"))

time: 359 us -> 400 us (1.11)
  starting transfers between devices: 63.5 us -> 89.5 us
  local copies, waits for them, and re-layouts: 36.1 us -> 59.1 us
  waiting for transfers between devices: 177 us -> 166 us
    ppermute x0 -> x6, waiting for transfers between devices: none -> 51.5 us  [wrapped(): return lax.ppermute(x, axis, pairs)]
    ppermute x34 -> x38, waiting for transfers between devices: 149 us -> 100 us  [cyclic(): return lax.ppermute(x, axis, [(i, (i + by) % count) for i in range(count)])]
    ppermute x0 -> x6, starting transfers between devices: none -> 15.1 us  [wrapped(): return lax.ppermute(x, axis, pairs)]
    reshape x1 -> x11, local copies, waits for them, and re-layouts: 5.88 us -> 20.4 us  [the longest x1 6.05 us: attend(): value_gradient.reshape(extent_rows, KEY_VALUE_HEADS * HEAD_SIZE)]
    ppermute x4 -> x10, waiting for transfers between devices: 28.6 us -> 14.3 us  [shift(): return lax.ppermute(x, axis, pairs)]
    ppermute x4 -> x10, starting transfers between devices: 11.1 us -> 23.4 us  [shift(): return lax.ppermute(x, axis, pairs)]
    unnamed x54 -> x64, local copies, waits for them, and re-layouts: 16.8 us -> 21.5 us
    dot_general x1, matrix products: 1.52 us -> 5.96 us  [attend(): jnp.einsum('grte,tgrd->egd', scores_low, query_four_axes, preferred_eleme...]
  transfers between devices with their start and end apart: 38 -> 54, of which waited for: 27 -> 28; matrix products, arithmetic and copies ran while one was open for 6% -> 10% of each run, Pallas kernels for 0% -> 0%
where the time goes in v5:
time: 400 us; the launch traced here: 395 us
  waiting for transfers between devices  166 us (42%)
  starting transfers between devices  89.5 us (22%)
  local copies, waits for them, and re-layouts  59.1 us (15%)
  matrix products  27.4 us (7%)
  other arithmetic  25.9 us (6%)
  blocking collectives  20.1 us (5%)
  between operations  7.29 us (2%)
    ppermute x38, waiting for transfers between devices, cyclic(): return lax.ppermute(x, axis, [(i, (i + by) % count) for i in range(count)])  100 us
    ppermute x6, waiting for transfers between devices, wrapped(): return lax.ppermute(x, axis, pairs)  51.5 us
    ppermute x38, starting transfers between devices, cyclic(): return lax.ppermute(x, axis, [(i, (i + by) % count) for i in range(count)])  51 us
    ppermute x10, starting transfers between devices, shift(): return lax.ppermute(x, axis, pairs)  23.4 us
    unnamed x64, local copies, waits for them, and re-layouts  21.5 us
    all_gather x1, blocking collectives, shards(): lax.all_gather(new_master.astype(jnp.bfloat16), DP, axis=0, tiled=True)  20.1 us
    ppermute x6, starting transfers between devices, wrapped(): return lax.ppermute(x, axis, pairs)  15.1 us
    ppermute x10, waiting for transfers between devices, shift(): return lax.ppermute(x, axis, pairs)  14.3 us
  transfers between devices with their start and end apart: 54, of which 28 were waited for; matrix products, arithmetic and copies ran while one was open for 10% of the time, Pallas kernels for 0%

profile of v5, /device:TPU:1, one launch (start us, length us, event | category | flops | bytes accessed | tf_op | source)
XLA Modules:
  0.0 395.3 jit_solution(1884612009826487469)
XLA Ops:
  4.7 4.4 %collective-permute-start = (bf16[128,2176]{0,1:T(8,128)(2,1)}, bf16[128,2176]{0,1:T(8,128)(2,1)S(1)}, u32[]{:S(2)}, u32[]{:S(2)}) collective-permute-start(bf16[128,2176]{0,1:T(8,128)(2,1)} %get-tuple-element.60), channel_id=1, source_target_pairs={{0,32},{32,64},{64,96},{96,128},{128,160},{160,192},{192,224},{1,3... | collective-permute-start | bytes 1671176 | tf_op jit(solution)/shard_map/ppermute | solution.py:115
  9.1 3.1 collective-permute-start.6
  12.3 4.4 %collective-permute-start.8 = (bf16[128,2176]{0,1:T(8,128)(2,1)}, bf16[128,2176]{0,1:T(8,128)(2,1)S(1)}, u32[]{:S(2)}, u32[]{:S(2)}) collective-permute-start(bf16[128,2176]{0,1:T(8,128)(2,1)} %get-tuple-element.60), channel_id=1, source_target_pairs={{0,16},{8,24},{1,17},{9,25},{2,18},{10,26},{3,19},{11,27},{4,20},{... | collective-permute-start | bytes 1671176 | tf_op jit(solution)/shard_map/ppermute | solution.py:115
  20.9 3.8 collective-permute-start.1
  26.9 8.2 %collective-permute-done.1 = bf16[128,2176]{0,1:T(8,128)(2,1)S(1)} collective-permute-done((bf16[128,2176]{0,1:T(8,128)(2,1)S(1)}, bf16[128,2176]{0,1:T(8,128)(2,1)S(1)}, u32[]{:S(2)}, u32[]{:S(2)}) %collective-permute-start.1) | collective-permute-done | bytes 557088 | tf_op jit(solution)/shard_map/ppermute | solution.py:115
  35.1 2.7 collective-permute-start.3
  38.7 8.6 %collective-permute-done.2 = bf16[128,2176]{0,1:T(8,128)(2,1)S(1)} collective-permute-done((bf16[128,2176]{0,1:T(8,128)(2,1)S(1)}, bf16[128,2176]{0,1:T(8,128)(2,1)S(1)}, u32[]{:S(2)}, u32[]{:S(2)}) %collective-permute-start.2) | collective-permute-done | bytes 557088 | tf_op jit(solution)/shard_map/ppermute | solution.py:40
  48.3 11.0 %collective-permute-done.3 = bf16[128,2176]{0,1:T(8,128)(2,1)S(1)} collective-permute-done((bf16[128,2176]{0,1:T(8,128)(2,1)S(1)}, bf16[128,2176]{0,1:T(8,128)(2,1)S(1)}, u32[]{:S(2)}, u32[]{:S(2)}) %collective-permute-start.3) | collective-permute-done | bytes 557088 | tf_op jit(solution)/shard_map/ppermute | solution.py:40
  67.1 19.6 %collective-permute-done.5 = bf16[128,2176]{0,1:T(8,128)(2,1)S(1)} collective-permute-done((bf16[128,2176]{0,1:T(8,128)(2,1)S(1)}, bf16[128,2176]{0,1:T(8,128)(2,1)S(1)}, u32[]{:S(2)}, u32[]{:S(2)}) %collective-permute-start.5) | collective-permute-done | bytes 557088 | tf_op jit(solution)/shard_map/ppermute | solution.py:123
  89.8 4.1 %fusion.39 = (bf16[1152,1024]{0,1:T(8,128)(2,1)}, bf16[1152,1024]{0,1:T(8,128)(2,1)S(1)}) fusion(bf16[1152,2176]{0,1:T(8,128)(2,1)} %select_dynamic-update-slice_fusion), kind=kLoop, calls=%fused_computation.116 | loop fusion | bytes 9437184 | tf_op jit(solution)/shard_map/slice | solution.py:174
  95.8 6.3 %fusion.42 = (f32[8,2,128]{2,1,0:T(2,128)}, f32[8,2,128,1152]{2,3,1,0:T(8,128)}) fusion(pred[128,1152]{0,1:T(8,128)(4,1)S(1)} %fusion.24, bf16[1152,8,128,1]{0,2,3,1:T(8,128)(2,1)S(1)} %bitcast.146, bf16[128,8,2,128]{0,3,2,1:T(8,128)(2,1)S(1)} %bitcast.156), kind=kOutput, calls=%fused_computation.119 | convolution fusion | flops 613418112 | bytes 12476416 | tf_op jit(solution)/shard_map/sub | solution.py:77
  102.1 4.8 %fusion.8 = bf16[8,2,128,1152]{2,3,1,0:T(8,128)(2,1)S(1)} fusion(f32[8,2,128,1152]{2,3,1,0:T(8,128)} %get-tuple-element.67, f32[8,2,128]{2,1,0:T(2,128)} %get-tuple-element.66), kind=kLoop, calls=%fused_computation.16 | loop fusion | flops 4718592 | bytes 14163968 | tf_op jit(solution)/shard_map/convert_element_type | solution.py:79
  107.0 3.9 fusion.43
  113.0 3.6 fusion.3
  116.6 6.1 %copy.62 = f32[1152,1024]{1,0:T(8,128)} copy(f32[1152,1024]{0,1:T(8,128)} %bitcast.144) | data formatting | bytes 9437184 | tf_op jit(solution)/shard_map/reshape | solution.py:108
  122.7 6.0 %bitcast_multiply_fusion = f32[8,1152,128]{1,2,0:T(8,128)} fusion(bf16[8,2,128,1152]{2,3,1,0:T(8,128)(2,1)} %fusion.3, bf16[128,8,2,128]{0,3,2,1:T(8,128)(2,1)S(1)} %bitcast.157), kind=kOutput, calls=%fused_computation.11 | convolution fusion | flops 605159424 | bytes 9961472 | tf_op jit(solution)/shard_map/grte,tgrd->egd/dot_general | solution.py:97
  128.6 6.1 %copy.61 = f32[1152,1024]{1,0:T(8,128)} copy(f32[1152,1024]{0,1:T(8,128)} %bitcast.145) | data formatting | bytes 9437184 | tf_op jit(solution)/shard_map/reshape | solution.py:107
  134.7 4.5 %fusion.1 = bf16[1152,2048]{1,0:T(8,128)(2,1)S(1)} fusion(f32[1152,1024]{1,0:T(8,128)} %copy.62, f32[1152,1024]{1,0:T(8,128)} %copy.61), kind=kLoop, calls=%fused_computation.4 | loop fusion | flops 9437184 | bytes 14155776 | tf_op jit(solution)/shard_map/convert.9
  140.8 8.3 %collective-permute-start.19 = (bf16[128,2048]{1,0:T(8,128)(2,1)S(1)}, bf16[128,2048]{1,0:T(8,128)(2,1)S(1)}, u32[]{:S(2)}, u32[]{:S(2)}) collective-permute-start(bf16[128,2048]{1,0:T(8,128)(2,1)S(1)} %get-tuple-element.39), channel_id=1, source_target_pairs={{0,8},{8,16},{16,24},{1,9},{9,17},{17,25},{2,10},{10,18},{18,26},{... | collective-permute-start | bytes 1572872 | tf_op jit(solution)/shard_map/ppermute | solution.py:123
  152.1 7.7 %collective-permute-done.19 = bf16[128,2048]{1,0:T(8,128)(2,1)S(1)} collective-permute-done((bf16[128,2048]{1,0:T(8,128)(2,1)S(1)}, bf16[128,2048]{1,0:T(8,128)(2,1)S(1)}, u32[]{:S(2)}, u32[]{:S(2)}) %collective-permute-start.19) | collective-permute-done | bytes 524320 | tf_op jit(solution)/shard_map/ppermute | solution.py:123
  160.0 11.1 %collective-permute-done.18 = bf16[128,2048]{1,0:T(8,128)(2,1)S(1)} collective-permute-done((bf16[128,2048]{1,0:T(8,128)(2,1)S(1)}, bf16[128,2048]{1,0:T(8,128)(2,1)S(1)}, u32[]{:S(2)}, u32[]{:S(2)}) %collective-permute-start.18) | collective-permute-done | bytes 524320 | tf_op jit(solution)/shard_map/ppermute | solution.py:123
  171.1 13.1 %collective-permute-done.17 = bf16[128,2048]{1,0:T(8,128)(2,1)S(1)} collective-permute-done((bf16[128,2048]{1,0:T(8,128)(2,1)S(1)}, bf16[128,2048]{1,0:T(8,128)(2,1)S(1)}, u32[]{:S(2)}, u32[]{:S(2)}) %collective-permute-start.17) | collective-permute-done | bytes 524320 | tf_op jit(solution)/shard_map/ppermute | solution.py:123
  186.7 2.5 copy.63
  189.3 3.4 reshape_squeeze.11
  206.6 2.9 add_convert_fusion
  219.0 5.2 %collective-permute-done.25 = bf16[128,672]{0,1:T(8,128)(2,1)S(1)} collective-permute-done((bf16[128,672]{0,1:T(8,128)(2,1)}, bf16[128,672]{0,1:T(8,128)(2,1)S(1)}, u32[]{:S(2)}, u32[]{:S(2)}) %collective-permute-start.25) | collective-permute-done | bytes 172064 | tf_op jit(solution)/shard_map/ppermute | solution.py:40
  226.5 6.1 %collective-permute-done.13 = bf16[128,2048]{1,0:T(8,128)(2,1)} collective-permute-done((bf16[128,2048]{1,0:T(8,128)(2,1)}, bf16[128,2048]{1,0:T(8,128)(2,1)}, u32[]{:S(2)}, u32[]{:S(2)}) %collective-permute-start.13) | collective-permute-done | bytes 524320 | tf_op jit(solution)/shard_map/ppermute | solution.py:115
  245.5 16.9 %collective-permute-done.30 = bf16[128,1024]{1,0:T(8,128)(2,1)S(1)} collective-permute-done((bf16[128,1024]{1,0:T(8,128)(2,1)S(1)}, bf16[128,1024]{1,0:T(8,128)(2,1)S(1)}, u32[]{:S(2)}, u32[]{:S(2)}) %collective-permute-start.30) | collective-permute-done | bytes 262176 | tf_op jit(solution)/shard_map/ppermute | solution.py:40
  263.8 4.4 %collective-permute-done.35 = bf16[128,1024]{1,0:T(8,128)(2,1)S(1)} collective-permute-done((bf16[128,1024]{1,0:T(8,128)(2,1)S(1)}, bf16[128,1024]{1,0:T(8,128)(2,1)S(1)}, u32[]{:S(2)}, u32[]{:S(2)}) %collective-permute-start.35) | collective-permute-done | bytes 262176 | tf_op jit(solution)/shard_map/ppermute | solution.py:40
  268.2 3.2 fusion.44
  271.4 3.2 reshape.147
  278.0 9.8 %collective-permute-done.38 = bf16[8,21,1024]{2,1,0:T(8,128)(2,1)} collective-permute-done((bf16[8,21,1024]{2,1,0:T(8,128)(2,1)S(1)}, bf16[8,21,1024]{2,1,0:T(8,128)(2,1)}, u32[]{:S(2)}, u32[]{:S(2)}) %collective-permute-start.38) | collective-permute-done | bytes 344096 | tf_op jit(solution)/shard_map/ppermute | solution.py:40
  289.1 7.0 %collective-permute-done.36 = bf16[8,21,1024]{2,1,0:T(8,128)(2,1)} collective-permute-done((bf16[8,21,1024]{2,1,0:T(8,128)(2,1)S(1)}, bf16[8,21,1024]{2,1,0:T(8,128)(2,1)}, u32[]{:S(2)}, u32[]{:S(2)}) %collective-permute-start.36) | collective-permute-done | bytes 344096 | tf_op jit(solution)/shard_map/ppermute | solution.py:40
  299.4 7.6 %collective-permute-start.45 = (f32[21,1024]{1,0:T(8,128)S(1)}, f32[21,1024]{1,0:T(8,128)S(1)}, u32[]{:S(2)}, u32[]{:S(2)}) collective-permute-start(f32[21,1024]{1,0:T(8,128)S(1)} %get-tuple-element.54), channel_id=1, source_target_pairs={{0,224},{32,0},{64,32},{96,64},{128,96},{160,128},{192,160},{224,1... | collective-permute-start | bytes 258056 | tf_op jit(solution)/shard_map/ppermute | solution.py:40
  307.0 2.8 collective-permute-start.44
  309.8 4.3 %collective-permute-start.42 = (f32[21,1024]{1,0:T(8,128)}, f32[21,1024]{1,0:T(8,128)}, u32[]{:S(2)}, u32[]{:S(2)}) collective-permute-start(f32[21,1024]{1,0:T(8,128)} %get-tuple-element.57), channel_id=1, source_target_pairs={{0,128},{32,160},{64,192},{96,224},{128,0},{160,32},{192,64},{224,... | collective-permute-start | bytes 258056 | tf_op jit(solution)/shard_map/ppermute | solution.py:40
  318.6 3.4 fusion.10
  323.0 3.2 collective-permute-done.41
  326.1 3.4 collective-permute-done.40
  329.6 3.8 collective-permute-done.39
  344.1 2.7 collective-permute-done.48
  348.4 2.8 collective-permute-done.49
  353.0 2.9 collective-permute-done.50
  357.8 2.6 collective-permute-done.51
  361.8 3.8 collective-permute-done.52
  366.3 3.0 collective-permute-start.53
  369.2 3.5 collective-permute-done.53
  374.2 20.1 %all-gather = bf16[8,21,1024]{2,1,0:T(8,128)(2,1)S(1)} all-gather(bf16[1,21,1024]{2,1,0:T(8,128)(2,1)S(1)} %get-tuple-element.28), channel_id=1, replica_groups=mesh['cz'=8,'cx'=4,'y'=4,'core'=2] {'y','core'}, dimensions={0}, use_global_device_ids=true | all-gather | bytes 387072 | tf_op jit(solution)/shard_map/all_gather | solution.py:247
  (181 shorter events, 102.4 us)
Async XLA Ops:
  4.7 16.2 %collective-permute-start = (bf16[128,2176]{0,1:T(8,128)(2,1)}, bf16[128,2176]{0,1:T(8,128)(2,1)S(1)}, u32[]{:S(2)}, u32[]{:S(2)}) collective-permute-start(bf16[128,2176]{0,1:T(8,128)(2,1)} %get-tuple-element.60), channel_id=1, source_target_pairs={{0,32},{32,64},{64,96},{96,128},{128,160},{160,192},{192,224},{1,3... | collective-permute-start | bytes 1671176 | tf_op jit(solution)/shard_map/ppermute | solution.py:115
  9.1 56.5 %collective-permute-start.6 = (bf16[128,2176]{0,1:T(8,128)(2,1)}, bf16[128,2176]{0,1:T(8,128)(2,1)S(1)}, u32[]{:S(2)}, u32[]{:S(2)}) collective-permute-start(bf16[128,2176]{0,1:T(8,128)(2,1)} %get-tuple-element.60), channel_id=1, source_target_pairs={{0,8},{8,16},{16,24},{1,9},{9,17},{17,25},{2,10},{10,18},{18,26},{... | collective-permute-start | bytes 1671176 | tf_op jit(solution)/shard_map/ppermute | solution.py:115
  12.3 75.5 %collective-permute-start.8 = (bf16[128,2176]{0,1:T(8,128)(2,1)}, bf16[128,2176]{0,1:T(8,128)(2,1)S(1)}, u32[]{:S(2)}, u32[]{:S(2)}) collective-permute-start(bf16[128,2176]{0,1:T(8,128)(2,1)} %get-tuple-element.60), channel_id=1, source_target_pairs={{0,16},{8,24},{1,17},{9,25},{2,18},{10,26},{3,19},{11,27},{4,20},{... | collective-permute-start | bytes 1671176 | tf_op jit(solution)/shard_map/ppermute | solution.py:115
  16.6 72.2 %collective-permute-start.10 = (bf16[128,2176]{0,1:T(8,128)(2,1)}, bf16[128,2176]{0,1:T(8,128)(2,1)S(1)}, u32[]{:S(2)}, u32[]{:S(2)}) collective-permute-start(bf16[128,2176]{0,1:T(8,128)(2,1)} %get-tuple-element.60), channel_id=1, source_target_pairs={{0,24},{1,25},{2,26},{3,27},{4,28},{5,29},{6,30},{7,31},{32,56},{3... | collective-permute-start | bytes 1671176 | tf_op jit(solution)/shard_map/ppermute | solution.py:115
  20.9 14.2 %collective-permute-start.1 = (bf16[128,2176]{0,1:T(8,128)(2,1)S(1)}, bf16[128,2176]{0,1:T(8,128)(2,1)S(1)}, u32[]{:S(2)}, u32[]{:S(2)}) collective-permute-start(bf16[128,2176]{0,1:T(8,128)(2,1)S(1)} %collective-permute-done), channel_id=1, source_target_pairs={{0,32},{32,64},{64,96},{96,128},{128,160},{160,192},{192,224},{1,3... | collective-permute-start | bytes 1671176 | tf_op jit(solution)/shard_map/ppermute | solution.py:115
  24.7 22.6 %collective-permute-start.2 = (bf16[128,2176]{0,1:T(8,128)(2,1)S(1)}, bf16[128,2176]{0,1:T(8,128)(2,1)S(1)}, u32[]{:S(2)}, u32[]{:S(2)}) collective-permute-start(bf16[128,2176]{0,1:T(8,128)(2,1)S(1)} %collective-permute-done), channel_id=1, source_target_pairs={{0,8},{8,16},{16,24},{24,0},{1,9},{9,17},{17,25},{25,1},{2,10},{10... | collective-permute-start | bytes 1671176 | tf_op jit(solution)/shard_map/ppermute | solution.py:40
  35.1 24.2 %collective-permute-start.3 = (bf16[128,2176]{0,1:T(8,128)(2,1)S(1)}, bf16[128,2176]{0,1:T(8,128)(2,1)S(1)}, u32[]{:S(2)}, u32[]{:S(2)}) collective-permute-start(bf16[128,2176]{0,1:T(8,128)(2,1)S(1)} %collective-permute-done), channel_id=1, source_target_pairs={{0,16},{8,24},{16,0},{24,8},{1,17},{9,25},{17,1},{25,9},{2,18},{10... | collective-permute-start | bytes 1671176 | tf_op jit(solution)/shard_map/ppermute | solution.py:40
  47.4 16.1 %collective-permute-start.4 = (bf16[128,2176]{0,1:T(8,128)(2,1)S(1)}, bf16[128,2176]{0,1:T(8,128)(2,1)S(1)}, u32[]{:S(2)}, u32[]{:S(2)}) collective-permute-start(bf16[128,2176]{0,1:T(8,128)(2,1)S(1)} %collective-permute-done), channel_id=1, source_target_pairs={{0,24},{8,0},{16,8},{24,16},{1,25},{9,1},{17,9},{25,17},{2,26},{10... | collective-permute-start | bytes 1671176 | tf_op jit(solution)/shard_map/ppermute | solution.py:40
  59.3 27.4 %collective-permute-start.5 = (bf16[128,2176]{0,1:T(8,128)(2,1)S(1)}, bf16[128,2176]{0,1:T(8,128)(2,1)S(1)}, u32[]{:S(2)}, u32[]{:S(2)}) collective-permute-start(bf16[128,2176]{0,1:T(8,128)(2,1)S(1)} %collective-permute-done.1), channel_id=1, source_target_pairs={{24,0},{25,1},{26,2},{27,3},{28,4},{29,5},{30,6},{31,7},{56,32},{5... | collective-permute-start | bytes 1671176 | tf_op jit(solution)/shard_map/ppermute | solution.py:123
  63.4 24.3 %collective-permute-start.7 = (bf16[128,2176]{0,1:T(8,128)(2,1)S(1)}, bf16[128,2176]{0,1:T(8,128)(2,1)S(1)}, u32[]{:S(2)}, u32[]{:S(2)}) collective-permute-start(bf16[128,2176]{0,1:T(8,128)(2,1)S(1)} %collective-permute-done.1), channel_id=1, source_target_pairs={{16,0},{24,8},{17,1},{25,9},{18,2},{26,10},{19,3},{27,11},{20,4},{... | collective-permute-start | bytes 1671176 | tf_op jit(solution)/shard_map/ppermute | solution.py:123
  65.6 23.2 %collective-permute-start.9 = (bf16[128,2176]{0,1:T(8,128)(2,1)S(1)}, bf16[128,2176]{0,1:T(8,128)(2,1)S(1)}, u32[]{:S(2)}, u32[]{:S(2)}) collective-permute-start(bf16[128,2176]{0,1:T(8,128)(2,1)S(1)} %collective-permute-done.1), channel_id=1, source_target_pairs={{8,0},{16,8},{24,16},{9,1},{17,9},{25,17},{10,2},{18,10},{26,18},{... | collective-permute-start | bytes 1671176 | tf_op jit(solution)/shard_map/ppermute | solution.py:123
  140.8 19.0 %collective-permute-start.19 = (bf16[128,2048]{1,0:T(8,128)(2,1)S(1)}, bf16[128,2048]{1,0:T(8,128)(2,1)S(1)}, u32[]{:S(2)}, u32[]{:S(2)}) collective-permute-start(bf16[128,2048]{1,0:T(8,128)(2,1)S(1)} %get-tuple-element.39), channel_id=1, source_target_pairs={{0,8},{8,16},{16,24},{1,9},{9,17},{17,25},{2,10},{10,18},{18,26},{... | collective-permute-start | bytes 1572872 | tf_op jit(solution)/shard_map/ppermute | solution.py:123
  149.1 22.0 %collective-permute-start.18 = (bf16[128,2048]{1,0:T(8,128)(2,1)S(1)}, bf16[128,2048]{1,0:T(8,128)(2,1)S(1)}, u32[]{:S(2)}, u32[]{:S(2)}) collective-permute-start(bf16[128,2048]{1,0:T(8,128)(2,1)S(1)} %get-tuple-element.40), channel_id=1, source_target_pairs={{0,16},{8,24},{1,17},{9,25},{2,18},{10,26},{3,19},{11,27},{4,20},{... | collective-permute-start | bytes 1572872 | tf_op jit(solution)/shard_map/ppermute | solution.py:123
  150.6 33.6 %collective-permute-start.17 = (bf16[128,2048]{1,0:T(8,128)(2,1)S(1)}, bf16[128,2048]{1,0:T(8,128)(2,1)S(1)}, u32[]{:S(2)}, u32[]{:S(2)}) collective-permute-start(bf16[128,2048]{1,0:T(8,128)(2,1)S(1)} %get-tuple-element.41), channel_id=1, source_target_pairs={{0,24},{1,25},{2,26},{3,27},{4,28},{5,29},{6,30},{7,31},{32,56},{3... | collective-permute-start | bytes 1572872 | tf_op jit(solution)/shard_map/ppermute | solution.py:123
  151.9 49.1 %collective-permute-start.16 = (bf16[128,2048]{1,0:T(8,128)(2,1)}, bf16[128,2048]{1,0:T(8,128)(2,1)}, u32[]{:S(2)}, u32[]{:S(2)}) collective-permute-start(bf16[128,2048]{1,0:T(8,128)(2,1)} %get-tuple-element.37), channel_id=1, source_target_pairs={{0,8},{8,16},{16,24},{24,0},{1,9},{9,17},{17,25},{25,1},{2,10},{10... | collective-permute-start | bytes 1572872 | tf_op jit(solution)/shard_map/ppermute | solution.py:40
  152.0 50.4 %collective-permute-start.15 = (bf16[128,2048]{1,0:T(8,128)(2,1)}, bf16[128,2048]{1,0:T(8,128)(2,1)}, u32[]{:S(2)}, u32[]{:S(2)}) collective-permute-start(bf16[128,2048]{1,0:T(8,128)(2,1)} %get-tuple-element.38), channel_id=1, source_target_pairs={{0,16},{8,24},{16,0},{24,8},{1,17},{9,25},{17,1},{25,9},{2,18},{10... | collective-permute-start | bytes 1572872 | tf_op jit(solution)/shard_map/ppermute | solution.py:40
  159.8 44.2 %collective-permute-start.14 = (bf16[128,2048]{1,0:T(8,128)(2,1)}, bf16[128,2048]{1,0:T(8,128)(2,1)}, u32[]{:S(2)}, u32[]{:S(2)}) collective-permute-start(bf16[128,2048]{1,0:T(8,128)(2,1)} %get-tuple-element.36), channel_id=1, source_target_pairs={{0,24},{8,0},{16,8},{24,16},{1,25},{9,1},{17,9},{25,17},{2,26},{10... | collective-permute-start | bytes 1572872 | tf_op jit(solution)/shard_map/ppermute | solution.py:40
  185.4 20.0 %collective-permute-start.20 = (bf16[128,2048]{1,0:T(8,128)(2,1)}, bf16[128,2048]{1,0:T(8,128)(2,1)}, u32[]{:S(2)}, u32[]{:S(2)}) collective-permute-start(bf16[128,2048]{1,0:T(8,128)(2,1)} %add_convert_fusion.1), channel_id=1, source_target_pairs={{32,0},{64,32},{96,64},{128,96},{160,128},{192,160},{224,192},{33,... | collective-permute-start | bytes 1572872 | tf_op jit(solution)/shard_map/ppermute | solution.py:115
  196.8 12.7 %collective-permute-start.22 = (bf16[128,672]{0,1:T(8,128)(2,1)}, bf16[128,672]{0,1:T(8,128)(2,1)}, u32[]{:S(2)}, u32[]{:S(2)}) collective-permute-start(bf16[128,672]{0,1:T(8,128)(2,1)} %reshape.140), channel_id=1, source_target_pairs={{0,1},{1,2},{2,3},{3,4},{4,5},{5,6},{6,7},{7,0},{8,9},{9,10},{10,1... | collective-permute-start | bytes 516104 | tf_op jit(solution)/shard_map/ppermute | solution.py:40
  201.0 9.8 %collective-permute-start.23 = (bf16[128,672]{0,1:T(8,128)(2,1)}, bf16[128,672]{0,1:T(8,128)(2,1)S(1)}, u32[]{:S(2)}, u32[]{:S(2)}) collective-permute-start(bf16[128,672]{0,1:T(8,128)(2,1)} %reshape.141), channel_id=1, source_target_pairs={{0,2},{1,3},{2,4},{3,5},{4,6},{5,7},{6,0},{7,1},{8,10},{9,11},{10,... | collective-permute-start | bytes 516104 | tf_op jit(solution)/shard_map/ppermute | solution.py:40
  202.4 14.0 %collective-permute-start.24 = (bf16[128,672]{0,1:T(8,128)(2,1)S(1)}, bf16[128,672]{0,1:T(8,128)(2,1)}, u32[]{:S(2)}, u32[]{:S(2)}) collective-permute-start(bf16[128,672]{0,1:T(8,128)(2,1)S(1)} %reshape.142), channel_id=1, source_target_pairs={{0,3},{1,4},{2,5},{3,6},{4,7},{5,0},{6,1},{7,2},{8,11},{9,12},{10,... | collective-permute-start | bytes 516104 | tf_op jit(solution)/shard_map/ppermute | solution.py:40
  204.0 28.6 %collective-permute-start.13 = (bf16[128,2048]{1,0:T(8,128)(2,1)}, bf16[128,2048]{1,0:T(8,128)(2,1)}, u32[]{:S(2)}, u32[]{:S(2)}) collective-permute-start(bf16[128,2048]{1,0:T(8,128)(2,1)} %copy-done.5), channel_id=1, source_target_pairs={{24,0},{25,1},{26,2},{27,3},{28,4},{29,5},{30,6},{31,7},{56,32},{5... | collective-permute-start | bytes 1572872 | tf_op jit(solution)/shard_map/ppermute | solution.py:115
  205.3 27.7 %collective-permute-start.12 = (bf16[128,2048]{1,0:T(8,128)(2,1)}, bf16[128,2048]{1,0:T(8,128)(2,1)}, u32[]{:S(2)}, u32[]{:S(2)}) collective-permute-start(bf16[128,2048]{1,0:T(8,128)(2,1)} %copy-done.4), channel_id=1, source_target_pairs={{16,0},{24,8},{17,1},{25,9},{18,2},{26,10},{19,3},{27,11},{20,4},{... | collective-permute-start | bytes 1572872 | tf_op jit(solution)/shard_map/ppermute | solution.py:115
  209.5 25.0 %collective-permute-start.11 = (bf16[128,2048]{1,0:T(8,128)(2,1)}, bf16[128,2048]{1,0:T(8,128)(2,1)}, u32[]{:S(2)}, u32[]{:S(2)}) collective-permute-start(bf16[128,2048]{1,0:T(8,128)(2,1)} %copy-done.3), channel_id=1, source_target_pairs={{8,0},{16,8},{24,16},{9,1},{17,9},{25,17},{10,2},{18,10},{26,18},{... | collective-permute-start | bytes 1572872 | tf_op jit(solution)/shard_map/ppermute | solution.py:115
  210.8 23.7 %collective-permute-start.21 = (bf16[128,2048]{1,0:T(8,128)(2,1)}, bf16[128,2048]{1,0:T(8,128)(2,1)}, u32[]{:S(2)}, u32[]{:S(2)}) collective-permute-start(bf16[128,2048]{1,0:T(8,128)(2,1)} %add_convert_fusion), channel_id=1, source_target_pairs={{32,0},{64,32},{96,64},{128,96},{160,128},{192,160},{224,192},{33,... | collective-permute-start | bytes 1572872 | tf_op jit(solution)/shard_map/ppermute | solution.py:115
  216.4 7.9 %collective-permute-start.25 = (bf16[128,672]{0,1:T(8,128)(2,1)}, bf16[128,672]{0,1:T(8,128)(2,1)S(1)}, u32[]{:S(2)}, u32[]{:S(2)}) collective-permute-start(bf16[128,672]{0,1:T(8,128)(2,1)} %reshape.143), channel_id=1, source_target_pairs={{0,4},{1,5},{2,6},{3,7},{4,0},{5,1},{6,2},{7,3},{8,12},{9,13},{10,... | collective-permute-start | bytes 516104 | tf_op jit(solution)/shard_map/ppermute | solution.py:40
  224.2 13.7 %collective-permute-start.26 = (bf16[128,672]{0,1:T(8,128)(2,1)S(1)}, bf16[128,672]{0,1:T(8,128)(2,1)S(1)}, u32[]{:S(2)}, u32[]{:S(2)}) collective-permute-start(bf16[128,672]{0,1:T(8,128)(2,1)S(1)} %reshape.144), channel_id=1, source_target_pairs={{0,5},{1,6},{2,7},{3,0},{4,1},{5,2},{6,3},{7,4},{8,13},{9,14},{10,... | collective-permute-start | bytes 516104 | tf_op jit(solution)/shard_map/ppermute | solution.py:40
  232.6 6.5 %collective-permute-start.27 = (bf16[128,672]{0,1:T(8,128)(2,1)S(1)}, bf16[128,672]{0,1:T(8,128)(2,1)S(1)}, u32[]{:S(2)}, u32[]{:S(2)}) collective-permute-start(bf16[128,672]{0,1:T(8,128)(2,1)S(1)} %reshape.145), channel_id=1, source_target_pairs={{0,6},{1,7},{2,0},{3,1},{4,2},{5,3},{6,4},{7,5},{8,14},{9,15},{10,... | collective-permute-start | bytes 516104 | tf_op jit(solution)/shard_map/ppermute | solution.py:40
  233.1 7.5 %collective-permute-start.28 = (bf16[128,672]{0,1:T(8,128)(2,1)S(1)}, bf16[128,672]{0,1:T(8,128)(2,1)S(1)}, u32[]{:S(2)}, u32[]{:S(2)}) collective-permute-start(bf16[128,672]{0,1:T(8,128)(2,1)S(1)} %reshape.146), channel_id=1, source_target_pairs={{0,7},{1,0},{2,1},{3,2},{4,3},{5,4},{6,5},{7,6},{8,15},{9,8},{10,9... | collective-permute-start | bytes 516104 | tf_op jit(solution)/shard_map/ppermute | solution.py:40
  237.6 6.8 %collective-permute-start.29 = (bf16[128,1024]{1,0:T(8,128)(2,1)S(1)}, bf16[128,1024]{1,0:T(8,128)(2,1)S(1)}, u32[]{:S(2)}, u32[]{:S(2)}) collective-permute-start(bf16[128,1024]{1,0:T(8,128)(2,1)S(1)} %get-tuple-element.62), channel_id=1, source_target_pairs={{0,1},{1,2},{2,3},{3,4},{4,5},{5,6},{6,7},{7,0},{8,9},{9,10},{10,1... | collective-permute-start | bytes 786440 | tf_op jit(solution)/shard_map/ppermute | solution.py:40
  238.0 24.4 %collective-permute-start.30 = (bf16[128,1024]{1,0:T(8,128)(2,1)S(1)}, bf16[128,1024]{1,0:T(8,128)(2,1)S(1)}, u32[]{:S(2)}, u32[]{:S(2)}) collective-permute-start(bf16[128,1024]{1,0:T(8,128)(2,1)S(1)} %get-tuple-element.62), channel_id=1, source_target_pairs={{0,2},{1,3},{2,4},{3,5},{4,6},{5,7},{6,0},{7,1},{8,10},{9,11},{10,... | collective-permute-start | bytes 786440 | tf_op jit(solution)/shard_map/ppermute | solution.py:40
  239.2 24.5 %collective-permute-start.31 = (bf16[128,1024]{1,0:T(8,128)(2,1)S(1)}, bf16[128,1024]{1,0:T(8,128)(2,1)S(1)}, u32[]{:S(2)}, u32[]{:S(2)}) collective-permute-start(bf16[128,1024]{1,0:T(8,128)(2,1)S(1)} %get-tuple-element.62), channel_id=1, source_target_pairs={{0,3},{1,4},{2,5},{3,6},{4,7},{5,0},{6,1},{7,2},{8,11},{9,12},{10,... | collective-permute-start | bytes 786440 | tf_op jit(solution)/shard_map/ppermute | solution.py:40
  240.6 23.0 %collective-permute-start.32 = (bf16[128,1024]{1,0:T(8,128)(2,1)S(1)}, bf16[128,1024]{1,0:T(8,128)(2,1)S(1)}, u32[]{:S(2)}, u32[]{:S(2)}) collective-permute-start(bf16[128,1024]{1,0:T(8,128)(2,1)S(1)} %get-tuple-element.62), channel_id=1, source_target_pairs={{0,4},{1,5},{2,6},{3,7},{4,0},{5,1},{6,2},{7,3},{8,12},{9,13},{10,... | collective-permute-start | bytes 786440 | tf_op jit(solution)/shard_map/ppermute | solution.py:40
  242.5 21.1 %collective-permute-start.33 = (bf16[128,1024]{1,0:T(8,128)(2,1)S(1)}, bf16[128,1024]{1,0:T(8,128)(2,1)S(1)}, u32[]{:S(2)}, u32[]{:S(2)}) collective-permute-start(bf16[128,1024]{1,0:T(8,128)(2,1)S(1)} %get-tuple-element.62), channel_id=1, source_target_pairs={{0,5},{1,6},{2,7},{3,0},{4,1},{5,2},{6,3},{7,4},{8,13},{9,14},{10,... | collective-permute-start | bytes 786440 | tf_op jit(solution)/shard_map/ppermute | solution.py:40
  244.4 19.3 %collective-permute-start.34 = (bf16[128,1024]{1,0:T(8,128)(2,1)S(1)}, bf16[128,1024]{1,0:T(8,128)(2,1)S(1)}, u32[]{:S(2)}, u32[]{:S(2)}) collective-permute-start(bf16[128,1024]{1,0:T(8,128)(2,1)S(1)} %get-tuple-element.62), channel_id=1, source_target_pairs={{0,6},{1,7},{2,0},{3,1},{4,2},{5,3},{6,4},{7,5},{8,14},{9,15},{10,... | collective-permute-start | bytes 786440 | tf_op jit(solution)/shard_map/ppermute | solution.py:40
  262.4 5.8 %collective-permute-start.35 = (bf16[128,1024]{1,0:T(8,128)(2,1)S(1)}, bf16[128,1024]{1,0:T(8,128)(2,1)S(1)}, u32[]{:S(2)}, u32[]{:S(2)}) collective-permute-start(bf16[128,1024]{1,0:T(8,128)(2,1)S(1)} %get-tuple-element.62), channel_id=1, source_target_pairs={{0,7},{1,0},{2,1},{3,2},{4,3},{5,4},{6,5},{7,6},{8,15},{9,8},{10,9... | collective-permute-start | bytes 786440 | tf_op jit(solution)/shard_map/ppermute | solution.py:40
  276.4 11.3 %collective-permute-start.38 = (bf16[8,21,1024]{2,1,0:T(8,128)(2,1)S(1)}, bf16[8,21,1024]{2,1,0:T(8,128)(2,1)}, u32[]{:S(2)}, u32[]{:S(2)}) collective-permute-start(bf16[8,21,1024]{2,1,0:T(8,128)(2,1)S(1)} %get-tuple-element.43), channel_id=1, source_target_pairs={{0,24},{8,0},{16,8},{24,16},{1,25},{9,1},{17,9},{25,17},{2,26},{10... | collective-permute-start | bytes 1032200 | tf_op jit(solution)/shard_map/ppermute | solution.py:40
  276.5 12.6 %collective-permute-start.37 = (bf16[8,21,1024]{2,1,0:T(8,128)(2,1)S(1)}, bf16[8,21,1024]{2,1,0:T(8,128)(2,1)}, u32[]{:S(2)}, u32[]{:S(2)}) collective-permute-start(bf16[8,21,1024]{2,1,0:T(8,128)(2,1)S(1)} %get-tuple-element.44), channel_id=1, source_target_pairs={{0,16},{8,24},{16,0},{24,8},{1,17},{9,25},{17,1},{25,9},{2,18},{10... | collective-permute-start | bytes 1032200 | tf_op jit(solution)/shard_map/ppermute | solution.py:40
  276.6 19.5 %collective-permute-start.36 = (bf16[8,21,1024]{2,1,0:T(8,128)(2,1)S(1)}, bf16[8,21,1024]{2,1,0:T(8,128)(2,1)}, u32[]{:S(2)}, u32[]{:S(2)}) collective-permute-start(bf16[8,21,1024]{2,1,0:T(8,128)(2,1)S(1)} %get-tuple-element.42), channel_id=1, source_target_pairs={{0,8},{8,16},{16,24},{24,0},{1,9},{9,17},{17,25},{25,1},{2,10},{10... | collective-permute-start | bytes 1032200 | tf_op jit(solution)/shard_map/ppermute | solution.py:40
  299.4 14.7 %collective-permute-start.45 = (f32[21,1024]{1,0:T(8,128)S(1)}, f32[21,1024]{1,0:T(8,128)S(1)}, u32[]{:S(2)}, u32[]{:S(2)}) collective-permute-start(f32[21,1024]{1,0:T(8,128)S(1)} %get-tuple-element.54), channel_id=1, source_target_pairs={{0,224},{32,0},{64,32},{96,64},{128,96},{160,128},{192,160},{224,1... | collective-permute-start | bytes 258056 | tf_op jit(solution)/shard_map/ppermute | solution.py:40
  307.0 9.4 %collective-permute-start.44 = (f32[21,1024]{1,0:T(8,128)S(1)}, f32[21,1024]{1,0:T(8,128)S(1)}, u32[]{:S(2)}, u32[]{:S(2)}) collective-permute-start(f32[21,1024]{1,0:T(8,128)S(1)} %get-tuple-element.55), channel_id=1, source_target_pairs={{0,192},{32,224},{64,0},{96,32},{128,64},{160,96},{192,128},{224,1... | collective-permute-start | bytes 258056 | tf_op jit(solution)/shard_map/ppermute | solution.py:40
  309.8 13.2 %collective-permute-start.43 = (f32[21,1024]{1,0:T(8,128)}, f32[21,1024]{1,0:T(8,128)}, u32[]{:S(2)}, u32[]{:S(2)}) collective-permute-start(f32[21,1024]{1,0:T(8,128)} %get-tuple-element.56), channel_id=1, source_target_pairs={{0,160},{32,192},{64,224},{96,0},{128,32},{160,64},{192,96},{224,1... | collective-permute-start | bytes 258056 | tf_op jit(solution)/shard_map/ppermute | solution.py:40
  309.8 13.2 %collective-permute-start.42 = (f32[21,1024]{1,0:T(8,128)}, f32[21,1024]{1,0:T(8,128)}, u32[]{:S(2)}, u32[]{:S(2)}) collective-permute-start(f32[21,1024]{1,0:T(8,128)} %get-tuple-element.57), channel_id=1, source_target_pairs={{0,128},{32,160},{64,192},{96,224},{128,0},{160,32},{192,64},{224,... | collective-permute-start | bytes 258056 | tf_op jit(solution)/shard_map/ppermute | solution.py:40
  314.1 12.0 %collective-permute-start.41 = (f32[21,1024]{1,0:T(8,128)S(1)}, f32[21,1024]{1,0:T(8,128)}, u32[]{:S(2)}, u32[]{:S(2)}) collective-permute-start(f32[21,1024]{1,0:T(8,128)S(1)} %get-tuple-element.58), channel_id=1, source_target_pairs={{0,96},{32,128},{64,160},{96,192},{128,224},{160,0},{192,32},{224,... | collective-permute-start | bytes 258056 | tf_op jit(solution)/shard_map/ppermute | solution.py:40
  314.1 15.4 %collective-permute-start.40 = (f32[21,1024]{1,0:T(8,128)S(1)}, f32[21,1024]{1,0:T(8,128)}, u32[]{:S(2)}, u32[]{:S(2)}) collective-permute-start(f32[21,1024]{1,0:T(8,128)S(1)} %get-tuple-element.59), channel_id=1, source_target_pairs={{0,64},{32,96},{64,128},{96,160},{128,192},{160,224},{192,0},{224,... | collective-permute-start | bytes 258056 | tf_op jit(solution)/shard_map/ppermute | solution.py:40
  317.0 16.3 %collective-permute-start.39 = (f32[21,1024]{1,0:T(8,128)S(1)}, f32[21,1024]{1,0:T(8,128)}, u32[]{:S(2)}, u32[]{:S(2)}) collective-permute-start(f32[21,1024]{1,0:T(8,128)S(1)} %get-tuple-element.53), channel_id=1, source_target_pairs={{0,32},{32,64},{64,96},{96,128},{128,160},{160,192},{192,224},{224... | collective-permute-start | bytes 258056 | tf_op jit(solution)/shard_map/ppermute | solution.py:40
  360.9 4.7 %collective-permute-start.52 = (f32[]{:T(128)}, f32[]{:T(128)}, u32[]{:S(2)}, u32[]{:S(2)}) collective-permute-start(f32[]{:T(128)} %add.497), channel_id=1, source_target_pairs={{0,64},{32,96},{64,128},{96,160},{128,192},{160,224},{192,0},{224,... | collective-permute-start | bytes 20 | tf_op jit(solution)/shard_map/ppermute | solution.py:40
  366.3 6.5 %collective-permute-start.53 = (f32[]{:T(128)}, f32[]{:T(128)}, u32[]{:S(2)}, u32[]{:S(2)}) collective-permute-start(f32[]{:T(128)} %add.498), channel_id=1, source_target_pairs={{0,128},{32,160},{64,192},{96,224},{128,0},{160,32},{192,64},{224,... | collective-permute-start | bytes 20 | tf_op jit(solution)/shard_map/ppermute | solution.py:40
  (26 other events, 492.3 us)

commit v6 on v3

--- a/solution.py
+++ b/solution.py
@@ -201,11 +201,13 @@
     nc = lax.axis_size("core")
     x_own = layer_input[0]
     rows = x_own.shape[1] // (nz * ncx * ny * nc)
-    x_view = x_own.reshape(shard_length, nz, ncx, ny * nc * rows)
+    tall = -(-rows // 8) * 8
+    x_view = x_own.reshape(shard_length, nz, ncx, ny * nc, rows)
+    x_view = jnp.pad(x_view, ((0, 0), (0, 0), (0, 0), (0, 0), (0, tall - rows)))
 
     def columns(target):
         picked = lax.dynamic_index_in_dim(x_view, target, 2, keepdims=False)
-        return picked.reshape(shard_length, nz * ny * nc * rows)
+        return picked.reshape(shard_length, nz * ny * nc * tall)
 
     x_list = [columns(icx)]
     v_list = [value_out]
@@ -220,7 +222,7 @@
         (((0,), (0,)), ((), ())),
         preferred_element_type=jnp.float32,
     )
-    partial = partial.reshape(nz, ny, nc, rows, kv_width)
+    partial = partial.reshape(nz, ny, nc, tall, kv_width)
     icore = lax.axis_index("core")
     stage = lax.dynamic_index_in_dim(partial, icore, 2, keepdims=False)
     for by in range(1, nc):
@@ -236,7 +238,9 @@
         sent = lax.dynamic_index_in_dim(stage_y, (iz + by) % nz, 0, keepdims=False)
         weight_grad = weight_grad + cyclic(sent, "cz", by)
 
-    square_total = all_sum(jnp.sum(weight_grad * weight_grad), ("core", "y", "cx", "cz"))
+    weight_grad = weight_grad[:rows]
+    square_total = lax.psum(jnp.sum(weight_grad * weight_grad), DP)
+    square_total = all_sum(square_total, ("cx", "cz"))
     norm_total = jnp.sqrt(square_total + 1e-06)
     clipped = weight_grad * jnp.minimum(1.0, clip_norm / norm_total)
     new_first = beta_first * first_moment_value + (1.0 - beta_first) * clipped

time: 359 us -> 360 us (level)
  blocking collectives: 22.3 us -> 33 us
  local copies, waits for them, and re-layouts: 36.1 us -> 25.6 us
    psum x0 -> x1, blocking collectives: none -> 14.6 us  [shards(): square_total = lax.psum(jnp.sum(weight_grad * weight_grad), DP)]
    reshape x1 -> x0, local copies, waits for them, and re-layouts: 5.88 us -> none  [shards(): partial = partial.reshape(nz, ny, nc, rows, kv_width)]
    all_gather x1, blocking collectives: 22.3 us -> 18.4 us  [shards(): lax.all_gather(new_master.astype(jnp.bfloat16), DP, axis=0, tiled=True)]
    ppermute x34 -> x31, starting transfers between devices: 52.4 us -> 55.9 us  [cyclic(): return lax.ppermute(x, axis, [(i, (i + by) % count) for i in range(count)])]
    ppermute x34 -> x31, waiting for transfers between devices: 149 us -> 147 us  [cyclic(): return lax.ppermute(x, axis, [(i, (i + by) % count) for i in range(count)])]
    unnamed x54 -> x57, local copies, waits for them, and re-layouts: 16.8 us -> 15.6 us
  transfers between devices with their start and end apart: 38 -> 35, of which waited for: 27 -> 25; matrix products, arithmetic and copies ran while one was open for 6% -> 4% of each run, Pallas kernels for 0% -> 0%
where the time goes in v6:
time: 360 us; the launch traced here: 355 us
  waiting for transfers between devices  176 us (49%)
  starting transfers between devices  67 us (19%)
  blocking collectives  33 us (9%)
  local copies, waits for them, and re-layouts  25.6 us (7%)
  other arithmetic  25.5 us (7%)
  matrix products  21.9 us (6%)
  between operations  5.66 us (2%)
    ppermute x31, waiting for transfers between devices, cyclic(): return lax.ppermute(x, axis, [(i, (i + by) % count) for i in range(count)])  147 us
    ppermute x31, starting transfers between devices, cyclic(): return lax.ppermute(x, axis, [(i, (i + by) % count) for i in range(count)])  55.9 us
    ppermute x4, waiting for transfers between devices, shift(): return lax.ppermute(x, axis, pairs)  29.9 us
    all_gather x1, blocking collectives, shards(): lax.all_gather(new_master.astype(jnp.bfloat16), DP, axis=0, tiled=True)  18.4 us
    unnamed x57, local copies, waits for them, and re-layouts  15.6 us
    psum x1, blocking collectives, shards(): square_total = lax.psum(jnp.sum(weight_grad * weight_grad), DP)  14.6 us
    ppermute x4, starting transfers between devices, shift(): return lax.ppermute(x, axis, pairs)  11.1 us
  transfers between devices with their start and end apart: 35, of which 25 were waited for; matrix products, arithmetic and copies ran while one was open for 4% of the time, Pallas kernels for 0%

profile of v6, /device:TPU:1, one launch (start us, length us, event | category | flops | bytes accessed | tf_op | source)
XLA Modules:
  0.0 354.9 jit_solution(11956348879800299025)
XLA Ops:
  3.6 4.4 %collective-permute-start = (bf16[128,2176]{0,1:T(8,128)(2,1)S(1)}, bf16[128,2176]{0,1:T(8,128)(2,1)S(1)}, u32[]{:S(2)}, u32[]{:S(2)}) collective-permute-start(bf16[128,2176]{0,1:T(8,128)(2,1)S(1)} %pad_maximum_fusion.4), channel_id=1, source_target_pairs={{0,32},{32,64},{64,96},{96,128},{128,160},{160,192},{192,224},{1,3... | collective-permute-start | bytes 1671176 | tf_op jit(solution)/shard_map/ppermute | solution.py:113
  10.9 8.4 %collective-permute-done = bf16[128,2176]{0,1:T(8,128)(2,1)S(1)} collective-permute-done((bf16[128,2176]{0,1:T(8,128)(2,1)S(1)}, bf16[128,2176]{0,1:T(8,128)(2,1)S(1)}, u32[]{:S(2)}, u32[]{:S(2)}) %collective-permute-start) | collective-permute-done | bytes 557088 | tf_op jit(solution)/shard_map/ppermute | solution.py:113
  19.3 4.1 %collective-permute-start.1 = (bf16[128,2176]{0,1:T(8,128)(2,1)S(1)}, bf16[128,2176]{0,1:T(8,128)(2,1)S(1)}, u32[]{:S(2)}, u32[]{:S(2)}) collective-permute-start(bf16[128,2176]{0,1:T(8,128)(2,1)S(1)} %collective-permute-done), channel_id=1, source_target_pairs={{0,32},{32,64},{64,96},{96,128},{128,160},{160,192},{192,224},{1,3... | collective-permute-start | bytes 1671176 | tf_op jit(solution)/shard_map/ppermute | solution.py:113
  24.8 2.5 collective-permute-start.3
  28.4 5.4 %collective-permute-done.1 = bf16[128,2176]{0,1:T(8,128)(2,1)S(1)} collective-permute-done((bf16[128,2176]{0,1:T(8,128)(2,1)S(1)}, bf16[128,2176]{0,1:T(8,128)(2,1)S(1)}, u32[]{:S(2)}, u32[]{:S(2)}) %collective-permute-start.1) | collective-permute-done | bytes 557088 | tf_op jit(solution)/shard_map/ppermute | solution.py:113
  35.4 2.5 collective-permute-start.6
  39.7 10.4 %collective-permute-done.3 = bf16[128,2176]{0,1:T(8,128)(2,1)S(1)} collective-permute-done((bf16[128,2176]{0,1:T(8,128)(2,1)S(1)}, bf16[128,2176]{0,1:T(8,128)(2,1)S(1)}, u32[]{:S(2)}, u32[]{:S(2)}) %collective-permute-start.3) | collective-permute-done | bytes 557088 | tf_op jit(solution)/shard_map/ppermute | solution.py:38
  50.3 2.5 collective-permute-done.4
  52.9 9.2 %collective-permute-done.5 = bf16[128,2176]{0,1:T(8,128)(2,1)S(1)} collective-permute-done((bf16[128,2176]{0,1:T(8,128)(2,1)S(1)}, bf16[128,2176]{0,1:T(8,128)(2,1)S(1)}, u32[]{:S(2)}, u32[]{:S(2)}) %collective-permute-start.5) | collective-permute-done | bytes 557088 | tf_op jit(solution)/shard_map/ppermute | solution.py:38
  62.2 11.8 %collective-permute-done.6 = bf16[128,2176]{0,1:T(8,128)(2,1)S(1)} collective-permute-done((bf16[128,2176]{0,1:T(8,128)(2,1)S(1)}, bf16[128,2176]{0,1:T(8,128)(2,1)S(1)}, u32[]{:S(2)}, u32[]{:S(2)}) %collective-permute-start.6) | collective-permute-done | bytes 557088 | tf_op jit(solution)/shard_map/ppermute | solution.py:38
  77.8 6.3 %fusion.56 = (f32[8,2,128]{2,1,0:T(2,128)}, f32[8,2,128,1152]{2,3,1,0:T(8,128)}) fusion(pred[128,1152]{0,1:T(8,128)(4,1)S(1)} %fusion.44, bf16[1152,8,128,1]{0,2,3,1:T(8,128)(2,1)S(1)} %bitcast.126, bf16[128,8,2,128]{0,3,2,1:T(8,128)(2,1)S(1)} %bitcast.140), kind=kOutput, calls=%fused_computation.133 | convolution fusion | flops 613418112 | bytes 12476416 | tf_op jit(solution)/shard_map/sub | solution.py:75
  84.1 4.8 %fusion.8 = bf16[8,2,128,1152]{2,3,1,0:T(8,128)(2,1)S(1)} fusion(f32[8,2,128,1152]{2,3,1,0:T(8,128)} %get-tuple-element.67, f32[8,2,128]{2,1,0:T(2,128)} %get-tuple-element.66), kind=kLoop, calls=%fused_computation.16 | loop fusion | flops 4718592 | bytes 14163968 | tf_op jit(solution)/shard_map/convert_element_type | solution.py:77
  91.7 5.3 %fusion.3 = bf16[8,2,128,1152]{2,3,1,0:T(8,128)(2,1)S(1)} fusion(bf16[1152,8,128,1]{0,2,3,1:T(8,128)(2,1)S(1)} %bitcast.129, bf16[128,8,2,128]{0,3,2,1:T(8,128)(2,1)S(1)} %bitcast.132, f32[8,2,128]{2,1,0:T(2,128)S(1)} %bitcast.146, f32[8,2,128,1152]{2,3,1,0:T(8,128)} %get-tuple-element.67, f32[8,2,128]{2,1,0:T(2,128)S(1)} %copy-done.18), kind=kOutput, calls=%fused_computation.7 | convolution fusion | flops 613416960 | bytes 17055744 | tf_op jit(solution)/shard_map/tgrd,egd->grte/dot_general | solution.py:82
  99.2 2.9 fusion.1
  102.8 2.1 fusion.54
  105.0 3.5 collective-permute-start.8
  109.1 2.2 collective-permute-start.13
  112.7 28.9 %collective-permute-done.8 = bf16[128,2048]{0,1:T(8,128)(2,1)S(1)} collective-permute-done((bf16[128,2048]{0,1:T(8,128)(2,1)S(1)}, bf16[128,2048]{0,1:T(8,128)(2,1)S(1)}, u32[]{:S(2)}, u32[]{:S(2)}) %collective-permute-start.8) | collective-permute-done | bytes 524320 | tf_op jit(solution)/shard_map/ppermute | solution.py:38
  141.6 3.6 %collective-permute-start.11 = (bf16[128,2048]{0,1:T(8,128)(2,1)S(1)}, bf16[128,2048]{0,1:T(8,128)(2,1)S(1)}, u32[]{:S(2)}, u32[]{:S(2)}) collective-permute-start(bf16[128,2048]{0,1:T(8,128)(2,1)S(1)} %get-tuple-element.36), channel_id=1, source_target_pairs={{0,24},{8,0},{16,8},{24,16},{1,25},{9,1},{17,9},{25,17},{2,26},{10... | collective-permute-start | bytes 1572872 | tf_op jit(solution)/shard_map/ppermute | solution.py:38
  148.9 7.6 %collective-permute-done.12 = bf16[128,2048]{0,1:T(8,128)(2,1)S(1)} collective-permute-done((bf16[128,2048]{0,1:T(8,128)(2,1)S(1)}, bf16[128,2048]{0,1:T(8,128)(2,1)S(1)}, u32[]{:S(2)}, u32[]{:S(2)}) %collective-permute-start.12) | collective-permute-done | bytes 524320 | tf_op jit(solution)/shard_map/ppermute | solution.py:38
  156.5 5.1 %collective-permute-done.14 = bf16[128,2048]{0,1:T(8,128)(2,1)S(1)} collective-permute-done((bf16[128,2048]{0,1:T(8,128)(2,1)S(1)}, bf16[128,2048]{0,1:T(8,128)(2,1)S(1)}, u32[]{:S(2)}, u32[]{:S(2)}) %collective-permute-start.14) | collective-permute-done | bytes 524320 | tf_op jit(solution)/shard_map/ppermute | solution.py:113
  161.6 2.2 add_convert_fusion
  167.6 10.9 %collective-permute-done.15 = bf16[128,2048]{0,1:T(8,128)(2,1)} collective-permute-done((bf16[128,2048]{0,1:T(8,128)(2,1)}, bf16[128,2048]{0,1:T(8,128)(2,1)}, u32[]{:S(2)}, u32[]{:S(2)}) %collective-permute-start.15) | collective-permute-done | bytes 524320 | tf_op jit(solution)/shard_map/ppermute | solution.py:113
  178.5 2.1 fusion.27
  184.2 12.3 %collective-permute-done.18 = bf16[128,2560]{0,1:T(8,128)(2,1)S(1)} collective-permute-done((bf16[128,2560]{0,1:T(8,128)(2,1)}, bf16[128,2560]{0,1:T(8,128)(2,1)S(1)}, u32[]{:S(2)}, u32[]{:S(2)}) %collective-permute-start.18) | collective-permute-done | bytes 655392 | tf_op jit(solution)/shard_map/ppermute | solution.py:38
  196.5 2.1 collective-permute-done.17
  198.7 17.0 %collective-permute-done.16 = bf16[128,2560]{0,1:T(8,128)(2,1)S(1)} collective-permute-done((bf16[128,2560]{0,1:T(8,128)(2,1)}, bf16[128,2560]{0,1:T(8,128)(2,1)S(1)}, u32[]{:S(2)}, u32[]{:S(2)}) %collective-permute-start.16) | collective-permute-done | bytes 655392 | tf_op jit(solution)/shard_map/ppermute | solution.py:38
  215.8 2.8 fusion.10
  218.7 2.7 copy-done.7
  222.2 3.0 collective-permute-done.19
  225.2 2.4 bitcast_add_fusion
  230.2 2.7 collective-permute-start.22
  233.9 15.7 %collective-permute-done.22 = bf16[8,24,1024]{2,1,0:T(8,128)(2,1)} collective-permute-done((bf16[8,24,1024]{2,1,0:T(8,128)(2,1)}, bf16[8,24,1024]{2,1,0:T(8,128)(2,1)}, u32[]{:S(2)}, u32[]{:S(2)}) %collective-permute-start.22) | collective-permute-done | bytes 393248 | tf_op jit(solution)/shard_map/ppermute | solution.py:38
  249.6 4.4 %collective-permute-done.20 = bf16[8,24,1024]{2,1,0:T(8,128)(2,1)} collective-permute-done((bf16[8,24,1024]{2,1,0:T(8,128)(2,1)S(1)}, bf16[8,24,1024]{2,1,0:T(8,128)(2,1)}, u32[]{:S(2)}, u32[]{:S(2)}) %collective-permute-start.20) | collective-permute-done | bytes 393248 | tf_op jit(solution)/shard_map/ppermute | solution.py:38
  258.2 2.2 collective-permute-start.23
  260.4 3.4 fusion.19
  267.7 7.7 %collective-permute-start.27 = (f32[24,1024]{1,0:T(8,128)}, f32[24,1024]{1,0:T(8,128)S(1)}, u32[]{:S(2)}, u32[]{:S(2)}) collective-permute-start(f32[24,1024]{1,0:T(8,128)} %get-tuple-element.55), channel_id=1, source_target_pairs={{0,160},{32,192},{64,224},{96,0},{128,32},{160,64},{192,96},{224,1... | collective-permute-start | bytes 294920 | tf_op jit(solution)/shard_map/ppermute | solution.py:38
  277.3 2.3 collective-permute-start.24
  282.5 2.7 collective-permute-done.26
  285.2 5.4 %collective-permute-done.25 = f32[24,1024]{1,0:T(8,128)S(1)} collective-permute-done((f32[24,1024]{1,0:T(8,128)}, f32[24,1024]{1,0:T(8,128)S(1)}, u32[]{:S(2)}, u32[]{:S(2)}) %collective-permute-start.25) | collective-permute-done | bytes 98336 | tf_op jit(solution)/shard_map/ppermute | solution.py:38
  292.1 14.6 %psum.7 = f32[]{:T(128)} all-reduce(f32[]{:T(128)} %get-tuple-element.32), channel_id=1, replica_groups=mesh['cz'=8,'cx'=4,'y'=4,'core'=2] {'y','core'}, use_global_device_ids=true, to_apply=%region_4.5 | all-reduce | flops 1 | bytes 8 | tf_op jit(solution)/shard_map/psum | solution.py:242
  306.7 3.9 %collective-permute-done.30 = f32[]{:T(128)} collective-permute-done((f32[]{:T(128)}, f32[]{:T(128)}, u32[]{:S(2)}, u32[]{:S(2)}) %collective-permute-start.30) | collective-permute-done | bytes 36 | tf_op jit(solution)/shard_map/ppermute | solution.py:38
  312.6 3.3 collective-permute-done.31
  316.6 3.6 %collective-permute-start.32 = (f32[]{:T(128)}, f32[]{:T(128)}, u32[]{:S(2)}, u32[]{:S(2)}) collective-permute-start(f32[]{:T(128)} %add.460), channel_id=1, source_target_pairs={{0,32},{32,64},{64,96},{96,128},{128,160},{160,192},{192,224},{224... | collective-permute-start | bytes 20 | tf_op jit(solution)/shard_map/ppermute | solution.py:38
  321.0 2.1 collective-permute-start.33
  323.1 2.6 collective-permute-done.33
  326.3 5.4 %collective-permute-start.34 = (f32[]{:T(128)}, f32[]{:T(128)}, u32[]{:S(2)}, u32[]{:S(2)}) collective-permute-start(f32[]{:T(128)} %add.462), channel_id=1, source_target_pairs={{0,128},{32,160},{64,192},{96,224},{128,0},{160,32},{192,64},{224,... | collective-permute-start | bytes 20 | tf_op jit(solution)/shard_map/ppermute | solution.py:38
  335.2 18.4 %all-gather = bf16[8,21,1024]{2,1,0:T(8,128)(2,1)S(1)} all-gather(bf16[1,21,1024]{2,1,0:T(8,128)(2,1)S(1)} %get-tuple-element.28), channel_id=1, replica_groups=mesh['cz'=8,'cx'=4,'y'=4,'core'=2] {'y','core'}, dimensions={0}, use_global_device_ids=true | all-gather | bytes 387072 | tf_op jit(solution)/shard_map/all_gather | solution.py:250
  (132 shorter events, 58.2 us)
Async XLA Ops:
  1.3 2.3 copy-start.19
  3.6 15.7 %collective-permute-start = (bf16[128,2176]{0,1:T(8,128)(2,1)S(1)}, bf16[128,2176]{0,1:T(8,128)(2,1)S(1)}, u32[]{:S(2)}, u32[]{:S(2)}) collective-permute-start(bf16[128,2176]{0,1:T(8,128)(2,1)S(1)} %pad_maximum_fusion.4), channel_id=1, source_target_pairs={{0,32},{32,64},{64,96},{96,128},{128,160},{160,192},{192,224},{1,3... | collective-permute-start | bytes 1671176 | tf_op jit(solution)/shard_map/ppermute | solution.py:113
  10.8 67.0 %copy-start.9 = (bf16[1,128,2048]{1,2,0:T(8,128)(2,1)}, bf16[1,128,2048]{1,2,0:T(8,128)(2,1)S(1)}, u32[]{:S(2)}) copy-start(bf16[1,128,2048]{1,2,0:T(8,128)(2,1)S(1)} %copy.85) | copy-start | bytes 1572868
  19.3 14.5 %collective-permute-start.1 = (bf16[128,2176]{0,1:T(8,128)(2,1)S(1)}, bf16[128,2176]{0,1:T(8,128)(2,1)S(1)}, u32[]{:S(2)}, u32[]{:S(2)}) collective-permute-start(bf16[128,2176]{0,1:T(8,128)(2,1)S(1)} %collective-permute-done), channel_id=1, source_target_pairs={{0,32},{32,64},{64,96},{96,128},{128,160},{160,192},{192,224},{1,3... | collective-permute-start | bytes 1671176 | tf_op jit(solution)/shard_map/ppermute | solution.py:113
  23.5 38.7 %copy-start.16 = (s32[1152]{0:T(1024)}, s32[1152]{0:T(1024)S(1)}, u32[]{:S(2)}) copy-start(s32[1152]{0:T(1024)S(1)} %get-tuple-element.68) | copy-start | bytes 13828
  23.5 14.7 %collective-permute-start.2 = (bf16[128,2176]{0,1:T(8,128)(2,1)S(1)}, bf16[128,2176]{0,1:T(8,128)(2,1)S(1)}, u32[]{:S(2)}, u32[]{:S(2)}) collective-permute-start(bf16[128,2176]{0,1:T(8,128)(2,1)S(1)} %collective-permute-done), channel_id=1, source_target_pairs={{0,8},{8,16},{16,24},{24,0},{1,9},{9,17},{17,25},{25,1},{2,10},{10... | collective-permute-start | bytes 1671176 | tf_op jit(solution)/shard_map/ppermute | solution.py:38
  24.8 25.3 %collective-permute-start.3 = (bf16[128,2176]{0,1:T(8,128)(2,1)S(1)}, bf16[128,2176]{0,1:T(8,128)(2,1)S(1)}, u32[]{:S(2)}, u32[]{:S(2)}) collective-permute-start(bf16[128,2176]{0,1:T(8,128)(2,1)S(1)} %collective-permute-done), channel_id=1, source_target_pairs={{0,16},{8,24},{16,0},{24,8},{1,17},{9,25},{17,1},{25,9},{2,18},{10... | collective-permute-start | bytes 1671176 | tf_op jit(solution)/shard_map/ppermute | solution.py:38
  27.2 25.5 %collective-permute-start.4 = (bf16[128,2176]{0,1:T(8,128)(2,1)S(1)}, bf16[128,2176]{0,1:T(8,128)(2,1)S(1)}, u32[]{:S(2)}, u32[]{:S(2)}) collective-permute-start(bf16[128,2176]{0,1:T(8,128)(2,1)S(1)} %collective-permute-done), channel_id=1, source_target_pairs={{0,24},{8,0},{16,8},{24,16},{1,25},{9,1},{17,9},{25,17},{2,26},{10... | collective-permute-start | bytes 1671176 | tf_op jit(solution)/shard_map/ppermute | solution.py:38
  34.2 27.9 %collective-permute-start.5 = (bf16[128,2176]{0,1:T(8,128)(2,1)S(1)}, bf16[128,2176]{0,1:T(8,128)(2,1)S(1)}, u32[]{:S(2)}, u32[]{:S(2)}) collective-permute-start(bf16[128,2176]{0,1:T(8,128)(2,1)S(1)} %get-tuple-element.51), channel_id=1, source_target_pairs={{0,8},{8,16},{16,24},{24,0},{1,9},{9,17},{17,25},{25,1},{2,10},{10... | collective-permute-start | bytes 1671176 | tf_op jit(solution)/shard_map/ppermute | solution.py:38
  35.4 38.5 %collective-permute-start.6 = (bf16[128,2176]{0,1:T(8,128)(2,1)S(1)}, bf16[128,2176]{0,1:T(8,128)(2,1)S(1)}, u32[]{:S(2)}, u32[]{:S(2)}) collective-permute-start(bf16[128,2176]{0,1:T(8,128)(2,1)S(1)} %get-tuple-element.50), channel_id=1, source_target_pairs={{0,16},{8,24},{16,0},{24,8},{1,17},{9,25},{17,1},{25,9},{2,18},{10... | collective-permute-start | bytes 1671176 | tf_op jit(solution)/shard_map/ppermute | solution.py:38
  38.2 36.5 %collective-permute-start.7 = (bf16[128,2176]{0,1:T(8,128)(2,1)S(1)}, bf16[128,2176]{0,1:T(8,128)(2,1)S(1)}, u32[]{:S(2)}, u32[]{:S(2)}) collective-permute-start(bf16[128,2176]{0,1:T(8,128)(2,1)S(1)} %get-tuple-element.49), channel_id=1, source_target_pairs={{0,24},{8,0},{16,8},{24,16},{1,25},{9,1},{17,9},{25,17},{2,26},{10... | collective-permute-start | bytes 1671176 | tf_op jit(solution)/shard_map/ppermute | solution.py:38
  76.6 7.5 %copy-start.3 = (bf16[1152,1024]{0,1:T(8,128)(2,1)}, bf16[1152,1024]{0,1:T(8,128)(2,1)S(1)}, u32[]{:S(2)}) copy-start(bf16[1152,1024]{0,1:T(8,128)(2,1)S(1)} %get-tuple-element.35) | copy-start | bytes 7077892
  90.5 8.7 %copy-start = (f32[8,1152,128,1]{1,2,3,0:T(8,128)}, f32[8,1152,128,1]{1,2,3,0:T(8,128)S(1)}, u32[]{:S(2)}) copy-start(f32[8,1152,128,1]{1,2,3,0:T(8,128)S(1)} %fusion.57) | copy-start | bytes 14155780
  91.7 5.3 %copy-start.10 = (bf16[1,128,2048]{1,2,0:T(8,128)(2,1)S(1)}, bf16[1,128,2048]{1,2,0:T(8,128)(2,1)}, u32[]{:S(2)}) copy-start(bf16[1,128,2048]{1,2,0:T(8,128)(2,1)} %copy-done.9) | copy-start | bytes 1572868
  99.2 3.7 %copy-start.1 = (f32[8,1152,128]{1,2,0:T(8,128)}, f32[8,1152,128]{1,2,0:T(8,128)S(1)}, u32[]{:S(2)}) copy-start(f32[8,1152,128]{1,2,0:T(8,128)S(1)} %bitcast_multiply_fusion) | copy-start | bytes 14155780
  105.0 60.1 %copy-start.13 = (bf16[1,128,5376]{2,1,0:T(8,128)(2,1)S(1)}, bf16[1,128,5376]{2,1,0:T(8,128)(2,1)}, u32[]{:S(2)}) copy-start(bf16[1,128,5376]{2,1,0:T(8,128)(2,1)} %param.9) | copy-start | bytes 4128772
  105.0 36.6 %collective-permute-start.8 = (bf16[128,2048]{0,1:T(8,128)(2,1)S(1)}, bf16[128,2048]{0,1:T(8,128)(2,1)S(1)}, u32[]{:S(2)}, u32[]{:S(2)}) collective-permute-start(bf16[128,2048]{0,1:T(8,128)(2,1)S(1)} %get-tuple-element.41), channel_id=1, source_target_pairs={{0,24},{8,0},{16,8},{24,16},{1,25},{9,1},{17,9},{25,17},{2,26},{10... | collective-permute-start | bytes 1572872 | tf_op jit(solution)/shard_map/ppermute | solution.py:38
  108.5 36.7 %collective-permute-start.9 = (bf16[128,2048]{0,1:T(8,128)(2,1)S(1)}, bf16[128,2048]{0,1:T(8,128)(2,1)S(1)}, u32[]{:S(2)}, u32[]{:S(2)}) collective-permute-start(bf16[128,2048]{0,1:T(8,128)(2,1)S(1)} %get-tuple-element.40), channel_id=1, source_target_pairs={{0,16},{8,24},{16,0},{24,8},{1,17},{9,25},{17,1},{25,9},{2,18},{10... | collective-permute-start | bytes 1572872 | tf_op jit(solution)/shard_map/ppermute | solution.py:38
  108.6 36.5 %collective-permute-start.10 = (bf16[128,2048]{0,1:T(8,128)(2,1)S(1)}, bf16[128,2048]{0,1:T(8,128)(2,1)S(1)}, u32[]{:S(2)}, u32[]{:S(2)}) collective-permute-start(bf16[128,2048]{0,1:T(8,128)(2,1)S(1)} %get-tuple-element.39), channel_id=1, source_target_pairs={{0,8},{8,16},{16,24},{24,0},{1,9},{9,17},{17,25},{25,1},{2,10},{10... | collective-permute-start | bytes 1572872 | tf_op jit(solution)/shard_map/ppermute | solution.py:38
  109.1 39.7 %collective-permute-start.13 = (bf16[128,2048]{0,1:T(8,128)(2,1)S(1)}, bf16[128,2048]{0,1:T(8,128)(2,1)S(1)}, u32[]{:S(2)}, u32[]{:S(2)}) collective-permute-start(bf16[128,2048]{0,1:T(8,128)(2,1)S(1)} %get-tuple-element.37), channel_id=1, source_target_pairs={{0,8},{8,16},{16,24},{24,0},{1,9},{9,17},{17,25},{25,1},{2,10},{10... | collective-permute-start | bytes 1572872 | tf_op jit(solution)/shard_map/ppermute | solution.py:38
  111.3 45.2 %collective-permute-start.12 = (bf16[128,2048]{0,1:T(8,128)(2,1)S(1)}, bf16[128,2048]{0,1:T(8,128)(2,1)S(1)}, u32[]{:S(2)}, u32[]{:S(2)}) collective-permute-start(bf16[128,2048]{0,1:T(8,128)(2,1)S(1)} %get-tuple-element.38), channel_id=1, source_target_pairs={{0,16},{8,24},{16,0},{24,8},{1,17},{9,25},{17,1},{25,9},{2,18},{10... | collective-permute-start | bytes 1572872 | tf_op jit(solution)/shard_map/ppermute | solution.py:38
  141.6 14.9 %collective-permute-start.11 = (bf16[128,2048]{0,1:T(8,128)(2,1)S(1)}, bf16[128,2048]{0,1:T(8,128)(2,1)S(1)}, u32[]{:S(2)}, u32[]{:S(2)}) collective-permute-start(bf16[128,2048]{0,1:T(8,128)(2,1)S(1)} %get-tuple-element.36), channel_id=1, source_target_pairs={{0,24},{8,0},{16,8},{24,16},{1,25},{9,1},{17,9},{25,17},{2,26},{10... | collective-permute-start | bytes 1572872 | tf_op jit(solution)/shard_map/ppermute | solution.py:38
  147.5 14.0 %collective-permute-start.14 = (bf16[128,2048]{0,1:T(8,128)(2,1)S(1)}, bf16[128,2048]{0,1:T(8,128)(2,1)S(1)}, u32[]{:S(2)}, u32[]{:S(2)}) collective-permute-start(bf16[128,2048]{0,1:T(8,128)(2,1)S(1)} %fusion.31), channel_id=1, source_target_pairs={{32,0},{64,32},{96,64},{128,96},{160,128},{192,160},{224,192},{33,... | collective-permute-start | bytes 1572872 | tf_op jit(solution)/shard_map/ppermute | solution.py:113
  163.8 14.7 %collective-permute-start.15 = (bf16[128,2048]{0,1:T(8,128)(2,1)}, bf16[128,2048]{0,1:T(8,128)(2,1)}, u32[]{:S(2)}, u32[]{:S(2)}) collective-permute-start(bf16[128,2048]{0,1:T(8,128)(2,1)} %add_convert_fusion), channel_id=1, source_target_pairs={{32,0},{64,32},{96,64},{128,96},{160,128},{192,160},{224,192},{33,... | collective-permute-start | bytes 1572872 | tf_op jit(solution)/shard_map/ppermute | solution.py:113
  182.8 13.7 %collective-permute-start.18 = (bf16[128,2560]{0,1:T(8,128)(2,1)}, bf16[128,2560]{0,1:T(8,128)(2,1)S(1)}, u32[]{:S(2)}, u32[]{:S(2)}) collective-permute-start(bf16[128,2560]{0,1:T(8,128)(2,1)} %get-tuple-element.64), channel_id=1, source_target_pairs={{0,24},{8,0},{16,8},{24,16},{1,25},{9,1},{17,9},{25,17},{2,26},{10... | collective-permute-start | bytes 1966088 | tf_op jit(solution)/shard_map/ppermute | solution.py:38
  183.3 15.3 %collective-permute-start.17 = (bf16[128,2560]{0,1:T(8,128)(2,1)}, bf16[128,2560]{0,1:T(8,128)(2,1)S(1)}, u32[]{:S(2)}, u32[]{:S(2)}) collective-permute-start(bf16[128,2560]{0,1:T(8,128)(2,1)} %get-tuple-element.65), channel_id=1, source_target_pairs={{0,16},{8,24},{16,0},{24,8},{1,17},{9,25},{17,1},{25,9},{2,18},{10... | collective-permute-start | bytes 1966088 | tf_op jit(solution)/shard_map/ppermute | solution.py:38
  183.3 32.4 %collective-permute-start.16 = (bf16[128,2560]{0,1:T(8,128)(2,1)}, bf16[128,2560]{0,1:T(8,128)(2,1)S(1)}, u32[]{:S(2)}, u32[]{:S(2)}) collective-permute-start(bf16[128,2560]{0,1:T(8,128)(2,1)} %get-tuple-element.63), channel_id=1, source_target_pairs={{0,8},{8,16},{16,24},{24,0},{1,9},{9,17},{17,25},{25,1},{2,10},{10... | collective-permute-start | bytes 1966088 | tf_op jit(solution)/shard_map/ppermute | solution.py:38
  218.6 2.7 copy-start.7
  221.6 3.6 %collective-permute-start.19 = (bf16[8,4,24,1024]{3,2,1,0:T(8,128)(2,1)S(1)}, bf16[8,4,24,1024]{3,2,1,0:T(8,128)(2,1)S(1)}, u32[]{:S(2)}, u32[]{:S(2)}) collective-permute-start(bf16[8,4,24,1024]{3,2,1,0:T(8,128)(2,1)S(1)} %fusion.9), channel_id=1, source_target_pairs={{0,1},{1,0},{2,3},{3,2},{4,5},{5,4},{6,7},{7,6},{8,9},{9,8},{10,11... | collective-permute-start | bytes 4718600 | tf_op jit(solution)/shard_map/ppermute | solution.py:38
  229.2 31.2 %copy-start.4 = (bf16[1152,1024]{0,1:T(8,128)(2,1)S(1)}, bf16[1152,1024]{0,1:T(8,128)(2,1)}, u32[]{:S(2)}) copy-start(bf16[1152,1024]{0,1:T(8,128)(2,1)} %copy-done.3) | copy-start | bytes 7077892
  230.2 19.4 %collective-permute-start.22 = (bf16[8,24,1024]{2,1,0:T(8,128)(2,1)}, bf16[8,24,1024]{2,1,0:T(8,128)(2,1)}, u32[]{:S(2)}, u32[]{:S(2)}) collective-permute-start(bf16[8,24,1024]{2,1,0:T(8,128)(2,1)} %get-tuple-element.43), channel_id=1, source_target_pairs={{0,6},{2,0},{4,2},{6,4},{1,7},{3,1},{5,3},{7,5},{8,14},{10,8},{12,... | collective-permute-start | bytes 1179656 | tf_op jit(solution)/shard_map/ppermute | solution.py:38
  232.9 16.7 %collective-permute-start.21 = (bf16[8,24,1024]{2,1,0:T(8,128)(2,1)S(1)}, bf16[8,24,1024]{2,1,0:T(8,128)(2,1)}, u32[]{:S(2)}, u32[]{:S(2)}) collective-permute-start(bf16[8,24,1024]{2,1,0:T(8,128)(2,1)S(1)} %get-tuple-element.44), channel_id=1, source_target_pairs={{0,4},{2,6},{4,0},{6,2},{1,5},{3,7},{5,1},{7,3},{8,12},{10,14},{12... | collective-permute-start | bytes 1179656 | tf_op jit(solution)/shard_map/ppermute | solution.py:38
  233.2 20.7 %collective-permute-start.20 = (bf16[8,24,1024]{2,1,0:T(8,128)(2,1)S(1)}, bf16[8,24,1024]{2,1,0:T(8,128)(2,1)}, u32[]{:S(2)}, u32[]{:S(2)}) collective-permute-start(bf16[8,24,1024]{2,1,0:T(8,128)(2,1)S(1)} %get-tuple-element.42), channel_id=1, source_target_pairs={{0,2},{2,4},{4,6},{6,0},{1,3},{3,5},{5,7},{7,1},{8,10},{10,12},{12... | collective-permute-start | bytes 1179656 | tf_op jit(solution)/shard_map/ppermute | solution.py:38
  255.7 2.5 copy-start.8
  256.6 18.7 %collective-permute-start.29 = (f32[24,1024]{1,0:T(8,128)}, f32[24,1024]{1,0:T(8,128)}, u32[]{:S(2)}, u32[]{:S(2)}) collective-permute-start(f32[24,1024]{1,0:T(8,128)} %get-tuple-element.53), channel_id=1, source_target_pairs={{0,224},{32,0},{64,32},{96,64},{128,96},{160,128},{192,160},{224,1... | collective-permute-start | bytes 294920 | tf_op jit(solution)/shard_map/ppermute | solution.py:38
  258.2 6.6 %copy-start.14 = (bf16[1,128,1024]{1,2,0:T(8,128)(2,1)S(1)}, bf16[1,128,1024]{1,2,0:T(8,128)(2,1)}, u32[]{:S(2)}) copy-start(bf16[1,128,1024]{1,2,0:T(8,128)(2,1)} %get-tuple-element.62) | copy-start | bytes 786436
  258.2 75.3 %copy-start.15 = (f32[21,1024]{1,0:T(8,128)S(1)}, f32[21,1024]{1,0:T(8,128)}, u32[]{:S(2)}) copy-start(f32[21,1024]{1,0:T(8,128)} %param.15) | copy-start | bytes 258052
  258.2 19.0 %collective-permute-start.23 = (f32[24,1024]{1,0:T(8,128)}, f32[24,1024]{1,0:T(8,128)}, u32[]{:S(2)}, u32[]{:S(2)}) collective-permute-start(f32[24,1024]{1,0:T(8,128)} %get-tuple-element.52), channel_id=1, source_target_pairs={{0,32},{32,64},{64,96},{96,128},{128,160},{160,192},{192,224},{224... | collective-permute-start | bytes 294920 | tf_op jit(solution)/shard_map/ppermute | solution.py:38
  266.5 14.1 %collective-permute-start.28 = (f32[24,1024]{1,0:T(8,128)}, f32[24,1024]{1,0:T(8,128)S(1)}, u32[]{:S(2)}, u32[]{:S(2)}) collective-permute-start(f32[24,1024]{1,0:T(8,128)} %get-tuple-element.54), channel_id=1, source_target_pairs={{0,192},{32,224},{64,0},{96,32},{128,64},{160,96},{192,128},{224,1... | collective-permute-start | bytes 294920 | tf_op jit(solution)/shard_map/ppermute | solution.py:38
  267.7 14.8 %collective-permute-start.27 = (f32[24,1024]{1,0:T(8,128)}, f32[24,1024]{1,0:T(8,128)S(1)}, u32[]{:S(2)}, u32[]{:S(2)}) collective-permute-start(f32[24,1024]{1,0:T(8,128)} %get-tuple-element.55), channel_id=1, source_target_pairs={{0,160},{32,192},{64,224},{96,0},{128,32},{160,64},{192,96},{224,1... | collective-permute-start | bytes 294920 | tf_op jit(solution)/shard_map/ppermute | solution.py:38
  275.4 9.8 %collective-permute-start.26 = (f32[24,1024]{1,0:T(8,128)}, f32[24,1024]{1,0:T(8,128)S(1)}, u32[]{:S(2)}, u32[]{:S(2)}) collective-permute-start(f32[24,1024]{1,0:T(8,128)} %get-tuple-element.56), channel_id=1, source_target_pairs={{0,128},{32,160},{64,192},{96,224},{128,0},{160,32},{192,64},{224,... | collective-permute-start | bytes 294920 | tf_op jit(solution)/shard_map/ppermute | solution.py:38
  275.4 15.2 %collective-permute-start.25 = (f32[24,1024]{1,0:T(8,128)}, f32[24,1024]{1,0:T(8,128)S(1)}, u32[]{:S(2)}, u32[]{:S(2)}) collective-permute-start(f32[24,1024]{1,0:T(8,128)} %get-tuple-element.57), channel_id=1, source_target_pairs={{0,96},{32,128},{64,160},{96,192},{128,224},{160,0},{192,32},{224,... | collective-permute-start | bytes 294920 | tf_op jit(solution)/shard_map/ppermute | solution.py:38
  277.3 13.3 %collective-permute-start.24 = (f32[24,1024]{1,0:T(8,128)}, f32[24,1024]{1,0:T(8,128)S(1)}, u32[]{:S(2)}, u32[]{:S(2)}) collective-permute-start(f32[24,1024]{1,0:T(8,128)} %get-tuple-element.58), channel_id=1, source_target_pairs={{0,64},{32,96},{64,128},{96,160},{128,192},{160,224},{192,0},{224,... | collective-permute-start | bytes 294920 | tf_op jit(solution)/shard_map/ppermute | solution.py:38
  306.7 3.9 %collective-permute-start.30 = (f32[]{:T(128)}, f32[]{:T(128)}, u32[]{:S(2)}, u32[]{:S(2)}) collective-permute-start(f32[]{:T(128)} %psum.7), channel_id=1, source_target_pairs={{0,8},{8,16},{16,24},{24,0},{1,9},{9,17},{17,25},{25,1},{2,10},{10... | collective-permute-start | bytes 20 | tf_op jit(solution)/shard_map/ppermute | solution.py:38
  311.8 4.1 %collective-permute-start.31 = (f32[]{:T(128)}, f32[]{:T(128)}, u32[]{:S(2)}, u32[]{:S(2)}) collective-permute-start(f32[]{:T(128)} %add.459), channel_id=1, source_target_pairs={{0,16},{8,24},{16,0},{24,8},{1,17},{9,25},{17,1},{25,9},{2,18},{10... | collective-permute-start | bytes 20 | tf_op jit(solution)/shard_map/ppermute | solution.py:38
  316.6 3.8 %collective-permute-start.32 = (f32[]{:T(128)}, f32[]{:T(128)}, u32[]{:S(2)}, u32[]{:S(2)}) collective-permute-start(f32[]{:T(128)} %add.460), channel_id=1, source_target_pairs={{0,32},{32,64},{64,96},{96,128},{128,160},{160,192},{192,224},{224... | collective-permute-start | bytes 20 | tf_op jit(solution)/shard_map/ppermute | solution.py:38
  321.0 4.7 %collective-permute-start.33 = (f32[]{:T(128)}, f32[]{:T(128)}, u32[]{:S(2)}, u32[]{:S(2)}) collective-permute-start(f32[]{:T(128)} %add.461), channel_id=1, source_target_pairs={{0,64},{32,96},{64,128},{96,160},{128,192},{160,224},{192,0},{224,... | collective-permute-start | bytes 20 | tf_op jit(solution)/shard_map/ppermute | solution.py:38
  326.3 6.5 %collective-permute-start.34 = (f32[]{:T(128)}, f32[]{:T(128)}, u32[]{:S(2)}, u32[]{:S(2)}) collective-permute-start(f32[]{:T(128)} %add.462), channel_id=1, source_target_pairs={{0,128},{32,160},{64,192},{96,224},{128,0},{160,32},{192,64},{224,... | collective-permute-start | bytes 20 | tf_op jit(solution)/shard_map/ppermute | solution.py:38
  (8 other events, 12.6 us)

commit v7 on v6

--- a/solution.py
+++ b/solution.py
@@ -242,12 +242,29 @@
     square_total = lax.psum(jnp.sum(weight_grad * weight_grad), DP)
     square_total = all_sum(square_total, ("cx", "cz"))
     norm_total = jnp.sqrt(square_total + 1e-06)
-    clipped = weight_grad * jnp.minimum(1.0, clip_norm / norm_total)
-    new_first = beta_first * first_moment_value + (1.0 - beta_first) * clipped
-    new_second = beta_second * second_moment_value + (1.0 - beta_second) * clipped * clipped
-    step_dir = new_first / correct_first / (jnp.sqrt(new_second / correct_second) + adam_eps)
-    new_master = master - learn_rate * (step_dir + decay_rate * master)
-    new_weight = lax.all_gather(new_master.astype(jnp.bfloat16), DP, axis=0, tiled=True)
+
+    ndp = ny * nc
+    idp = iy * nc + icore
+
+    def dp_rows(x, axis):
+        got = [x] + [cyclic(x, DP, by) for by in range(ndp - 1, 0, -1)]
+        rolled = jnp.roll(jnp.stack(got, axis=axis), idp, axis=axis)
+        shape = x.shape[:axis] + (ndp * x.shape[axis],) + x.shape[axis + 1 :]
+        return rolled.reshape(shape)
+
+    state_all = dp_rows(jnp.stack([master, first_moment_value, second_moment_value]), 1)
+    grad_all = dp_rows(weight_grad, 0)
+    master_all, first_all, second_all = state_all[0], state_all[1], state_all[2]
+    clipped = grad_all * jnp.minimum(1.0, clip_norm / norm_total)
+    first_new = beta_first * first_all + (1.0 - beta_first) * clipped
+    second_new = beta_second * second_all + (1.0 - beta_second) * clipped * clipped
+    step_dir = first_new / correct_first / (jnp.sqrt(second_new / correct_second) + adam_eps)
+    master_new = master_all - learn_rate * (step_dir + decay_rate * master_all)
+    new_weight = master_new.astype(jnp.bfloat16)
+    mine = idp * rows
+    new_master = lax.dynamic_slice_in_dim(master_new, mine, rows, 0)
+    new_first = lax.dynamic_slice_in_dim(first_new, mine, rows, 0)
+    new_second = lax.dynamic_slice_in_dim(second_new, mine, rows, 0)
     return (
         query_gradient[None],
         key_out[None],

time: 360 us -> 368 us (1.022)
  starting transfers between devices: 67 us -> 96.8 us
  blocking collectives: 33 us -> 12.6 us
  waiting for transfers between devices: 176 us -> 157 us
  local copies, waits for them, and re-layouts: 25.6 us -> 41 us
    ppermute x31 -> x45, starting transfers between devices: 55.9 us -> 85.7 us  [cyclic(): return lax.ppermute(x, axis, [(i, (i + by) % count) for i in range(count)])]
    all_gather x1 -> x0, blocking collectives: 18.4 us -> none  [shards(): lax.all_gather(new_master.astype(jnp.bfloat16), DP, axis=0, tiled=True)]
    ppermute x4, waiting for transfers between devices: 29.9 us -> 17.1 us  [shift(): return lax.ppermute(x, axis, pairs)]
    unnamed x57 -> x106, local copies, waits for them, and re-layouts: 15.6 us -> 22.6 us
    ppermute x31 -> x45, waiting for transfers between devices: 147 us -> 140 us  [cyclic(): return lax.ppermute(x, axis, [(i, (i + by) % count) for i in range(count)])]
  transfers between devices with their start and end apart: 35 -> 49, of which waited for: 25 -> 26; matrix products, arithmetic and copies ran while one was open for 4% -> 11% of each run, Pallas kernels for 0% -> 0%
where the time goes in v7:
time: 368 us; the launch traced here: 362 us
  waiting for transfers between devices  157 us (43%)
  starting transfers between devices  96.8 us (26%)
  local copies, waits for them, and re-layouts  41 us (11%)
  other arithmetic  27.9 us (8%)
  matrix products  20.9 us (6%)
  blocking collectives  12.6 us (3%)
  between operations  5.89 us (2%)
    ppermute x45, waiting for transfers between devices, cyclic(): return lax.ppermute(x, axis, [(i, (i + by) % count) for i in range(count)])  140 us
    ppermute x45, starting transfers between devices, cyclic(): return lax.ppermute(x, axis, [(i, (i + by) % count) for i in range(count)])  85.7 us
    unnamed x106, local copies, waits for them, and re-layouts  22.6 us
    ppermute x4, waiting for transfers between devices, shift(): return lax.ppermute(x, axis, pairs)  17.1 us
    psum x1, blocking collectives, shards(): square_total = lax.psum(jnp.sum(weight_grad * weight_grad), DP)  12.6 us
    ppermute x4, starting transfers between devices, shift(): return lax.ppermute(x, axis, pairs)  11.1 us
  transfers between devices with their start and end apart: 49, of which 26 were waited for; matrix products, arithmetic and copies ran while one was open for 11% of the time, Pallas kernels for 0%

profile of v7, /device:TPU:1, one launch (start us, length us, event | category | flops | bytes accessed | tf_op | source)
XLA Modules:
  0.0 362.1 jit_solution(15160293151723458273)
XLA Ops:
  3.6 4.4 %collective-permute-start = (bf16[128,2176]{0,1:T(8,128)(2,1)S(1)}, bf16[128,2176]{0,1:T(8,128)(2,1)S(1)}, u32[]{:S(2)}, u32[]{:S(2)}) collective-permute-start(bf16[128,2176]{0,1:T(8,128)(2,1)S(1)} %pad_maximum_fusion.4), channel_id=1, source_target_pairs={{0,32},{32,64},{64,96},{96,128},{128,160},{160,192},{192,224},{1,3... | collective-permute-start | bytes 1671176 | tf_op jit(solution)/shard_map/ppermute | solution.py:113
  10.9 8.4 %collective-permute-done = bf16[128,2176]{0,1:T(8,128)(2,1)S(1)} collective-permute-done((bf16[128,2176]{0,1:T(8,128)(2,1)S(1)}, bf16[128,2176]{0,1:T(8,128)(2,1)S(1)}, u32[]{:S(2)}, u32[]{:S(2)}) %collective-permute-start) | collective-permute-done | bytes 557088 | tf_op jit(solution)/shard_map/ppermute | solution.py:113
  19.3 4.1 %collective-permute-start.1 = (bf16[128,2176]{0,1:T(8,128)(2,1)S(1)}, bf16[128,2176]{0,1:T(8,128)(2,1)S(1)}, u32[]{:S(2)}, u32[]{:S(2)}) collective-permute-start(bf16[128,2176]{0,1:T(8,128)(2,1)S(1)} %collective-permute-done), channel_id=1, source_target_pairs={{0,32},{32,64},{64,96},{96,128},{128,160},{160,192},{192,224},{1,3... | collective-permute-start | bytes 1671176 | tf_op jit(solution)/shard_map/ppermute | solution.py:113
  24.8 2.5 collective-permute-start.3
  28.4 5.4 %collective-permute-done.1 = bf16[128,2176]{0,1:T(8,128)(2,1)S(1)} collective-permute-done((bf16[128,2176]{0,1:T(8,128)(2,1)S(1)}, bf16[128,2176]{0,1:T(8,128)(2,1)S(1)}, u32[]{:S(2)}, u32[]{:S(2)}) %collective-permute-start.1) | collective-permute-done | bytes 557088 | tf_op jit(solution)/shard_map/ppermute | solution.py:113
  35.4 2.5 collective-permute-start.6
  39.7 10.4 %collective-permute-done.3 = bf16[128,2176]{0,1:T(8,128)(2,1)S(1)} collective-permute-done((bf16[128,2176]{0,1:T(8,128)(2,1)S(1)}, bf16[128,2176]{0,1:T(8,128)(2,1)S(1)}, u32[]{:S(2)}, u32[]{:S(2)}) %collective-permute-start.3) | collective-permute-done | bytes 557088 | tf_op jit(solution)/shard_map/ppermute | solution.py:38
  50.3 2.5 collective-permute-done.4
  52.9 9.2 %collective-permute-done.5 = bf16[128,2176]{0,1:T(8,128)(2,1)S(1)} collective-permute-done((bf16[128,2176]{0,1:T(8,128)(2,1)S(1)}, bf16[128,2176]{0,1:T(8,128)(2,1)S(1)}, u32[]{:S(2)}, u32[]{:S(2)}) %collective-permute-start.5) | collective-permute-done | bytes 557088 | tf_op jit(solution)/shard_map/ppermute | solution.py:38
  62.2 11.8 %collective-permute-done.6 = bf16[128,2176]{0,1:T(8,128)(2,1)S(1)} collective-permute-done((bf16[128,2176]{0,1:T(8,128)(2,1)S(1)}, bf16[128,2176]{0,1:T(8,128)(2,1)S(1)}, u32[]{:S(2)}, u32[]{:S(2)}) %collective-permute-start.6) | collective-permute-done | bytes 557088 | tf_op jit(solution)/shard_map/ppermute | solution.py:38
  77.7 6.3 %fusion.57 = (f32[8,2,128]{2,1,0:T(2,128)}, f32[8,2,128,1152]{2,3,1,0:T(8,128)}) fusion(pred[128,1152]{0,1:T(8,128)(4,1)S(1)} %fusion.45, bf16[1152,8,128,1]{0,2,3,1:T(8,128)(2,1)S(1)} %bitcast.183, bf16[128,8,2,128]{0,3,2,1:T(8,128)(2,1)S(1)} %bitcast.197), kind=kOutput, calls=%fused_computation.173 | convolution fusion | flops 613418112 | bytes 12476416 | tf_op jit(solution)/shard_map/sub | solution.py:75
  84.1 4.8 %fusion.8 = bf16[8,2,128,1152]{2,3,1,0:T(8,128)(2,1)S(1)} fusion(f32[8,2,128,1152]{2,3,1,0:T(8,128)} %get-tuple-element.63, f32[8,2,128]{2,1,0:T(2,128)} %get-tuple-element.62), kind=kLoop, calls=%fused_computation.16 | loop fusion | flops 4718592 | bytes 14163968 | tf_op jit(solution)/shard_map/convert_element_type | solution.py:77
  91.7 5.2 %fusion.3 = bf16[8,2,128,1152]{2,3,1,0:T(8,128)(2,1)S(1)} fusion(bf16[1152,8,128,1]{0,2,3,1:T(8,128)(2,1)S(1)} %bitcast.186, bf16[128,8,2,128]{0,3,2,1:T(8,128)(2,1)S(1)} %bitcast.189, f32[8,2,128]{2,1,0:T(2,128)S(1)} %bitcast.212, f32[8,2,128,1152]{2,3,1,0:T(8,128)} %get-tuple-element.63, f32[8,2,128]{2,1,0:T(2,128)S(1)} %copy-done.27), kind=kOutput, calls=%fused_computation.7 | convolution fusion | flops 613416960 | bytes 17055744 | tf_op jit(solution)/shard_map/tgrd,egd->grte/dot_general | solution.py:82
  99.1 2.9 fusion.1
  102.7 3.1 fusion.55
  105.9 3.4 collective-permute-start.8
  109.9 2.5 collective-permute-start.13
  113.7 28.7 %collective-permute-done.8 = bf16[128,2048]{0,1:T(8,128)(2,1)S(1)} collective-permute-done((bf16[128,2048]{0,1:T(8,128)(2,1)S(1)}, bf16[128,2048]{0,1:T(8,128)(2,1)S(1)}, u32[]{:S(2)}, u32[]{:S(2)}) %collective-permute-start.8) | collective-permute-done | bytes 524320 | tf_op jit(solution)/shard_map/ppermute | solution.py:38
  142.4 3.6 collective-permute-start.11
  146.0 2.6 fusion.31
  156.2 2.8 collective-permute-start.17
  159.0 2.6 collective-permute-start.18
  163.0 5.1 %collective-permute-start.20 = (f32[3,21,1024]{2,1,0:T(8,128)}, f32[3,21,1024]{2,1,0:T(8,128)S(1)}, u32[]{:S(2)}, u32[]{:S(2)}) collective-permute-start(f32[3,21,1024]{2,1,0:T(8,128)} %pad_maximum_fusion.5), channel_id=1, source_target_pairs={{0,3},{1,4},{2,5},{3,6},{4,7},{5,0},{6,1},{7,2},{8,11},{9,12},{10,... | collective-permute-start | bytes 774152 | tf_op jit(solution)/shard_map/ppermute | solution.py:38
  172.9 9.0 %collective-permute-done.18 = f32[3,21,1024]{2,1,0:T(8,128)S(1)} collective-permute-done((f32[3,21,1024]{2,1,0:T(8,128)}, f32[3,21,1024]{2,1,0:T(8,128)S(1)}, u32[]{:S(2)}, u32[]{:S(2)}) %collective-permute-start.18) | collective-permute-done | bytes 258080 | tf_op jit(solution)/shard_map/ppermute | solution.py:38
  182.0 2.2 collective-permute-done.15
  188.7 14.7 %collective-permute-done.25 = bf16[128,2560]{0,1:T(8,128)(2,1)S(1)} collective-permute-done((bf16[128,2560]{0,1:T(8,128)(2,1)S(1)}, bf16[128,2560]{0,1:T(8,128)(2,1)S(1)}, u32[]{:S(2)}, u32[]{:S(2)}) %collective-permute-start.25) | collective-permute-done | bytes 655392 | tf_op jit(solution)/shard_map/ppermute | solution.py:38
  205.3 12.7 %collective-permute-done.23 = bf16[128,2560]{0,1:T(8,128)(2,1)S(1)} collective-permute-done((bf16[128,2560]{0,1:T(8,128)(2,1)S(1)}, bf16[128,2560]{0,1:T(8,128)(2,1)S(1)}, u32[]{:S(2)}, u32[]{:S(2)}) %collective-permute-start.23) | collective-permute-done | bytes 655392 | tf_op jit(solution)/shard_map/ppermute | solution.py:38
  226.0 4.0 %collective-permute-start.29 = (bf16[8,24,1024]{2,1,0:T(8,128)(2,1)}, bf16[8,24,1024]{2,1,0:T(8,128)(2,1)}, u32[]{:S(2)}, u32[]{:S(2)}) collective-permute-start(bf16[8,24,1024]{2,1,0:T(8,128)(2,1)} %get-tuple-element.39), channel_id=1, source_target_pairs={{0,6},{2,0},{4,2},{6,4},{1,7},{3,1},{5,3},{7,5},{8,14},{10,8},{12,... | collective-permute-start | bytes 1179656 | tf_op jit(solution)/shard_map/ppermute | solution.py:38
  232.3 2.2 squeeze.56
  237.6 9.1 %collective-permute-done.29 = bf16[8,24,1024]{2,1,0:T(8,128)(2,1)} collective-permute-done((bf16[8,24,1024]{2,1,0:T(8,128)(2,1)}, bf16[8,24,1024]{2,1,0:T(8,128)(2,1)}, u32[]{:S(2)}, u32[]{:S(2)}) %collective-permute-start.29) | collective-permute-done | bytes 393248 | tf_op jit(solution)/shard_map/ppermute | solution.py:38
  246.7 4.0 %collective-permute-done.27 = bf16[8,24,1024]{2,1,0:T(8,128)(2,1)} collective-permute-done((bf16[8,24,1024]{2,1,0:T(8,128)(2,1)}, bf16[8,24,1024]{2,1,0:T(8,128)(2,1)}, u32[]{:S(2)}, u32[]{:S(2)}) %collective-permute-start.27) | collective-permute-done | bytes 393248 | tf_op jit(solution)/shard_map/ppermute | solution.py:38
  253.4 2.7 collective-permute-start.36
  257.0 3.4 fusion.19
  263.1 2.5 collective-permute-start.35
  265.6 7.9 %collective-permute-start.34 = (f32[24,1024]{1,0:T(8,128)}, f32[24,1024]{1,0:T(8,128)S(1)}, u32[]{:S(2)}, u32[]{:S(2)}) collective-permute-start(f32[24,1024]{1,0:T(8,128)} %get-tuple-element.51), channel_id=1, source_target_pairs={{0,160},{32,192},{64,224},{96,0},{128,32},{160,64},{192,96},{224,1... | collective-permute-start | bytes 294920 | tf_op jit(solution)/shard_map/ppermute | solution.py:38
  275.5 2.2 collective-permute-start.31
  280.9 2.5 collective-permute-done.33
  283.3 5.4 %collective-permute-done.32 = f32[24,1024]{1,0:T(8,128)S(1)} collective-permute-done((f32[24,1024]{1,0:T(8,128)}, f32[24,1024]{1,0:T(8,128)S(1)}, u32[]{:S(2)}, u32[]{:S(2)}) %collective-permute-start.32) | collective-permute-done | bytes 98336 | tf_op jit(solution)/shard_map/ppermute | solution.py:38
  294.0 2.6 collective-permute-start.40
  296.6 12.6 %psum.7 = f32[]{:T(128)} all-reduce(f32[]{:T(128)} %get-tuple-element.25), channel_id=1, replica_groups=mesh['cz'=8,'cx'=4,'y'=4,'core'=2] {'y','core'}, use_global_device_ids=true, to_apply=%region_4.5 | all-reduce | flops 1 | bytes 8 | tf_op jit(solution)/shard_map/psum | solution.py:242
  309.3 3.7 %collective-permute-done.44 = f32[]{:T(128)} collective-permute-done((f32[]{:T(128)}, f32[]{:T(128)}, u32[]{:S(2)}, u32[]{:S(2)}) %collective-permute-start.44) | collective-permute-done | bytes 36 | tf_op jit(solution)/shard_map/ppermute | solution.py:38
  315.1 3.1 collective-permute-done.45
  318.9 3.7 %collective-permute-start.46 = (f32[]{:T(128)}, f32[]{:T(128)}, u32[]{:S(2)}, u32[]{:S(2)}) collective-permute-start(f32[]{:T(128)} %add.485), channel_id=1, source_target_pairs={{0,32},{32,64},{64,96},{96,128},{128,160},{160,192},{192,224},{224... | collective-permute-start | bytes 20 | tf_op jit(solution)/shard_map/ppermute | solution.py:38
  325.4 2.5 collective-permute-done.47
  328.5 5.4 %collective-permute-start.48 = (f32[]{:T(128)}, f32[]{:T(128)}, u32[]{:S(2)}, u32[]{:S(2)}) collective-permute-start(f32[]{:T(128)} %add.487), channel_id=1, source_target_pairs={{0,128},{32,160},{64,192},{96,224},{128,0},{160,32},{192,64},{224,... | collective-permute-start | bytes 20 | tf_op jit(solution)/shard_map/ppermute | solution.py:38
  334.9 7.7 %collective-permute-start.41 = (f32[21,1024]{1,0:T(8,128)S(1)}, f32[21,1024]{1,0:T(8,128)S(1)}, u32[]{:S(2)}, u32[]{:S(2)}) collective-permute-start(f32[21,1024]{1,0:T(8,128)S(1)} %get-tuple-element.26), channel_id=1, source_target_pairs={{0,3},{1,4},{2,5},{3,6},{4,7},{5,0},{6,1},{7,2},{8,11},{9,12},{10,... | collective-permute-start | bytes 258056 | tf_op jit(solution)/shard_map/ppermute | solution.py:38
  346.6 3.1 collective-permute-done.42
  357.5 2.3 fusion.52
  (223 shorter events, 90.0 us)
Async XLA Ops:
  3.6 15.7 %collective-permute-start = (bf16[128,2176]{0,1:T(8,128)(2,1)S(1)}, bf16[128,2176]{0,1:T(8,128)(2,1)S(1)}, u32[]{:S(2)}, u32[]{:S(2)}) collective-permute-start(bf16[128,2176]{0,1:T(8,128)(2,1)S(1)} %pad_maximum_fusion.4), channel_id=1, source_target_pairs={{0,32},{32,64},{64,96},{96,128},{128,160},{160,192},{192,224},{1,3... | collective-permute-start | bytes 1671176 | tf_op jit(solution)/shard_map/ppermute | solution.py:113
  19.3 14.5 %collective-permute-start.1 = (bf16[128,2176]{0,1:T(8,128)(2,1)S(1)}, bf16[128,2176]{0,1:T(8,128)(2,1)S(1)}, u32[]{:S(2)}, u32[]{:S(2)}) collective-permute-start(bf16[128,2176]{0,1:T(8,128)(2,1)S(1)} %collective-permute-done), channel_id=1, source_target_pairs={{0,32},{32,64},{64,96},{96,128},{128,160},{160,192},{192,224},{1,3... | collective-permute-start | bytes 1671176 | tf_op jit(solution)/shard_map/ppermute | solution.py:113
  23.5 14.7 %collective-permute-start.2 = (bf16[128,2176]{0,1:T(8,128)(2,1)S(1)}, bf16[128,2176]{0,1:T(8,128)(2,1)S(1)}, u32[]{:S(2)}, u32[]{:S(2)}) collective-permute-start(bf16[128,2176]{0,1:T(8,128)(2,1)S(1)} %collective-permute-done), channel_id=1, source_target_pairs={{0,8},{8,16},{16,24},{24,0},{1,9},{9,17},{17,25},{25,1},{2,10},{10... | collective-permute-start | bytes 1671176 | tf_op jit(solution)/shard_map/ppermute | solution.py:38
  24.8 25.3 %collective-permute-start.3 = (bf16[128,2176]{0,1:T(8,128)(2,1)S(1)}, bf16[128,2176]{0,1:T(8,128)(2,1)S(1)}, u32[]{:S(2)}, u32[]{:S(2)}) collective-permute-start(bf16[128,2176]{0,1:T(8,128)(2,1)S(1)} %collective-permute-done), channel_id=1, source_target_pairs={{0,16},{8,24},{16,0},{24,8},{1,17},{9,25},{17,1},{25,9},{2,18},{10... | collective-permute-start | bytes 1671176 | tf_op jit(solution)/shard_map/ppermute | solution.py:38
  27.2 25.5 %collective-permute-start.4 = (bf16[128,2176]{0,1:T(8,128)(2,1)S(1)}, bf16[128,2176]{0,1:T(8,128)(2,1)S(1)}, u32[]{:S(2)}, u32[]{:S(2)}) collective-permute-start(bf16[128,2176]{0,1:T(8,128)(2,1)S(1)} %collective-permute-done), channel_id=1, source_target_pairs={{0,24},{8,0},{16,8},{24,16},{1,25},{9,1},{17,9},{25,17},{2,26},{10... | collective-permute-start | bytes 1671176 | tf_op jit(solution)/shard_map/ppermute | solution.py:38
  34.2 27.9 %collective-permute-start.5 = (bf16[128,2176]{0,1:T(8,128)(2,1)S(1)}, bf16[128,2176]{0,1:T(8,128)(2,1)S(1)}, u32[]{:S(2)}, u32[]{:S(2)}) collective-permute-start(bf16[128,2176]{0,1:T(8,128)(2,1)S(1)} %get-tuple-element.47), channel_id=1, source_target_pairs={{0,8},{8,16},{16,24},{24,0},{1,9},{9,17},{17,25},{25,1},{2,10},{10... | collective-permute-start | bytes 1671176 | tf_op jit(solution)/shard_map/ppermute | solution.py:38
  35.4 38.5 %collective-permute-start.6 = (bf16[128,2176]{0,1:T(8,128)(2,1)S(1)}, bf16[128,2176]{0,1:T(8,128)(2,1)S(1)}, u32[]{:S(2)}, u32[]{:S(2)}) collective-permute-start(bf16[128,2176]{0,1:T(8,128)(2,1)S(1)} %get-tuple-element.46), channel_id=1, source_target_pairs={{0,16},{8,24},{16,0},{24,8},{1,17},{9,25},{17,1},{25,9},{2,18},{10... | collective-permute-start | bytes 1671176 | tf_op jit(solution)/shard_map/ppermute | solution.py:38
  38.2 36.5 %collective-permute-start.7 = (bf16[128,2176]{0,1:T(8,128)(2,1)S(1)}, bf16[128,2176]{0,1:T(8,128)(2,1)S(1)}, u32[]{:S(2)}, u32[]{:S(2)}) collective-permute-start(bf16[128,2176]{0,1:T(8,128)(2,1)S(1)} %get-tuple-element.45), channel_id=1, source_target_pairs={{0,24},{8,0},{16,8},{24,16},{1,25},{9,1},{17,9},{25,17},{2,26},{10... | collective-permute-start | bytes 1671176 | tf_op jit(solution)/shard_map/ppermute | solution.py:38
  105.9 36.5 %collective-permute-start.8 = (bf16[128,2048]{0,1:T(8,128)(2,1)S(1)}, bf16[128,2048]{0,1:T(8,128)(2,1)S(1)}, u32[]{:S(2)}, u32[]{:S(2)}) collective-permute-start(bf16[128,2048]{0,1:T(8,128)(2,1)S(1)} %get-tuple-element.37), channel_id=1, source_target_pairs={{0,24},{8,0},{16,8},{24,16},{1,25},{9,1},{17,9},{25,17},{2,26},{10... | collective-permute-start | bytes 1572872 | tf_op jit(solution)/shard_map/ppermute | solution.py:38
  109.3 36.7 %collective-permute-start.9 = (bf16[128,2048]{0,1:T(8,128)(2,1)S(1)}, bf16[128,2048]{0,1:T(8,128)(2,1)S(1)}, u32[]{:S(2)}, u32[]{:S(2)}) collective-permute-start(bf16[128,2048]{0,1:T(8,128)(2,1)S(1)} %get-tuple-element.36), channel_id=1, source_target_pairs={{0,16},{8,24},{16,0},{24,8},{1,17},{9,25},{17,1},{25,9},{2,18},{10... | collective-permute-start | bytes 1572872 | tf_op jit(solution)/shard_map/ppermute | solution.py:38
  109.5 36.5 %collective-permute-start.10 = (bf16[128,2048]{0,1:T(8,128)(2,1)S(1)}, bf16[128,2048]{0,1:T(8,128)(2,1)S(1)}, u32[]{:S(2)}, u32[]{:S(2)}) collective-permute-start(bf16[128,2048]{0,1:T(8,128)(2,1)S(1)} %get-tuple-element.35), channel_id=1, source_target_pairs={{0,8},{8,16},{16,24},{24,0},{1,9},{9,17},{17,25},{25,1},{2,10},{10... | collective-permute-start | bytes 1572872 | tf_op jit(solution)/shard_map/ppermute | solution.py:38
  109.9 46.3 %collective-permute-start.13 = (bf16[128,2048]{0,1:T(8,128)(2,1)}, bf16[128,2048]{0,1:T(8,128)(2,1)}, u32[]{:S(2)}, u32[]{:S(2)}) collective-permute-start(bf16[128,2048]{0,1:T(8,128)(2,1)} %get-tuple-element.33), channel_id=1, source_target_pairs={{0,8},{8,16},{16,24},{24,0},{1,9},{9,17},{17,25},{25,1},{2,10},{10... | collective-permute-start | bytes 1572872 | tf_op jit(solution)/shard_map/ppermute | solution.py:38
  112.3 46.7 %collective-permute-start.12 = (bf16[128,2048]{0,1:T(8,128)(2,1)}, bf16[128,2048]{0,1:T(8,128)(2,1)}, u32[]{:S(2)}, u32[]{:S(2)}) collective-permute-start(bf16[128,2048]{0,1:T(8,128)(2,1)} %get-tuple-element.34), channel_id=1, source_target_pairs={{0,16},{8,24},{16,0},{24,8},{1,17},{9,25},{17,1},{25,9},{2,18},{10... | collective-permute-start | bytes 1572872 | tf_op jit(solution)/shard_map/ppermute | solution.py:38
  142.4 19.2 %collective-permute-start.11 = (bf16[128,2048]{0,1:T(8,128)(2,1)}, bf16[128,2048]{0,1:T(8,128)(2,1)}, u32[]{:S(2)}, u32[]{:S(2)}) collective-permute-start(bf16[128,2048]{0,1:T(8,128)(2,1)} %get-tuple-element.32), channel_id=1, source_target_pairs={{0,24},{8,0},{16,8},{24,16},{1,25},{9,1},{17,9},{25,17},{2,26},{10... | collective-permute-start | bytes 1572872 | tf_op jit(solution)/shard_map/ppermute | solution.py:38
  148.6 14.4 %collective-permute-start.14 = (bf16[128,2048]{0,1:T(8,128)(2,1)}, bf16[128,2048]{0,1:T(8,128)(2,1)}, u32[]{:S(2)}, u32[]{:S(2)}) collective-permute-start(bf16[128,2048]{0,1:T(8,128)(2,1)} %fusion.31), channel_id=1, source_target_pairs={{32,0},{64,32},{96,64},{128,96},{160,128},{192,160},{224,192},{33,... | collective-permute-start | bytes 1572872 | tf_op jit(solution)/shard_map/ppermute | solution.py:113
  150.7 19.5 %collective-permute-start.16 = (f32[3,21,1024]{2,1,0:T(8,128)}, f32[3,21,1024]{2,1,0:T(8,128)}, u32[]{:S(2)}, u32[]{:S(2)}) collective-permute-start(f32[3,21,1024]{2,1,0:T(8,128)} %pad_maximum_fusion.5), channel_id=1, source_target_pairs={{0,7},{1,0},{2,1},{3,2},{4,3},{5,4},{6,5},{7,6},{8,15},{9,8},{10,9... | collective-permute-start | bytes 774152 | tf_op jit(solution)/shard_map/ppermute | solution.py:38
  156.2 16.2 %collective-permute-start.17 = (f32[3,21,1024]{2,1,0:T(8,128)}, f32[3,21,1024]{2,1,0:T(8,128)S(1)}, u32[]{:S(2)}, u32[]{:S(2)}) collective-permute-start(f32[3,21,1024]{2,1,0:T(8,128)} %pad_maximum_fusion.5), channel_id=1, source_target_pairs={{0,6},{1,7},{2,0},{3,1},{4,2},{5,3},{6,4},{7,5},{8,14},{9,15},{10,... | collective-permute-start | bytes 774152 | tf_op jit(solution)/shard_map/ppermute | solution.py:38
  159.0 22.9 %collective-permute-start.18 = (f32[3,21,1024]{2,1,0:T(8,128)}, f32[3,21,1024]{2,1,0:T(8,128)S(1)}, u32[]{:S(2)}, u32[]{:S(2)}) collective-permute-start(f32[3,21,1024]{2,1,0:T(8,128)} %pad_maximum_fusion.5), channel_id=1, source_target_pairs={{0,5},{1,6},{2,7},{3,0},{4,1},{5,2},{6,3},{7,4},{8,13},{9,14},{10,... | collective-permute-start | bytes 774152 | tf_op jit(solution)/shard_map/ppermute | solution.py:38
  161.6 25.7 %collective-permute-start.19 = (f32[3,21,1024]{2,1,0:T(8,128)}, f32[3,21,1024]{2,1,0:T(8,128)S(1)}, u32[]{:S(2)}, u32[]{:S(2)}) collective-permute-start(f32[3,21,1024]{2,1,0:T(8,128)} %pad_maximum_fusion.5), channel_id=1, source_target_pairs={{0,4},{1,5},{2,6},{3,7},{4,0},{5,1},{6,2},{7,3},{8,12},{9,13},{10,... | collective-permute-start | bytes 774152 | tf_op jit(solution)/shard_map/ppermute | solution.py:38
  163.0 25.2 %collective-permute-start.20 = (f32[3,21,1024]{2,1,0:T(8,128)}, f32[3,21,1024]{2,1,0:T(8,128)S(1)}, u32[]{:S(2)}, u32[]{:S(2)}) collective-permute-start(f32[3,21,1024]{2,1,0:T(8,128)} %pad_maximum_fusion.5), channel_id=1, source_target_pairs={{0,3},{1,4},{2,5},{3,6},{4,7},{5,0},{6,1},{7,2},{8,11},{9,12},{10,... | collective-permute-start | bytes 774152 | tf_op jit(solution)/shard_map/ppermute | solution.py:38
  170.1 14.1 %collective-permute-start.15 = (bf16[128,2048]{0,1:T(8,128)(2,1)S(1)}, bf16[128,2048]{0,1:T(8,128)(2,1)S(1)}, u32[]{:S(2)}, u32[]{:S(2)}) collective-permute-start(bf16[128,2048]{0,1:T(8,128)(2,1)S(1)} %add_convert_fusion), channel_id=1, source_target_pairs={{32,0},{64,32},{96,64},{128,96},{160,128},{192,160},{224,192},{33,... | collective-permute-start | bytes 1572872 | tf_op jit(solution)/shard_map/ppermute | solution.py:113
  172.4 16.3 %collective-permute-start.21 = (f32[3,21,1024]{2,1,0:T(8,128)}, f32[3,21,1024]{2,1,0:T(8,128)S(1)}, u32[]{:S(2)}, u32[]{:S(2)}) collective-permute-start(f32[3,21,1024]{2,1,0:T(8,128)} %pad_maximum_fusion.5), channel_id=1, source_target_pairs={{0,2},{1,3},{2,4},{3,5},{4,6},{5,7},{6,0},{7,1},{8,10},{9,11},{10,... | collective-permute-start | bytes 774152 | tf_op jit(solution)/shard_map/ppermute | solution.py:38
  186.6 16.8 %collective-permute-start.25 = (bf16[128,2560]{0,1:T(8,128)(2,1)S(1)}, bf16[128,2560]{0,1:T(8,128)(2,1)S(1)}, u32[]{:S(2)}, u32[]{:S(2)}) collective-permute-start(bf16[128,2560]{0,1:T(8,128)(2,1)S(1)} %get-tuple-element.60), channel_id=1, source_target_pairs={{0,24},{8,0},{16,8},{24,16},{1,25},{9,1},{17,9},{25,17},{2,26},{10... | collective-permute-start | bytes 1966088 | tf_op jit(solution)/shard_map/ppermute | solution.py:38
  187.3 18.0 %collective-permute-start.24 = (bf16[128,2560]{0,1:T(8,128)(2,1)S(1)}, bf16[128,2560]{0,1:T(8,128)(2,1)S(1)}, u32[]{:S(2)}, u32[]{:S(2)}) collective-permute-start(bf16[128,2560]{0,1:T(8,128)(2,1)S(1)} %get-tuple-element.61), channel_id=1, source_target_pairs={{0,16},{8,24},{16,0},{24,8},{1,17},{9,25},{17,1},{25,9},{2,18},{10... | collective-permute-start | bytes 1966088 | tf_op jit(solution)/shard_map/ppermute | solution.py:38
  187.3 30.7 %collective-permute-start.23 = (bf16[128,2560]{0,1:T(8,128)(2,1)S(1)}, bf16[128,2560]{0,1:T(8,128)(2,1)S(1)}, u32[]{:S(2)}, u32[]{:S(2)}) collective-permute-start(bf16[128,2560]{0,1:T(8,128)(2,1)S(1)} %get-tuple-element.59), channel_id=1, source_target_pairs={{0,8},{8,16},{16,24},{24,0},{1,9},{9,17},{17,25},{25,1},{2,10},{10... | collective-permute-start | bytes 1966088 | tf_op jit(solution)/shard_map/ppermute | solution.py:38
  188.2 32.7 %collective-permute-start.22 = (f32[3,21,1024]{2,1,0:T(8,128)}, f32[3,21,1024]{2,1,0:T(8,128)S(1)}, u32[]{:S(2)}, u32[]{:S(2)}) collective-permute-start(f32[3,21,1024]{2,1,0:T(8,128)} %pad_maximum_fusion.5), channel_id=1, source_target_pairs={{0,1},{1,2},{2,3},{3,4},{4,5},{5,6},{6,7},{7,0},{8,9},{9,10},{10,1... | collective-permute-start | bytes 774152 | tf_op jit(solution)/shard_map/ppermute | solution.py:38
  226.0 20.7 %collective-permute-start.29 = (bf16[8,24,1024]{2,1,0:T(8,128)(2,1)}, bf16[8,24,1024]{2,1,0:T(8,128)(2,1)}, u32[]{:S(2)}, u32[]{:S(2)}) collective-permute-start(bf16[8,24,1024]{2,1,0:T(8,128)(2,1)} %get-tuple-element.39), channel_id=1, source_target_pairs={{0,6},{2,0},{4,2},{6,4},{1,7},{3,1},{5,3},{7,5},{8,14},{10,8},{12,... | collective-permute-start | bytes 1179656 | tf_op jit(solution)/shard_map/ppermute | solution.py:38
  230.0 16.7 %collective-permute-start.28 = (bf16[8,24,1024]{2,1,0:T(8,128)(2,1)}, bf16[8,24,1024]{2,1,0:T(8,128)(2,1)}, u32[]{:S(2)}, u32[]{:S(2)}) collective-permute-start(bf16[8,24,1024]{2,1,0:T(8,128)(2,1)} %get-tuple-element.40), channel_id=1, source_target_pairs={{0,4},{2,6},{4,0},{6,2},{1,5},{3,7},{5,1},{7,3},{8,12},{10,14},{12... | collective-permute-start | bytes 1179656 | tf_op jit(solution)/shard_map/ppermute | solution.py:38
  230.0 20.7 %collective-permute-start.27 = (bf16[8,24,1024]{2,1,0:T(8,128)(2,1)}, bf16[8,24,1024]{2,1,0:T(8,128)(2,1)}, u32[]{:S(2)}, u32[]{:S(2)}) collective-permute-start(bf16[8,24,1024]{2,1,0:T(8,128)(2,1)} %get-tuple-element.38), channel_id=1, source_target_pairs={{0,2},{2,4},{4,6},{6,0},{1,3},{3,5},{5,7},{7,1},{8,10},{10,12},{12... | collective-permute-start | bytes 1179656 | tf_op jit(solution)/shard_map/ppermute | solution.py:38
  253.4 20.2 %collective-permute-start.36 = (f32[24,1024]{1,0:T(8,128)}, f32[24,1024]{1,0:T(8,128)}, u32[]{:S(2)}, u32[]{:S(2)}) collective-permute-start(f32[24,1024]{1,0:T(8,128)} %get-tuple-element.49), channel_id=1, source_target_pairs={{0,224},{32,0},{64,32},{96,64},{128,96},{160,128},{192,160},{224,1... | collective-permute-start | bytes 294920 | tf_op jit(solution)/shard_map/ppermute | solution.py:38
  256.1 19.4 %collective-permute-start.30 = (f32[24,1024]{1,0:T(8,128)}, f32[24,1024]{1,0:T(8,128)}, u32[]{:S(2)}, u32[]{:S(2)}) collective-permute-start(f32[24,1024]{1,0:T(8,128)} %get-tuple-element.48), channel_id=1, source_target_pairs={{0,32},{32,64},{64,96},{96,128},{128,160},{160,192},{192,224},{224... | collective-permute-start | bytes 294920 | tf_op jit(solution)/shard_map/ppermute | solution.py:38
  263.1 15.6 %collective-permute-start.35 = (f32[24,1024]{1,0:T(8,128)}, f32[24,1024]{1,0:T(8,128)S(1)}, u32[]{:S(2)}, u32[]{:S(2)}) collective-permute-start(f32[24,1024]{1,0:T(8,128)} %get-tuple-element.50), channel_id=1, source_target_pairs={{0,192},{32,224},{64,0},{96,32},{128,64},{160,96},{192,128},{224,1... | collective-permute-start | bytes 294920 | tf_op jit(solution)/shard_map/ppermute | solution.py:38
  265.6 15.3 %collective-permute-start.34 = (f32[24,1024]{1,0:T(8,128)}, f32[24,1024]{1,0:T(8,128)S(1)}, u32[]{:S(2)}, u32[]{:S(2)}) collective-permute-start(f32[24,1024]{1,0:T(8,128)} %get-tuple-element.51), channel_id=1, source_target_pairs={{0,160},{32,192},{64,224},{96,0},{128,32},{160,64},{192,96},{224,1... | collective-permute-start | bytes 294920 | tf_op jit(solution)/shard_map/ppermute | solution.py:38
  273.5 9.8 %collective-permute-start.33 = (f32[24,1024]{1,0:T(8,128)}, f32[24,1024]{1,0:T(8,128)S(1)}, u32[]{:S(2)}, u32[]{:S(2)}) collective-permute-start(f32[24,1024]{1,0:T(8,128)} %get-tuple-element.52), channel_id=1, source_target_pairs={{0,128},{32,160},{64,192},{96,224},{128,0},{160,32},{192,64},{224,... | collective-permute-start | bytes 294920 | tf_op jit(solution)/shard_map/ppermute | solution.py:38
  273.5 15.2 %collective-permute-start.32 = (f32[24,1024]{1,0:T(8,128)}, f32[24,1024]{1,0:T(8,128)S(1)}, u32[]{:S(2)}, u32[]{:S(2)}) collective-permute-start(f32[24,1024]{1,0:T(8,128)} %get-tuple-element.53), channel_id=1, source_target_pairs={{0,96},{32,128},{64,160},{96,192},{128,224},{160,0},{192,32},{224,... | collective-permute-start | bytes 294920 | tf_op jit(solution)/shard_map/ppermute | solution.py:38
  275.5 13.2 %collective-permute-start.31 = (f32[24,1024]{1,0:T(8,128)S(1)}, f32[24,1024]{1,0:T(8,128)S(1)}, u32[]{:S(2)}, u32[]{:S(2)}) collective-permute-start(f32[24,1024]{1,0:T(8,128)S(1)} %get-tuple-element.54), channel_id=1, source_target_pairs={{0,64},{32,96},{64,128},{96,160},{128,192},{160,224},{192,0},{224,... | collective-permute-start | bytes 294920 | tf_op jit(solution)/shard_map/ppermute | solution.py:38
  290.3 53.0 %collective-permute-start.37 = (f32[21,1024]{1,0:T(8,128)S(1)}, f32[21,1024]{1,0:T(8,128)S(1)}, u32[]{:S(2)}, u32[]{:S(2)}) collective-permute-start(f32[21,1024]{1,0:T(8,128)S(1)} %get-tuple-element.26), channel_id=1, source_target_pairs={{0,7},{1,0},{2,1},{3,2},{4,3},{5,4},{6,5},{7,6},{8,15},{9,8},{10,9... | collective-permute-start | bytes 258056 | tf_op jit(solution)/shard_map/ppermute | solution.py:38
  293.0 51.0 %collective-permute-start.38 = (f32[21,1024]{1,0:T(8,128)S(1)}, f32[21,1024]{1,0:T(8,128)S(1)}, u32[]{:S(2)}, u32[]{:S(2)}) collective-permute-start(f32[21,1024]{1,0:T(8,128)S(1)} %get-tuple-element.26), channel_id=1, source_target_pairs={{0,6},{1,7},{2,0},{3,1},{4,2},{5,3},{6,4},{7,5},{8,14},{9,15},{10,... | collective-permute-start | bytes 258056 | tf_op jit(solution)/shard_map/ppermute | solution.py:38
  293.0 51.6 %collective-permute-start.39 = (f32[21,1024]{1,0:T(8,128)S(1)}, f32[21,1024]{1,0:T(8,128)S(1)}, u32[]{:S(2)}, u32[]{:S(2)}) collective-permute-start(f32[21,1024]{1,0:T(8,128)S(1)} %get-tuple-element.26), channel_id=1, source_target_pairs={{0,5},{1,6},{2,7},{3,0},{4,1},{5,2},{6,3},{7,4},{8,13},{9,14},{10,... | collective-permute-start | bytes 258056 | tf_op jit(solution)/shard_map/ppermute | solution.py:38
  294.0 51.3 %collective-permute-start.40 = (f32[21,1024]{1,0:T(8,128)S(1)}, f32[21,1024]{1,0:T(8,128)S(1)}, u32[]{:S(2)}, u32[]{:S(2)}) collective-permute-start(f32[21,1024]{1,0:T(8,128)S(1)} %get-tuple-element.26), channel_id=1, source_target_pairs={{0,4},{1,5},{2,6},{3,7},{4,0},{5,1},{6,2},{7,3},{8,12},{9,13},{10,... | collective-permute-start | bytes 258056 | tf_op jit(solution)/shard_map/ppermute | solution.py:38
  309.3 3.7 %collective-permute-start.44 = (f32[]{:T(128)}, f32[]{:T(128)}, u32[]{:S(2)}, u32[]{:S(2)}) collective-permute-start(f32[]{:T(128)} %psum.7), channel_id=1, source_target_pairs={{0,8},{8,16},{16,24},{24,0},{1,9},{9,17},{17,25},{25,1},{2,10},{10... | collective-permute-start | bytes 20 | tf_op jit(solution)/shard_map/ppermute | solution.py:38
  314.3 4.0 %collective-permute-start.45 = (f32[]{:T(128)}, f32[]{:T(128)}, u32[]{:S(2)}, u32[]{:S(2)}) collective-permute-start(f32[]{:T(128)} %add.484), channel_id=1, source_target_pairs={{0,16},{8,24},{16,0},{24,8},{1,17},{9,25},{17,1},{25,9},{2,18},{10... | collective-permute-start | bytes 20 | tf_op jit(solution)/shard_map/ppermute | solution.py:38
  318.9 3.8 %collective-permute-start.46 = (f32[]{:T(128)}, f32[]{:T(128)}, u32[]{:S(2)}, u32[]{:S(2)}) collective-permute-start(f32[]{:T(128)} %add.485), channel_id=1, source_target_pairs={{0,32},{32,64},{64,96},{96,128},{128,160},{160,192},{192,224},{224... | collective-permute-start | bytes 20 | tf_op jit(solution)/shard_map/ppermute | solution.py:38
  323.3 4.6 %collective-permute-start.47 = (f32[]{:T(128)}, f32[]{:T(128)}, u32[]{:S(2)}, u32[]{:S(2)}) collective-permute-start(f32[]{:T(128)} %add.486), channel_id=1, source_target_pairs={{0,64},{32,96},{64,128},{96,160},{128,192},{160,224},{192,0},{224,... | collective-permute-start | bytes 20 | tf_op jit(solution)/shard_map/ppermute | solution.py:38
  328.5 6.4 %collective-permute-start.48 = (f32[]{:T(128)}, f32[]{:T(128)}, u32[]{:S(2)}, u32[]{:S(2)}) collective-permute-start(f32[]{:T(128)} %add.487), channel_id=1, source_target_pairs={{0,128},{32,160},{64,192},{96,224},{128,0},{160,32},{192,64},{224,... | collective-permute-start | bytes 20 | tf_op jit(solution)/shard_map/ppermute | solution.py:38
  334.9 11.1 %collective-permute-start.41 = (f32[21,1024]{1,0:T(8,128)S(1)}, f32[21,1024]{1,0:T(8,128)S(1)}, u32[]{:S(2)}, u32[]{:S(2)}) collective-permute-start(f32[21,1024]{1,0:T(8,128)S(1)} %get-tuple-element.26), channel_id=1, source_target_pairs={{0,3},{1,4},{2,5},{3,6},{4,7},{5,0},{6,1},{7,2},{8,11},{9,12},{10,... | collective-permute-start | bytes 258056 | tf_op jit(solution)/shard_map/ppermute | solution.py:38
  343.3 6.5 %collective-permute-start.42 = (f32[21,1024]{1,0:T(8,128)S(1)}, f32[21,1024]{1,0:T(8,128)S(1)}, u32[]{:S(2)}, u32[]{:S(2)}) collective-permute-start(f32[21,1024]{1,0:T(8,128)S(1)} %get-tuple-element.26), channel_id=1, source_target_pairs={{0,2},{1,3},{2,4},{3,5},{4,6},{5,7},{6,0},{7,1},{8,10},{9,11},{10,... | collective-permute-start | bytes 258056 | tf_op jit(solution)/shard_map/ppermute | solution.py:38
  344.0 6.4 %collective-permute-start.43 = (f32[21,1024]{1,0:T(8,128)S(1)}, f32[21,1024]{1,0:T(8,128)S(1)}, u32[]{:S(2)}, u32[]{:S(2)}) collective-permute-start(f32[21,1024]{1,0:T(8,128)S(1)} %get-tuple-element.26), channel_id=1, source_target_pairs={{0,1},{1,2},{2,3},{3,4},{4,5},{5,6},{6,7},{7,0},{8,9},{9,10},{10,1... | collective-permute-start | bytes 258056 | tf_op jit(solution)/shard_map/ppermute | solution.py:38
  (33 other events, 686.5 us)

commit v8 on v6

--- a/solution.py
+++ b/solution.py
@@ -211,11 +211,10 @@
 
     x_list = [columns(icx)]
     v_list = [value_out]
+    landed = (kv_rows[0, 0] * 0).astype(x_own.dtype)
     for by in range(1, ncx):
-        piece = jnp.concatenate([columns((icx + by) % ncx), value_out], axis=1)
-        got = cyclic(piece, "cx", by)
-        x_list.append(got[:, : -kv_width])
-        v_list.append(got[:, -kv_width:])
+        x_list.append(cyclic(columns((icx + by) % ncx) + landed, "cx", by))
+        v_list.append(cyclic(value_out, "cx", by))
     partial = lax.dot_general(
         jnp.concatenate(x_list, axis=0),
         jnp.concatenate(v_list, axis=0),

time: 360 us -> 369 us (1.025)
  waiting for transfers between devices: 176 us -> 162 us
  local copies, waits for them, and re-layouts: 25.6 us -> 38.7 us
  matrix products: 21.9 us -> 29 us
    reshape x0 -> x2, local copies, waits for them, and re-layouts: none -> 12.2 us  [the longest x1 6.17 us: attend(): value_gradient.reshape(extent_rows, KEY_VALUE_HEADS * HEAD_SIZE)]
    ppermute x4, waiting for transfers between devices: 29.9 us -> 18.5 us  [shift(): return lax.ppermute(x, axis, pairs)]
    dot_general x1, matrix products: 1.52 us -> 5.99 us  [attend(): jnp.einsum('grte,tgrd->egd', scores_low, query_four_axes, preferred_eleme...]
    ppermute x31 -> x34, waiting for transfers between devices: 147 us -> 144 us  [cyclic(): return lax.ppermute(x, axis, [(i, (i + by) % count) for i in range(count)])]
    ppermute x31 -> x34, starting transfers between devices: 55.9 us -> 57.2 us  [cyclic(): return lax.ppermute(x, axis, [(i, (i + by) % count) for i in range(count)])]
    unnamed x57 -> x43, local copies, waits for them, and re-layouts: 15.6 us -> 15.1 us
  transfers between devices with their start and end apart: 35 -> 38, of which waited for: 25 -> 28; matrix products, arithmetic and copies ran while one was open for 4% -> 6% of each run, Pallas kernels for 0% -> 0%
where the time goes in v8:
time: 369 us; the launch traced here: 364 us
  waiting for transfers between devices  162 us (44%)
  starting transfers between devices  68.3 us (19%)
  local copies, waits for them, and re-layouts  38.7 us (10%)
  blocking collectives  34.1 us (9%)
  matrix products  29 us (8%)
  other arithmetic  25.5 us (7%)
  between operations  5.95 us (2%)
    ppermute x34, waiting for transfers between devices, cyclic(): return lax.ppermute(x, axis, [(i, (i + by) % count) for i in range(count)])  144 us
    ppermute x34, starting transfers between devices, cyclic(): return lax.ppermute(x, axis, [(i, (i + by) % count) for i in range(count)])  57.2 us
    all_gather x1, blocking collectives, shards(): lax.all_gather(new_master.astype(jnp.bfloat16), DP, axis=0, tiled=True)  19.7 us
    ppermute x4, waiting for transfers between devices, shift(): return lax.ppermute(x, axis, pairs)  18.5 us
    unnamed x43, local copies, waits for them, and re-layouts  15.1 us
    psum x1, blocking collectives, shards(): square_total = lax.psum(jnp.sum(weight_grad * weight_grad), DP)  14.5 us
    ppermute x4, starting transfers between devices, shift(): return lax.ppermute(x, axis, pairs)  11.1 us
    sub x1, matrix products, attend(): weights = jnp.exp(scores - row_max)  7.88 us
  transfers between devices with their start and end apart: 38, of which 28 were waited for; matrix products, arithmetic and copies ran while one was open for 6% of the time, Pallas kernels for 0%

profile of v8, /device:TPU:1, one launch (start us, length us, event | category | flops | bytes accessed | tf_op | source)
XLA Modules:
  0.0 363.9 jit_solution(13292229387298299329)
XLA Ops:
  3.6 4.4 %collective-permute-start = (bf16[128,2176]{0,1:T(8,128)(2,1)S(1)}, bf16[128,2176]{0,1:T(8,128)(2,1)S(1)}, u32[]{:S(2)}, u32[]{:S(2)}) collective-permute-start(bf16[128,2176]{0,1:T(8,128)(2,1)S(1)} %pad_maximum_fusion.1), channel_id=1, source_target_pairs={{0,32},{32,64},{64,96},{96,128},{128,160},{160,192},{192,224},{1,3... | collective-permute-start | bytes 1671176 | tf_op jit(solution)/shard_map/ppermute | solution.py:113
  11.6 7.7 %collective-permute-done = bf16[128,2176]{0,1:T(8,128)(2,1)S(1)} collective-permute-done((bf16[128,2176]{0,1:T(8,128)(2,1)S(1)}, bf16[128,2176]{0,1:T(8,128)(2,1)S(1)}, u32[]{:S(2)}, u32[]{:S(2)}) %collective-permute-start) | collective-permute-done | bytes 557088 | tf_op jit(solution)/shard_map/ppermute | solution.py:113
  19.3 4.1 %collective-permute-start.1 = (bf16[128,2176]{0,1:T(8,128)(2,1)S(1)}, bf16[128,2176]{0,1:T(8,128)(2,1)S(1)}, u32[]{:S(2)}, u32[]{:S(2)}) collective-permute-start(bf16[128,2176]{0,1:T(8,128)(2,1)S(1)} %collective-permute-done), channel_id=1, source_target_pairs={{0,32},{32,64},{64,96},{96,128},{128,160},{160,192},{192,224},{1,3... | collective-permute-start | bytes 1671176 | tf_op jit(solution)/shard_map/ppermute | solution.py:113
  24.7 2.5 collective-permute-start.3
  28.4 5.4 %collective-permute-done.1 = bf16[128,2176]{0,1:T(8,128)(2,1)S(1)} collective-permute-done((bf16[128,2176]{0,1:T(8,128)(2,1)S(1)}, bf16[128,2176]{0,1:T(8,128)(2,1)S(1)}, u32[]{:S(2)}, u32[]{:S(2)}) %collective-permute-start.1) | collective-permute-done | bytes 557088 | tf_op jit(solution)/shard_map/ppermute | solution.py:113
  35.4 2.5 collective-permute-start.6
  39.7 10.4 %collective-permute-done.3 = bf16[128,2176]{0,1:T(8,128)(2,1)S(1)} collective-permute-done((bf16[128,2176]{0,1:T(8,128)(2,1)S(1)}, bf16[128,2176]{0,1:T(8,128)(2,1)S(1)}, u32[]{:S(2)}, u32[]{:S(2)}) %collective-permute-start.3) | collective-permute-done | bytes 557088 | tf_op jit(solution)/shard_map/ppermute | solution.py:38
  50.2 2.5 collective-permute-done.4
  52.8 9.2 %collective-permute-done.5 = bf16[128,2176]{0,1:T(8,128)(2,1)S(1)} collective-permute-done((bf16[128,2176]{0,1:T(8,128)(2,1)S(1)}, bf16[128,2176]{0,1:T(8,128)(2,1)S(1)}, u32[]{:S(2)}, u32[]{:S(2)}) %collective-permute-start.5) | collective-permute-done | bytes 557088 | tf_op jit(solution)/shard_map/ppermute | solution.py:38
  62.1 11.8 %collective-permute-done.6 = bf16[128,2176]{0,1:T(8,128)(2,1)S(1)} collective-permute-done((bf16[128,2176]{0,1:T(8,128)(2,1)S(1)}, bf16[128,2176]{0,1:T(8,128)(2,1)S(1)}, u32[]{:S(2)}, u32[]{:S(2)}) %collective-permute-start.6) | collective-permute-done | bytes 557088 | tf_op jit(solution)/shard_map/ppermute | solution.py:38
  77.7 7.9 %fusion.59 = (f32[8,2,128]{2,1,0:T(2,128)S(1)}, f32[8,2,128,1152]{2,3,1,0:T(8,128)}) fusion(pred[128,1152]{0,1:T(8,128)(4,1)S(1)} %fusion.44, bf16[1152,8,128,1]{0,2,3,1:T(8,128)(2,1)S(1)} %bitcast.125, bf16[128,8,2,128]{0,3,2,1:T(8,128)(2,1)} %bitcast.142), kind=kOutput, calls=%fused_computation.133 | convolution fusion | flops 613418112 | bytes 12476416 | tf_op jit(solution)/shard_map/sub | solution.py:75
  85.5 4.8 %fusion.8 = bf16[8,2,128,1152]{2,3,1,0:T(8,128)(2,1)S(1)} fusion(f32[8,2,128,1152]{2,3,1,0:T(8,128)} %get-tuple-element.64, f32[8,2,128]{2,1,0:T(2,128)S(1)} %get-tuple-element.63), kind=kLoop, calls=%fused_computation.16 | loop fusion | flops 4718592 | bytes 14163968 | tf_op jit(solution)/shard_map/convert_element_type | solution.py:77
  90.4 3.9 %fusion.60 = f32[8,1152,128,1]{1,2,3,0:T(8,128)} fusion(bf16[8,2,128,1152]{2,3,1,0:T(8,128)(2,1)S(1)} %fusion.8, bf16[128,8,2,128]{0,3,2,1:T(8,128)(2,1)S(1)} %bitcast.131), kind=kOutput, calls=%fused_computation.134 | convolution fusion | flops 603979776 | bytes 9961472 | tf_op jit(solution)/shard_map/grte,tgrd->egd/dot_general | solution.py:100
  96.5 3.6 fusion.3
  100.1 6.2 %copy.62 = f32[1152,1024]{1,0:T(8,128)} copy(f32[1152,1024]{0,1:T(8,128)} %bitcast.123) | data formatting | bytes 9437184 | tf_op jit(solution)/shard_map/reshape | solution.py:106
  106.2 6.0 %bitcast_multiply_fusion = f32[8,1152,128]{1,2,0:T(8,128)} fusion(bf16[8,2,128,1152]{2,3,1,0:T(8,128)(2,1)} %fusion.3, bf16[128,8,2,128]{0,3,2,1:T(8,128)(2,1)S(1)} %bitcast.143), kind=kOutput, calls=%fused_computation.11 | convolution fusion | flops 605159424 | bytes 9961472 | tf_op jit(solution)/shard_map/grte,tgrd->egd/dot_general | solution.py:95
  112.2 6.0 %copy.61 = f32[1152,1024]{1,0:T(8,128)} copy(f32[1152,1024]{0,1:T(8,128)} %bitcast.124) | data formatting | bytes 9437184 | tf_op jit(solution)/shard_map/reshape | solution.py:105
  118.3 4.5 %fusion.1 = bf16[1152,2048]{1,0:T(8,128)(2,1)S(1)} fusion(f32[1152,1024]{1,0:T(8,128)} %copy.62, f32[1152,1024]{1,0:T(8,128)} %copy.61), kind=kLoop, calls=%fused_computation.4 | loop fusion | flops 9437184 | bytes 14155776 | tf_op jit(solution)/shard_map/convert.9
  123.0 3.7 %collective-permute-start.8 = (bf16[128,2048]{1,0:T(8,128)(2,1)S(1)}, bf16[128,2048]{1,0:T(8,128)(2,1)S(1)}, u32[]{:S(2)}, u32[]{:S(2)}) collective-permute-start(bf16[128,2048]{1,0:T(8,128)(2,1)S(1)} %get-tuple-element.41), channel_id=1, source_target_pairs={{0,24},{8,0},{16,8},{24,16},{1,25},{9,1},{17,9},{25,17},{2,26},{10... | collective-permute-start | bytes 1572872 | tf_op jit(solution)/shard_map/ppermute | solution.py:38
  130.8 29.1 %collective-permute-done.8 = bf16[128,2048]{1,0:T(8,128)(2,1)S(1)} collective-permute-done((bf16[128,2048]{1,0:T(8,128)(2,1)S(1)}, bf16[128,2048]{1,0:T(8,128)(2,1)S(1)}, u32[]{:S(2)}, u32[]{:S(2)}) %collective-permute-start.8) | collective-permute-done | bytes 524320 | tf_op jit(solution)/shard_map/ppermute | solution.py:38
  159.8 3.6 collective-permute-start.11
  165.2 9.6 %collective-permute-done.12 = bf16[128,2048]{1,0:T(8,128)(2,1)S(1)} collective-permute-done((bf16[128,2048]{1,0:T(8,128)(2,1)S(1)}, bf16[128,2048]{1,0:T(8,128)(2,1)S(1)}, u32[]{:S(2)}, u32[]{:S(2)}) %collective-permute-start.12) | collective-permute-done | bytes 524320 | tf_op jit(solution)/shard_map/ppermute | solution.py:38
  174.7 3.1 collective-permute-done.14
  181.0 2.6 copy.63
  183.6 3.3 reshape_squeeze.11
  187.6 2.6 pad_dynamic-slice_fusion.3
  200.7 13.6 %collective-permute-done.16 = bf16[128,1536]{0,1:T(8,128)(2,1)} collective-permute-done((bf16[128,1536]{0,1:T(8,128)(2,1)}, bf16[128,1536]{0,1:T(8,128)(2,1)}, u32[]{:S(2)}, u32[]{:S(2)}) %collective-permute-start.16) | collective-permute-done | bytes 393248 | tf_op jit(solution)/shard_map/ppermute | solution.py:38
  214.6 8.2 %collective-permute-done.19 = bf16[128,1024]{1,0:T(8,128)(2,1)S(1)} collective-permute-done((bf16[128,1024]{1,0:T(8,128)(2,1)S(1)}, bf16[128,1024]{1,0:T(8,128)(2,1)S(1)}, u32[]{:S(2)}, u32[]{:S(2)}) %collective-permute-start.19) | collective-permute-done | bytes 262176 | tf_op jit(solution)/shard_map/ppermute | solution.py:38
  222.8 3.2 fusion.10
  226.0 2.7 copy-done.2
  230.6 3.4 collective-permute-done.22
  234.0 2.9 bitcast_add_fusion
  238.7 2.8 collective-permute-start.25
  242.5 15.3 %collective-permute-done.25 = bf16[8,24,1024]{2,1,0:T(8,128)(2,1)} collective-permute-done((bf16[8,24,1024]{2,1,0:T(8,128)(2,1)S(1)}, bf16[8,24,1024]{2,1,0:T(8,128)(2,1)}, u32[]{:S(2)}, u32[]{:S(2)}) %collective-permute-start.25) | collective-permute-done | bytes 393248 | tf_op jit(solution)/shard_map/ppermute | solution.py:38
  257.9 4.7 %collective-permute-done.23 = bf16[8,24,1024]{2,1,0:T(8,128)(2,1)} collective-permute-done((bf16[8,24,1024]{2,1,0:T(8,128)(2,1)S(1)}, bf16[8,24,1024]{2,1,0:T(8,128)(2,1)}, u32[]{:S(2)}, u32[]{:S(2)}) %collective-permute-start.23) | collective-permute-done | bytes 393248 | tf_op jit(solution)/shard_map/ppermute | solution.py:38
  265.2 6.6 %collective-permute-start.32 = (f32[24,1024]{1,0:T(8,128)}, f32[24,1024]{1,0:T(8,128)}, u32[]{:S(2)}, u32[]{:S(2)}) collective-permute-start(f32[24,1024]{1,0:T(8,128)} %get-tuple-element.53), channel_id=1, source_target_pairs={{0,224},{32,0},{64,32},{96,64},{128,96},{160,128},{192,160},{224,1... | collective-permute-start | bytes 294920 | tf_op jit(solution)/shard_map/ppermute | solution.py:38
  271.8 3.4 fusion.19
  277.6 5.5 %collective-permute-start.30 = (f32[24,1024]{1,0:T(8,128)}, f32[24,1024]{1,0:T(8,128)S(1)}, u32[]{:S(2)}, u32[]{:S(2)}) collective-permute-start(f32[24,1024]{1,0:T(8,128)} %get-tuple-element.55), channel_id=1, source_target_pairs={{0,160},{32,192},{64,224},{96,0},{128,32},{160,64},{192,96},{224,1... | collective-permute-start | bytes 294920 | tf_op jit(solution)/shard_map/ppermute | solution.py:38
  285.1 3.6 collective-permute-start.27
  291.4 7.5 %collective-permute-done.28 = f32[24,1024]{1,0:T(8,128)S(1)} collective-permute-done((f32[24,1024]{1,0:T(8,128)S(1)}, f32[24,1024]{1,0:T(8,128)S(1)}, u32[]{:S(2)}, u32[]{:S(2)}) %collective-permute-start.28) | collective-permute-done | bytes 98336 | tf_op jit(solution)/shard_map/ppermute | solution.py:38
  300.4 14.5 %psum.7 = f32[]{:T(128)} all-reduce(f32[]{:T(128)} %get-tuple-element.32), channel_id=1, replica_groups=mesh['cz'=8,'cx'=4,'y'=4,'core'=2] {'y','core'}, use_global_device_ids=true, to_apply=%region_4.5 | all-reduce | flops 1 | bytes 8 | tf_op jit(solution)/shard_map/psum | solution.py:241
  315.0 3.7 %collective-permute-done.33 = f32[]{:T(128)} collective-permute-done((f32[]{:T(128)}, f32[]{:T(128)}, u32[]{:S(2)}, u32[]{:S(2)}) %collective-permute-start.33) | collective-permute-done | bytes 36 | tf_op jit(solution)/shard_map/ppermute | solution.py:38
  320.8 3.1 collective-permute-done.34
  324.6 3.9 %collective-permute-start.35 = (f32[]{:T(128)}, f32[]{:T(128)}, u32[]{:S(2)}, u32[]{:S(2)}) collective-permute-start(f32[]{:T(128)} %add.490), channel_id=1, source_target_pairs={{0,32},{32,64},{64,96},{96,128},{128,160},{160,192},{192,224},{224... | collective-permute-start | bytes 20 | tf_op jit(solution)/shard_map/ppermute | solution.py:38
  331.4 3.4 collective-permute-done.36
  335.4 3.0 collective-permute-start.37
  338.4 3.4 collective-permute-done.37
  343.2 19.7 %all-gather = bf16[8,21,1024]{2,1,0:T(8,128)(2,1)S(1)} all-gather(bf16[1,21,1024]{2,1,0:T(8,128)(2,1)S(1)} %get-tuple-element.28), channel_id=1, replica_groups=mesh['cz'=8,'cx'=4,'y'=4,'core'=2] {'y','core'}, dimensions={0}, use_global_device_ids=true | all-gather | bytes 387072 | tf_op jit(solution)/shard_map/all_gather | solution.py:249
  (121 shorter events, 59.2 us)
Async XLA Ops:
  3.6 15.7 %collective-permute-start = (bf16[128,2176]{0,1:T(8,128)(2,1)S(1)}, bf16[128,2176]{0,1:T(8,128)(2,1)S(1)}, u32[]{:S(2)}, u32[]{:S(2)}) collective-permute-start(bf16[128,2176]{0,1:T(8,128)(2,1)S(1)} %pad_maximum_fusion.1), channel_id=1, source_target_pairs={{0,32},{32,64},{64,96},{96,128},{128,160},{160,192},{192,224},{1,3... | collective-permute-start | bytes 1671176 | tf_op jit(solution)/shard_map/ppermute | solution.py:113
  19.3 14.5 %collective-permute-start.1 = (bf16[128,2176]{0,1:T(8,128)(2,1)S(1)}, bf16[128,2176]{0,1:T(8,128)(2,1)S(1)}, u32[]{:S(2)}, u32[]{:S(2)}) collective-permute-start(bf16[128,2176]{0,1:T(8,128)(2,1)S(1)} %collective-permute-done), channel_id=1, source_target_pairs={{0,32},{32,64},{64,96},{96,128},{128,160},{160,192},{192,224},{1,3... | collective-permute-start | bytes 1671176 | tf_op jit(solution)/shard_map/ppermute | solution.py:113
  23.5 14.7 %collective-permute-start.2 = (bf16[128,2176]{0,1:T(8,128)(2,1)S(1)}, bf16[128,2176]{0,1:T(8,128)(2,1)S(1)}, u32[]{:S(2)}, u32[]{:S(2)}) collective-permute-start(bf16[128,2176]{0,1:T(8,128)(2,1)S(1)} %collective-permute-done), channel_id=1, source_target_pairs={{0,8},{8,16},{16,24},{24,0},{1,9},{9,17},{17,25},{25,1},{2,10},{10... | collective-permute-start | bytes 1671176 | tf_op jit(solution)/shard_map/ppermute | solution.py:38
  24.7 25.3 %collective-permute-start.3 = (bf16[128,2176]{0,1:T(8,128)(2,1)S(1)}, bf16[128,2176]{0,1:T(8,128)(2,1)S(1)}, u32[]{:S(2)}, u32[]{:S(2)}) collective-permute-start(bf16[128,2176]{0,1:T(8,128)(2,1)S(1)} %collective-permute-done), channel_id=1, source_target_pairs={{0,16},{8,24},{16,0},{24,8},{1,17},{9,25},{17,1},{25,9},{2,18},{10... | collective-permute-start | bytes 1671176 | tf_op jit(solution)/shard_map/ppermute | solution.py:38
  27.2 25.5 %collective-permute-start.4 = (bf16[128,2176]{0,1:T(8,128)(2,1)S(1)}, bf16[128,2176]{0,1:T(8,128)(2,1)S(1)}, u32[]{:S(2)}, u32[]{:S(2)}) collective-permute-start(bf16[128,2176]{0,1:T(8,128)(2,1)S(1)} %collective-permute-done), channel_id=1, source_target_pairs={{0,24},{8,0},{16,8},{24,16},{1,25},{9,1},{17,9},{25,17},{2,26},{10... | collective-permute-start | bytes 1671176 | tf_op jit(solution)/shard_map/ppermute | solution.py:38
  34.1 27.9 %collective-permute-start.5 = (bf16[128,2176]{0,1:T(8,128)(2,1)S(1)}, bf16[128,2176]{0,1:T(8,128)(2,1)S(1)}, u32[]{:S(2)}, u32[]{:S(2)}) collective-permute-start(bf16[128,2176]{0,1:T(8,128)(2,1)S(1)} %get-tuple-element.51), channel_id=1, source_target_pairs={{0,8},{8,16},{16,24},{24,0},{1,9},{9,17},{17,25},{25,1},{2,10},{10... | collective-permute-start | bytes 1671176 | tf_op jit(solution)/shard_map/ppermute | solution.py:38
  35.4 38.5 %collective-permute-start.6 = (bf16[128,2176]{0,1:T(8,128)(2,1)S(1)}, bf16[128,2176]{0,1:T(8,128)(2,1)S(1)}, u32[]{:S(2)}, u32[]{:S(2)}) collective-permute-start(bf16[128,2176]{0,1:T(8,128)(2,1)S(1)} %get-tuple-element.50), channel_id=1, source_target_pairs={{0,16},{8,24},{16,0},{24,8},{1,17},{9,25},{17,1},{25,9},{2,18},{10... | collective-permute-start | bytes 1671176 | tf_op jit(solution)/shard_map/ppermute | solution.py:38
  38.2 36.5 %collective-permute-start.7 = (bf16[128,2176]{0,1:T(8,128)(2,1)S(1)}, bf16[128,2176]{0,1:T(8,128)(2,1)S(1)}, u32[]{:S(2)}, u32[]{:S(2)}) collective-permute-start(bf16[128,2176]{0,1:T(8,128)(2,1)S(1)} %get-tuple-element.49), channel_id=1, source_target_pairs={{0,24},{8,0},{16,8},{24,16},{1,25},{9,1},{17,9},{25,17},{2,26},{10... | collective-permute-start | bytes 1671176 | tf_op jit(solution)/shard_map/ppermute | solution.py:38
  90.4 5.0 %slice-start = ((s8[9437184]{0:T(1024)(128)(4,1)}), s8[4194304]{0:T(1024)(128)(4,1)S(1)}, s32[]{:S(2)}) async-start(s8[9437184]{0:T(1024)(128)(4,1)} %bitcast.129), calls=%async_computation | async-start | bytes 8388608
  90.4 5.8 %slice-start.1 = ((s8[9437184]{0:T(1024)(128)(4,1)}), s8[4194304]{0:T(1024)(128)(4,1)S(1)}, s32[]{:S(2)}) async-start(s8[9437184]{0:T(1024)(128)(4,1)} %bitcast.129), calls=%async_computation.1 | async-start | bytes 8388608
  100.1 6.2 %copy-start.4 = (bf16[1,128,2048]{1,2,0:T(8,128)(2,1)S(1)}, bf16[1,128,2048]{1,2,0:T(8,128)(2,1)}, u32[]{:S(2)}) copy-start(bf16[1,128,2048]{1,2,0:T(8,128)(2,1)} %copy.84) | copy-start | bytes 1572868
  123.0 36.8 %collective-permute-start.8 = (bf16[128,2048]{1,0:T(8,128)(2,1)S(1)}, bf16[128,2048]{1,0:T(8,128)(2,1)S(1)}, u32[]{:S(2)}, u32[]{:S(2)}) collective-permute-start(bf16[128,2048]{1,0:T(8,128)(2,1)S(1)} %get-tuple-element.41), channel_id=1, source_target_pairs={{0,24},{8,0},{16,8},{24,16},{1,25},{9,1},{17,9},{25,17},{2,26},{10... | collective-permute-start | bytes 1572872 | tf_op jit(solution)/shard_map/ppermute | solution.py:38
  126.7 36.7 %collective-permute-start.9 = (bf16[128,2048]{1,0:T(8,128)(2,1)S(1)}, bf16[128,2048]{1,0:T(8,128)(2,1)S(1)}, u32[]{:S(2)}, u32[]{:S(2)}) collective-permute-start(bf16[128,2048]{1,0:T(8,128)(2,1)S(1)} %get-tuple-element.40), channel_id=1, source_target_pairs={{0,16},{8,24},{16,0},{24,8},{1,17},{9,25},{17,1},{25,9},{2,18},{10... | collective-permute-start | bytes 1572872 | tf_op jit(solution)/shard_map/ppermute | solution.py:38
  126.9 36.5 %collective-permute-start.10 = (bf16[128,2048]{1,0:T(8,128)(2,1)S(1)}, bf16[128,2048]{1,0:T(8,128)(2,1)S(1)}, u32[]{:S(2)}, u32[]{:S(2)}) collective-permute-start(bf16[128,2048]{1,0:T(8,128)(2,1)S(1)} %get-tuple-element.39), channel_id=1, source_target_pairs={{0,8},{8,16},{16,24},{24,0},{1,9},{9,17},{17,25},{25,1},{2,10},{10... | collective-permute-start | bytes 1572872 | tf_op jit(solution)/shard_map/ppermute | solution.py:38
  127.4 37.8 %collective-permute-start.13 = (bf16[128,2048]{1,0:T(8,128)(2,1)S(1)}, bf16[128,2048]{1,0:T(8,128)(2,1)S(1)}, u32[]{:S(2)}, u32[]{:S(2)}) collective-permute-start(bf16[128,2048]{1,0:T(8,128)(2,1)S(1)} %get-tuple-element.37), channel_id=1, source_target_pairs={{0,8},{8,16},{16,24},{24,0},{1,9},{9,17},{17,25},{25,1},{2,10},{10... | collective-permute-start | bytes 1572872 | tf_op jit(solution)/shard_map/ppermute | solution.py:38
  129.4 45.4 %collective-permute-start.12 = (bf16[128,2048]{1,0:T(8,128)(2,1)S(1)}, bf16[128,2048]{1,0:T(8,128)(2,1)S(1)}, u32[]{:S(2)}, u32[]{:S(2)}) collective-permute-start(bf16[128,2048]{1,0:T(8,128)(2,1)S(1)} %get-tuple-element.38), channel_id=1, source_target_pairs={{0,16},{8,24},{16,0},{24,8},{1,17},{9,25},{17,1},{25,9},{2,18},{10... | collective-permute-start | bytes 1572872 | tf_op jit(solution)/shard_map/ppermute | solution.py:38
  159.8 14.9 %collective-permute-start.11 = (bf16[128,2048]{1,0:T(8,128)(2,1)S(1)}, bf16[128,2048]{1,0:T(8,128)(2,1)S(1)}, u32[]{:S(2)}, u32[]{:S(2)}) collective-permute-start(bf16[128,2048]{1,0:T(8,128)(2,1)S(1)} %get-tuple-element.36), channel_id=1, source_target_pairs={{0,24},{8,0},{16,8},{24,16},{1,25},{9,1},{17,9},{25,17},{2,26},{10... | collective-permute-start | bytes 1572872 | tf_op jit(solution)/shard_map/ppermute | solution.py:38
  163.4 15.8 %copy-start.5 = (bf16[128,2048]{1,0:T(8,128)(2,1)}, bf16[128,2048]{1,0:T(8,128)(2,1)S(1)}, u32[]{:S(2)}) copy-start(bf16[128,2048]{1,0:T(8,128)(2,1)S(1)} %collective-permute-done.9) | copy-start | bytes 1572868
  163.4 15.8 %copy-start.7 = (bf16[128,2048]{1,0:T(8,128)(2,1)}, bf16[128,2048]{1,0:T(8,128)(2,1)S(1)}, u32[]{:S(2)}) copy-start(bf16[128,2048]{1,0:T(8,128)(2,1)S(1)} %collective-permute-done.10) | copy-start | bytes 1572868
  163.8 14.1 %collective-permute-start.14 = (bf16[128,2048]{1,0:T(8,128)(2,1)S(1)}, bf16[128,2048]{1,0:T(8,128)(2,1)S(1)}, u32[]{:S(2)}, u32[]{:S(2)}) collective-permute-start(bf16[128,2048]{1,0:T(8,128)(2,1)S(1)} %fusion.31), channel_id=1, source_target_pairs={{32,0},{64,32},{96,64},{128,96},{160,128},{192,160},{224,192},{33,... | collective-permute-start | bytes 1572872 | tf_op jit(solution)/shard_map/ppermute | solution.py:113
  179.2 14.7 %collective-permute-start.15 = (bf16[128,2048]{1,0:T(8,128)(2,1)}, bf16[128,2048]{1,0:T(8,128)(2,1)}, u32[]{:S(2)}, u32[]{:S(2)}) collective-permute-start(bf16[128,2048]{1,0:T(8,128)(2,1)} %add_convert_fusion), channel_id=1, source_target_pairs={{32,0},{64,32},{96,64},{128,96},{160,128},{192,160},{224,192},{33,... | collective-permute-start | bytes 1572872 | tf_op jit(solution)/shard_map/ppermute | solution.py:113
  181.0 12.9 %copy-start.6 = (bf16[128,2048]{1,0:T(8,128)(2,1)S(1)}, bf16[128,2048]{1,0:T(8,128)(2,1)}, u32[]{:S(2)}) copy-start(bf16[128,2048]{1,0:T(8,128)(2,1)} %copy-done.5) | copy-start | bytes 1572868
  190.1 8.5 %collective-permute-start.18 = (bf16[128,1536]{0,1:T(8,128)(2,1)S(1)}, bf16[128,1536]{0,1:T(8,128)(2,1)S(1)}, u32[]{:S(2)}, u32[]{:S(2)}) collective-permute-start(bf16[128,1536]{0,1:T(8,128)(2,1)S(1)} %bitcast.145), channel_id=1, source_target_pairs={{0,24},{8,0},{16,8},{24,16},{1,25},{9,1},{17,9},{25,17},{2,26},{10... | collective-permute-start | bytes 1179656 | tf_op jit(solution)/shard_map/ppermute | solution.py:38
  190.4 10.2 %collective-permute-start.17 = (bf16[128,1536]{0,1:T(8,128)(2,1)}, bf16[128,1536]{0,1:T(8,128)(2,1)}, u32[]{:S(2)}, u32[]{:S(2)}) collective-permute-start(bf16[128,1536]{0,1:T(8,128)(2,1)} %bitcast.31), channel_id=1, source_target_pairs={{0,16},{8,24},{16,0},{24,8},{1,17},{9,25},{17,1},{25,9},{2,18},{10... | collective-permute-start | bytes 1179656 | tf_op jit(solution)/shard_map/ppermute | solution.py:38
  190.4 23.9 %collective-permute-start.16 = (bf16[128,1536]{0,1:T(8,128)(2,1)}, bf16[128,1536]{0,1:T(8,128)(2,1)}, u32[]{:S(2)}, u32[]{:S(2)}) collective-permute-start(bf16[128,1536]{0,1:T(8,128)(2,1)} %bitcast.30), channel_id=1, source_target_pairs={{0,8},{8,16},{16,24},{24,0},{1,9},{9,17},{17,25},{25,1},{2,10},{10... | collective-permute-start | bytes 1179656 | tf_op jit(solution)/shard_map/ppermute | solution.py:38
  196.7 17.6 %collective-permute-start.21 = (bf16[128,1024]{1,0:T(8,128)(2,1)S(1)}, bf16[128,1024]{1,0:T(8,128)(2,1)S(1)}, u32[]{:S(2)}, u32[]{:S(2)}) collective-permute-start(bf16[128,1024]{1,0:T(8,128)(2,1)S(1)} %get-tuple-element.60), channel_id=1, source_target_pairs={{0,24},{8,0},{16,8},{24,16},{1,25},{9,1},{17,9},{25,17},{2,26},{10... | collective-permute-start | bytes 786440 | tf_op jit(solution)/shard_map/ppermute | solution.py:38
  197.3 17.4 %collective-permute-start.20 = (bf16[128,1024]{1,0:T(8,128)(2,1)S(1)}, bf16[128,1024]{1,0:T(8,128)(2,1)S(1)}, u32[]{:S(2)}, u32[]{:S(2)}) collective-permute-start(bf16[128,1024]{1,0:T(8,128)(2,1)S(1)} %get-tuple-element.60), channel_id=1, source_target_pairs={{0,16},{8,24},{16,0},{24,8},{1,17},{9,25},{17,1},{25,9},{2,18},{10... | collective-permute-start | bytes 786440 | tf_op jit(solution)/shard_map/ppermute | solution.py:38
  199.3 23.5 %collective-permute-start.19 = (bf16[128,1024]{1,0:T(8,128)(2,1)S(1)}, bf16[128,1024]{1,0:T(8,128)(2,1)S(1)}, u32[]{:S(2)}, u32[]{:S(2)}) collective-permute-start(bf16[128,1024]{1,0:T(8,128)(2,1)S(1)} %get-tuple-element.60), channel_id=1, source_target_pairs={{0,8},{8,16},{16,24},{24,0},{1,9},{9,17},{17,25},{25,1},{2,10},{10... | collective-permute-start | bytes 786440 | tf_op jit(solution)/shard_map/ppermute | solution.py:38
  230.1 3.9 %collective-permute-start.22 = (bf16[8,4,24,1024]{3,2,1,0:T(8,128)(2,1)}, bf16[8,4,24,1024]{3,2,1,0:T(8,128)(2,1)}, u32[]{:S(2)}, u32[]{:S(2)}) collective-permute-start(bf16[8,4,24,1024]{3,2,1,0:T(8,128)(2,1)} %fusion.9), channel_id=1, source_target_pairs={{0,1},{1,0},{2,3},{3,2},{4,5},{5,4},{6,7},{7,6},{8,9},{9,8},{10,11... | collective-permute-start | bytes 4718600 | tf_op jit(solution)/shard_map/ppermute | solution.py:38
  238.7 19.1 %collective-permute-start.25 = (bf16[8,24,1024]{2,1,0:T(8,128)(2,1)S(1)}, bf16[8,24,1024]{2,1,0:T(8,128)(2,1)}, u32[]{:S(2)}, u32[]{:S(2)}) collective-permute-start(bf16[8,24,1024]{2,1,0:T(8,128)(2,1)S(1)} %get-tuple-element.43), channel_id=1, source_target_pairs={{0,6},{2,0},{4,2},{6,4},{1,7},{3,1},{5,3},{7,5},{8,14},{10,8},{12,... | collective-permute-start | bytes 1179656 | tf_op jit(solution)/shard_map/ppermute | solution.py:38
  241.5 16.4 %collective-permute-start.24 = (bf16[8,24,1024]{2,1,0:T(8,128)(2,1)S(1)}, bf16[8,24,1024]{2,1,0:T(8,128)(2,1)}, u32[]{:S(2)}, u32[]{:S(2)}) collective-permute-start(bf16[8,24,1024]{2,1,0:T(8,128)(2,1)S(1)} %get-tuple-element.44), channel_id=1, source_target_pairs={{0,4},{2,6},{4,0},{6,2},{1,5},{3,7},{5,1},{7,3},{8,12},{10,14},{12... | collective-permute-start | bytes 1179656 | tf_op jit(solution)/shard_map/ppermute | solution.py:38
  241.9 20.7 %collective-permute-start.23 = (bf16[8,24,1024]{2,1,0:T(8,128)(2,1)S(1)}, bf16[8,24,1024]{2,1,0:T(8,128)(2,1)}, u32[]{:S(2)}, u32[]{:S(2)}) collective-permute-start(bf16[8,24,1024]{2,1,0:T(8,128)(2,1)S(1)} %get-tuple-element.42), channel_id=1, source_target_pairs={{0,2},{2,4},{4,6},{6,0},{1,3},{3,5},{5,7},{7,1},{8,10},{10,12},{12... | collective-permute-start | bytes 1179656 | tf_op jit(solution)/shard_map/ppermute | solution.py:38
  264.3 7.5 %copy-start.3 = (f32[8,24,1024]{2,1,0:T(8,128)}, f32[8,24,1024]{2,1,0:T(8,128)S(1)}, u32[]{:S(2)}) copy-start(f32[8,24,1024]{2,1,0:T(8,128)S(1)} %fusion.41) | copy-start | bytes 2359300
  265.2 19.1 %collective-permute-start.32 = (f32[24,1024]{1,0:T(8,128)}, f32[24,1024]{1,0:T(8,128)}, u32[]{:S(2)}, u32[]{:S(2)}) collective-permute-start(f32[24,1024]{1,0:T(8,128)} %get-tuple-element.53), channel_id=1, source_target_pairs={{0,224},{32,0},{64,32},{96,64},{128,96},{160,128},{192,160},{224,1... | collective-permute-start | bytes 294920 | tf_op jit(solution)/shard_map/ppermute | solution.py:38
  271.7 70.7 %copy-start.8 = (f32[21,1024]{1,0:T(8,128)S(1)}, f32[21,1024]{1,0:T(8,128)}, u32[]{:S(2)}) copy-start(f32[21,1024]{1,0:T(8,128)} %param.15) | copy-start | bytes 258052
  271.7 70.7 %copy-start.9 = (f32[21,1024]{1,0:T(8,128)S(1)}, f32[21,1024]{1,0:T(8,128)}, u32[]{:S(2)}) copy-start(f32[21,1024]{1,0:T(8,128)} %param.16) | copy-start | bytes 258052
  271.8 70.7 %copy-start.10 = (f32[21,1024]{1,0:T(8,128)S(1)}, f32[21,1024]{1,0:T(8,128)}, u32[]{:S(2)}) copy-start(f32[21,1024]{1,0:T(8,128)} %param.17) | copy-start | bytes 258052
  271.8 13.3 %collective-permute-start.26 = (f32[24,1024]{1,0:T(8,128)}, f32[24,1024]{1,0:T(8,128)}, u32[]{:S(2)}, u32[]{:S(2)}) collective-permute-start(f32[24,1024]{1,0:T(8,128)} %get-tuple-element.52), channel_id=1, source_target_pairs={{0,32},{32,64},{64,96},{96,128},{128,160},{160,192},{192,224},{224... | collective-permute-start | bytes 294920 | tf_op jit(solution)/shard_map/ppermute | solution.py:38
  276.3 13.3 %collective-permute-start.31 = (f32[24,1024]{1,0:T(8,128)}, f32[24,1024]{1,0:T(8,128)S(1)}, u32[]{:S(2)}, u32[]{:S(2)}) collective-permute-start(f32[24,1024]{1,0:T(8,128)} %get-tuple-element.54), channel_id=1, source_target_pairs={{0,192},{32,224},{64,0},{96,32},{128,64},{160,96},{192,128},{224,1... | collective-permute-start | bytes 294920 | tf_op jit(solution)/shard_map/ppermute | solution.py:38
  277.6 13.1 %collective-permute-start.30 = (f32[24,1024]{1,0:T(8,128)}, f32[24,1024]{1,0:T(8,128)S(1)}, u32[]{:S(2)}, u32[]{:S(2)}) collective-permute-start(f32[24,1024]{1,0:T(8,128)} %get-tuple-element.55), channel_id=1, source_target_pairs={{0,160},{32,192},{64,224},{96,0},{128,32},{160,64},{192,96},{224,1... | collective-permute-start | bytes 294920 | tf_op jit(solution)/shard_map/ppermute | solution.py:38
  283.1 8.3 %collective-permute-start.29 = (f32[24,1024]{1,0:T(8,128)S(1)}, f32[24,1024]{1,0:T(8,128)S(1)}, u32[]{:S(2)}, u32[]{:S(2)}) collective-permute-start(f32[24,1024]{1,0:T(8,128)S(1)} %get-tuple-element.56), channel_id=1, source_target_pairs={{0,128},{32,160},{64,192},{96,224},{128,0},{160,32},{192,64},{224,... | collective-permute-start | bytes 294920 | tf_op jit(solution)/shard_map/ppermute | solution.py:38
  284.3 14.6 %collective-permute-start.28 = (f32[24,1024]{1,0:T(8,128)S(1)}, f32[24,1024]{1,0:T(8,128)S(1)}, u32[]{:S(2)}, u32[]{:S(2)}) collective-permute-start(f32[24,1024]{1,0:T(8,128)S(1)} %get-tuple-element.57), channel_id=1, source_target_pairs={{0,96},{32,128},{64,160},{96,192},{128,224},{160,0},{192,32},{224,... | collective-permute-start | bytes 294920 | tf_op jit(solution)/shard_map/ppermute | solution.py:38
  285.1 13.8 %collective-permute-start.27 = (f32[24,1024]{1,0:T(8,128)S(1)}, f32[24,1024]{1,0:T(8,128)S(1)}, u32[]{:S(2)}, u32[]{:S(2)}) collective-permute-start(f32[24,1024]{1,0:T(8,128)S(1)} %get-tuple-element.58), channel_id=1, source_target_pairs={{0,64},{32,96},{64,128},{96,160},{128,192},{160,224},{192,0},{224,... | collective-permute-start | bytes 294920 | tf_op jit(solution)/shard_map/ppermute | solution.py:38
  314.9 3.9 %collective-permute-start.33 = (f32[]{:T(128)}, f32[]{:T(128)}, u32[]{:S(2)}, u32[]{:S(2)}) collective-permute-start(f32[]{:T(128)} %psum.7), channel_id=1, source_target_pairs={{0,8},{8,16},{16,24},{24,0},{1,9},{9,17},{17,25},{25,1},{2,10},{10... | collective-permute-start | bytes 20 | tf_op jit(solution)/shard_map/ppermute | solution.py:38
  320.0 4.0 %collective-permute-start.34 = (f32[]{:T(128)}, f32[]{:T(128)}, u32[]{:S(2)}, u32[]{:S(2)}) collective-permute-start(f32[]{:T(128)} %add.489), channel_id=1, source_target_pairs={{0,16},{8,24},{16,0},{24,8},{1,17},{9,25},{17,1},{25,9},{2,18},{10... | collective-permute-start | bytes 20 | tf_op jit(solution)/shard_map/ppermute | solution.py:38
  324.6 4.9 %collective-permute-start.35 = (f32[]{:T(128)}, f32[]{:T(128)}, u32[]{:S(2)}, u32[]{:S(2)}) collective-permute-start(f32[]{:T(128)} %add.490), channel_id=1, source_target_pairs={{0,32},{32,64},{64,96},{96,128},{128,160},{160,192},{192,224},{224... | collective-permute-start | bytes 20 | tf_op jit(solution)/shard_map/ppermute | solution.py:38
  330.2 4.6 %collective-permute-start.36 = (f32[]{:T(128)}, f32[]{:T(128)}, u32[]{:S(2)}, u32[]{:S(2)}) collective-permute-start(f32[]{:T(128)} %add.491), channel_id=1, source_target_pairs={{0,64},{32,96},{64,128},{96,160},{128,192},{160,224},{192,0},{224,... | collective-permute-start | bytes 20 | tf_op jit(solution)/shard_map/ppermute | solution.py:38
  335.4 6.4 %collective-permute-start.37 = (f32[]{:T(128)}, f32[]{:T(128)}, u32[]{:S(2)}, u32[]{:S(2)}) collective-permute-start(f32[]{:T(128)} %add.492), channel_id=1, source_target_pairs={{0,128},{32,160},{64,192},{96,224},{128,0},{160,32},{192,64},{224,... | collective-permute-start | bytes 20 | tf_op jit(solution)/shard_map/ppermute | solution.py:38
  (5 other events, 11.2 us)

commit v9 on v6

--- a/solution.py
+++ b/solution.py
@@ -239,8 +239,8 @@
         weight_grad = weight_grad + cyclic(sent, "cz", by)
 
     weight_grad = weight_grad[:rows]
-    square_total = lax.psum(jnp.sum(weight_grad * weight_grad), DP)
-    square_total = all_sum(square_total, ("cx", "cz"))
+    square_total = lax.psum(jnp.sum(weight_grad * weight_grad), ("cx", "y", "core"))
+    square_total = all_sum(square_total, ("cz",))
     norm_total = jnp.sqrt(square_total + 1e-06)
     clipped = weight_grad * jnp.minimum(1.0, clip_norm / norm_total)
     new_first = beta_first * first_moment_value + (1.0 - beta_first) * clipped

time: 360 us -> 400 us (1.11)
  blocking collectives: 33 us -> 82.2 us
  waiting for transfers between devices: 176 us -> 170 us
    psum x1, blocking collectives: 14.6 us -> 64.8 us  [shards(): lax.psum(jnp.sum(weight_grad * weight_grad), ('cx', 'y', 'core'))]
    ppermute x31 -> x29, waiting for transfers between devices: 147 us -> 140 us  [cyclic(): return lax.ppermute(x, axis, [(i, (i + by) % count) for i in range(count)])]
    ppermute x31 -> x29, starting transfers between devices: 55.9 us -> 54.2 us  [cyclic(): return lax.ppermute(x, axis, [(i, (i + by) % count) for i in range(count)])]
  transfers between devices with their start and end apart: 35 -> 33, of which waited for: 25 -> 23; matrix products, arithmetic and copies ran while one was open for 4% -> 4% of each run, Pallas kernels for 0% -> 0%
where the time goes in v9:
time: 400 us; the launch traced here: 394 us
  waiting for transfers between devices  170 us (42%)
  blocking collectives  82.2 us (21%)
  starting transfers between devices  65.3 us (16%)
  local copies, waits for them, and re-layouts  25.6 us (6%)
  other arithmetic  25.5 us (6%)
  matrix products  21.9 us (5%)
  between operations  4.18 us (1%)
    ppermute x29, waiting for transfers between devices, cyclic(): return lax.ppermute(x, axis, [(i, (i + by) % count) for i in range(count)])  140 us
    psum x1, blocking collectives, shards(): lax.psum(jnp.sum(weight_grad * weight_grad), ('cx', 'y', 'core'))  64.8 us
    ppermute x29, starting transfers between devices, cyclic(): return lax.ppermute(x, axis, [(i, (i + by) % count) for i in range(count)])  54.2 us
    ppermute x4, waiting for transfers between devices, shift(): return lax.ppermute(x, axis, pairs)  29.9 us
    all_gather x1, blocking collectives, shards(): lax.all_gather(new_master.astype(jnp.bfloat16), DP, axis=0, tiled=True)  17.3 us
    unnamed x57, local copies, waits for them, and re-layouts  15.6 us
    ppermute x4, starting transfers between devices, shift(): return lax.ppermute(x, axis, pairs)  11.1 us
  transfers between devices with their start and end apart: 33, of which 23 were waited for; matrix products, arithmetic and copies ran while one was open for 4% of the time, Pallas kernels for 0%

profile of v9, /device:TPU:1, one launch (start us, length us, event | category | flops | bytes accessed | tf_op | source)
XLA Modules:
  0.0 394.3 jit_solution(6440995133308021837)
XLA Ops:
  3.6 4.4 %collective-permute-start = (bf16[128,2176]{0,1:T(8,128)(2,1)S(1)}, bf16[128,2176]{0,1:T(8,128)(2,1)S(1)}, u32[]{:S(2)}, u32[]{:S(2)}) collective-permute-start(bf16[128,2176]{0,1:T(8,128)(2,1)S(1)} %pad_maximum_fusion.4), channel_id=1, source_target_pairs={{0,32},{32,64},{64,96},{96,128},{128,160},{160,192},{192,224},{1,3... | collective-permute-start | bytes 1671176 | tf_op jit(solution)/shard_map/ppermute | solution.py:113
  10.9 8.4 %collective-permute-done = bf16[128,2176]{0,1:T(8,128)(2,1)S(1)} collective-permute-done((bf16[128,2176]{0,1:T(8,128)(2,1)S(1)}, bf16[128,2176]{0,1:T(8,128)(2,1)S(1)}, u32[]{:S(2)}, u32[]{:S(2)}) %collective-permute-start) | collective-permute-done | bytes 557088 | tf_op jit(solution)/shard_map/ppermute | solution.py:113
  19.3 4.1 %collective-permute-start.1 = (bf16[128,2176]{0,1:T(8,128)(2,1)S(1)}, bf16[128,2176]{0,1:T(8,128)(2,1)S(1)}, u32[]{:S(2)}, u32[]{:S(2)}) collective-permute-start(bf16[128,2176]{0,1:T(8,128)(2,1)S(1)} %collective-permute-done), channel_id=1, source_target_pairs={{0,32},{32,64},{64,96},{96,128},{128,160},{160,192},{192,224},{1,3... | collective-permute-start | bytes 1671176 | tf_op jit(solution)/shard_map/ppermute | solution.py:113
  24.8 2.5 collective-permute-start.3
  28.4 5.4 %collective-permute-done.1 = bf16[128,2176]{0,1:T(8,128)(2,1)S(1)} collective-permute-done((bf16[128,2176]{0,1:T(8,128)(2,1)S(1)}, bf16[128,2176]{0,1:T(8,128)(2,1)S(1)}, u32[]{:S(2)}, u32[]{:S(2)}) %collective-permute-start.1) | collective-permute-done | bytes 557088 | tf_op jit(solution)/shard_map/ppermute | solution.py:113
  35.4 2.5 collective-permute-start.6
  39.7 10.4 %collective-permute-done.3 = bf16[128,2176]{0,1:T(8,128)(2,1)S(1)} collective-permute-done((bf16[128,2176]{0,1:T(8,128)(2,1)S(1)}, bf16[128,2176]{0,1:T(8,128)(2,1)S(1)}, u32[]{:S(2)}, u32[]{:S(2)}) %collective-permute-start.3) | collective-permute-done | bytes 557088 | tf_op jit(solution)/shard_map/ppermute | solution.py:38
  50.3 2.5 collective-permute-done.4
  52.9 9.2 %collective-permute-done.5 = bf16[128,2176]{0,1:T(8,128)(2,1)S(1)} collective-permute-done((bf16[128,2176]{0,1:T(8,128)(2,1)S(1)}, bf16[128,2176]{0,1:T(8,128)(2,1)S(1)}, u32[]{:S(2)}, u32[]{:S(2)}) %collective-permute-start.5) | collective-permute-done | bytes 557088 | tf_op jit(solution)/shard_map/ppermute | solution.py:38
  62.2 11.8 %collective-permute-done.6 = bf16[128,2176]{0,1:T(8,128)(2,1)S(1)} collective-permute-done((bf16[128,2176]{0,1:T(8,128)(2,1)S(1)}, bf16[128,2176]{0,1:T(8,128)(2,1)S(1)}, u32[]{:S(2)}, u32[]{:S(2)}) %collective-permute-start.6) | collective-permute-done | bytes 557088 | tf_op jit(solution)/shard_map/ppermute | solution.py:38
  77.8 6.3 %fusion.56 = (f32[8,2,128]{2,1,0:T(2,128)}, f32[8,2,128,1152]{2,3,1,0:T(8,128)}) fusion(pred[128,1152]{0,1:T(8,128)(4,1)S(1)} %fusion.44, bf16[1152,8,128,1]{0,2,3,1:T(8,128)(2,1)S(1)} %bitcast.126, bf16[128,8,2,128]{0,3,2,1:T(8,128)(2,1)S(1)} %bitcast.140), kind=kOutput, calls=%fused_computation.133 | convolution fusion | flops 613418112 | bytes 12476416 | tf_op jit(solution)/shard_map/sub | solution.py:75
  84.1 4.8 %fusion.8 = bf16[8,2,128,1152]{2,3,1,0:T(8,128)(2,1)S(1)} fusion(f32[8,2,128,1152]{2,3,1,0:T(8,128)} %get-tuple-element.67, f32[8,2,128]{2,1,0:T(2,128)} %get-tuple-element.66), kind=kLoop, calls=%fused_computation.16 | loop fusion | flops 4718592 | bytes 14163968 | tf_op jit(solution)/shard_map/convert_element_type | solution.py:77
  91.7 5.3 %fusion.3 = bf16[8,2,128,1152]{2,3,1,0:T(8,128)(2,1)S(1)} fusion(bf16[1152,8,128,1]{0,2,3,1:T(8,128)(2,1)S(1)} %bitcast.129, bf16[128,8,2,128]{0,3,2,1:T(8,128)(2,1)S(1)} %bitcast.132, f32[8,2,128]{2,1,0:T(2,128)S(1)} %bitcast.146, f32[8,2,128,1152]{2,3,1,0:T(8,128)} %get-tuple-element.67, f32[8,2,128]{2,1,0:T(2,128)S(1)} %copy-done.18), kind=kOutput, calls=%fused_computation.7 | convolution fusion | flops 613416960 | bytes 17055744 | tf_op jit(solution)/shard_map/tgrd,egd->grte/dot_general | solution.py:82
  99.2 2.9 fusion.1
  102.8 2.1 fusion.54
  105.0 3.5 collective-permute-start.8
  109.1 2.2 collective-permute-start.13
  112.7 28.9 %collective-permute-done.8 = bf16[128,2048]{0,1:T(8,128)(2,1)S(1)} collective-permute-done((bf16[128,2048]{0,1:T(8,128)(2,1)S(1)}, bf16[128,2048]{0,1:T(8,128)(2,1)S(1)}, u32[]{:S(2)}, u32[]{:S(2)}) %collective-permute-start.8) | collective-permute-done | bytes 524320 | tf_op jit(solution)/shard_map/ppermute | solution.py:38
  141.6 3.6 collective-permute-start.11
  148.9 7.6 %collective-permute-done.12 = bf16[128,2048]{0,1:T(8,128)(2,1)S(1)} collective-permute-done((bf16[128,2048]{0,1:T(8,128)(2,1)S(1)}, bf16[128,2048]{0,1:T(8,128)(2,1)S(1)}, u32[]{:S(2)}, u32[]{:S(2)}) %collective-permute-start.12) | collective-permute-done | bytes 524320 | tf_op jit(solution)/shard_map/ppermute | solution.py:38
  156.5 5.1 %collective-permute-done.14 = bf16[128,2048]{0,1:T(8,128)(2,1)S(1)} collective-permute-done((bf16[128,2048]{0,1:T(8,128)(2,1)S(1)}, bf16[128,2048]{0,1:T(8,128)(2,1)S(1)}, u32[]{:S(2)}, u32[]{:S(2)}) %collective-permute-start.14) | collective-permute-done | bytes 524320 | tf_op jit(solution)/shard_map/ppermute | solution.py:113
  161.6 2.2 add_convert_fusion
  167.6 10.9 %collective-permute-done.15 = bf16[128,2048]{0,1:T(8,128)(2,1)} collective-permute-done((bf16[128,2048]{0,1:T(8,128)(2,1)}, bf16[128,2048]{0,1:T(8,128)(2,1)}, u32[]{:S(2)}, u32[]{:S(2)}) %collective-permute-start.15) | collective-permute-done | bytes 524320 | tf_op jit(solution)/shard_map/ppermute | solution.py:113
  178.5 2.1 fusion.27
  184.3 12.3 %collective-permute-done.18 = bf16[128,2560]{0,1:T(8,128)(2,1)S(1)} collective-permute-done((bf16[128,2560]{0,1:T(8,128)(2,1)}, bf16[128,2560]{0,1:T(8,128)(2,1)S(1)}, u32[]{:S(2)}, u32[]{:S(2)}) %collective-permute-start.18) | collective-permute-done | bytes 655392 | tf_op jit(solution)/shard_map/ppermute | solution.py:38
  196.6 2.1 collective-permute-done.17
  198.7 17.0 %collective-permute-done.16 = bf16[128,2560]{0,1:T(8,128)(2,1)S(1)} collective-permute-done((bf16[128,2560]{0,1:T(8,128)(2,1)}, bf16[128,2560]{0,1:T(8,128)(2,1)S(1)}, u32[]{:S(2)}, u32[]{:S(2)}) %collective-permute-start.16) | collective-permute-done | bytes 655392 | tf_op jit(solution)/shard_map/ppermute | solution.py:38
  215.8 2.8 fusion.10
  218.7 2.7 copy-done.7
  222.2 3.0 collective-permute-done.19
  225.2 2.4 bitcast_add_fusion
  230.2 2.7 collective-permute-start.22
  234.0 15.7 %collective-permute-done.22 = bf16[8,24,1024]{2,1,0:T(8,128)(2,1)} collective-permute-done((bf16[8,24,1024]{2,1,0:T(8,128)(2,1)}, bf16[8,24,1024]{2,1,0:T(8,128)(2,1)}, u32[]{:S(2)}, u32[]{:S(2)}) %collective-permute-start.22) | collective-permute-done | bytes 393248 | tf_op jit(solution)/shard_map/ppermute | solution.py:38
  249.6 4.4 %collective-permute-done.20 = bf16[8,24,1024]{2,1,0:T(8,128)(2,1)} collective-permute-done((bf16[8,24,1024]{2,1,0:T(8,128)(2,1)S(1)}, bf16[8,24,1024]{2,1,0:T(8,128)(2,1)}, u32[]{:S(2)}, u32[]{:S(2)}) %collective-permute-start.20) | collective-permute-done | bytes 393248 | tf_op jit(solution)/shard_map/ppermute | solution.py:38
  258.3 2.2 collective-permute-start.23
  260.4 3.4 fusion.19
  267.7 7.7 %collective-permute-start.27 = (f32[24,1024]{1,0:T(8,128)}, f32[24,1024]{1,0:T(8,128)S(1)}, u32[]{:S(2)}, u32[]{:S(2)}) collective-permute-start(f32[24,1024]{1,0:T(8,128)} %get-tuple-element.55), channel_id=1, source_target_pairs={{0,160},{32,192},{64,224},{96,0},{128,32},{160,64},{192,96},{224,1... | collective-permute-start | bytes 294920 | tf_op jit(solution)/shard_map/ppermute | solution.py:38
  275.4 1.9 collective-permute-start.25
  277.3 2.3 collective-permute-start.24
  280.6 1.9 collective-permute-done.27
  282.5 2.7 collective-permute-done.26
  285.2 5.4 %collective-permute-done.25 = f32[24,1024]{1,0:T(8,128)S(1)} collective-permute-done((f32[24,1024]{1,0:T(8,128)}, f32[24,1024]{1,0:T(8,128)S(1)}, u32[]{:S(2)}, u32[]{:S(2)}) %collective-permute-start.25) | collective-permute-done | bytes 98336 | tf_op jit(solution)/shard_map/ppermute | solution.py:38
  292.1 64.8 %psum.7 = f32[]{:T(128)} all-reduce(f32[]{:T(128)} %get-tuple-element.32), channel_id=1, replica_groups=mesh['cz'=8,'cx'=4,'y'=4,'core'=2] {'cx','y','core'}, use_global_device_ids=true, to_apply=%region_4.5 | all-reduce | flops 1 | bytes 8 | tf_op jit(solution)/shard_map/psum | solution.py:242
  357.0 2.8 collective-permute-start.30
  361.9 2.1 collective-permute-start.31
  363.9 2.5 collective-permute-done.31
  367.0 5.4 %collective-permute-start.32 = (f32[]{:T(128)}, f32[]{:T(128)}, u32[]{:S(2)}, u32[]{:S(2)}) collective-permute-start(f32[]{:T(128)} %add.454), channel_id=1, source_target_pairs={{0,128},{32,160},{64,192},{96,224},{128,0},{160,32},{192,64},{224,... | collective-permute-start | bytes 20 | tf_op jit(solution)/shard_map/ppermute | solution.py:38
  375.7 17.3 %all-gather = bf16[8,21,1024]{2,1,0:T(8,128)(2,1)S(1)} all-gather(bf16[1,21,1024]{2,1,0:T(8,128)(2,1)S(1)} %get-tuple-element.28), channel_id=1, replica_groups=mesh['cz'=8,'cx'=4,'y'=4,'core'=2] {'y','core'}, dimensions={0}, use_global_device_ids=true | all-gather | bytes 387072 | tf_op jit(solution)/shard_map/all_gather | solution.py:250
  (128 shorter events, 54.2 us)
Async XLA Ops:
  1.3 2.3 copy-start.19
  3.6 15.7 %collective-permute-start = (bf16[128,2176]{0,1:T(8,128)(2,1)S(1)}, bf16[128,2176]{0,1:T(8,128)(2,1)S(1)}, u32[]{:S(2)}, u32[]{:S(2)}) collective-permute-start(bf16[128,2176]{0,1:T(8,128)(2,1)S(1)} %pad_maximum_fusion.4), channel_id=1, source_target_pairs={{0,32},{32,64},{64,96},{96,128},{128,160},{160,192},{192,224},{1,3... | collective-permute-start | bytes 1671176 | tf_op jit(solution)/shard_map/ppermute | solution.py:113
  10.8 67.0 %copy-start.9 = (bf16[1,128,2048]{1,2,0:T(8,128)(2,1)}, bf16[1,128,2048]{1,2,0:T(8,128)(2,1)S(1)}, u32[]{:S(2)}) copy-start(bf16[1,128,2048]{1,2,0:T(8,128)(2,1)S(1)} %copy.85) | copy-start | bytes 1572868
  19.3 14.5 %collective-permute-start.1 = (bf16[128,2176]{0,1:T(8,128)(2,1)S(1)}, bf16[128,2176]{0,1:T(8,128)(2,1)S(1)}, u32[]{:S(2)}, u32[]{:S(2)}) collective-permute-start(bf16[128,2176]{0,1:T(8,128)(2,1)S(1)} %collective-permute-done), channel_id=1, source_target_pairs={{0,32},{32,64},{64,96},{96,128},{128,160},{160,192},{192,224},{1,3... | collective-permute-start | bytes 1671176 | tf_op jit(solution)/shard_map/ppermute | solution.py:113
  23.5 38.7 %copy-start.16 = (s32[1152]{0:T(1024)}, s32[1152]{0:T(1024)S(1)}, u32[]{:S(2)}) copy-start(s32[1152]{0:T(1024)S(1)} %get-tuple-element.68) | copy-start | bytes 13828
  23.5 14.7 %collective-permute-start.2 = (bf16[128,2176]{0,1:T(8,128)(2,1)S(1)}, bf16[128,2176]{0,1:T(8,128)(2,1)S(1)}, u32[]{:S(2)}, u32[]{:S(2)}) collective-permute-start(bf16[128,2176]{0,1:T(8,128)(2,1)S(1)} %collective-permute-done), channel_id=1, source_target_pairs={{0,8},{8,16},{16,24},{24,0},{1,9},{9,17},{17,25},{25,1},{2,10},{10... | collective-permute-start | bytes 1671176 | tf_op jit(solution)/shard_map/ppermute | solution.py:38
  24.8 25.3 %collective-permute-start.3 = (bf16[128,2176]{0,1:T(8,128)(2,1)S(1)}, bf16[128,2176]{0,1:T(8,128)(2,1)S(1)}, u32[]{:S(2)}, u32[]{:S(2)}) collective-permute-start(bf16[128,2176]{0,1:T(8,128)(2,1)S(1)} %collective-permute-done), channel_id=1, source_target_pairs={{0,16},{8,24},{16,0},{24,8},{1,17},{9,25},{17,1},{25,9},{2,18},{10... | collective-permute-start | bytes 1671176 | tf_op jit(solution)/shard_map/ppermute | solution.py:38
  27.2 25.5 %collective-permute-start.4 = (bf16[128,2176]{0,1:T(8,128)(2,1)S(1)}, bf16[128,2176]{0,1:T(8,128)(2,1)S(1)}, u32[]{:S(2)}, u32[]{:S(2)}) collective-permute-start(bf16[128,2176]{0,1:T(8,128)(2,1)S(1)} %collective-permute-done), channel_id=1, source_target_pairs={{0,24},{8,0},{16,8},{24,16},{1,25},{9,1},{17,9},{25,17},{2,26},{10... | collective-permute-start | bytes 1671176 | tf_op jit(solution)/shard_map/ppermute | solution.py:38
  34.2 27.9 %collective-permute-start.5 = (bf16[128,2176]{0,1:T(8,128)(2,1)S(1)}, bf16[128,2176]{0,1:T(8,128)(2,1)S(1)}, u32[]{:S(2)}, u32[]{:S(2)}) collective-permute-start(bf16[128,2176]{0,1:T(8,128)(2,1)S(1)} %get-tuple-element.51), channel_id=1, source_target_pairs={{0,8},{8,16},{16,24},{24,0},{1,9},{9,17},{17,25},{25,1},{2,10},{10... | collective-permute-start | bytes 1671176 | tf_op jit(solution)/shard_map/ppermute | solution.py:38
  35.4 38.5 %collective-permute-start.6 = (bf16[128,2176]{0,1:T(8,128)(2,1)S(1)}, bf16[128,2176]{0,1:T(8,128)(2,1)S(1)}, u32[]{:S(2)}, u32[]{:S(2)}) collective-permute-start(bf16[128,2176]{0,1:T(8,128)(2,1)S(1)} %get-tuple-element.50), channel_id=1, source_target_pairs={{0,16},{8,24},{16,0},{24,8},{1,17},{9,25},{17,1},{25,9},{2,18},{10... | collective-permute-start | bytes 1671176 | tf_op jit(solution)/shard_map/ppermute | solution.py:38
  38.2 36.5 %collective-permute-start.7 = (bf16[128,2176]{0,1:T(8,128)(2,1)S(1)}, bf16[128,2176]{0,1:T(8,128)(2,1)S(1)}, u32[]{:S(2)}, u32[]{:S(2)}) collective-permute-start(bf16[128,2176]{0,1:T(8,128)(2,1)S(1)} %get-tuple-element.49), channel_id=1, source_target_pairs={{0,24},{8,0},{16,8},{24,16},{1,25},{9,1},{17,9},{25,17},{2,26},{10... | collective-permute-start | bytes 1671176 | tf_op jit(solution)/shard_map/ppermute | solution.py:38
  74.8 1.8 copy-start.17
  76.6 7.4 %copy-start.3 = (bf16[1152,1024]{0,1:T(8,128)(2,1)}, bf16[1152,1024]{0,1:T(8,128)(2,1)S(1)}, u32[]{:S(2)}) copy-start(bf16[1152,1024]{0,1:T(8,128)(2,1)S(1)} %get-tuple-element.35) | copy-start | bytes 7077892
  90.4 8.7 %copy-start = (f32[8,1152,128,1]{1,2,3,0:T(8,128)}, f32[8,1152,128,1]{1,2,3,0:T(8,128)S(1)}, u32[]{:S(2)}) copy-start(f32[8,1152,128,1]{1,2,3,0:T(8,128)S(1)} %fusion.57) | copy-start | bytes 14155780
  91.7 5.3 %copy-start.10 = (bf16[1,128,2048]{1,2,0:T(8,128)(2,1)S(1)}, bf16[1,128,2048]{1,2,0:T(8,128)(2,1)}, u32[]{:S(2)}) copy-start(bf16[1,128,2048]{1,2,0:T(8,128)(2,1)} %copy-done.9) | copy-start | bytes 1572868
  96.9 2.2 copy-start.2
  99.2 3.7 copy-start.1
  105.0 60.1 %copy-start.13 = (bf16[1,128,5376]{2,1,0:T(8,128)(2,1)S(1)}, bf16[1,128,5376]{2,1,0:T(8,128)(2,1)}, u32[]{:S(2)}) copy-start(bf16[1,128,5376]{2,1,0:T(8,128)(2,1)} %param.9) | copy-start | bytes 4128772
  105.0 36.6 %collective-permute-start.8 = (bf16[128,2048]{0,1:T(8,128)(2,1)S(1)}, bf16[128,2048]{0,1:T(8,128)(2,1)S(1)}, u32[]{:S(2)}, u32[]{:S(2)}) collective-permute-start(bf16[128,2048]{0,1:T(8,128)(2,1)S(1)} %get-tuple-element.41), channel_id=1, source_target_pairs={{0,24},{8,0},{16,8},{24,16},{1,25},{9,1},{17,9},{25,17},{2,26},{10... | collective-permute-start | bytes 1572872 | tf_op jit(solution)/shard_map/ppermute | solution.py:38
  108.5 36.7 %collective-permute-start.9 = (bf16[128,2048]{0,1:T(8,128)(2,1)S(1)}, bf16[128,2048]{0,1:T(8,128)(2,1)S(1)}, u32[]{:S(2)}, u32[]{:S(2)}) collective-permute-start(bf16[128,2048]{0,1:T(8,128)(2,1)S(1)} %get-tuple-element.40), channel_id=1, source_target_pairs={{0,16},{8,24},{16,0},{24,8},{1,17},{9,25},{17,1},{25,9},{2,18},{10... | collective-permute-start | bytes 1572872 | tf_op jit(solution)/shard_map/ppermute | solution.py:38
  108.7 36.5 %collective-permute-start.10 = (bf16[128,2048]{0,1:T(8,128)(2,1)S(1)}, bf16[128,2048]{0,1:T(8,128)(2,1)S(1)}, u32[]{:S(2)}, u32[]{:S(2)}) collective-permute-start(bf16[128,2048]{0,1:T(8,128)(2,1)S(1)} %get-tuple-element.39), channel_id=1, source_target_pairs={{0,8},{8,16},{16,24},{24,0},{1,9},{9,17},{17,25},{25,1},{2,10},{10... | collective-permute-start | bytes 1572872 | tf_op jit(solution)/shard_map/ppermute | solution.py:38
  109.1 39.7 %collective-permute-start.13 = (bf16[128,2048]{0,1:T(8,128)(2,1)S(1)}, bf16[128,2048]{0,1:T(8,128)(2,1)S(1)}, u32[]{:S(2)}, u32[]{:S(2)}) collective-permute-start(bf16[128,2048]{0,1:T(8,128)(2,1)S(1)} %get-tuple-element.37), channel_id=1, source_target_pairs={{0,8},{8,16},{16,24},{24,0},{1,9},{9,17},{17,25},{25,1},{2,10},{10... | collective-permute-start | bytes 1572872 | tf_op jit(solution)/shard_map/ppermute | solution.py:38
  111.3 45.2 %collective-permute-start.12 = (bf16[128,2048]{0,1:T(8,128)(2,1)S(1)}, bf16[128,2048]{0,1:T(8,128)(2,1)S(1)}, u32[]{:S(2)}, u32[]{:S(2)}) collective-permute-start(bf16[128,2048]{0,1:T(8,128)(2,1)S(1)} %get-tuple-element.38), channel_id=1, source_target_pairs={{0,16},{8,24},{16,0},{24,8},{1,17},{9,25},{17,1},{25,9},{2,18},{10... | collective-permute-start | bytes 1572872 | tf_op jit(solution)/shard_map/ppermute | solution.py:38
  141.6 14.9 %collective-permute-start.11 = (bf16[128,2048]{0,1:T(8,128)(2,1)S(1)}, bf16[128,2048]{0,1:T(8,128)(2,1)S(1)}, u32[]{:S(2)}, u32[]{:S(2)}) collective-permute-start(bf16[128,2048]{0,1:T(8,128)(2,1)S(1)} %get-tuple-element.36), channel_id=1, source_target_pairs={{0,24},{8,0},{16,8},{24,16},{1,25},{9,1},{17,9},{25,17},{2,26},{10... | collective-permute-start | bytes 1572872 | tf_op jit(solution)/shard_map/ppermute | solution.py:38
  147.6 14.0 %collective-permute-start.14 = (bf16[128,2048]{0,1:T(8,128)(2,1)S(1)}, bf16[128,2048]{0,1:T(8,128)(2,1)S(1)}, u32[]{:S(2)}, u32[]{:S(2)}) collective-permute-start(bf16[128,2048]{0,1:T(8,128)(2,1)S(1)} %fusion.31), channel_id=1, source_target_pairs={{32,0},{64,32},{96,64},{128,96},{160,128},{192,160},{224,192},{33,... | collective-permute-start | bytes 1572872 | tf_op jit(solution)/shard_map/ppermute | solution.py:113
  163.8 14.7 %collective-permute-start.15 = (bf16[128,2048]{0,1:T(8,128)(2,1)}, bf16[128,2048]{0,1:T(8,128)(2,1)}, u32[]{:S(2)}, u32[]{:S(2)}) collective-permute-start(bf16[128,2048]{0,1:T(8,128)(2,1)} %add_convert_fusion), channel_id=1, source_target_pairs={{32,0},{64,32},{96,64},{128,96},{160,128},{192,160},{224,192},{33,... | collective-permute-start | bytes 1572872 | tf_op jit(solution)/shard_map/ppermute | solution.py:113
  182.8 13.7 %collective-permute-start.18 = (bf16[128,2560]{0,1:T(8,128)(2,1)}, bf16[128,2560]{0,1:T(8,128)(2,1)S(1)}, u32[]{:S(2)}, u32[]{:S(2)}) collective-permute-start(bf16[128,2560]{0,1:T(8,128)(2,1)} %get-tuple-element.64), channel_id=1, source_target_pairs={{0,24},{8,0},{16,8},{24,16},{1,25},{9,1},{17,9},{25,17},{2,26},{10... | collective-permute-start | bytes 1966088 | tf_op jit(solution)/shard_map/ppermute | solution.py:38
  183.4 15.3 %collective-permute-start.17 = (bf16[128,2560]{0,1:T(8,128)(2,1)}, bf16[128,2560]{0,1:T(8,128)(2,1)S(1)}, u32[]{:S(2)}, u32[]{:S(2)}) collective-permute-start(bf16[128,2560]{0,1:T(8,128)(2,1)} %get-tuple-element.65), channel_id=1, source_target_pairs={{0,16},{8,24},{16,0},{24,8},{1,17},{9,25},{17,1},{25,9},{2,18},{10... | collective-permute-start | bytes 1966088 | tf_op jit(solution)/shard_map/ppermute | solution.py:38
  183.4 32.4 %collective-permute-start.16 = (bf16[128,2560]{0,1:T(8,128)(2,1)}, bf16[128,2560]{0,1:T(8,128)(2,1)S(1)}, u32[]{:S(2)}, u32[]{:S(2)}) collective-permute-start(bf16[128,2560]{0,1:T(8,128)(2,1)} %get-tuple-element.63), channel_id=1, source_target_pairs={{0,8},{8,16},{16,24},{24,0},{1,9},{9,17},{17,25},{25,1},{2,10},{10... | collective-permute-start | bytes 1966088 | tf_op jit(solution)/shard_map/ppermute | solution.py:38
  218.7 2.7 copy-start.7
  221.6 3.6 collective-permute-start.19
  229.3 31.1 %copy-start.4 = (bf16[1152,1024]{0,1:T(8,128)(2,1)S(1)}, bf16[1152,1024]{0,1:T(8,128)(2,1)}, u32[]{:S(2)}) copy-start(bf16[1152,1024]{0,1:T(8,128)(2,1)} %copy-done.3) | copy-start | bytes 7077892
  230.2 19.4 %collective-permute-start.22 = (bf16[8,24,1024]{2,1,0:T(8,128)(2,1)}, bf16[8,24,1024]{2,1,0:T(8,128)(2,1)}, u32[]{:S(2)}, u32[]{:S(2)}) collective-permute-start(bf16[8,24,1024]{2,1,0:T(8,128)(2,1)} %get-tuple-element.43), channel_id=1, source_target_pairs={{0,6},{2,0},{4,2},{6,4},{1,7},{3,1},{5,3},{7,5},{8,14},{10,8},{12,... | collective-permute-start | bytes 1179656 | tf_op jit(solution)/shard_map/ppermute | solution.py:38
  232.9 16.7 %collective-permute-start.21 = (bf16[8,24,1024]{2,1,0:T(8,128)(2,1)S(1)}, bf16[8,24,1024]{2,1,0:T(8,128)(2,1)}, u32[]{:S(2)}, u32[]{:S(2)}) collective-permute-start(bf16[8,24,1024]{2,1,0:T(8,128)(2,1)S(1)} %get-tuple-element.44), channel_id=1, source_target_pairs={{0,4},{2,6},{4,0},{6,2},{1,5},{3,7},{5,1},{7,3},{8,12},{10,14},{12... | collective-permute-start | bytes 1179656 | tf_op jit(solution)/shard_map/ppermute | solution.py:38
  233.3 20.7 %collective-permute-start.20 = (bf16[8,24,1024]{2,1,0:T(8,128)(2,1)S(1)}, bf16[8,24,1024]{2,1,0:T(8,128)(2,1)}, u32[]{:S(2)}, u32[]{:S(2)}) collective-permute-start(bf16[8,24,1024]{2,1,0:T(8,128)(2,1)S(1)} %get-tuple-element.42), channel_id=1, source_target_pairs={{0,2},{2,4},{4,6},{6,0},{1,3},{3,5},{5,7},{7,1},{8,10},{10,12},{12... | collective-permute-start | bytes 1179656 | tf_op jit(solution)/shard_map/ppermute | solution.py:38
  255.7 2.5 copy-start.8
  256.7 18.7 %collective-permute-start.29 = (f32[24,1024]{1,0:T(8,128)}, f32[24,1024]{1,0:T(8,128)}, u32[]{:S(2)}, u32[]{:S(2)}) collective-permute-start(f32[24,1024]{1,0:T(8,128)} %get-tuple-element.53), channel_id=1, source_target_pairs={{0,224},{32,0},{64,32},{96,64},{128,96},{160,128},{192,160},{224,1... | collective-permute-start | bytes 294920 | tf_op jit(solution)/shard_map/ppermute | solution.py:38
  258.3 6.5 %copy-start.14 = (bf16[1,128,1024]{1,2,0:T(8,128)(2,1)S(1)}, bf16[1,128,1024]{1,2,0:T(8,128)(2,1)}, u32[]{:S(2)}) copy-start(bf16[1,128,1024]{1,2,0:T(8,128)(2,1)} %get-tuple-element.62) | copy-start | bytes 786436
  258.3 115.7 %copy-start.15 = (f32[21,1024]{1,0:T(8,128)S(1)}, f32[21,1024]{1,0:T(8,128)}, u32[]{:S(2)}) copy-start(f32[21,1024]{1,0:T(8,128)} %param.15) | copy-start | bytes 258052
  258.3 19.0 %collective-permute-start.23 = (f32[24,1024]{1,0:T(8,128)}, f32[24,1024]{1,0:T(8,128)}, u32[]{:S(2)}, u32[]{:S(2)}) collective-permute-start(f32[24,1024]{1,0:T(8,128)} %get-tuple-element.52), channel_id=1, source_target_pairs={{0,32},{32,64},{64,96},{96,128},{128,160},{160,192},{192,224},{224... | collective-permute-start | bytes 294920 | tf_op jit(solution)/shard_map/ppermute | solution.py:38
  266.5 14.1 %collective-permute-start.28 = (f32[24,1024]{1,0:T(8,128)}, f32[24,1024]{1,0:T(8,128)S(1)}, u32[]{:S(2)}, u32[]{:S(2)}) collective-permute-start(f32[24,1024]{1,0:T(8,128)} %get-tuple-element.54), channel_id=1, source_target_pairs={{0,192},{32,224},{64,0},{96,32},{128,64},{160,96},{192,128},{224,1... | collective-permute-start | bytes 294920 | tf_op jit(solution)/shard_map/ppermute | solution.py:38
  267.7 14.8 %collective-permute-start.27 = (f32[24,1024]{1,0:T(8,128)}, f32[24,1024]{1,0:T(8,128)S(1)}, u32[]{:S(2)}, u32[]{:S(2)}) collective-permute-start(f32[24,1024]{1,0:T(8,128)} %get-tuple-element.55), channel_id=1, source_target_pairs={{0,160},{32,192},{64,224},{96,0},{128,32},{160,64},{192,96},{224,1... | collective-permute-start | bytes 294920 | tf_op jit(solution)/shard_map/ppermute | solution.py:38
  275.4 9.8 %collective-permute-start.26 = (f32[24,1024]{1,0:T(8,128)}, f32[24,1024]{1,0:T(8,128)S(1)}, u32[]{:S(2)}, u32[]{:S(2)}) collective-permute-start(f32[24,1024]{1,0:T(8,128)} %get-tuple-element.56), channel_id=1, source_target_pairs={{0,128},{32,160},{64,192},{96,224},{128,0},{160,32},{192,64},{224,... | collective-permute-start | bytes 294920 | tf_op jit(solution)/shard_map/ppermute | solution.py:38
  275.4 15.2 %collective-permute-start.25 = (f32[24,1024]{1,0:T(8,128)}, f32[24,1024]{1,0:T(8,128)S(1)}, u32[]{:S(2)}, u32[]{:S(2)}) collective-permute-start(f32[24,1024]{1,0:T(8,128)} %get-tuple-element.57), channel_id=1, source_target_pairs={{0,96},{32,128},{64,160},{96,192},{128,224},{160,0},{192,32},{224,... | collective-permute-start | bytes 294920 | tf_op jit(solution)/shard_map/ppermute | solution.py:38
  277.3 13.3 %collective-permute-start.24 = (f32[24,1024]{1,0:T(8,128)}, f32[24,1024]{1,0:T(8,128)S(1)}, u32[]{:S(2)}, u32[]{:S(2)}) collective-permute-start(f32[24,1024]{1,0:T(8,128)} %get-tuple-element.58), channel_id=1, source_target_pairs={{0,64},{32,96},{64,128},{96,160},{128,192},{160,224},{192,0},{224,... | collective-permute-start | bytes 294920 | tf_op jit(solution)/shard_map/ppermute | solution.py:38
  357.0 3.7 collective-permute-start.30
  361.9 4.6 %collective-permute-start.31 = (f32[]{:T(128)}, f32[]{:T(128)}, u32[]{:S(2)}, u32[]{:S(2)}) collective-permute-start(f32[]{:T(128)} %add.453), channel_id=1, source_target_pairs={{0,64},{32,96},{64,128},{96,160},{128,192},{160,224},{192,0},{224,... | collective-permute-start | bytes 20 | tf_op jit(solution)/shard_map/ppermute | solution.py:38
  367.0 6.4 %collective-permute-start.32 = (f32[]{:T(128)}, f32[]{:T(128)}, u32[]{:S(2)}, u32[]{:S(2)}) collective-permute-start(f32[]{:T(128)} %add.454), channel_id=1, source_target_pairs={{0,128},{32,160},{64,192},{96,224},{128,0},{160,32},{192,64},{224,... | collective-permute-start | bytes 20 | tf_op jit(solution)/shard_map/ppermute | solution.py:38
  (6 other events, 8.6 us)
